TPU v7x, 256 devices: a whole 4x4x8 slice. The times are simulated.
256 devices in a mesh: gx: 16 (over z, y_lo), gy: 16 (over x, y_hi, core).
Axes of the slice: x: 4, y: 4 (y_hi: 2, y_lo: 2; y = y_hi * 2 + y_lo), z: 8, core: 2. Of those that a mesh axis runs over, the one named last changes fastest.
Arguments:
- stored_slab: bfloat16 [2, 32, 128, 2048], P(None, None, 'gx', 'gy'), may hold values from -6 to 6
- block_scales: bfloat16 [2, 32, 16, 16], P(None, None, 'gx', 'gy'), may hold values from 0.5 to 2
- holder: int32 [16], replicated, may hold values from 0 to 15, each once
- soil_class: int32 [128, 2048], P('gx', 'gy'), may hold values from 0 to 11
- soil_table: float32 [12, 4], replicated, may hold values from 0.01 to 0.05
- cotangent: float32 [2, 32, 128, 2048], P(None, None, 'gx', 'gy'), may hold values from -6 to 6
Outputs:
- recomputed: float32 [2, 32, 128, 2048], P(None, None, 'gx', 'gy')
- sensitivity: float32 [2, 32, 128, 2048], P(None, None, 'gx', 'gy')
Inputs may be any that keep to these rules, and one draw needn't show every extreme that they name: holder is a permutation: every gy index holds exactly one checkpoint block.
All inputs are finite; a program needn't handle non-finite values.
Results may differ from a plain program's by a relative error of at most 0.0003.
Values may be sent and summed in bfloat16 or wider, within the bound.
No kernel may reach another device: no remote copies, remote signals or barrier semaphores. Data moves between devices by JAX's collectives and lax.ppermute only.
A program may use at most 128 MiB of HBM per device.

v0:
```python
import jax
import jax.numpy as jnp
from jax import lax
from jax.experimental import pallas as pl
from jax.experimental.pallas import tpu as pltpu
from jax.sharding import PartitionSpec as P

F32 = jnp.float32
NCOEF = 4
VMEM = pltpu.MemorySpace.VMEM
SMEM = pltpu.MemorySpace.SMEM


def _roll(v, shift, axis):
    shift = shift % v.shape[axis]
    if shift == 0:
        return v
    return pltpu.roll(v, shift, axis)


def _iotas(shape):
    return lax.broadcasted_iota(jnp.int32, shape, 0), lax.broadcasted_iota(jnp.int32, shape, 1)


def _pack_edges(vals, xf_ref, xl_ref, yf_ref, yl_ref):
    x, y = vals[0].shape
    _, lane = _iotas((x, y))
    xf_ref[...] = jnp.zeros(xf_ref.shape, F32)
    xl_ref[...] = jnp.zeros(xl_ref.shape, F32)
    yf = jnp.zeros((x, y), F32)
    yl = jnp.zeros((x, y), F32)
    for k, v in enumerate(vals):
        xf_ref[k : k + 1, :] = v[0:1, :]
        xl_ref[k : k + 1, :] = v[x - 1 : x, :]
        yf = jnp.where(lane == k, _roll(v, k, 1), yf)
        yl = jnp.where(lane == k, _roll(v, k - (y - 1), 1), yl)
    yf_ref[...] = yf
    yl_ref[...] = yl


def _expand_halo(xm_ref, xp_ref, ym_ref, yp_ref, first, nf, nz, dst):
    hxm, hxp, hym, hyp = dst
    x, y = hxm.shape[2], hxm.shape[3]
    ymv = ym_ref[...]
    ypv = yp_ref[...]
    for f in range(nf):
        for z in range(nz):
            k = first + f * nz + z
            hxm[f, z] = jnp.broadcast_to(xm_ref[k : k + 1, :], (x, y))
            hxp[f, z] = jnp.broadcast_to(xp_ref[k : k + 1, :], (x, y))
            hym[f, z] = _roll(ymv, -k, 1)
            hyp[f, z] = _roll(ypv, (y - 1) - k, 1)


def _coef_table(c_ref, cxm_ref, cxp_ref, cym_ref, cyp_ref, first, cs):
    x, y = c_ref.shape[1], c_ref.shape[2]
    ymv = cym_ref[...]
    ypv = cyp_ref[...]
    masks = _iotas((x, y))
    for k in range(NCOEF):
        r = first + k
        cv = c_ref[k]
        cs[k] = cv
        halo = (
            jnp.broadcast_to(cxm_ref[r : r + 1, :], (x, y)),
            jnp.broadcast_to(cxp_ref[r : r + 1, :], (x, y)),
            _roll(ymv, -r, 1),
            _roll(ypv, (y - 1) - r, 1),
        )
        for d, v in enumerate(_neighbours(cv, 0, [h[None] for h in halo], masks)):
            cs[4 + 4 * d + k] = v


def _neighbours(v, z, h, masks):
    row, lane = masks
    x, y = v.shape
    hxm, hxp, hym, hyp = h
    return (
        jnp.where(row == 0, hxm[z], _roll(v, 1, 0)),
        jnp.where(row == x - 1, hxp[z], _roll(v, x - 1, 0)),
        jnp.where(lane == 0, hym[z], _roll(v, 1, 1)),
        jnp.where(lane == y - 1, hyp[z], _roll(v, y - 1, 1)),
    )


def _field_at(ref, f, z, nz):
    zm = jnp.maximum(z - 1, 0)
    zp = jnp.minimum(z + 1, nz - 1)
    vm = jnp.where(z > 0, 1.0, 0.0).astype(F32)
    vp = jnp.where(z < nz - 1, 1.0, 0.0).astype(F32)
    return ref[f, z], ref[f, zm] * vm, ref[f, zp] * vp, vm, vp


def _gains(b):
    return 1.5 + b, 1.5 + 0.5 * b


def _step_body(s_ref, sh, cs, o_ref, nz, masks):
    def body(z, carry):
        u, u_m, u_p, vm, vp = _field_at(s_ref, 0, z, nz)
        t, t_m, t_p, _, _ = _field_at(s_ref, 1, z, nz)
        c = [cs[k] for k in range(NCOEF)]
        g1, g2 = _gains(jnp.tanh(u))
        kw, dtv, lamb, kv = c[0] * g1, c[1] * g2, c[2] * g2, c[3] * g1
        a1 = jnp.zeros_like(u)
        a2 = jnp.zeros_like(u)
        for un, tn, valid in ((u_m, t_m, vm), (u_p, t_p, vp)):
            g1n, g2n = _gains(jnp.tanh(un))
            a1 = a1 + (g1 + valid * g1n) * (un - u)
            a2 = a2 + (g2 + valid * g2n) * (tn - t)
        f0 = c[0] * a1 + c[1] * a2
        f1 = c[2] * a2 + c[3] * a1
        uns = _neighbours(u, z, sh[0], masks)
        tns = _neighbours(t, z, sh[1], masks)
        for d in range(4):
            un, tn = uns[d], tns[d]
            g1n, g2n = _gains(jnp.tanh(un))
            cn = [cs[4 + 4 * d + k] for k in range(NCOEF)]
            du = un - u
            dt = tn - t
            f0 = f0 + (kw + cn[0] * g1n) * du + (dtv + cn[1] * g2n) * dt
            f1 = f1 + (lamb + cn[2] * g2n) * dt + (kv + cn[3] * g1n) * du
        o_ref[0, z] = u + 0.5 * f0
        o_ref[1, z] = t + 0.5 * f1
        return carry

    lax.fori_loop(0, nz, body, 0)


def _adjoint_body(s_ref, sh, a_ref, ah, cs, o_ref, nz, masks):
    def body(z, carry):
        u, u_m, u_p, vm, vp = _field_at(s_ref, 0, z, nz)
        t, t_m, t_p, _, _ = _field_at(s_ref, 1, z, nz)
        a0, a0_m, a0_p, _, _ = _field_at(a_ref, 0, z, nz)
        a1, a1_m, a1_p, _, _ = _field_at(a_ref, 1, z, nz)
        c = [cs[k] for k in range(NCOEF)]
        b = jnp.tanh(u)
        g1, g2 = _gains(b)
        kw, dtv, lamb, kv = c[0] * g1, c[1] * g2, c[2] * g2, c[3] * g1
        zero = jnp.zeros_like(u)
        p10, p11, p20, p21 = zero, zero, zero, zero
        gu0, gu1, gt0, gt1 = zero, zero, zero, zero
        for un, tn, a0n, a1n, valid in ((u_m, t_m, a0_m, a1_m, vm), (u_p, t_p, a0_p, a1_p, vp)):
            g1n, g2n = _gains(jnp.tanh(un))
            s1 = g1 + valid * g1n
            s2 = g2 + valid * g2n
            du, dt, da0, da1 = un - u, tn - t, a0n - a0, a1n - a1
            p10 = p10 + s1 * da0
            p11 = p11 + s1 * da1
            p20 = p20 + s2 * da0
            p21 = p21 + s2 * da1
            gu0 = gu0 + du * da0
            gu1 = gu1 + du * da1
            gt0 = gt0 + dt * da0
            gt1 = gt1 + dt * da1
        ju = c[0] * p10 + c[3] * p11
        jt = c[1] * p20 + c[2] * p21
        uns = _neighbours(u, z, sh[0], masks)
        tns = _neighbours(t, z, sh[1], masks)
        a0ns = _neighbours(a0, z, ah[0], masks)
        a1ns = _neighbours(a1, z, ah[1], masks)
        for d in range(4):
            un, tn, a0n, a1n = uns[d], tns[d], a0ns[d], a1ns[d]
            g1n, g2n = _gains(jnp.tanh(un))
            cn = [cs[4 + 4 * d + k] for k in range(NCOEF)]
            du, dt, da0, da1 = un - u, tn - t, a0n - a0, a1n - a1
            ju = ju + (kw + cn[0] * g1n) * da0 + (kv + cn[3] * g1n) * da1
            jt = jt + (dtv + cn[1] * g2n) * da0 + (lamb + cn[2] * g2n) * da1
            gu0 = gu0 + du * da0
            gu1 = gu1 + du * da1
            gt0 = gt0 + dt * da0
            gt1 = gt1 + dt * da1
        gsum = c[0] * gu0 + c[3] * gu1 + 0.5 * (c[1] * gt0 + c[2] * gt1)
        o_ref[0, z] = a0 + 0.5 * ju - 0.5 * (1.0 - b * b) * gsum
        o_ref[1, z] = a1 + 0.5 * jt
        return carry

    lax.fori_loop(0, nz, body, 0)


def _halo_scratch(nf, nz, x, y):
    return [pltpu.VMEM((nf, nz, x, y), F32) for _ in range(4)]


def _edge_shapes(rows, x, y):
    return (
        jax.ShapeDtypeStruct((rows, y), F32),
        jax.ShapeDtypeStruct((rows, y), F32),
        jax.ShapeDtypeStruct((x, y), F32),
        jax.ShapeDtypeStruct((x, y), F32),
    )


def _rows(n):
    return -(-n // 8) * 8


def prep_call(soil_class, soil_table, cot):
    nf, nz, x, y = cot.shape
    nclass = soil_table.shape[0]

    def kernel(cls_ref, tab_ref, cot_ref, coef_ref, xf_ref, xl_ref, yf_ref, yl_ref):
        cls = cls_ref[...]
        coefs = []
        for k in range(NCOEF):
            cv = jnp.zeros(cls.shape, F32)
            for j in range(nclass):
                cv = jnp.where(cls == j, tab_ref[j, k], cv)
            coef_ref[k] = cv
            coefs.append(cv)
        vals = [cot_ref[f, z] for f in range(nf) for z in range(nz)] + coefs
        _pack_edges(vals, xf_ref, xl_ref, yf_ref, yl_ref)

    rows = _rows(nf * nz + NCOEF)
    return pl.pallas_call(
        kernel,
        out_shape=(jax.ShapeDtypeStruct((NCOEF, x, y), F32),) + _edge_shapes(rows, x, y),
        in_specs=[
            pl.BlockSpec(memory_space=VMEM),
            pl.BlockSpec(memory_space=SMEM),
            pl.BlockSpec(memory_space=VMEM),
        ],
    )(soil_class, soil_table, cot)


def state0_call(gathered, scales, index):
    _, nf, planes, x, y = gathered.shape
    nz = planes - 1

    def kernel(idx_ref, sc_ref, own_ref, left_ref, right_ref, s_ref, xf_ref, xl_ref, ym_ref, yp_ref):
        hown, hl, hr = idx_ref[0], idx_ref[1], idx_ref[2]
        has_l = jnp.where(idx_ref[3] > 0, 1.0, 0.0).astype(F32)
        has_r = jnp.where(idx_ref[4] > 0, 1.0, 0.0).astype(F32)
        _, lane = _iotas((x, y))
        vals = []
        ym = jnp.zeros((x, y), F32)
        yp = jnp.zeros((x, y), F32)
        for f in range(nf):
            for z in range(nz):
                k = f * nz + z
                v = own_ref[f, z].astype(F32) * sc_ref[hown * (nf * nz) + k]
                s_ref[f, z] = v
                vals.append(v)
                lv = left_ref[f, z].astype(F32) * (sc_ref[hl * (nf * nz) + k] * has_l)
                rv = right_ref[f, z].astype(F32) * (sc_ref[hr * (nf * nz) + k] * has_r)
                ym = jnp.where(lane == k, _roll(lv, k - (y - 1), 1), ym)
                yp = jnp.where(lane == k, _roll(rv, k, 1), yp)
        ym_ref[...] = ym
        yp_ref[...] = yp
        xf_ref[...] = jnp.zeros(xf_ref.shape, F32)
        xl_ref[...] = jnp.zeros(xl_ref.shape, F32)
        for k, v in enumerate(vals):
            xf_ref[k : k + 1, :] = v[0:1, :]
            xl_ref[k : k + 1, :] = v[x - 1 : x, :]

    block = (None, nf, planes, x, y)
    rows = _rows(nf * nz)
    grid_spec = pltpu.PrefetchScalarGridSpec(
        num_scalar_prefetch=2,
        grid=(1,),
        in_specs=[
            pl.BlockSpec(block, lambda i, idx, sc: (idx[0], 0, 0, 0, 0)),
            pl.BlockSpec(block, lambda i, idx, sc: (idx[1], 0, 0, 0, 0)),
            pl.BlockSpec(block, lambda i, idx, sc: (idx[2], 0, 0, 0, 0)),
        ],
        out_specs=[
            pl.BlockSpec((nf, nz, x, y), lambda i, idx, sc: (0, 0, 0, 0)),
            pl.BlockSpec((rows, y), lambda i, idx, sc: (0, 0)),
            pl.BlockSpec((rows, y), lambda i, idx, sc: (0, 0)),
            pl.BlockSpec((x, y), lambda i, idx, sc: (0, 0)),
            pl.BlockSpec((x, y), lambda i, idx, sc: (0, 0)),
        ],
    )
    return pl.pallas_call(
        kernel,
        grid_spec=grid_spec,
        out_shape=(jax.ShapeDtypeStruct((nf, nz, x, y), F32),) + _edge_shapes(rows, x, y),
    )(index, scales, gathered, gathered, gathered)


def step_call(s, s_halo, coef, c_halo, c_first, with_edges):
    nf, nz, x, y = s.shape

    def kernel(*refs):
        s_ref, sxm, sxp, sym, syp, c_ref, cxm, cxp, cym, cyp = refs[:10]
        rest = refs[10:]
        if with_edges:
            o_ref, xf_ref, xl_ref, yf_ref, yl_ref = rest[:5]
            scratch = rest[5:]
        else:
            o_ref = rest[0]
            scratch = rest[1:]
        sh_all = scratch[0:4]
        cs = scratch[4]
        _expand_halo(sxm, sxp, sym, syp, 0, nf, nz, sh_all)
        _coef_table(c_ref, cxm, cxp, cym, cyp, c_first, cs)
        masks = _iotas((x, y))
        sh = [tuple(h.at[f] for h in sh_all) for f in range(nf)]
        _step_body(s_ref, sh, cs, o_ref, nz, masks)
        if with_edges:
            vals = [o_ref[f, z] for f in range(nf) for z in range(nz)]
            _pack_edges(vals, xf_ref, xl_ref, yf_ref, yl_ref)

    out_shape = (jax.ShapeDtypeStruct(s.shape, F32),)
    if with_edges:
        out_shape = out_shape + _edge_shapes(_rows(nf * nz), x, y)
    res = pl.pallas_call(
        kernel,
        out_shape=out_shape,
        scratch_shapes=_halo_scratch(nf, nz, x, y) + [pltpu.VMEM((5 * NCOEF, x, y), F32)],
    )(s, *s_halo, coef, *c_halo)
    return res if with_edges else res[0]


def adjoint_call(s, s_halo, a, a_halo, a_first, coef, c_halo, c_first, with_edges):
    nf, nz, x, y = s.shape

    def kernel(*refs):
        s_ref, sxm, sxp, sym, syp, a_ref, axm, axp, aym, ayp, c_ref, cxm, cxp, cym, cyp = refs[:15]
        rest = refs[15:]
        if with_edges:
            o_ref, xf_ref, xl_ref, yf_ref, yl_ref = rest[:5]
            scratch = rest[5:]
        else:
            o_ref = rest[0]
            scratch = rest[1:]
        sh_all = scratch[0:4]
        ah_all = scratch[4:8]
        cs = scratch[8]
        _expand_halo(sxm, sxp, sym, syp, 0, nf, nz, sh_all)
        _expand_halo(axm, axp, aym, ayp, a_first, nf, nz, ah_all)
        _coef_table(c_ref, cxm, cxp, cym, cyp, c_first, cs)
        masks = _iotas((x, y))
        sh = [tuple(h.at[f] for h in sh_all) for f in range(nf)]
        ah = [tuple(h.at[f] for h in ah_all) for f in range(nf)]
        _adjoint_body(s_ref, sh, a_ref, ah, cs, o_ref, nz, masks)
        if with_edges:
            vals = [o_ref[f, z] for f in range(nf) for z in range(nz)]
            _pack_edges(vals, xf_ref, xl_ref, yf_ref, yl_ref)

    out_shape = (jax.ShapeDtypeStruct(s.shape, F32),)
    if with_edges:
        out_shape = out_shape + _edge_shapes(_rows(nf * nz), x, y)
    res = pl.pallas_call(
        kernel,
        out_shape=out_shape,
        scratch_shapes=_halo_scratch(nf, nz, x, y)
        + _halo_scratch(nf, nz, x, y)
        + [pltpu.VMEM((5 * NCOEF, x, y), F32)],
    )(s, *s_halo, a, *a_halo, coef, *c_halo)
    return res if with_edges else res[0]


def _shift(v, axis, step):
    n = lax.axis_size(axis)
    if step > 0:
        pairs = [(i, i + 1) for i in range(n - 1)]
    else:
        pairs = [(i + 1, i) for i in range(n - 1)]
    return lax.ppermute(v, axis, pairs)


def exchange(xf, xl, yf, yl):
    return (
        _shift(xl, "gx", 1),
        _shift(xf, "gx", -1),
        _shift(yl, "gy", 1),
        _shift(yf, "gy", -1),
    )


def on_device(stored_slab, block_scales, holder, soil_class, soil_table, cotangent):
    nf, nz, x, y = stored_slab.shape
    ngy = lax.axis_size("gy")
    gy = lax.axis_index("gy")

    planes = jnp.pad(
        block_scales.reshape(nf, 1, 1, nz), ((0, 0), (0, 0), (0, x - 1), (0, y - nz))
    )
    packed = jnp.concatenate([stored_slab, planes], axis=1)
    gathered = lax.all_gather(packed, "gy", axis=0)

    coef, cxf, cxl, cyf, cyl = prep_call(soil_class, soil_table, cotangent)
    c_halo = exchange(cxf, cxl, cyf, cyl)
    c_first = nf * nz

    index = jnp.stack(
        [
            holder[gy],
            holder[jnp.maximum(gy - 1, 0)],
            holder[jnp.minimum(gy + 1, ngy - 1)],
            (gy > 0).astype(jnp.int32),
            (gy < ngy - 1).astype(jnp.int32),
        ]
    )
    scales = gathered[:, :, nz, 0, :nz].astype(F32).reshape(-1)
    s0, s0xf, s0xl, s0ym, s0yp = state0_call(gathered, scales, index)
    s0_halo = (_shift(s0xl, "gx", 1), _shift(s0xf, "gx", -1), s0ym, s0yp)

    s1, *s1_edges = step_call(s0, s0_halo, coef, c_halo, c_first, True)
    s1_halo = exchange(*s1_edges)

    a1, *a1_edges = adjoint_call(
        s1, s1_halo, cotangent, c_halo, 0, coef, c_halo, c_first, True
    )
    a1_halo = exchange(*a1_edges)
    s2 = step_call(s1, s1_halo, coef, c_halo, c_first, False)

    sens = adjoint_call(s0, s0_halo, a1, a1_halo, 0, coef, c_halo, c_first, False)
    return (s2, sens)


def solution(mesh):
    placed = (
        P(None, None, "gx", "gy"),
        P(None, None, "gx", "gy"),
        P(),
        P("gx", "gy"),
        P(),
        P(None, None, "gx", "gy"),
    )
    return jax.shard_map(
        on_device,
        mesh=mesh,
        in_specs=placed,
        out_specs=(P(None, None, "gx", "gy"), P(None, None, "gx", "gy")),
        check_vma=False,
    )
```

profile of v0, /device:TPU:130, one launch (start us, length us, event | category | flops | bytes accessed | tf_op | source)
XLA Modules:
  0.0 151.4 jit_solution(12356102141273229927)
XLA Ops:
  7.2 0.0 all-gather.3.cloned.1.call-start
  7.2 0.7 copy.12
  7.9 1.6 %fusion.1 = bf16[2,33,8,128]{3,2,1,0:T(8,128)(2,1)} fusion(bf16[2,1,1,32]{3,2,1,0:T(2,128)(2,1)S(1)} %copy.12, bf16[2,32,8,128]{3,2,1,0:T(8,128)(2,1)} %param.6), kind=kLoop, calls=%fused_computation.2 | loop fusion | flops 405504 | bytes 266368 | tf_op jit(solution)/shard_map/concatenate | solution.py:380
  9.4 0.0 all-gather.3.cloned.1.call-update
  9.5 1.4 copy.11.tab_ref
  10.8 1.8 %shard_map.78 = (f32[4,8,128]{2,1,0:T(8,128)}, f32[72,128]{1,0:T(8,128)}, f32[72,128]{1,0:T(8,128)}, f32[8,128]{1,0:T(8,128)}, f32[8,128]{1,0:T(8,128)}) custom-call(s32[8,128]{1,0:T(8,128)} %cls_ref.1, f32[12,4]{1,0:T(8,128)} %copy.11.tab_ref, f32[2,32,8,128]{3,2,1,0:T(8,128)} %refs_5_.1), custom_call_target="tpu_custom_call" | custom-call | tf_op jit(solution)/shard_map/pallas_call | solution.py:215
  12.6 3.5 %collective-permute-start.2 = (f32[72,128]{1,0:T(8,128)}, f32[72,128]{1,0:T(8,128)S(1)}, u32[]{:S(2)}, u32[]{:S(2)}) collective-permute-start(f32[72,128]{1,0:T(8,128)} %get-tuple-element.28), channel_id=1, source_target_pairs={{0,16},{16,32},{32,48},{48,64},{64,80},{80,96},{96,112},{112,128},... | collective-permute-start | bytes 110600 | tf_op jit(solution)/shard_map/ppermute | solution.py:360
  16.1 4.5 %collective-permute-start.3 = (f32[72,128]{1,0:T(8,128)}, f32[72,128]{1,0:T(8,128)S(1)}, u32[]{:S(2)}, u32[]{:S(2)}) collective-permute-start(f32[72,128]{1,0:T(8,128)} %get-tuple-element.29), channel_id=1, source_target_pairs={{16,0},{32,16},{48,32},{64,48},{80,64},{96,80},{112,96},{128,112},... | collective-permute-start | bytes 110600 | tf_op jit(solution)/shard_map/ppermute | solution.py:360
  20.6 1.4 fusion.3
  22.0 2.6 %stack.19.idx_ref = s32[5]{0:T(128)} concatenate(s32[1]{0:T(128)} %get-tuple-element.43, s32[1]{0:T(128)} %get-tuple-element.44, s32[1]{0:T(128)} %get-tuple-element.42, s32[1]{0:T(128)} %bitcast, s32[1]{0:T(128)} %bitcast.1), dimensions={0} | concatenate | bytes 40 | tf_op jit(solution)/shard_map/stack | solution.py:387
  24.6 41.7 %all-gather.3.cloned.1.call-done = bf16[32,33,8,128]{3,2,1,0:T(8,128)(2,1)} async-done(((bf16[2,33,8,128]{3,2,1,0:T(8,128)(2,1)}), bf16[32,33,8,128]{3,2,1,0:T(8,128)(2,1)}) %all-gather.3.cloned.1.call-update) | async-done | bytes 2162704 | tf_op jit(solution)/shard_map/all_gather | solution.py:381
  66.3 0.9 fusion.2
  67.2 0.7 reshape.14.sc_ref
  67.8 2.8 %shard_map.77 = (f32[2,32,8,128]{3,2,1,0:T(8,128)}, f32[64,128]{1,0:T(8,128)}, f32[64,128]{1,0:T(8,128)}, f32[8,128]{1,0:T(8,128)}, f32[8,128]{1,0:T(8,128)}) custom-call(s32[5]{0:T(128)} %stack.19.idx_ref, f32[1024]{0:T(1024)} %reshape.14.sc_ref, bf16[16,2,33,8,128]{4,3,2,1,0:T(8,128)(2,1)} %bitcast.5, bf16[16,2,33,8,128]{4,3,2,1,0:T(8,128)(2,1)} %bitcast.6, ...), custom_call_target="tpu_custom_call" | custom-call | tf_op jit(solution)/shard_map/pallas_call | solution.py:274
  70.7 2.5 %collective-permute-start = (f32[64,128]{1,0:T(8,128)}, f32[64,128]{1,0:T(8,128)S(1)}, u32[]{:S(2)}, u32[]{:S(2)}) collective-permute-start(f32[64,128]{1,0:T(8,128)} %get-tuple-element.23), channel_id=1, source_target_pairs={{0,16},{16,32},{32,48},{48,64},{64,80},{80,96},{96,112},{112,128},... | collective-permute-start | bytes 98312 | tf_op jit(solution)/shard_map/ppermute | solution.py:360
  73.1 5.5 %collective-permute-start.1 = (f32[64,128]{1,0:T(8,128)}, f32[64,128]{1,0:T(8,128)S(1)}, u32[]{:S(2)}, u32[]{:S(2)}) collective-permute-start(f32[64,128]{1,0:T(8,128)} %get-tuple-element.24), channel_id=1, source_target_pairs={{16,0},{32,16},{48,32},{64,48},{80,64},{96,80},{112,96},{128,112},... | collective-permute-start | bytes 98312 | tf_op jit(solution)/shard_map/ppermute | solution.py:360
  78.6 1.9 %collective-permute-start.4 = (f32[8,128]{1,0:T(8,128)S(1)}, f32[8,128]{1,0:T(8,128)S(1)}, u32[]{:S(2)}, u32[]{:S(2)}) collective-permute-start(f32[8,128]{1,0:T(8,128)S(1)} %copy-done.15), channel_id=1, source_target_pairs={{0,1},{1,2},{2,3},{3,4},{4,5},{5,6},{6,7},{7,8},{8,9},{9,10},{10,1... | collective-permute-start | bytes 12296 | tf_op jit(solution)/shard_map/ppermute | solution.py:360
  80.5 5.4 %collective-permute-done.4.refs_8_.refs_13_ = f32[8,128]{1,0:T(8,128)S(1)} collective-permute-done((f32[8,128]{1,0:T(8,128)S(1)}, f32[8,128]{1,0:T(8,128)S(1)}, u32[]{:S(2)}, u32[]{:S(2)}) %collective-permute-start.4) | collective-permute-done | bytes 4128 | tf_op jit(solution)/shard_map/ppermute | solution.py:360
  86.0 1.9 %collective-permute-start.5 = (f32[8,128]{1,0:T(8,128)S(1)}, f32[8,128]{1,0:T(8,128)S(1)}, u32[]{:S(2)}, u32[]{:S(2)}) collective-permute-start(f32[8,128]{1,0:T(8,128)S(1)} %copy-done.14), channel_id=1, source_target_pairs={{1,0},{2,1},{3,2},{4,3},{5,4},{6,5},{7,6},{8,7},{9,8},{10,9},{11,1... | collective-permute-start | bytes 12296 | tf_op jit(solution)/shard_map/ppermute | solution.py:360
  87.9 1.3 collective-permute-done.5.refs_9_.refs_14_
  89.2 0.0 collective-permute-done.2.refs_6_.refs_11_
  89.2 0.0 collective-permute-done.3.refs_7_.refs_12_
  89.2 0.0 collective-permute-done.1.refs_2_
  89.3 0.5 copy-done.7
  89.8 0.0 copy-done
  89.8 0.0 copy-done.1
  89.8 0.0 copy-done.4
  89.8 0.0 copy-done.5
  89.9 4.9 %shard_map.79 = (f32[2,32,8,128]{3,2,1,0:T(8,128)}, f32[64,128]{1,0:T(8,128)}, f32[64,128]{1,0:T(8,128)}, f32[8,128]{1,0:T(8,128)}, f32[8,128]{1,0:T(8,128)}) custom-call(f32[2,32,8,128]{3,2,1,0:T(8,128)} %get-tuple-element.22.refs_0_, f32[64,128]{1,0:T(8,128)} %copy-done.4, f32[64,128]{1,0:T(8,128)} %copy-done.5, f32[8,128]{1,0:T(8,128)} %get-tuple-element.25.refs_3_, ...), custom_call_target="tpu_custom_call" | custom-call | tf_op jit(solution)/shard_map/pallas_call | solution.py:307
  94.7 1.9 %collective-permute-start.6 = (f32[64,128]{1,0:T(8,128)}, f32[64,128]{1,0:T(8,128)S(1)}, u32[]{:S(2)}, u32[]{:S(2)}) collective-permute-start(f32[64,128]{1,0:T(8,128)} %get-tuple-element.33), channel_id=1, source_target_pairs={{0,16},{16,32},{32,48},{48,64},{64,80},{80,96},{96,112},{112,128},... | collective-permute-start | bytes 98312 | tf_op jit(solution)/shard_map/ppermute | solution.py:360
  96.7 6.0 %collective-permute-start.7 = (f32[64,128]{1,0:T(8,128)}, f32[64,128]{1,0:T(8,128)S(1)}, u32[]{:S(2)}, u32[]{:S(2)}) collective-permute-start(f32[64,128]{1,0:T(8,128)} %get-tuple-element.34), channel_id=1, source_target_pairs={{16,0},{32,16},{48,32},{64,48},{80,64},{96,80},{112,96},{128,112},... | collective-permute-start | bytes 98312 | tf_op jit(solution)/shard_map/ppermute | solution.py:360
  102.7 1.9 %collective-permute-start.8 = (f32[8,128]{1,0:T(8,128)}, f32[8,128]{1,0:T(8,128)S(1)}, u32[]{:S(2)}, u32[]{:S(2)}) collective-permute-start(f32[8,128]{1,0:T(8,128)} %get-tuple-element.35), channel_id=1, source_target_pairs={{0,1},{1,2},{2,3},{3,4},{4,5},{5,6},{6,7},{7,8},{8,9},{9,10},{10,1... | collective-permute-start | bytes 12296 | tf_op jit(solution)/shard_map/ppermute | solution.py:360
  104.6 6.0 %collective-permute-start.9 = (f32[8,128]{1,0:T(8,128)}, f32[8,128]{1,0:T(8,128)S(1)}, u32[]{:S(2)}, u32[]{:S(2)}) collective-permute-start(f32[8,128]{1,0:T(8,128)} %get-tuple-element.36), channel_id=1, source_target_pairs={{1,0},{2,1},{3,2},{4,3},{5,4},{6,5},{7,6},{8,7},{9,8},{10,9},{11,1... | collective-permute-start | bytes 12296 | tf_op jit(solution)/shard_map/ppermute | solution.py:360
  110.7 1.5 collective-permute-done.9.refs_4_
  112.2 0.6 copy-done.11
  112.8 0.0 copy-done.2
  112.8 0.0 copy-done.3
  112.8 5.2 %shard_map.81 = (f32[2,32,8,128]{3,2,1,0:T(8,128)}, f32[64,128]{1,0:T(8,128)}, f32[64,128]{1,0:T(8,128)}, f32[8,128]{1,0:T(8,128)}, f32[8,128]{1,0:T(8,128)}) custom-call(f32[2,32,8,128]{3,2,1,0:T(8,128)} %get-tuple-element.32.refs_0_, f32[64,128]{1,0:T(8,128)} %copy-done.2, f32[64,128]{1,0:T(8,128)} %copy-done.3, f32[8,128]{1,0:T(8,128)} %copy-done.10, ...), custom_call_target="tpu_custom_call" | custom-call | tf_op jit(solution)/shard_map/pallas_call | solution.py:344
  118.1 1.9 %collective-permute-start.10 = (f32[64,128]{1,0:T(8,128)}, f32[64,128]{1,0:T(8,128)S(1)}, u32[]{:S(2)}, u32[]{:S(2)}) collective-permute-start(f32[64,128]{1,0:T(8,128)} %get-tuple-element.38), channel_id=1, source_target_pairs={{0,16},{16,32},{32,48},{48,64},{64,80},{80,96},{96,112},{112,128},... | collective-permute-start | bytes 98312 | tf_op jit(solution)/shard_map/ppermute | solution.py:360
  120.0 6.0 %collective-permute-start.11 = (f32[64,128]{1,0:T(8,128)}, f32[64,128]{1,0:T(8,128)S(1)}, u32[]{:S(2)}, u32[]{:S(2)}) collective-permute-start(f32[64,128]{1,0:T(8,128)} %get-tuple-element.39), channel_id=1, source_target_pairs={{16,0},{32,16},{48,32},{64,48},{80,64},{96,80},{112,96},{128,112},... | collective-permute-start | bytes 98312 | tf_op jit(solution)/shard_map/ppermute | solution.py:360
  126.0 1.9 %collective-permute-start.12 = (f32[8,128]{1,0:T(8,128)}, f32[8,128]{1,0:T(8,128)S(1)}, u32[]{:S(2)}, u32[]{:S(2)}) collective-permute-start(f32[8,128]{1,0:T(8,128)} %get-tuple-element.40), channel_id=1, source_target_pairs={{0,1},{1,2},{2,3},{3,4},{4,5},{5,6},{6,7},{7,8},{8,9},{9,10},{10,1... | collective-permute-start | bytes 12296 | tf_op jit(solution)/shard_map/ppermute | solution.py:360
  127.9 6.0 %collective-permute-start.13 = (f32[8,128]{1,0:T(8,128)}, f32[8,128]{1,0:T(8,128)S(1)}, u32[]{:S(2)}, u32[]{:S(2)}) collective-permute-start(f32[8,128]{1,0:T(8,128)} %get-tuple-element.41), channel_id=1, source_target_pairs={{1,0},{2,1},{3,2},{4,3},{5,4},{6,5},{7,6},{8,7},{9,8},{10,9},{11,1... | collective-permute-start | bytes 12296 | tf_op jit(solution)/shard_map/ppermute | solution.py:360
  134.0 4.8 %shard_map.80 = f32[2,32,8,128]{3,2,1,0:T(8,128)} custom-call(f32[2,32,8,128]{3,2,1,0:T(8,128)} %get-tuple-element.32.refs_0_, f32[64,128]{1,0:T(8,128)} %copy-done.2, f32[64,128]{1,0:T(8,128)} %copy-done.3, f32[8,128]{1,0:T(8,128)} %copy-done.10, f32[8,128]{1,0:T(8,128)} %copy-done.11, f32[4,8,128]{2,1,0:T(8,128)} %get-tuple-element.27.refs_5_.refs_10_, ...), custom_call_target="tpu_custom_call" | custom-call | tf_op jit(solution)/shard_map/pallas_call | solution.py:307
  138.9 0.5 copy-done.12
  139.4 0.0 copy-done.13
  139.4 0.0 copy-done.8
  139.4 0.0 copy-done.9
  139.5 5.1 %shard_map.82 = f32[2,32,8,128]{3,2,1,0:T(8,128)} custom-call(f32[2,32,8,128]{3,2,1,0:T(8,128)} %get-tuple-element.22.refs_0_, f32[64,128]{1,0:T(8,128)} %copy-done.4, f32[64,128]{1,0:T(8,128)} %copy-done.5, f32[8,128]{1,0:T(8,128)} %get-tuple-element.25.refs_3_, f32[8,128]{1,0:T(8,128)} %get-tuple-element.26.refs_4_, ...), custom_call_target="tpu_custom_call" | custom-call | tf_op jit(solution)/shard_map/pallas_call | solution.py:344
  (28 shorter events, 0.1 us)
Async XLA Ops:
  7.2 59.1 %all-gather.3.cloned.1.call-start = ((), (), s32[]{:S(2)}) async-start(), calls=%async_computation | async-start | bytes 2297856 | tf_op jit(solution)/shard_map/all_gather | solution.py:381
  12.6 76.6 %collective-permute-start.2 = (f32[72,128]{1,0:T(8,128)}, f32[72,128]{1,0:T(8,128)S(1)}, u32[]{:S(2)}, u32[]{:S(2)}) collective-permute-start(f32[72,128]{1,0:T(8,128)} %get-tuple-element.28), channel_id=1, source_target_pairs={{0,16},{16,32},{32,48},{48,64},{64,80},{80,96},{96,112},{112,128},... | collective-permute-start | bytes 110600 | tf_op jit(solution)/shard_map/ppermute | solution.py:360
  16.1 73.1 %collective-permute-start.3 = (f32[72,128]{1,0:T(8,128)}, f32[72,128]{1,0:T(8,128)S(1)}, u32[]{:S(2)}, u32[]{:S(2)}) collective-permute-start(f32[72,128]{1,0:T(8,128)} %get-tuple-element.29), channel_id=1, source_target_pairs={{16,0},{32,16},{48,32},{64,48},{80,64},{96,80},{112,96},{128,112},... | collective-permute-start | bytes 110600 | tf_op jit(solution)/shard_map/ppermute | solution.py:360
  67.8 10.8 %copy-start.15 = (f32[8,128]{1,0:T(8,128)S(1)}, f32[8,128]{1,0:T(8,128)}, u32[]{:S(2)}) copy-start(f32[8,128]{1,0:T(8,128)} %get-tuple-element.30) | copy-start | bytes 12292
  67.8 18.1 %copy-start.14 = (f32[8,128]{1,0:T(8,128)S(1)}, f32[8,128]{1,0:T(8,128)}, u32[]{:S(2)}) copy-start(f32[8,128]{1,0:T(8,128)} %get-tuple-element.31) | copy-start | bytes 12292
  70.7 18.6 %collective-permute-start = (f32[64,128]{1,0:T(8,128)}, f32[64,128]{1,0:T(8,128)S(1)}, u32[]{:S(2)}, u32[]{:S(2)}) collective-permute-start(f32[64,128]{1,0:T(8,128)} %get-tuple-element.23), channel_id=1, source_target_pairs={{0,16},{16,32},{32,48},{48,64},{64,80},{80,96},{96,112},{112,128},... | collective-permute-start | bytes 98312 | tf_op jit(solution)/shard_map/ppermute | solution.py:360
  73.1 16.1 %collective-permute-start.1 = (f32[64,128]{1,0:T(8,128)}, f32[64,128]{1,0:T(8,128)S(1)}, u32[]{:S(2)}, u32[]{:S(2)}) collective-permute-start(f32[64,128]{1,0:T(8,128)} %get-tuple-element.24), channel_id=1, source_target_pairs={{16,0},{32,16},{48,32},{64,48},{80,64},{96,80},{112,96},{128,112},... | collective-permute-start | bytes 98312 | tf_op jit(solution)/shard_map/ppermute | solution.py:360
  78.6 7.3 %collective-permute-start.4 = (f32[8,128]{1,0:T(8,128)S(1)}, f32[8,128]{1,0:T(8,128)S(1)}, u32[]{:S(2)}, u32[]{:S(2)}) collective-permute-start(f32[8,128]{1,0:T(8,128)S(1)} %copy-done.15), channel_id=1, source_target_pairs={{0,1},{1,2},{2,3},{3,4},{4,5},{5,6},{6,7},{7,8},{8,9},{9,10},{10,1... | collective-permute-start | bytes 12296 | tf_op jit(solution)/shard_map/ppermute | solution.py:360
  86.0 3.3 %copy-start.6 = (f32[8,128]{1,0:T(8,128)}, f32[8,128]{1,0:T(8,128)S(1)}, u32[]{:S(2)}) copy-start(f32[8,128]{1,0:T(8,128)S(1)} %collective-permute-done.4.refs_8_.refs_13_) | copy-start | bytes 12292
  86.0 3.2 %collective-permute-start.5 = (f32[8,128]{1,0:T(8,128)S(1)}, f32[8,128]{1,0:T(8,128)S(1)}, u32[]{:S(2)}, u32[]{:S(2)}) collective-permute-start(f32[8,128]{1,0:T(8,128)S(1)} %copy-done.14), channel_id=1, source_target_pairs={{1,0},{2,1},{3,2},{4,3},{5,4},{6,5},{7,6},{8,7},{9,8},{10,9},{11,1... | collective-permute-start | bytes 12296 | tf_op jit(solution)/shard_map/ppermute | solution.py:360
  89.2 0.6 copy-start.7
  89.2 0.6 copy-start
  89.2 0.6 copy-start.1
  89.2 0.6 copy-start.4
  89.2 0.6 copy-start.5
  94.7 17.5 %collective-permute-start.6 = (f32[64,128]{1,0:T(8,128)}, f32[64,128]{1,0:T(8,128)S(1)}, u32[]{:S(2)}, u32[]{:S(2)}) collective-permute-start(f32[64,128]{1,0:T(8,128)} %get-tuple-element.33), channel_id=1, source_target_pairs={{0,16},{16,32},{32,48},{48,64},{64,80},{80,96},{96,112},{112,128},... | collective-permute-start | bytes 98312 | tf_op jit(solution)/shard_map/ppermute | solution.py:360
  96.7 15.5 %collective-permute-start.7 = (f32[64,128]{1,0:T(8,128)}, f32[64,128]{1,0:T(8,128)S(1)}, u32[]{:S(2)}, u32[]{:S(2)}) collective-permute-start(f32[64,128]{1,0:T(8,128)} %get-tuple-element.34), channel_id=1, source_target_pairs={{16,0},{32,16},{48,32},{64,48},{80,64},{96,80},{112,96},{128,112},... | collective-permute-start | bytes 98312 | tf_op jit(solution)/shard_map/ppermute | solution.py:360
  102.7 8.0 %collective-permute-start.8 = (f32[8,128]{1,0:T(8,128)}, f32[8,128]{1,0:T(8,128)S(1)}, u32[]{:S(2)}, u32[]{:S(2)}) collective-permute-start(f32[8,128]{1,0:T(8,128)} %get-tuple-element.35), channel_id=1, source_target_pairs={{0,1},{1,2},{2,3},{3,4},{4,5},{5,6},{6,7},{7,8},{8,9},{9,10},{10,1... | collective-permute-start | bytes 12296 | tf_op jit(solution)/shard_map/ppermute | solution.py:360
  104.6 7.6 %collective-permute-start.9 = (f32[8,128]{1,0:T(8,128)}, f32[8,128]{1,0:T(8,128)S(1)}, u32[]{:S(2)}, u32[]{:S(2)}) collective-permute-start(f32[8,128]{1,0:T(8,128)} %get-tuple-element.36), channel_id=1, source_target_pairs={{1,0},{2,1},{3,2},{4,3},{5,4},{6,5},{7,6},{8,7},{9,8},{10,9},{11,1... | collective-permute-start | bytes 12296 | tf_op jit(solution)/shard_map/ppermute | solution.py:360
  110.7 1.5 %copy-start.10 = (f32[8,128]{1,0:T(8,128)}, f32[8,128]{1,0:T(8,128)S(1)}, u32[]{:S(2)}) copy-start(f32[8,128]{1,0:T(8,128)S(1)} %collective-permute-done.8.refs_3_) | copy-start | bytes 12292
  112.2 0.6 copy-start.11
  112.2 0.6 copy-start.2
  112.2 0.6 copy-start.3
  118.1 20.8 %collective-permute-start.10 = (f32[64,128]{1,0:T(8,128)}, f32[64,128]{1,0:T(8,128)S(1)}, u32[]{:S(2)}, u32[]{:S(2)}) collective-permute-start(f32[64,128]{1,0:T(8,128)} %get-tuple-element.38), channel_id=1, source_target_pairs={{0,16},{16,32},{32,48},{48,64},{64,80},{80,96},{96,112},{112,128},... | collective-permute-start | bytes 98312 | tf_op jit(solution)/shard_map/ppermute | solution.py:360
  120.0 18.9 %collective-permute-start.11 = (f32[64,128]{1,0:T(8,128)}, f32[64,128]{1,0:T(8,128)S(1)}, u32[]{:S(2)}, u32[]{:S(2)}) collective-permute-start(f32[64,128]{1,0:T(8,128)} %get-tuple-element.39), channel_id=1, source_target_pairs={{16,0},{32,16},{48,32},{64,48},{80,64},{96,80},{112,96},{128,112},... | collective-permute-start | bytes 98312 | tf_op jit(solution)/shard_map/ppermute | solution.py:360
  126.0 12.8 %collective-permute-start.12 = (f32[8,128]{1,0:T(8,128)}, f32[8,128]{1,0:T(8,128)S(1)}, u32[]{:S(2)}, u32[]{:S(2)}) collective-permute-start(f32[8,128]{1,0:T(8,128)} %get-tuple-element.40), channel_id=1, source_target_pairs={{0,1},{1,2},{2,3},{3,4},{4,5},{5,6},{6,7},{7,8},{8,9},{9,10},{10,1... | collective-permute-start | bytes 12296 | tf_op jit(solution)/shard_map/ppermute | solution.py:360
  127.9 10.9 %collective-permute-start.13 = (f32[8,128]{1,0:T(8,128)}, f32[8,128]{1,0:T(8,128)S(1)}, u32[]{:S(2)}, u32[]{:S(2)}) collective-permute-start(f32[8,128]{1,0:T(8,128)} %get-tuple-element.41), channel_id=1, source_target_pairs={{1,0},{2,1},{3,2},{4,3},{5,4},{6,5},{7,6},{8,7},{9,8},{10,9},{11,1... | collective-permute-start | bytes 12296 | tf_op jit(solution)/shard_map/ppermute | solution.py:360
  138.8 0.6 copy-start.12
  138.8 0.6 copy-start.13
  138.8 0.6 copy-start.8
  138.9 0.6 copy-start.9
Sparse Core Ops, SparseCore 0:
  11.3 54.9 all-gather.2
where the time goes:
time: 152 us; the launch traced here: 151 us
  starting transfers between devices  51.6 us (34%)
  waiting for transfers between devices  49.9 us (33%)
  Pallas kernels  24.6 us (16%)
  between operations  14.3 us (9%)
  local copies, waits for them, and re-layouts  8.52 us (6%)
  other arithmetic  2.47 us (2%)
    ppermute x14, starting transfers between devices, _shift(): return lax.ppermute(v, axis, pairs)  51.5 us
    all_gather x1, waiting for transfers between devices, on_device(): gathered = lax.all_gather(packed, 'gy', axis=0)  41.7 us
    pallas_call x2, Pallas kernels, adjoint_call(): pl.pallas_call(kernel, out_shape=out_shape, scratch_shapes=_halo_scratch(...  10.3 us
    pallas_call x2, Pallas kernels, step_call(): pl.pallas_call(kernel, out_shape=out_shape, scratch_shapes=_halo_scratch(...  9.7 us
    ppermute x14, waiting for transfers between devices, _shift(): return lax.ppermute(v, axis, pairs)  8.23 us
    unnamed x34, local copies, waits for them, and re-layouts  3.84 us
  transfers between devices with their start and end apart: 15, of which 4 were waited for; matrix products, arithmetic and copies ran while one was open for 5% of the time, Pallas kernels for 6%

commit v1 on v0

--- a/solution.py
+++ b/solution.py
@@ -223,59 +223,27 @@
     )(soil_class, soil_table, cot)
 
 
-def state0_call(gathered, scales, index):
-    _, nf, planes, x, y = gathered.shape
-    nz = planes - 1
-
-    def kernel(idx_ref, sc_ref, own_ref, left_ref, right_ref, s_ref, xf_ref, xl_ref, ym_ref, yp_ref):
-        hown, hl, hr = idx_ref[0], idx_ref[1], idx_ref[2]
-        has_l = jnp.where(idx_ref[3] > 0, 1.0, 0.0).astype(F32)
-        has_r = jnp.where(idx_ref[4] > 0, 1.0, 0.0).astype(F32)
-        _, lane = _iotas((x, y))
+def state0_call(pieces, scales):
+    npiece, pp, x, y = pieces.shape
+    per = pp - 1
+    nplanes = npiece * per
+
+    def kernel(sc_ref, r_ref, s_ref, xf_ref, xl_ref, yf_ref, yl_ref):
+        nz = s_ref.shape[1]
         vals = []
-        ym = jnp.zeros((x, y), F32)
-        yp = jnp.zeros((x, y), F32)
-        for f in range(nf):
-            for z in range(nz):
-                k = f * nz + z
-                v = own_ref[f, z].astype(F32) * sc_ref[hown * (nf * nz) + k]
-                s_ref[f, z] = v
-                vals.append(v)
-                lv = left_ref[f, z].astype(F32) * (sc_ref[hl * (nf * nz) + k] * has_l)
-                rv = right_ref[f, z].astype(F32) * (sc_ref[hr * (nf * nz) + k] * has_r)
-                ym = jnp.where(lane == k, _roll(lv, k - (y - 1), 1), ym)
-                yp = jnp.where(lane == k, _roll(rv, k, 1), yp)
-        ym_ref[...] = ym
-        yp_ref[...] = yp
-        xf_ref[...] = jnp.zeros(xf_ref.shape, F32)
-        xl_ref[...] = jnp.zeros(xl_ref.shape, F32)
-        for k, v in enumerate(vals):
-            xf_ref[k : k + 1, :] = v[0:1, :]
-            xl_ref[k : k + 1, :] = v[x - 1 : x, :]
-
-    block = (None, nf, planes, x, y)
-    rows = _rows(nf * nz)
-    grid_spec = pltpu.PrefetchScalarGridSpec(
-        num_scalar_prefetch=2,
-        grid=(1,),
-        in_specs=[
-            pl.BlockSpec(block, lambda i, idx, sc: (idx[0], 0, 0, 0, 0)),
-            pl.BlockSpec(block, lambda i, idx, sc: (idx[1], 0, 0, 0, 0)),
-            pl.BlockSpec(block, lambda i, idx, sc: (idx[2], 0, 0, 0, 0)),
-        ],
-        out_specs=[
-            pl.BlockSpec((nf, nz, x, y), lambda i, idx, sc: (0, 0, 0, 0)),
-            pl.BlockSpec((rows, y), lambda i, idx, sc: (0, 0)),
-            pl.BlockSpec((rows, y), lambda i, idx, sc: (0, 0)),
-            pl.BlockSpec((x, y), lambda i, idx, sc: (0, 0)),
-            pl.BlockSpec((x, y), lambda i, idx, sc: (0, 0)),
-        ],
-    )
+        for k in range(nplanes):
+            v = r_ref[k // per, k % per].astype(F32) * sc_ref[k]
+            s_ref[k // nz, k % nz] = v
+            vals.append(v)
+        _pack_edges(vals, xf_ref, xl_ref, yf_ref, yl_ref)
+
+    nf = 2
+    nz = nplanes // nf
     return pl.pallas_call(
         kernel,
-        grid_spec=grid_spec,
-        out_shape=(jax.ShapeDtypeStruct((nf, nz, x, y), F32),) + _edge_shapes(rows, x, y),
-    )(index, scales, gathered, gathered, gathered)
+        out_shape=(jax.ShapeDtypeStruct((nf, nz, x, y), F32),) + _edge_shapes(_rows(nplanes), x, y),
+        in_specs=[pl.BlockSpec(memory_space=SMEM), pl.BlockSpec(memory_space=VMEM)],
+    )(scales, pieces)
 
 
 def step_call(s, s_halo, coef, c_halo, c_first, with_edges):
@@ -369,33 +337,30 @@
     )
 
 
+def route_blocks(stored_slab, block_scales, holder):
+    nf, nz, x, y = stored_slab.shape
+    n = lax.axis_size("gy")
+    per = nf * nz // n
+    slab = stored_slab.reshape(n, per, x, y)
+    sc = jnp.pad(block_scales.reshape(n, 1, 1, per), ((0, 0), (0, 0), (0, x - 1), (0, y - per)))
+    send = jnp.concatenate([slab, sc], axis=1)
+    held = lax.all_to_all(send, "gy", 0, 0, tiled=True)
+    forward = jnp.take(held, holder, axis=0)
+    return lax.all_to_all(forward, "gy", 0, 0, tiled=True)
+
+
 def on_device(stored_slab, block_scales, holder, soil_class, soil_table, cotangent):
     nf, nz, x, y = stored_slab.shape
-    ngy = lax.axis_size("gy")
-    gy = lax.axis_index("gy")
-
-    planes = jnp.pad(
-        block_scales.reshape(nf, 1, 1, nz), ((0, 0), (0, 0), (0, x - 1), (0, y - nz))
-    )
-    packed = jnp.concatenate([stored_slab, planes], axis=1)
-    gathered = lax.all_gather(packed, "gy", axis=0)
 
     coef, cxf, cxl, cyf, cyl = prep_call(soil_class, soil_table, cotangent)
     c_halo = exchange(cxf, cxl, cyf, cyl)
     c_first = nf * nz
 
-    index = jnp.stack(
-        [
-            holder[gy],
-            holder[jnp.maximum(gy - 1, 0)],
-            holder[jnp.minimum(gy + 1, ngy - 1)],
-            (gy > 0).astype(jnp.int32),
-            (gy < ngy - 1).astype(jnp.int32),
-        ]
-    )
-    scales = gathered[:, :, nz, 0, :nz].astype(F32).reshape(-1)
-    s0, s0xf, s0xl, s0ym, s0yp = state0_call(gathered, scales, index)
-    s0_halo = (_shift(s0xl, "gx", 1), _shift(s0xf, "gx", -1), s0ym, s0yp)
+    pieces = route_blocks(stored_slab, block_scales, holder)
+    per = pieces.shape[1] - 1
+    scales = pieces[:, per, 0, :per].astype(F32).reshape(-1)
+    s0, *s0_edges = state0_call(pieces, scales)
+    s0_halo = exchange(*s0_edges)
 
     s1, *s1_edges = step_call(s0, s0_halo, coef, c_halo, c_first, True)
     s1_halo = exchange(*s1_edges)

time: 152 us -> 121 us (0.80)
  waiting for transfers between devices: 49.9 us -> 15.6 us
  starting transfers between devices: 51.6 us -> 72.7 us
  between operations: 14.3 us -> 1.06 us
  local copies, waits for them, and re-layouts: 8.52 us -> 4.43 us
    all_gather x1 -> x0, waiting for transfers between devices: 41.7 us -> none  [on_device(): gathered = lax.all_gather(packed, 'gy', axis=0)]
    all_to_all x0 -> x2, starting transfers between devices: none -> 13.1 us  [the longest x1 7.61 us: route_blocks(): held = lax.all_to_all(send, 'gy', 0, 0, tiled=True)]
    ppermute x14 -> x16, starting transfers between devices: 51.5 us -> 59.6 us  [_shift(): return lax.ppermute(v, axis, pairs)]
    all_to_all x0 -> x2, waiting for transfers between devices: none -> 6.33 us  [the longest x1 6.32 us: route_blocks(): held = lax.all_to_all(send, 'gy', 0, 0, tiled=True)]
    another operation x1 -> x0, local copies, waits for them, and re-layouts: 2.55 us -> none  [on_device(): jnp.stack([holder[gy], holder[jnp.maximum(gy - 1, 0)], holder[jnp.minimum...]
    unnamed x34 -> x49, local copies, waits for them, and re-layouts: 3.84 us -> 2.49 us
    ppermute x14 -> x16, waiting for transfers between devices: 8.23 us -> 9.29 us  [_shift(): return lax.ppermute(v, axis, pairs)]
  transfers between devices with their start and end apart: 15 -> 18, of which waited for: 4 -> 5; matrix products, arithmetic and copies ran while one was open for 5% -> 1% of each run, Pallas kernels for 6% -> 7%
where the time goes in v1:
time: 121 us; the launch traced here: 120 us
  starting transfers between devices  72.7 us (60%)
  Pallas kernels  23.5 us (19%)
  waiting for transfers between devices  15.6 us (13%)
  local copies, waits for them, and re-layouts  4.43 us (4%)
  other arithmetic  2.39 us (2%)
    ppermute x16, starting transfers between devices, _shift(): return lax.ppermute(v, axis, pairs)  59.6 us
    pallas_call x2, Pallas kernels, adjoint_call(): pl.pallas_call(kernel, out_shape=out_shape, scratch_shapes=_halo_scratch(...  10.3 us
    pallas_call x2, Pallas kernels, step_call(): pl.pallas_call(kernel, out_shape=out_shape, scratch_shapes=_halo_scratch(...  9.7 us
    ppermute x16, waiting for transfers between devices, _shift(): return lax.ppermute(v, axis, pairs)  9.29 us
    all_to_all x1, starting transfers between devices, route_blocks(): held = lax.all_to_all(send, 'gy', 0, 0, tiled=True)  7.61 us
    all_to_all x1, waiting for transfers between devices, route_blocks(): held = lax.all_to_all(send, 'gy', 0, 0, tiled=True)  6.32 us
    all_to_all x1, starting transfers between devices, route_blocks(): return lax.all_to_all(forward, 'gy', 0, 0, tiled=True)  5.47 us
    unnamed x49, local copies, waits for them, and re-layouts  2.49 us
  transfers between devices with their start and end apart: 18, of which 5 were waited for; matrix products, arithmetic and copies ran while one was open for 1% of the time, Pallas kernels for 7%

profile of v1, /device:TPU:130, one launch (start us, length us, event | category | flops | bytes accessed | tf_op | source)
XLA Modules:
  0.0 119.8 jit_solution(8327777664175890577)
XLA Ops:
  0.6 0.7 reshape.31
  1.4 1.6 %fusion.1 = bf16[16,5,8,128]{3,2,1,0:T(8,128)(2,1)} fusion(bf16[16,1,1,4]{3,2,1,0:T(2,128)(2,1)S(1)} %reshape.31, bf16[16,4,8,128]{3,2,1,0:T(8,128)(2,1)} %bitcast.3), kind=kLoop, calls=%fused_computation.3 | loop fusion | flops 491520 | bytes 295040 | tf_op jit(solution)/shard_map/concatenate | solution.py:346
  3.0 7.6 %all-to-all-start = ((bf16[16,5,8,128]{3,2,1,0:T(8,128)(2,1)}), bf16[16,5,8,128]{3,2,1,0:T(8,128)(2,1)S(1)}, u32[]{:S(2)}, u32[]{:S(2)}) async-start(bf16[16,5,8,128]{3,2,1,0:T(8,128)(2,1)} %fusion.1), calls=%async_computation | async-start | bytes 327680 | tf_op jit(solution)/shard_map/all_to_all | solution.py:347
  10.6 6.3 %all-to-all-done = bf16[16,5,8,128]{3,2,1,0:T(8,128)(2,1)S(1)} async-done(((bf16[16,5,8,128]{3,2,1,0:T(8,128)(2,1)}), bf16[16,5,8,128]{3,2,1,0:T(8,128)(2,1)S(1)}, u32[]{:S(2)}, u32[]{:S(2)}) %all-to-all-start) | async-done | bytes 163872 | tf_op jit(solution)/shard_map/all_to_all | solution.py:347
  16.9 0.6 gather_fusion
  17.5 0.8 broadcast_select_fusion
  18.3 5.5 %all-to-all-start.1 = ((bf16[16,5,8,128]{3,2,1,0:T(8,128)(2,1)}), bf16[16,5,8,128]{3,2,1,0:T(8,128)(2,1)S(1)}, u32[]{:S(2)}, u32[]{:S(2)}) async-start(bf16[16,5,8,128]{3,2,1,0:T(8,128)(2,1)} %broadcast_select_fusion), calls=%async_computation.1 | async-start | bytes 327680 | tf_op jit(solution)/shard_map/all_to_all | solution.py:349
  23.8 0.7 copy.11.tab_ref
  24.4 1.8 %shard_map.78 = (f32[4,8,128]{2,1,0:T(8,128)}, f32[72,128]{1,0:T(8,128)}, f32[72,128]{1,0:T(8,128)}, f32[8,128]{1,0:T(8,128)}, f32[8,128]{1,0:T(8,128)}) custom-call(s32[8,128]{1,0:T(8,128)} %cls_ref.1, f32[12,4]{1,0:T(8,128)} %copy.11.tab_ref, f32[2,32,8,128]{3,2,1,0:T(8,128)} %refs_5_.1), custom_call_target="tpu_custom_call" | custom-call | tf_op jit(solution)/shard_map/pallas_call | solution.py:215
  26.2 2.6 %collective-permute-start.4 = (f32[72,128]{1,0:T(8,128)}, f32[72,128]{1,0:T(8,128)S(1)}, u32[]{:S(2)}, u32[]{:S(2)}) collective-permute-start(f32[72,128]{1,0:T(8,128)} %get-tuple-element.28), channel_id=1, source_target_pairs={{0,16},{16,32},{32,48},{48,64},{64,80},{80,96},{96,112},{112,128},... | collective-permute-start | bytes 110600 | tf_op jit(solution)/shard_map/ppermute | solution.py:328
  28.8 5.4 %collective-permute-start.5 = (f32[72,128]{1,0:T(8,128)}, f32[72,128]{1,0:T(8,128)S(1)}, u32[]{:S(2)}, u32[]{:S(2)}) collective-permute-start(f32[72,128]{1,0:T(8,128)} %get-tuple-element.29), channel_id=1, source_target_pairs={{16,0},{32,16},{48,32},{64,48},{80,64},{96,80},{112,96},{128,112},... | collective-permute-start | bytes 110600 | tf_op jit(solution)/shard_map/ppermute | solution.py:328
  34.2 0.0 all-to-all-done.1.r_ref
  34.2 0.0 copy-start.2
  34.2 0.6 reshape.21.sc_ref
  34.8 0.0 copy-done.2
  34.9 1.7 %shard_map.77 = (f32[2,32,8,128]{3,2,1,0:T(8,128)}, f32[64,128]{1,0:T(8,128)}, f32[64,128]{1,0:T(8,128)}, f32[8,128]{1,0:T(8,128)}, f32[8,128]{1,0:T(8,128)}) custom-call(f32[64]{0:T(128)} %reshape.21.sc_ref, bf16[16,5,8,128]{3,2,1,0:T(8,128)(2,1)} %copy-done.2), custom_call_target="tpu_custom_call" | custom-call | tf_op jit(solution)/shard_map/pallas_call | solution.py:242
  36.6 2.0 %collective-permute-start = (f32[64,128]{1,0:T(8,128)}, f32[64,128]{1,0:T(8,128)S(1)}, u32[]{:S(2)}, u32[]{:S(2)}) collective-permute-start(f32[64,128]{1,0:T(8,128)} %get-tuple-element.23), channel_id=1, source_target_pairs={{0,16},{16,32},{32,48},{48,64},{64,80},{80,96},{96,112},{112,128},... | collective-permute-start | bytes 98312 | tf_op jit(solution)/shard_map/ppermute | solution.py:328
  38.7 6.0 %collective-permute-start.1 = (f32[64,128]{1,0:T(8,128)}, f32[64,128]{1,0:T(8,128)S(1)}, u32[]{:S(2)}, u32[]{:S(2)}) collective-permute-start(f32[64,128]{1,0:T(8,128)} %get-tuple-element.24), channel_id=1, source_target_pairs={{16,0},{32,16},{48,32},{64,48},{80,64},{96,80},{112,96},{128,112},... | collective-permute-start | bytes 98312 | tf_op jit(solution)/shard_map/ppermute | solution.py:328
  44.7 1.9 %collective-permute-start.6 = (f32[8,128]{1,0:T(8,128)S(1)}, f32[8,128]{1,0:T(8,128)S(1)}, u32[]{:S(2)}, u32[]{:S(2)}) collective-permute-start(f32[8,128]{1,0:T(8,128)S(1)} %copy-done.20), channel_id=1, source_target_pairs={{0,1},{1,2},{2,3},{3,4},{4,5},{5,6},{6,7},{7,8},{8,9},{9,10},{10,1... | collective-permute-start | bytes 12296 | tf_op jit(solution)/shard_map/ppermute | solution.py:328
  46.6 5.4 %collective-permute-done.6.refs_8_.refs_13_ = f32[8,128]{1,0:T(8,128)S(1)} collective-permute-done((f32[8,128]{1,0:T(8,128)S(1)}, f32[8,128]{1,0:T(8,128)S(1)}, u32[]{:S(2)}, u32[]{:S(2)}) %collective-permute-start.6) | collective-permute-done | bytes 4128 | tf_op jit(solution)/shard_map/ppermute | solution.py:328
  52.0 1.9 %collective-permute-start.7 = (f32[8,128]{1,0:T(8,128)S(1)}, f32[8,128]{1,0:T(8,128)S(1)}, u32[]{:S(2)}, u32[]{:S(2)}) collective-permute-start(f32[8,128]{1,0:T(8,128)S(1)} %copy-done.19), channel_id=1, source_target_pairs={{1,0},{2,1},{3,2},{4,3},{5,4},{6,5},{7,6},{8,7},{9,8},{10,9},{11,1... | collective-permute-start | bytes 12296 | tf_op jit(solution)/shard_map/ppermute | solution.py:328
  54.0 1.3 %collective-permute-done.7.refs_9_.refs_14_ = f32[8,128]{1,0:T(8,128)S(1)} collective-permute-done((f32[8,128]{1,0:T(8,128)S(1)}, f32[8,128]{1,0:T(8,128)S(1)}, u32[]{:S(2)}, u32[]{:S(2)}) %collective-permute-start.7) | collective-permute-done | bytes 4128 | tf_op jit(solution)/shard_map/ppermute | solution.py:328
  55.3 4.1 %collective-permute-start.2 = (f32[8,128]{1,0:T(8,128)}, f32[8,128]{1,0:T(8,128)S(1)}, u32[]{:S(2)}, u32[]{:S(2)}) collective-permute-start(f32[8,128]{1,0:T(8,128)} %get-tuple-element.25), channel_id=1, source_target_pairs={{0,1},{1,2},{2,3},{3,4},{4,5},{5,6},{6,7},{7,8},{8,9},{9,10},{10,1... | collective-permute-start | bytes 12296 | tf_op jit(solution)/shard_map/ppermute | solution.py:328
  59.4 3.9 %collective-permute-start.3 = (f32[8,128]{1,0:T(8,128)S(1)}, f32[8,128]{1,0:T(8,128)S(1)}, u32[]{:S(2)}, u32[]{:S(2)}) collective-permute-start(f32[8,128]{1,0:T(8,128)S(1)} %copy-done.18), channel_id=1, source_target_pairs={{1,0},{2,1},{3,2},{4,3},{5,4},{6,5},{7,6},{8,7},{9,8},{10,9},{11,1... | collective-permute-start | bytes 12296 | tf_op jit(solution)/shard_map/ppermute | solution.py:328
  63.3 1.3 %collective-permute-done.3.refs_4_ = f32[8,128]{1,0:T(8,128)S(1)} collective-permute-done((f32[8,128]{1,0:T(8,128)S(1)}, f32[8,128]{1,0:T(8,128)S(1)}, u32[]{:S(2)}, u32[]{:S(2)}) %collective-permute-start.3) | collective-permute-done | bytes 4128 | tf_op jit(solution)/shard_map/ppermute | solution.py:328
  64.6 0.5 copy-done.12
  65.2 0.0 copy-done.5
  65.2 0.0 copy-done.6
  65.2 4.9 %shard_map.79 = (f32[2,32,8,128]{3,2,1,0:T(8,128)}, f32[64,128]{1,0:T(8,128)}, f32[64,128]{1,0:T(8,128)}, f32[8,128]{1,0:T(8,128)}, f32[8,128]{1,0:T(8,128)}) custom-call(f32[2,32,8,128]{3,2,1,0:T(8,128)} %get-tuple-element.22.refs_0_, f32[64,128]{1,0:T(8,128)} %copy-done.5, f32[64,128]{1,0:T(8,128)} %copy-done.6, f32[8,128]{1,0:T(8,128)} %copy-done.11, ...), custom_call_target="tpu_custom_call" | custom-call | tf_op jit(solution)/shard_map/pallas_call | solution.py:275
  70.1 1.9 %collective-permute-start.8 = (f32[64,128]{1,0:T(8,128)}, f32[64,128]{1,0:T(8,128)S(1)}, u32[]{:S(2)}, u32[]{:S(2)}) collective-permute-start(f32[64,128]{1,0:T(8,128)} %get-tuple-element.33), channel_id=1, source_target_pairs={{0,16},{16,32},{32,48},{48,64},{64,80},{80,96},{96,112},{112,128},... | collective-permute-start | bytes 98312 | tf_op jit(solution)/shard_map/ppermute | solution.py:328
  72.0 6.0 %collective-permute-start.9 = (f32[64,128]{1,0:T(8,128)}, f32[64,128]{1,0:T(8,128)S(1)}, u32[]{:S(2)}, u32[]{:S(2)}) collective-permute-start(f32[64,128]{1,0:T(8,128)} %get-tuple-element.34), channel_id=1, source_target_pairs={{16,0},{32,16},{48,32},{64,48},{80,64},{96,80},{112,96},{128,112},... | collective-permute-start | bytes 98312 | tf_op jit(solution)/shard_map/ppermute | solution.py:328
  78.1 2.6 %collective-permute-start.10 = (f32[8,128]{1,0:T(8,128)}, f32[8,128]{1,0:T(8,128)S(1)}, u32[]{:S(2)}, u32[]{:S(2)}) collective-permute-start(f32[8,128]{1,0:T(8,128)} %get-tuple-element.35), channel_id=1, source_target_pairs={{0,1},{1,2},{2,3},{3,4},{4,5},{5,6},{6,7},{7,8},{8,9},{9,10},{10,1... | collective-permute-start | bytes 12296 | tf_op jit(solution)/shard_map/ppermute | solution.py:328
  80.7 5.4 %collective-permute-start.11 = (f32[8,128]{1,0:T(8,128)S(1)}, f32[8,128]{1,0:T(8,128)S(1)}, u32[]{:S(2)}, u32[]{:S(2)}) collective-permute-start(f32[8,128]{1,0:T(8,128)S(1)} %copy-done.22), channel_id=1, source_target_pairs={{1,0},{2,1},{3,2},{4,3},{5,4},{6,5},{7,6},{8,7},{9,8},{10,9},{11,1... | collective-permute-start | bytes 12296 | tf_op jit(solution)/shard_map/ppermute | solution.py:328
  86.1 1.3 %collective-permute-done.11.refs_4_ = f32[8,128]{1,0:T(8,128)S(1)} collective-permute-done((f32[8,128]{1,0:T(8,128)S(1)}, f32[8,128]{1,0:T(8,128)S(1)}, u32[]{:S(2)}, u32[]{:S(2)}) %collective-permute-start.11) | collective-permute-done | bytes 4128 | tf_op jit(solution)/shard_map/ppermute | solution.py:328
  87.4 0.6 copy-done.14
  87.9 0.0 copy-done.3
  88.0 0.0 copy-done.4
  88.0 5.3 %shard_map.81 = (f32[2,32,8,128]{3,2,1,0:T(8,128)}, f32[64,128]{1,0:T(8,128)}, f32[64,128]{1,0:T(8,128)}, f32[8,128]{1,0:T(8,128)}, f32[8,128]{1,0:T(8,128)}) custom-call(f32[2,32,8,128]{3,2,1,0:T(8,128)} %get-tuple-element.32.refs_0_, f32[64,128]{1,0:T(8,128)} %copy-done.3, f32[64,128]{1,0:T(8,128)} %copy-done.4, f32[8,128]{1,0:T(8,128)} %copy-done.13, ...), custom_call_target="tpu_custom_call" | custom-call | tf_op jit(solution)/shard_map/pallas_call | solution.py:312
  93.2 1.9 %collective-permute-start.12 = (f32[64,128]{1,0:T(8,128)}, f32[64,128]{1,0:T(8,128)S(1)}, u32[]{:S(2)}, u32[]{:S(2)}) collective-permute-start(f32[64,128]{1,0:T(8,128)} %get-tuple-element.38), channel_id=1, source_target_pairs={{0,16},{16,32},{32,48},{48,64},{64,80},{80,96},{96,112},{112,128},... | collective-permute-start | bytes 98312 | tf_op jit(solution)/shard_map/ppermute | solution.py:328
  95.2 6.0 %collective-permute-start.13 = (f32[64,128]{1,0:T(8,128)}, f32[64,128]{1,0:T(8,128)S(1)}, u32[]{:S(2)}, u32[]{:S(2)}) collective-permute-start(f32[64,128]{1,0:T(8,128)} %get-tuple-element.39), channel_id=1, source_target_pairs={{16,0},{32,16},{48,32},{64,48},{80,64},{96,80},{112,96},{128,112},... | collective-permute-start | bytes 98312 | tf_op jit(solution)/shard_map/ppermute | solution.py:328
  101.2 1.9 %collective-permute-start.14 = (f32[8,128]{1,0:T(8,128)}, f32[8,128]{1,0:T(8,128)S(1)}, u32[]{:S(2)}, u32[]{:S(2)}) collective-permute-start(f32[8,128]{1,0:T(8,128)} %get-tuple-element.40), channel_id=1, source_target_pairs={{0,1},{1,2},{2,3},{3,4},{4,5},{5,6},{6,7},{7,8},{8,9},{9,10},{10,1... | collective-permute-start | bytes 12296 | tf_op jit(solution)/shard_map/ppermute | solution.py:328
  103.2 6.0 %collective-permute-start.15 = (f32[8,128]{1,0:T(8,128)S(1)}, f32[8,128]{1,0:T(8,128)S(1)}, u32[]{:S(2)}, u32[]{:S(2)}) collective-permute-start(f32[8,128]{1,0:T(8,128)S(1)} %copy-done.21), channel_id=1, source_target_pairs={{1,0},{2,1},{3,2},{4,3},{5,4},{6,5},{7,6},{8,7},{9,8},{10,9},{11,1... | collective-permute-start | bytes 12296 | tf_op jit(solution)/shard_map/ppermute | solution.py:328
  109.2 4.8 %shard_map.80 = f32[2,32,8,128]{3,2,1,0:T(8,128)} custom-call(f32[2,32,8,128]{3,2,1,0:T(8,128)} %get-tuple-element.32.refs_0_, f32[64,128]{1,0:T(8,128)} %copy-done.3, f32[64,128]{1,0:T(8,128)} %copy-done.4, f32[8,128]{1,0:T(8,128)} %copy-done.13, f32[8,128]{1,0:T(8,128)} %copy-done.14, f32[4,8,128]{2,1,0:T(8,128)} %get-tuple-element.27.refs_5_.refs_10_, ...), custom_call_target="tpu_custom_call" | custom-call | tf_op jit(solution)/shard_map/pallas_call | solution.py:275
  114.1 0.5 copy-done.15
  114.6 0.0 copy-done.16
  114.6 0.0 copy-done.9
  114.7 0.0 copy-done.10
  114.7 5.1 %shard_map.82 = f32[2,32,8,128]{3,2,1,0:T(8,128)} custom-call(f32[2,32,8,128]{3,2,1,0:T(8,128)} %get-tuple-element.22.refs_0_, f32[64,128]{1,0:T(8,128)} %copy-done.5, f32[64,128]{1,0:T(8,128)} %copy-done.6, f32[8,128]{1,0:T(8,128)} %copy-done.11, f32[8,128]{1,0:T(8,128)} %copy-done.12, f32[2,32,8,128]{3,2,1,0:T(8,128)} %get-tuple-element.37.refs_5_, ...), custom_call_target="tpu_custom_call" | custom-call | tf_op jit(solution)/shard_map/pallas_call | solution.py:312
  (52 shorter events, 0.1 us)
Async XLA Ops:
  3.0 7.6 %copy-start.23 = (s32[16]{0:T(128)S(1)}, s32[16]{0:T(128)}, u32[]{:S(2)}) copy-start(s32[16]{0:T(128)} %param.8) | copy-start | bytes 196
  3.0 14.0 %all-to-all-start = ((bf16[16,5,8,128]{3,2,1,0:T(8,128)(2,1)}), bf16[16,5,8,128]{3,2,1,0:T(8,128)(2,1)S(1)}, u32[]{:S(2)}, u32[]{:S(2)}) async-start(bf16[16,5,8,128]{3,2,1,0:T(8,128)(2,1)} %fusion.1), calls=%async_computation | async-start | bytes 327680 | tf_op jit(solution)/shard_map/all_to_all | solution.py:347
  18.3 5.5 %copy-start.17 = (f32[12,4]{0,1:T(4,128)S(1)}, f32[12,4]{0,1:T(4,128)}, u32[]{:S(2)}) copy-start(f32[12,4]{0,1:T(4,128)} %param.10) | copy-start | bytes 580
  18.3 15.9 %all-to-all-start.1 = ((bf16[16,5,8,128]{3,2,1,0:T(8,128)(2,1)}), bf16[16,5,8,128]{3,2,1,0:T(8,128)(2,1)S(1)}, u32[]{:S(2)}, u32[]{:S(2)}) async-start(bf16[16,5,8,128]{3,2,1,0:T(8,128)(2,1)} %broadcast_select_fusion), calls=%async_computation.1 | async-start | bytes 327680 | tf_op jit(solution)/shard_map/all_to_all | solution.py:349
  26.2 33.1 %collective-permute-start.4 = (f32[72,128]{1,0:T(8,128)}, f32[72,128]{1,0:T(8,128)S(1)}, u32[]{:S(2)}, u32[]{:S(2)}) collective-permute-start(f32[72,128]{1,0:T(8,128)} %get-tuple-element.28), channel_id=1, source_target_pairs={{0,16},{16,32},{32,48},{48,64},{64,80},{80,96},{96,112},{112,128},... | collective-permute-start | bytes 110600 | tf_op jit(solution)/shard_map/ppermute | solution.py:328
  28.8 34.5 %collective-permute-start.5 = (f32[72,128]{1,0:T(8,128)}, f32[72,128]{1,0:T(8,128)S(1)}, u32[]{:S(2)}, u32[]{:S(2)}) collective-permute-start(f32[72,128]{1,0:T(8,128)} %get-tuple-element.29), channel_id=1, source_target_pairs={{16,0},{32,16},{48,32},{64,48},{80,64},{96,80},{112,96},{128,112},... | collective-permute-start | bytes 110600 | tf_op jit(solution)/shard_map/ppermute | solution.py:328
  34.2 0.7 copy-start.2
  34.9 9.8 %copy-start.20 = (f32[8,128]{1,0:T(8,128)S(1)}, f32[8,128]{1,0:T(8,128)}, u32[]{:S(2)}) copy-start(f32[8,128]{1,0:T(8,128)} %get-tuple-element.30) | copy-start | bytes 12292
  36.6 15.4 %copy-start.19 = (f32[8,128]{1,0:T(8,128)S(1)}, f32[8,128]{1,0:T(8,128)}, u32[]{:S(2)}) copy-start(f32[8,128]{1,0:T(8,128)} %get-tuple-element.31) | copy-start | bytes 12292
  36.6 28.0 %collective-permute-start = (f32[64,128]{1,0:T(8,128)}, f32[64,128]{1,0:T(8,128)S(1)}, u32[]{:S(2)}, u32[]{:S(2)}) collective-permute-start(f32[64,128]{1,0:T(8,128)} %get-tuple-element.23), channel_id=1, source_target_pairs={{0,16},{16,32},{32,48},{48,64},{64,80},{80,96},{96,112},{112,128},... | collective-permute-start | bytes 98312 | tf_op jit(solution)/shard_map/ppermute | solution.py:328
  38.6 20.7 %copy-start.18 = (f32[8,128]{1,0:T(8,128)S(1)}, f32[8,128]{1,0:T(8,128)}, u32[]{:S(2)}) copy-start(f32[8,128]{1,0:T(8,128)} %get-tuple-element.26) | copy-start | bytes 12292
  38.7 25.9 %collective-permute-start.1 = (f32[64,128]{1,0:T(8,128)}, f32[64,128]{1,0:T(8,128)S(1)}, u32[]{:S(2)}, u32[]{:S(2)}) collective-permute-start(f32[64,128]{1,0:T(8,128)} %get-tuple-element.24), channel_id=1, source_target_pairs={{16,0},{32,16},{48,32},{64,48},{80,64},{96,80},{112,96},{128,112},... | collective-permute-start | bytes 98312 | tf_op jit(solution)/shard_map/ppermute | solution.py:328
  44.7 7.3 %collective-permute-start.6 = (f32[8,128]{1,0:T(8,128)S(1)}, f32[8,128]{1,0:T(8,128)S(1)}, u32[]{:S(2)}, u32[]{:S(2)}) collective-permute-start(f32[8,128]{1,0:T(8,128)S(1)} %copy-done.20), channel_id=1, source_target_pairs={{0,1},{1,2},{2,3},{3,4},{4,5},{5,6},{6,7},{7,8},{8,9},{9,10},{10,1... | collective-permute-start | bytes 12296 | tf_op jit(solution)/shard_map/ppermute | solution.py:328
  52.0 12.6 %copy-start.7 = (f32[8,128]{1,0:T(8,128)}, f32[8,128]{1,0:T(8,128)S(1)}, u32[]{:S(2)}) copy-start(f32[8,128]{1,0:T(8,128)S(1)} %collective-permute-done.6.refs_8_.refs_13_) | copy-start | bytes 12292
  52.0 3.2 %collective-permute-start.7 = (f32[8,128]{1,0:T(8,128)S(1)}, f32[8,128]{1,0:T(8,128)S(1)}, u32[]{:S(2)}, u32[]{:S(2)}) collective-permute-start(f32[8,128]{1,0:T(8,128)S(1)} %copy-done.19), channel_id=1, source_target_pairs={{1,0},{2,1},{3,2},{4,3},{5,4},{6,5},{7,6},{8,7},{9,8},{10,9},{11,1... | collective-permute-start | bytes 12296 | tf_op jit(solution)/shard_map/ppermute | solution.py:328
  55.3 9.3 %copy-start.8 = (f32[8,128]{1,0:T(8,128)}, f32[8,128]{1,0:T(8,128)S(1)}, u32[]{:S(2)}) copy-start(f32[8,128]{1,0:T(8,128)S(1)} %collective-permute-done.7.refs_9_.refs_14_) | copy-start | bytes 12292
  55.3 8.0 %collective-permute-start.2 = (f32[8,128]{1,0:T(8,128)}, f32[8,128]{1,0:T(8,128)S(1)}, u32[]{:S(2)}, u32[]{:S(2)}) collective-permute-start(f32[8,128]{1,0:T(8,128)} %get-tuple-element.25), channel_id=1, source_target_pairs={{0,1},{1,2},{2,3},{3,4},{4,5},{5,6},{6,7},{7,8},{8,9},{9,10},{10,1... | collective-permute-start | bytes 12296 | tf_op jit(solution)/shard_map/ppermute | solution.py:328
  59.3 5.3 %copy-start = (f32[72,128]{1,0:T(8,128)}, f32[72,128]{1,0:T(8,128)S(1)}, u32[]{:S(2)}) copy-start(f32[72,128]{1,0:T(8,128)S(1)} %collective-permute-done.4.refs_6_.refs_11_) | copy-start | bytes 110596
  59.4 5.2 %collective-permute-start.3 = (f32[8,128]{1,0:T(8,128)S(1)}, f32[8,128]{1,0:T(8,128)S(1)}, u32[]{:S(2)}, u32[]{:S(2)}) collective-permute-start(f32[8,128]{1,0:T(8,128)S(1)} %copy-done.18), channel_id=1, source_target_pairs={{1,0},{2,1},{3,2},{4,3},{5,4},{6,5},{7,6},{8,7},{9,8},{10,9},{11,1... | collective-permute-start | bytes 12296 | tf_op jit(solution)/shard_map/ppermute | solution.py:328
  63.3 1.4 %copy-start.1 = (f32[72,128]{1,0:T(8,128)}, f32[72,128]{1,0:T(8,128)S(1)}, u32[]{:S(2)}) copy-start(f32[72,128]{1,0:T(8,128)S(1)} %collective-permute-done.5.refs_7_.refs_12_) | copy-start | bytes 110596
  63.3 1.3 %copy-start.11 = (f32[8,128]{1,0:T(8,128)}, f32[8,128]{1,0:T(8,128)S(1)}, u32[]{:S(2)}) copy-start(f32[8,128]{1,0:T(8,128)S(1)} %collective-permute-done.2.refs_3_) | copy-start | bytes 12292
  64.6 0.6 copy-start.12
  64.6 0.6 copy-start.5
  64.6 0.6 copy-start.6
  70.1 10.6 %copy-start.22 = (f32[8,128]{1,0:T(8,128)S(1)}, f32[8,128]{1,0:T(8,128)}, u32[]{:S(2)}) copy-start(f32[8,128]{1,0:T(8,128)} %get-tuple-element.36) | copy-start | bytes 12292
  70.1 17.3 %collective-permute-start.8 = (f32[64,128]{1,0:T(8,128)}, f32[64,128]{1,0:T(8,128)S(1)}, u32[]{:S(2)}, u32[]{:S(2)}) collective-permute-start(f32[64,128]{1,0:T(8,128)} %get-tuple-element.33), channel_id=1, source_target_pairs={{0,16},{16,32},{32,48},{48,64},{64,80},{80,96},{96,112},{112,128},... | collective-permute-start | bytes 98312 | tf_op jit(solution)/shard_map/ppermute | solution.py:328
  72.0 15.3 %collective-permute-start.9 = (f32[64,128]{1,0:T(8,128)}, f32[64,128]{1,0:T(8,128)S(1)}, u32[]{:S(2)}, u32[]{:S(2)}) collective-permute-start(f32[64,128]{1,0:T(8,128)} %get-tuple-element.34), channel_id=1, source_target_pairs={{16,0},{32,16},{48,32},{64,48},{80,64},{96,80},{112,96},{128,112},... | collective-permute-start | bytes 98312 | tf_op jit(solution)/shard_map/ppermute | solution.py:328
  78.1 8.0 %collective-permute-start.10 = (f32[8,128]{1,0:T(8,128)}, f32[8,128]{1,0:T(8,128)S(1)}, u32[]{:S(2)}, u32[]{:S(2)}) collective-permute-start(f32[8,128]{1,0:T(8,128)} %get-tuple-element.35), channel_id=1, source_target_pairs={{0,1},{1,2},{2,3},{3,4},{4,5},{5,6},{6,7},{7,8},{8,9},{9,10},{10,1... | collective-permute-start | bytes 12296 | tf_op jit(solution)/shard_map/ppermute | solution.py:328
  80.7 6.7 %collective-permute-start.11 = (f32[8,128]{1,0:T(8,128)S(1)}, f32[8,128]{1,0:T(8,128)S(1)}, u32[]{:S(2)}, u32[]{:S(2)}) collective-permute-start(f32[8,128]{1,0:T(8,128)S(1)} %copy-done.22), channel_id=1, source_target_pairs={{1,0},{2,1},{3,2},{4,3},{5,4},{6,5},{7,6},{8,7},{9,8},{10,9},{11,1... | collective-permute-start | bytes 12296 | tf_op jit(solution)/shard_map/ppermute | solution.py:328
  86.1 1.3 %copy-start.13 = (f32[8,128]{1,0:T(8,128)}, f32[8,128]{1,0:T(8,128)S(1)}, u32[]{:S(2)}) copy-start(f32[8,128]{1,0:T(8,128)S(1)} %collective-permute-done.10.refs_3_) | copy-start | bytes 12292
  87.4 0.6 copy-start.14
  87.4 0.6 copy-start.3
  87.4 0.6 copy-start.4
  93.2 9.9 %copy-start.21 = (f32[8,128]{1,0:T(8,128)S(1)}, f32[8,128]{1,0:T(8,128)}, u32[]{:S(2)}) copy-start(f32[8,128]{1,0:T(8,128)} %get-tuple-element.41) | copy-start | bytes 12292
  93.2 20.8 %collective-permute-start.12 = (f32[64,128]{1,0:T(8,128)}, f32[64,128]{1,0:T(8,128)S(1)}, u32[]{:S(2)}, u32[]{:S(2)}) collective-permute-start(f32[64,128]{1,0:T(8,128)} %get-tuple-element.38), channel_id=1, source_target_pairs={{0,16},{16,32},{32,48},{48,64},{64,80},{80,96},{96,112},{112,128},... | collective-permute-start | bytes 98312 | tf_op jit(solution)/shard_map/ppermute | solution.py:328
  95.2 18.9 %collective-permute-start.13 = (f32[64,128]{1,0:T(8,128)}, f32[64,128]{1,0:T(8,128)S(1)}, u32[]{:S(2)}, u32[]{:S(2)}) collective-permute-start(f32[64,128]{1,0:T(8,128)} %get-tuple-element.39), channel_id=1, source_target_pairs={{16,0},{32,16},{48,32},{64,48},{80,64},{96,80},{112,96},{128,112},... | collective-permute-start | bytes 98312 | tf_op jit(solution)/shard_map/ppermute | solution.py:328
  101.2 12.8 %collective-permute-start.14 = (f32[8,128]{1,0:T(8,128)}, f32[8,128]{1,0:T(8,128)S(1)}, u32[]{:S(2)}, u32[]{:S(2)}) collective-permute-start(f32[8,128]{1,0:T(8,128)} %get-tuple-element.40), channel_id=1, source_target_pairs={{0,1},{1,2},{2,3},{3,4},{4,5},{5,6},{6,7},{7,8},{8,9},{9,10},{10,1... | collective-permute-start | bytes 12296 | tf_op jit(solution)/shard_map/ppermute | solution.py:328
  103.2 10.9 %collective-permute-start.15 = (f32[8,128]{1,0:T(8,128)S(1)}, f32[8,128]{1,0:T(8,128)S(1)}, u32[]{:S(2)}, u32[]{:S(2)}) collective-permute-start(f32[8,128]{1,0:T(8,128)S(1)} %copy-done.21), channel_id=1, source_target_pairs={{1,0},{2,1},{3,2},{4,3},{5,4},{6,5},{7,6},{8,7},{9,8},{10,9},{11,1... | collective-permute-start | bytes 12296 | tf_op jit(solution)/shard_map/ppermute | solution.py:328
  114.0 0.6 copy-start.15
  114.0 0.6 copy-start.16
  114.1 0.6 copy-start.9
  114.1 0.6 copy-start.10

commit v2 on v1

--- a/solution.py
+++ b/solution.py
@@ -195,11 +195,12 @@
     return -(-n // 8) * 8
 
 
-def prep_call(soil_class, soil_table, cot):
+def prep_call(soil_class, soil_table, cot, slab, scales):
     nf, nz, x, y = cot.shape
     nclass = soil_table.shape[0]
-
-    def kernel(cls_ref, tab_ref, cot_ref, coef_ref, xf_ref, xl_ref, yf_ref, yl_ref):
+    nplanes = nf * nz
+
+    def kernel(cls_ref, tab_ref, sc_ref, cot_ref, slab_ref, coef_ref, xf_ref, xl_ref, yf_ref, yl_ref):
         cls = cls_ref[...]
         coefs = []
         for k in range(NCOEF):
@@ -210,38 +211,58 @@
             coefs.append(cv)
         vals = [cot_ref[f, z] for f in range(nf) for z in range(nz)] + coefs
         _pack_edges(vals, xf_ref, xl_ref, yf_ref, yl_ref)
-
-    rows = _rows(nf * nz + NCOEF)
+        base = len(vals)
+        for k in range(nplanes):
+            v = slab_ref[k // nz, k % nz].astype(F32)
+            xf_ref[base + k : base + k + 1, :] = v[0:1, :]
+            xl_ref[base + k : base + k + 1, :] = v[x - 1 : x, :]
+        _, lane = _iotas((1, y))
+        row = jnp.zeros((1, y), F32)
+        for k in range(nplanes):
+            row = jnp.where(lane == k, sc_ref[k], row)
+        xf_ref[base + nplanes : base + nplanes + 1, :] = row
+        xl_ref[base + nplanes : base + nplanes + 1, :] = row
+
+    rows = _rows(2 * nplanes + NCOEF + 1)
     return pl.pallas_call(
         kernel,
-        out_shape=(jax.ShapeDtypeStruct((NCOEF, x, y), F32),) + _edge_shapes(rows, x, y),
+        out_shape=(jax.ShapeDtypeStruct((NCOEF, x, y), F32),)
+        + _edge_shapes(rows, x, y)[:2]
+        + _edge_shapes(8, x, y)[2:],
         in_specs=[
             pl.BlockSpec(memory_space=VMEM),
             pl.BlockSpec(memory_space=SMEM),
+            pl.BlockSpec(memory_space=SMEM),
+            pl.BlockSpec(memory_space=VMEM),
             pl.BlockSpec(memory_space=VMEM),
         ],
-    )(soil_class, soil_table, cot)
-
-
-def state0_call(pieces, scales):
-    npiece, pp, x, y = pieces.shape
-    per = pp - 1
+    )(soil_class, soil_table, scales, cot, slab)
+
+
+def state0_call(pieces, scales, nf, per):
+    npiece, _, x, y = pieces.shape
     nplanes = npiece * per
-
-    def kernel(sc_ref, r_ref, s_ref, xf_ref, xl_ref, yf_ref, yl_ref):
-        nz = s_ref.shape[1]
-        vals = []
+    nz = nplanes // nf
+
+    def kernel(sc_ref, r_ref, s_ref, xm_ref, xp_ref, ym_ref, yp_ref):
+        _, lane = _iotas((x, y))
+        ym = jnp.zeros((x, y), F32)
+        yp = jnp.zeros((x, y), F32)
         for k in range(nplanes):
-            v = r_ref[k // per, k % per].astype(F32) * sc_ref[k]
-            s_ref[k // nz, k % nz] = v
-            vals.append(v)
-        _pack_edges(vals, xf_ref, xl_ref, yf_ref, yl_ref)
-
-    nf = 2
-    nz = nplanes // nf
+            p, i = k // per, k % per
+            s_ref[k // nz, k % nz] = r_ref[p, i].astype(F32) * sc_ref[k]
+            hx = r_ref[p, per].astype(F32)
+            xm_ref[k : k + 1, :] = hx[i : i + 1, :] * sc_ref[nplanes + k]
+            xp_ref[k : k + 1, :] = hx[per + i : per + i + 1, :] * sc_ref[2 * nplanes + k]
+            hy = r_ref[p, per + 2].astype(F32)
+            ym = jnp.where(lane == k, _roll(hy, k - i, 1) * sc_ref[3 * nplanes + k], ym)
+            yp = jnp.where(lane == k, _roll(hy, k - (per + i), 1) * sc_ref[4 * nplanes + k], yp)
+        ym_ref[...] = ym
+        yp_ref[...] = yp
+
     return pl.pallas_call(
         kernel,
-        out_shape=(jax.ShapeDtypeStruct((nf, nz, x, y), F32),) + _edge_shapes(_rows(nplanes), x, y),
+        out_shape=(jax.ShapeDtypeStruct((nf, nz, x, y), F32),) + _edge_shapes(nplanes, x, y),
         in_specs=[pl.BlockSpec(memory_space=SMEM), pl.BlockSpec(memory_space=VMEM)],
     )(scales, pieces)
 
@@ -337,30 +358,64 @@
     )
 
 
-def route_blocks(stored_slab, block_scales, holder):
+def route_blocks(stored_slab, block_scales, holder, xm_all, xp_all, first):
     nf, nz, x, y = stored_slab.shape
     n = lax.axis_size("gy")
-    per = nf * nz // n
+    nplanes = nf * nz
+    per = nplanes // n
+    bf = stored_slab.dtype
     slab = stored_slab.reshape(n, per, x, y)
-    sc = jnp.pad(block_scales.reshape(n, 1, 1, per), ((0, 0), (0, 0), (0, x - 1), (0, y - per)))
-    send = jnp.concatenate([slab, sc], axis=1)
-    held = lax.all_to_all(send, "gy", 0, 0, tiled=True)
-    forward = jnp.take(held, holder, axis=0)
+    rows_m = xm_all[first : first + nplanes].astype(bf).reshape(n, per, y)
+    rows_p = xp_all[first : first + nplanes].astype(bf).reshape(n, per, y)
+    halo = jnp.concatenate([rows_m, rows_p], axis=1)[:, None]
+    sc_m = xm_all[first + nplanes, :nplanes].astype(bf).reshape(n, 1, per)
+    sc_p = xp_all[first + nplanes, :nplanes].astype(bf).reshape(n, 1, per)
+    sc = jnp.concatenate([block_scales.reshape(n, 1, per), sc_m, sc_p], axis=1)
+    sc = jnp.pad(sc, ((0, 0), (0, x - 3), (0, y - per)))[:, None]
+    held = lax.all_to_all(jnp.concatenate([slab, halo, sc], axis=1), "gy", 0, 0, tiled=True)
+
+    g = jnp.arange(n, dtype=jnp.int32)
+    left = jnp.take(holder, jnp.maximum(g - 1, 0))
+    right = jnp.take(holder, jnp.minimum(g + 1, n - 1))
+    has_l = (g > 0)[:, None, None]
+    has_r = (g < n - 1)[:, None, None]
+    zero = jnp.zeros((), bf)
+    cols_l = jnp.where(has_l, jnp.take(held[:, :per, :, y - 1], left, axis=0), zero)
+    cols_r = jnp.where(has_r, jnp.take(held[:, :per, :, 0], right, axis=0), zero)
+    scl_l = jnp.where(has_l, jnp.take(held[:, per + 1, 0:1, :per], left, axis=0), zero)
+    scl_r = jnp.where(has_r, jnp.take(held[:, per + 1, 0:1, :per], right, axis=0), zero)
+    cols = jnp.concatenate([cols_l, cols_r], axis=1).transpose(0, 2, 1)
+    scl = jnp.concatenate([scl_l, scl_r], axis=2)
+    yplane = jnp.concatenate(
+        [
+            jnp.pad(cols, ((0, 0), (0, 0), (0, y - 2 * per))),
+            jnp.pad(scl, ((0, 0), (0, x - 1), (0, y - 2 * per))),
+        ],
+        axis=1,
+    )
+    forward = jnp.concatenate([jnp.take(held, holder, axis=0), yplane.reshape(n, 2, x, y)], axis=1)
     return lax.all_to_all(forward, "gy", 0, 0, tiled=True)
 
 
 def on_device(stored_slab, block_scales, holder, soil_class, soil_table, cotangent):
     nf, nz, x, y = stored_slab.shape
-
-    coef, cxf, cxl, cyf, cyl = prep_call(soil_class, soil_table, cotangent)
+    nplanes = nf * nz
+
+    coef, cxf, cxl, cyf, cyl = prep_call(
+        soil_class, soil_table, cotangent, stored_slab, block_scales.reshape(-1).astype(F32)
+    )
     c_halo = exchange(cxf, cxl, cyf, cyl)
-    c_first = nf * nz
-
-    pieces = route_blocks(stored_slab, block_scales, holder)
-    per = pieces.shape[1] - 1
-    scales = pieces[:, per, 0, :per].astype(F32).reshape(-1)
-    s0, *s0_edges = state0_call(pieces, scales)
-    s0_halo = exchange(*s0_edges)
+    c_first = nplanes
+
+    pieces = route_blocks(stored_slab, block_scales, holder, c_halo[0], c_halo[1], nplanes + NCOEF)
+    per = nplanes // pieces.shape[0]
+    scales = jnp.concatenate(
+        [
+            pieces[:, per + 1, 0:3, :per].transpose(1, 0, 2).reshape(3, nplanes),
+            pieces[:, per + 3, 0, : 2 * per].reshape(-1, 2, per).transpose(1, 0, 2).reshape(2, nplanes),
+        ]
+    ).astype(F32).reshape(-1)
+    s0, *s0_halo = state0_call(pieces, scales, nf, per)
 
     s1, *s1_edges = step_call(s0, s0_halo, coef, c_halo, c_first, True)
     s1_halo = exchange(*s1_edges)

time: 121 us -> 109 us (0.901)
  starting transfers between devices: 72.7 us -> 60.8 us
  waiting for transfers between devices: 15.6 us -> 7.91 us
  local copies, waits for them, and re-layouts: 4.43 us -> 12.1 us
    ppermute x16 -> x12, starting transfers between devices: 59.6 us -> 47.7 us  [_shift(): return lax.ppermute(v, axis, pairs)]
    ppermute x16 -> x12, waiting for transfers between devices: 9.29 us -> 1.31 us  [_shift(): return lax.ppermute(v, axis, pairs)]
    gather x1 -> x9, local copies, waits for them, and re-layouts: 0.58 us -> 4.41 us  [the longest x2 0.67 us: route_blocks(): jnp.take(held[:, per + 1, 0:1, :per], right, axis=0)]
    unnamed x49 -> x43, local copies, waits for them, and re-layouts: 2.49 us -> 4.55 us
  transfers between devices with their start and end apart: 18 -> 14, of which waited for: 5 -> 2; matrix products, arithmetic and copies ran while one was open for 1% -> 2% of each run, Pallas kernels for 7% -> 6%
where the time goes in v2:
time: 109 us; the launch traced here: 108 us
  starting transfers between devices  60.8 us (56%)
  Pallas kernels  23.9 us (22%)
  local copies, waits for them, and re-layouts  12.1 us (11%)
  waiting for transfers between devices  7.91 us (7%)
  other arithmetic  1.99 us (2%)
  between operations  1.17 us (1%)
    ppermute x12, starting transfers between devices, _shift(): return lax.ppermute(v, axis, pairs)  47.7 us
    pallas_call x2, Pallas kernels, adjoint_call(): pl.pallas_call(kernel, out_shape=out_shape, scratch_shapes=_halo_scratch(...  10.4 us
    pallas_call x2, Pallas kernels, step_call(): pl.pallas_call(kernel, out_shape=out_shape, scratch_shapes=_halo_scratch(...  9.78 us
    all_to_all x1, starting transfers between devices, route_blocks(): lax.all_to_all(jnp.concatenate([slab, halo, sc], axis=1), 'gy', 0, 0, til...  7.48 us
    all_to_all x1, waiting for transfers between devices, route_blocks(): lax.all_to_all(jnp.concatenate([slab, halo, sc], axis=1), 'gy', 0, 0, til...  6.59 us
    all_to_all x1, starting transfers between devices, route_blocks(): return lax.all_to_all(forward, 'gy', 0, 0, tiled=True)  5.56 us
    unnamed x43, local copies, waits for them, and re-layouts  4.55 us
  transfers between devices with their start and end apart: 14, of which 2 were waited for; matrix products, arithmetic and copies ran while one was open for 2% of the time, Pallas kernels for 6%

profile of v2, /device:TPU:130, one launch (start us, length us, event | category | flops | bytes accessed | tf_op | source)
XLA Modules:
  0.0 107.8 jit_solution(9024663226898393226)
XLA Ops:
  0.6 1.4 %copy.58.tab_ref = f32[12,4]{1,0:T(8,128)} copy(f32[12,4]{0,1:T(4,128)} %param.16) | data formatting | bytes 384 | tf_op args[4]
  2.0 0.7 reshape.112.sc_ref
  2.7 1.8 %shard_map.77 = (f32[4,8,128]{2,1,0:T(8,128)}, f32[136,128]{1,0:T(8,128)}, f32[136,128]{1,0:T(8,128)}, f32[8,128]{1,0:T(8,128)}, f32[8,128]{1,0:T(8,128)}) custom-call(s32[8,128]{1,0:T(8,128)} %cls_ref.1, f32[12,4]{1,0:T(8,128)} %copy.58.tab_ref, f32[64]{0:T(128)} %reshape.112.sc_ref, f32[2,32,8,128]{3,2,1,0:T(8,128)} %refs_5_.1, ...), custom_call_target="tpu_custom_call" | custom-call | tf_op jit(solution)/shard_map/pallas_call | solution.py:227
  4.5 3.5 %collective-permute-start = (f32[136,128]{1,0:T(8,128)}, f32[136,128]{1,0:T(8,128)S(1)}, u32[]{:S(2)}, u32[]{:S(2)}) collective-permute-start(f32[136,128]{1,0:T(8,128)} %get-tuple-element.25), channel_id=1, source_target_pairs={{0,16},{16,32},{32,48},{48,64},{64,80},{80,96},{96,112},{112,128},... | collective-permute-start | bytes 208904 | tf_op jit(solution)/shard_map/ppermute | solution.py:349
  8.0 4.5 %collective-permute-start.1 = (f32[136,128]{1,0:T(8,128)}, f32[136,128]{1,0:T(8,128)S(1)}, u32[]{:S(2)}, u32[]{:S(2)}) collective-permute-start(f32[136,128]{1,0:T(8,128)} %get-tuple-element.26), channel_id=1, source_target_pairs={{16,0},{32,16},{48,32},{64,48},{80,64},{96,80},{112,96},{128,112},... | collective-permute-start | bytes 208904 | tf_op jit(solution)/shard_map/ppermute | solution.py:349
  12.6 0.6 copy-done
  13.2 0.7 gather_fusion.3
  13.9 0.7 gather_fusion.1
  14.7 0.5 copy-done.1
  15.6 0.7 pad_maximum_fusion.1
  16.3 7.5 %all-to-all-start = ((bf16[16,6,8,128]{3,2,1,0:T(8,128)(2,1)}), bf16[16,6,8,128]{3,2,1,0:T(8,128)(2,1)S(1)}, u32[]{:S(2)}, u32[]{:S(2)}) async-start(bf16[16,6,8,128]{3,2,1,0:T(8,128)(2,1)} %pad_maximum_fusion.1), calls=%async_computation | async-start | bytes 393216 | tf_op jit(solution)/shard_map/all_to_all | solution.py:375
  23.8 6.6 %all-to-all-done = bf16[16,6,8,128]{3,2,1,0:T(8,128)(2,1)S(1)} async-done(((bf16[16,6,8,128]{3,2,1,0:T(8,128)(2,1)}), bf16[16,6,8,128]{3,2,1,0:T(8,128)(2,1)S(1)}, u32[]{:S(2)}, u32[]{:S(2)}) %all-to-all-start) | async-done | bytes 196640 | tf_op jit(solution)/shard_map/all_to_all | solution.py:375
  30.4 0.1 fusion.16
  30.5 0.3 copy.64
  30.8 0.1 copy.65
  30.9 0.3 copy.62
  31.2 0.1 copy.63
  31.4 0.1 copy.67
  31.5 0.6 gather_fusion.4
  32.1 0.6 gather_fusion.6
  32.7 0.6 gather_fusion.5
  33.3 0.6 gather_fusion.2
  33.8 0.1 select_select_fusion
  34.0 0.1 select_select_fusion.1
  34.5 0.6 gather_fusion
  35.2 0.7 pad_maximum_fusion
  36.0 5.6 %all-to-all-start.1 = ((bf16[16,8,8,128]{3,2,1,0:T(8,128)(2,1)}), bf16[16,8,8,128]{3,2,1,0:T(8,128)(2,1)S(1)}, u32[]{:S(2)}, u32[]{:S(2)}) async-start(bf16[16,8,8,128]{3,2,1,0:T(8,128)(2,1)} %pad_maximum_fusion), calls=%async_computation.1 | async-start | bytes 524288 | tf_op jit(solution)/shard_map/all_to_all | solution.py:397
  41.5 2.1 %collective-permute-start.2 = (f32[8,128]{1,0:T(8,128)S(1)}, f32[8,128]{1,0:T(8,128)S(1)}, u32[]{:S(2)}, u32[]{:S(2)}) collective-permute-start(f32[8,128]{1,0:T(8,128)S(1)} %copy-done.17), channel_id=1, source_target_pairs={{0,1},{1,2},{2,3},{3,4},{4,5},{5,6},{6,7},{7,8},{8,9},{9,10},{10,1... | collective-permute-start | bytes 12296 | tf_op jit(solution)/shard_map/ppermute | solution.py:349
  43.6 5.9 %collective-permute-start.3 = (f32[8,128]{1,0:T(8,128)S(1)}, f32[8,128]{1,0:T(8,128)S(1)}, u32[]{:S(2)}, u32[]{:S(2)}) collective-permute-start(f32[8,128]{1,0:T(8,128)S(1)} %copy-done.16), channel_id=1, source_target_pairs={{1,0},{2,1},{3,2},{4,3},{5,4},{6,5},{7,6},{8,7},{9,8},{10,9},{11,1... | collective-permute-start | bytes 12296 | tf_op jit(solution)/shard_map/ppermute | solution.py:349
  49.8 0.1 copy.75
  50.0 0.7 reshape.113.sc_ref
  50.7 1.9 %shard_map.78 = (f32[2,32,8,128]{3,2,1,0:T(8,128)}, f32[64,128]{1,0:T(8,128)}, f32[64,128]{1,0:T(8,128)}, f32[8,128]{1,0:T(8,128)}, f32[8,128]{1,0:T(8,128)}) custom-call(f32[320]{0:T(512)} %reshape.113.sc_ref, bf16[16,8,8,128]{3,2,1,0:T(8,128)(2,1)} %copy-done.3), custom_call_target="tpu_custom_call" | custom-call | tf_op jit(solution)/shard_map/pallas_call | solution.py:263
  52.6 0.6 copy-done.7
  53.1 4.9 %shard_map.79 = (f32[2,32,8,128]{3,2,1,0:T(8,128)}, f32[64,128]{1,0:T(8,128)}, f32[64,128]{1,0:T(8,128)}, f32[8,128]{1,0:T(8,128)}, f32[8,128]{1,0:T(8,128)}) custom-call(f32[2,32,8,128]{3,2,1,0:T(8,128)} %get-tuple-element.27.refs_0_, f32[64,128]{1,0:T(8,128)} %get-tuple-element.28.refs_1_, f32[64,128]{1,0:T(8,128)} %get-tuple-element.29.refs_2_, ...), custom_call_target="tpu_custom_call" | custom-call | tf_op jit(solution)/shard_map/pallas_call | solution.py:296
  58.1 2.7 %collective-permute-start.4 = (f32[64,128]{1,0:T(8,128)}, f32[64,128]{1,0:T(8,128)S(1)}, u32[]{:S(2)}, u32[]{:S(2)}) collective-permute-start(f32[64,128]{1,0:T(8,128)} %get-tuple-element.36), channel_id=1, source_target_pairs={{0,16},{16,32},{32,48},{48,64},{64,80},{80,96},{96,112},{112,128},... | collective-permute-start | bytes 98312 | tf_op jit(solution)/shard_map/ppermute | solution.py:349
  60.8 5.2 %collective-permute-start.5 = (f32[64,128]{1,0:T(8,128)}, f32[64,128]{1,0:T(8,128)S(1)}, u32[]{:S(2)}, u32[]{:S(2)}) collective-permute-start(f32[64,128]{1,0:T(8,128)} %get-tuple-element.37), channel_id=1, source_target_pairs={{16,0},{32,16},{48,32},{64,48},{80,64},{96,80},{112,96},{128,112},... | collective-permute-start | bytes 98312 | tf_op jit(solution)/shard_map/ppermute | solution.py:349
  66.0 1.9 %collective-permute-start.6 = (f32[8,128]{1,0:T(8,128)}, f32[8,128]{1,0:T(8,128)S(1)}, u32[]{:S(2)}, u32[]{:S(2)}) collective-permute-start(f32[8,128]{1,0:T(8,128)} %get-tuple-element.38), channel_id=1, source_target_pairs={{0,1},{1,2},{2,3},{3,4},{4,5},{5,6},{6,7},{7,8},{8,9},{9,10},{10,1... | collective-permute-start | bytes 12296 | tf_op jit(solution)/shard_map/ppermute | solution.py:349
  68.0 6.0 %collective-permute-start.7 = (f32[8,128]{1,0:T(8,128)S(1)}, f32[8,128]{1,0:T(8,128)S(1)}, u32[]{:S(2)}, u32[]{:S(2)}) collective-permute-start(f32[8,128]{1,0:T(8,128)S(1)} %copy-done.19), channel_id=1, source_target_pairs={{1,0},{2,1},{3,2},{4,3},{5,4},{6,5},{7,6},{8,7},{9,8},{10,9},{11,1... | collective-permute-start | bytes 12296 | tf_op jit(solution)/shard_map/ppermute | solution.py:349
  74.1 1.3 %collective-permute-done.7.refs_4_ = f32[8,128]{1,0:T(8,128)S(1)} collective-permute-done((f32[8,128]{1,0:T(8,128)S(1)}, f32[8,128]{1,0:T(8,128)S(1)}, u32[]{:S(2)}, u32[]{:S(2)}) %collective-permute-start.7) | collective-permute-done | bytes 4128 | tf_op jit(solution)/shard_map/ppermute | solution.py:349
  75.4 0.6 copy-done.12
  76.0 5.3 %shard_map.81 = (f32[2,32,8,128]{3,2,1,0:T(8,128)}, f32[64,128]{1,0:T(8,128)}, f32[64,128]{1,0:T(8,128)}, f32[8,128]{1,0:T(8,128)}, f32[8,128]{1,0:T(8,128)}) custom-call(f32[2,32,8,128]{3,2,1,0:T(8,128)} %get-tuple-element.35.refs_0_, f32[64,128]{1,0:T(8,128)} %copy-done.5, f32[64,128]{1,0:T(8,128)} %copy-done.6, f32[8,128]{1,0:T(8,128)} %copy-done.11, ...), custom_call_target="tpu_custom_call" | custom-call | tf_op jit(solution)/shard_map/pallas_call | solution.py:333
  81.3 1.9 %collective-permute-start.8 = (f32[64,128]{1,0:T(8,128)}, f32[64,128]{1,0:T(8,128)S(1)}, u32[]{:S(2)}, u32[]{:S(2)}) collective-permute-start(f32[64,128]{1,0:T(8,128)} %get-tuple-element.41), channel_id=1, source_target_pairs={{0,16},{16,32},{32,48},{48,64},{64,80},{80,96},{96,112},{112,128},... | collective-permute-start | bytes 98312 | tf_op jit(solution)/shard_map/ppermute | solution.py:349
  83.2 6.0 %collective-permute-start.9 = (f32[64,128]{1,0:T(8,128)}, f32[64,128]{1,0:T(8,128)S(1)}, u32[]{:S(2)}, u32[]{:S(2)}) collective-permute-start(f32[64,128]{1,0:T(8,128)} %get-tuple-element.42), channel_id=1, source_target_pairs={{16,0},{32,16},{48,32},{64,48},{80,64},{96,80},{112,96},{128,112},... | collective-permute-start | bytes 98312 | tf_op jit(solution)/shard_map/ppermute | solution.py:349
  89.2 2.7 %collective-permute-start.10 = (f32[8,128]{1,0:T(8,128)}, f32[8,128]{1,0:T(8,128)S(1)}, u32[]{:S(2)}, u32[]{:S(2)}) collective-permute-start(f32[8,128]{1,0:T(8,128)} %get-tuple-element.43), channel_id=1, source_target_pairs={{0,1},{1,2},{2,3},{3,4},{4,5},{5,6},{6,7},{7,8},{8,9},{9,10},{10,1... | collective-permute-start | bytes 12296 | tf_op jit(solution)/shard_map/ppermute | solution.py:349
  92.0 5.2 %collective-permute-start.11 = (f32[8,128]{1,0:T(8,128)S(1)}, f32[8,128]{1,0:T(8,128)S(1)}, u32[]{:S(2)}, u32[]{:S(2)}) collective-permute-start(f32[8,128]{1,0:T(8,128)S(1)} %copy-done.18), channel_id=1, source_target_pairs={{1,0},{2,1},{3,2},{4,3},{5,4},{6,5},{7,6},{8,7},{9,8},{10,9},{11,1... | collective-permute-start | bytes 12296 | tf_op jit(solution)/shard_map/ppermute | solution.py:349
  97.2 4.8 %shard_map.80 = f32[2,32,8,128]{3,2,1,0:T(8,128)} custom-call(f32[2,32,8,128]{3,2,1,0:T(8,128)} %get-tuple-element.35.refs_0_, f32[64,128]{1,0:T(8,128)} %copy-done.5, f32[64,128]{1,0:T(8,128)} %copy-done.6, f32[8,128]{1,0:T(8,128)} %copy-done.11, f32[8,128]{1,0:T(8,128)} %copy-done.12, f32[4,8,128]{2,1,0:T(8,128)} %get-tuple-element.32.refs_5_.refs_10_, ...), custom_call_target="tpu_custom_call" | custom-call | tf_op jit(solution)/shard_map/pallas_call | solution.py:296
  102.1 0.5 copy-done.13
  102.7 5.1 %shard_map.82 = f32[2,32,8,128]{3,2,1,0:T(8,128)} custom-call(f32[2,32,8,128]{3,2,1,0:T(8,128)} %get-tuple-element.27.refs_0_, f32[64,128]{1,0:T(8,128)} %get-tuple-element.28.refs_1_, f32[64,128]{1,0:T(8,128)} %get-tuple-element.29.refs_2_, f32[8,128]{1,0:T(8,128)} %get-tuple-element.30.refs_3_, f32[8,128]{1,0:T(8,128)} %get-tuple-element.31.refs_4_, ...), custom_call_target="tpu_custom_call" | custom-call | tf_op jit(solution)/shard_map/pallas_call | solution.py:333
  (88 shorter events, 1.7 us)
Async XLA Ops:
  0.6 1.4 %copy-start.15 = (bf16[2,32,1,1]{1,0,3,2:T(2,128)(2,1)S(1)}, bf16[2,32,1,1]{1,0,3,2:T(2,128)(2,1)}, u32[]{:S(2)}) copy-start(bf16[2,32,1,1]{1,0,3,2:T(2,128)(2,1)} %param.13) | copy-start | bytes 388
  4.5 10.1 %collective-permute-start = (f32[136,128]{1,0:T(8,128)}, f32[136,128]{1,0:T(8,128)S(1)}, u32[]{:S(2)}, u32[]{:S(2)}) collective-permute-start(f32[136,128]{1,0:T(8,128)} %get-tuple-element.25), channel_id=1, source_target_pairs={{0,16},{16,32},{32,48},{48,64},{64,80},{80,96},{96,112},{112,128},... | collective-permute-start | bytes 208904 | tf_op jit(solution)/shard_map/ppermute | solution.py:349
  8.0 6.7 %collective-permute-start.1 = (f32[136,128]{1,0:T(8,128)}, f32[136,128]{1,0:T(8,128)S(1)}, u32[]{:S(2)}, u32[]{:S(2)}) collective-permute-start(f32[136,128]{1,0:T(8,128)} %get-tuple-element.26), channel_id=1, source_target_pairs={{16,0},{32,16},{48,32},{64,48},{80,64},{96,80},{112,96},{128,112},... | collective-permute-start | bytes 208904 | tf_op jit(solution)/shard_map/ppermute | solution.py:349
  12.5 0.7 copy-start
  14.6 0.6 copy-start.1
  14.7 0.9 copy-start.4
  14.7 0.7 copy-start.2
  16.3 14.1 %all-to-all-start = ((bf16[16,6,8,128]{3,2,1,0:T(8,128)(2,1)}), bf16[16,6,8,128]{3,2,1,0:T(8,128)(2,1)S(1)}, u32[]{:S(2)}, u32[]{:S(2)}) async-start(bf16[16,6,8,128]{3,2,1,0:T(8,128)(2,1)} %pad_maximum_fusion.1), calls=%async_computation | async-start | bytes 393216 | tf_op jit(solution)/shard_map/all_to_all | solution.py:375
  36.0 5.6 %copy-start.17 = (f32[8,128]{1,0:T(8,128)S(1)}, f32[8,128]{1,0:T(8,128)}, u32[]{:S(2)}) copy-start(f32[8,128]{1,0:T(8,128)} %get-tuple-element.33) | copy-start | bytes 12292
  36.0 7.6 %copy-start.16 = (f32[8,128]{1,0:T(8,128)S(1)}, f32[8,128]{1,0:T(8,128)}, u32[]{:S(2)}) copy-start(f32[8,128]{1,0:T(8,128)} %get-tuple-element.34) | copy-start | bytes 12292
  36.0 13.6 %all-to-all-start.1 = ((bf16[16,8,8,128]{3,2,1,0:T(8,128)(2,1)}), bf16[16,8,8,128]{3,2,1,0:T(8,128)(2,1)S(1)}, u32[]{:S(2)}, u32[]{:S(2)}) async-start(bf16[16,8,8,128]{3,2,1,0:T(8,128)(2,1)} %pad_maximum_fusion), calls=%async_computation.1 | async-start | bytes 524288 | tf_op jit(solution)/shard_map/all_to_all | solution.py:397
  41.5 11.0 %collective-permute-start.2 = (f32[8,128]{1,0:T(8,128)S(1)}, f32[8,128]{1,0:T(8,128)S(1)}, u32[]{:S(2)}, u32[]{:S(2)}) collective-permute-start(f32[8,128]{1,0:T(8,128)S(1)} %copy-done.17), channel_id=1, source_target_pairs={{0,1},{1,2},{2,3},{3,4},{4,5},{5,6},{6,7},{7,8},{8,9},{9,10},{10,1... | collective-permute-start | bytes 12296 | tf_op jit(solution)/shard_map/ppermute | solution.py:349
  43.6 8.9 %collective-permute-start.3 = (f32[8,128]{1,0:T(8,128)S(1)}, f32[8,128]{1,0:T(8,128)S(1)}, u32[]{:S(2)}, u32[]{:S(2)}) collective-permute-start(f32[8,128]{1,0:T(8,128)S(1)} %copy-done.16), channel_id=1, source_target_pairs={{1,0},{2,1},{3,2},{4,3},{5,4},{6,5},{7,6},{8,7},{9,8},{10,9},{11,1... | collective-permute-start | bytes 12296 | tf_op jit(solution)/shard_map/ppermute | solution.py:349
  49.5 1.1 %copy-start.3 = (bf16[16,8,8,128]{3,2,1,0:T(8,128)(2,1)}, bf16[16,8,8,128]{3,2,1,0:T(8,128)(2,1)S(1)}, u32[]{:S(2)}) copy-start(bf16[16,8,8,128]{3,2,1,0:T(8,128)(2,1)S(1)} %all-to-all-done.1.r_ref) | copy-start | bytes 786436
  52.5 0.6 copy-start.7
  52.5 0.6 copy-start.8
  58.1 9.9 %copy-start.19 = (f32[8,128]{1,0:T(8,128)S(1)}, f32[8,128]{1,0:T(8,128)}, u32[]{:S(2)}) copy-start(f32[8,128]{1,0:T(8,128)} %get-tuple-element.39) | copy-start | bytes 12292
  58.1 17.3 %collective-permute-start.4 = (f32[64,128]{1,0:T(8,128)}, f32[64,128]{1,0:T(8,128)S(1)}, u32[]{:S(2)}, u32[]{:S(2)}) collective-permute-start(f32[64,128]{1,0:T(8,128)} %get-tuple-element.36), channel_id=1, source_target_pairs={{0,16},{16,32},{32,48},{48,64},{64,80},{80,96},{96,112},{112,128},... | collective-permute-start | bytes 98312 | tf_op jit(solution)/shard_map/ppermute | solution.py:349
  60.8 14.6 %collective-permute-start.5 = (f32[64,128]{1,0:T(8,128)}, f32[64,128]{1,0:T(8,128)S(1)}, u32[]{:S(2)}, u32[]{:S(2)}) collective-permute-start(f32[64,128]{1,0:T(8,128)} %get-tuple-element.37), channel_id=1, source_target_pairs={{16,0},{32,16},{48,32},{64,48},{80,64},{96,80},{112,96},{128,112},... | collective-permute-start | bytes 98312 | tf_op jit(solution)/shard_map/ppermute | solution.py:349
  66.0 8.0 %collective-permute-start.6 = (f32[8,128]{1,0:T(8,128)}, f32[8,128]{1,0:T(8,128)S(1)}, u32[]{:S(2)}, u32[]{:S(2)}) collective-permute-start(f32[8,128]{1,0:T(8,128)} %get-tuple-element.38), channel_id=1, source_target_pairs={{0,1},{1,2},{2,3},{3,4},{4,5},{5,6},{6,7},{7,8},{8,9},{9,10},{10,1... | collective-permute-start | bytes 12296 | tf_op jit(solution)/shard_map/ppermute | solution.py:349
  68.0 7.4 %collective-permute-start.7 = (f32[8,128]{1,0:T(8,128)S(1)}, f32[8,128]{1,0:T(8,128)S(1)}, u32[]{:S(2)}, u32[]{:S(2)}) collective-permute-start(f32[8,128]{1,0:T(8,128)S(1)} %copy-done.19), channel_id=1, source_target_pairs={{1,0},{2,1},{3,2},{4,3},{5,4},{6,5},{7,6},{8,7},{9,8},{10,9},{11,1... | collective-permute-start | bytes 12296 | tf_op jit(solution)/shard_map/ppermute | solution.py:349
  74.0 1.3 %copy-start.11 = (f32[8,128]{1,0:T(8,128)}, f32[8,128]{1,0:T(8,128)S(1)}, u32[]{:S(2)}) copy-start(f32[8,128]{1,0:T(8,128)S(1)} %collective-permute-done.6.refs_3_) | copy-start | bytes 12292
  75.3 0.6 copy-start.12
  75.3 0.6 copy-start.5
  75.4 0.6 copy-start.6
  81.3 10.7 %copy-start.18 = (f32[8,128]{1,0:T(8,128)S(1)}, f32[8,128]{1,0:T(8,128)}, u32[]{:S(2)}) copy-start(f32[8,128]{1,0:T(8,128)} %get-tuple-element.44) | copy-start | bytes 12292
  81.3 20.8 %collective-permute-start.8 = (f32[64,128]{1,0:T(8,128)}, f32[64,128]{1,0:T(8,128)S(1)}, u32[]{:S(2)}, u32[]{:S(2)}) collective-permute-start(f32[64,128]{1,0:T(8,128)} %get-tuple-element.41), channel_id=1, source_target_pairs={{0,16},{16,32},{32,48},{48,64},{64,80},{80,96},{96,112},{112,128},... | collective-permute-start | bytes 98312 | tf_op jit(solution)/shard_map/ppermute | solution.py:349
  83.2 18.9 %collective-permute-start.9 = (f32[64,128]{1,0:T(8,128)}, f32[64,128]{1,0:T(8,128)S(1)}, u32[]{:S(2)}, u32[]{:S(2)}) collective-permute-start(f32[64,128]{1,0:T(8,128)} %get-tuple-element.42), channel_id=1, source_target_pairs={{16,0},{32,16},{48,32},{64,48},{80,64},{96,80},{112,96},{128,112},... | collective-permute-start | bytes 98312 | tf_op jit(solution)/shard_map/ppermute | solution.py:349
  89.2 12.8 %collective-permute-start.10 = (f32[8,128]{1,0:T(8,128)}, f32[8,128]{1,0:T(8,128)S(1)}, u32[]{:S(2)}, u32[]{:S(2)}) collective-permute-start(f32[8,128]{1,0:T(8,128)} %get-tuple-element.43), channel_id=1, source_target_pairs={{0,1},{1,2},{2,3},{3,4},{4,5},{5,6},{6,7},{7,8},{8,9},{9,10},{10,1... | collective-permute-start | bytes 12296 | tf_op jit(solution)/shard_map/ppermute | solution.py:349
  92.0 10.1 %collective-permute-start.11 = (f32[8,128]{1,0:T(8,128)S(1)}, f32[8,128]{1,0:T(8,128)S(1)}, u32[]{:S(2)}, u32[]{:S(2)}) collective-permute-start(f32[8,128]{1,0:T(8,128)S(1)} %copy-done.18), channel_id=1, source_target_pairs={{1,0},{2,1},{3,2},{4,3},{5,4},{6,5},{7,6},{8,7},{9,8},{10,9},{11,1... | collective-permute-start | bytes 12296 | tf_op jit(solution)/shard_map/ppermute | solution.py:349
  102.1 0.6 copy-start.13
  102.1 0.6 copy-start.14
  102.1 0.6 copy-start.9
  102.1 0.6 copy-start.10

commit v3 on v2

--- a/solution.py
+++ b/solution.py
@@ -7,6 +7,7 @@
 
 F32 = jnp.float32
 NCOEF = 4
+UNROLL = 4
 VMEM = pltpu.MemorySpace.VMEM
 SMEM = pltpu.MemorySpace.SMEM
 
@@ -124,7 +125,7 @@
         o_ref[1, z] = t + 0.5 * f1
         return carry
 
-    lax.fori_loop(0, nz, body, 0)
+    lax.fori_loop(0, nz, body, 0, unroll=UNROLL)
 
 
 def _adjoint_body(s_ref, sh, a_ref, ah, cs, o_ref, nz, masks):
@@ -175,7 +176,7 @@
         o_ref[1, z] = a1 + 0.5 * jt
         return carry
 
-    lax.fori_loop(0, nz, body, 0)
+    lax.fori_loop(0, nz, body, 0, unroll=UNROLL)
 
 
 def _halo_scratch(nf, nz, x, y):

time: 109 us -> 101 us (0.927)
  Pallas kernels: 23.9 us -> 16.5 us
    pallas_call x2, Pallas kernels: 9.78 us -> 5.83 us  [step_call(): pl.pallas_call(kernel, out_shape=out_shape, scratch_shapes=_halo_scratch(...]
    pallas_call x2, Pallas kernels: 10.4 us -> 7.02 us  [adjoint_call(): pl.pallas_call(kernel, out_shape=out_shape, scratch_shapes=_halo_scratch(...]
  transfers between devices with their start and end apart: 14 -> 14, of which waited for: 2 -> 2; matrix products, arithmetic and copies ran while one was open for 2% -> 3% of each run, Pallas kernels for 6% -> 5%
where the time goes in v3:
time: 101 us
  starting transfers between devices  60.8 us (60%)
  Pallas kernels  16.5 us (16%)
  local copies, waits for them, and re-layouts  12.1 us (12%)
  waiting for transfers between devices  7.91 us (8%)
  other arithmetic  1.99 us (2%)
  between operations  1.18 us (1%)
    ppermute x12, starting transfers between devices, _shift(): return lax.ppermute(v, axis, pairs)  47.7 us
    all_to_all x1, starting transfers between devices, route_blocks(): lax.all_to_all(jnp.concatenate([slab, halo, sc], axis=1), 'gy', 0, 0, til...  7.48 us
    pallas_call x2, Pallas kernels, adjoint_call(): pl.pallas_call(kernel, out_shape=out_shape, scratch_shapes=_halo_scratch(...  7.02 us
    all_to_all x1, waiting for transfers between devices, route_blocks(): lax.all_to_all(jnp.concatenate([slab, halo, sc], axis=1), 'gy', 0, 0, til...  6.59 us
    pallas_call x2, Pallas kernels, step_call(): pl.pallas_call(kernel, out_shape=out_shape, scratch_shapes=_halo_scratch(...  5.83 us
    all_to_all x1, starting transfers between devices, route_blocks(): return lax.all_to_all(forward, 'gy', 0, 0, tiled=True)  5.56 us
    unnamed x43, local copies, waits for them, and re-layouts  4.55 us
  transfers between devices with their start and end apart: 14, of which 2 were waited for; matrix products, arithmetic and copies ran while one was open for 3% of the time, Pallas kernels for 5%

profile of v3, /device:TPU:130, one launch (start us, length us, event | category | flops | bytes accessed | tf_op | source)
XLA Modules:
  0.0 100.5 jit_solution(5745017769844728690)
XLA Ops:
  0.6 1.4 %copy.58.tab_ref = f32[12,4]{1,0:T(8,128)} copy(f32[12,4]{0,1:T(4,128)} %param.16) | data formatting | bytes 384 | tf_op args[4]
  2.0 0.7 reshape.112.sc_ref
  2.7 1.8 %shard_map.77 = (f32[4,8,128]{2,1,0:T(8,128)}, f32[136,128]{1,0:T(8,128)}, f32[136,128]{1,0:T(8,128)}, f32[8,128]{1,0:T(8,128)}, f32[8,128]{1,0:T(8,128)}) custom-call(s32[8,128]{1,0:T(8,128)} %cls_ref.1, f32[12,4]{1,0:T(8,128)} %copy.58.tab_ref, f32[64]{0:T(128)} %reshape.112.sc_ref, f32[2,32,8,128]{3,2,1,0:T(8,128)} %refs_5_.1, ...), custom_call_target="tpu_custom_call" | custom-call | tf_op jit(solution)/shard_map/pallas_call | solution.py:228
  4.5 3.5 %collective-permute-start = (f32[136,128]{1,0:T(8,128)}, f32[136,128]{1,0:T(8,128)S(1)}, u32[]{:S(2)}, u32[]{:S(2)}) collective-permute-start(f32[136,128]{1,0:T(8,128)} %get-tuple-element.25), channel_id=1, source_target_pairs={{0,16},{16,32},{32,48},{48,64},{64,80},{80,96},{96,112},{112,128},... | collective-permute-start | bytes 208904 | tf_op jit(solution)/shard_map/ppermute | solution.py:350
  8.0 4.5 %collective-permute-start.1 = (f32[136,128]{1,0:T(8,128)}, f32[136,128]{1,0:T(8,128)S(1)}, u32[]{:S(2)}, u32[]{:S(2)}) collective-permute-start(f32[136,128]{1,0:T(8,128)} %get-tuple-element.26), channel_id=1, source_target_pairs={{16,0},{32,16},{48,32},{64,48},{80,64},{96,80},{112,96},{128,112},... | collective-permute-start | bytes 208904 | tf_op jit(solution)/shard_map/ppermute | solution.py:350
  12.6 0.6 copy-done
  13.2 0.7 gather_fusion.3
  13.9 0.7 gather_fusion.1
  14.7 0.5 copy-done.1
  15.6 0.7 pad_maximum_fusion.1
  16.3 7.5 %all-to-all-start = ((bf16[16,6,8,128]{3,2,1,0:T(8,128)(2,1)}), bf16[16,6,8,128]{3,2,1,0:T(8,128)(2,1)S(1)}, u32[]{:S(2)}, u32[]{:S(2)}) async-start(bf16[16,6,8,128]{3,2,1,0:T(8,128)(2,1)} %pad_maximum_fusion.1), calls=%async_computation | async-start | bytes 393216 | tf_op jit(solution)/shard_map/all_to_all | solution.py:376
  23.8 6.6 %all-to-all-done = bf16[16,6,8,128]{3,2,1,0:T(8,128)(2,1)S(1)} async-done(((bf16[16,6,8,128]{3,2,1,0:T(8,128)(2,1)}), bf16[16,6,8,128]{3,2,1,0:T(8,128)(2,1)S(1)}, u32[]{:S(2)}, u32[]{:S(2)}) %all-to-all-start) | async-done | bytes 196640 | tf_op jit(solution)/shard_map/all_to_all | solution.py:376
  30.4 0.1 fusion.16
  30.5 0.3 copy.64
  30.8 0.1 copy.65
  30.9 0.3 copy.62
  31.2 0.1 copy.63
  31.4 0.1 copy.67
  31.5 0.6 gather_fusion.4
  32.1 0.6 gather_fusion.6
  32.7 0.6 gather_fusion.5
  33.3 0.6 gather_fusion.2
  33.8 0.1 select_select_fusion
  34.0 0.1 select_select_fusion.1
  34.5 0.6 gather_fusion
  35.2 0.7 pad_maximum_fusion
  36.0 5.6 %all-to-all-start.1 = ((bf16[16,8,8,128]{3,2,1,0:T(8,128)(2,1)}), bf16[16,8,8,128]{3,2,1,0:T(8,128)(2,1)S(1)}, u32[]{:S(2)}, u32[]{:S(2)}) async-start(bf16[16,8,8,128]{3,2,1,0:T(8,128)(2,1)} %pad_maximum_fusion), calls=%async_computation.1 | async-start | bytes 524288 | tf_op jit(solution)/shard_map/all_to_all | solution.py:398
  41.5 2.1 %collective-permute-start.2 = (f32[8,128]{1,0:T(8,128)S(1)}, f32[8,128]{1,0:T(8,128)S(1)}, u32[]{:S(2)}, u32[]{:S(2)}) collective-permute-start(f32[8,128]{1,0:T(8,128)S(1)} %copy-done.17), channel_id=1, source_target_pairs={{0,1},{1,2},{2,3},{3,4},{4,5},{5,6},{6,7},{7,8},{8,9},{9,10},{10,1... | collective-permute-start | bytes 12296 | tf_op jit(solution)/shard_map/ppermute | solution.py:350
  43.6 5.9 %collective-permute-start.3 = (f32[8,128]{1,0:T(8,128)S(1)}, f32[8,128]{1,0:T(8,128)S(1)}, u32[]{:S(2)}, u32[]{:S(2)}) collective-permute-start(f32[8,128]{1,0:T(8,128)S(1)} %copy-done.16), channel_id=1, source_target_pairs={{1,0},{2,1},{3,2},{4,3},{5,4},{6,5},{7,6},{8,7},{9,8},{10,9},{11,1... | collective-permute-start | bytes 12296 | tf_op jit(solution)/shard_map/ppermute | solution.py:350
  49.8 0.1 copy.75
  50.0 0.7 reshape.113.sc_ref
  50.7 1.9 %shard_map.78 = (f32[2,32,8,128]{3,2,1,0:T(8,128)}, f32[64,128]{1,0:T(8,128)}, f32[64,128]{1,0:T(8,128)}, f32[8,128]{1,0:T(8,128)}, f32[8,128]{1,0:T(8,128)}) custom-call(f32[320]{0:T(512)} %reshape.113.sc_ref, bf16[16,8,8,128]{3,2,1,0:T(8,128)(2,1)} %copy-done.3), custom_call_target="tpu_custom_call" | custom-call | tf_op jit(solution)/shard_map/pallas_call | solution.py:264
  52.6 0.6 copy-done.7
  53.1 3.0 %shard_map.79 = (f32[2,32,8,128]{3,2,1,0:T(8,128)}, f32[64,128]{1,0:T(8,128)}, f32[64,128]{1,0:T(8,128)}, f32[8,128]{1,0:T(8,128)}, f32[8,128]{1,0:T(8,128)}) custom-call(f32[2,32,8,128]{3,2,1,0:T(8,128)} %get-tuple-element.27.refs_0_, f32[64,128]{1,0:T(8,128)} %get-tuple-element.28.refs_1_, f32[64,128]{1,0:T(8,128)} %get-tuple-element.29.refs_2_, ...), custom_call_target="tpu_custom_call" | custom-call | tf_op jit(solution)/shard_map/pallas_call | solution.py:297
  56.1 2.7 %collective-permute-start.4 = (f32[64,128]{1,0:T(8,128)}, f32[64,128]{1,0:T(8,128)S(1)}, u32[]{:S(2)}, u32[]{:S(2)}) collective-permute-start(f32[64,128]{1,0:T(8,128)} %get-tuple-element.36), channel_id=1, source_target_pairs={{0,16},{16,32},{32,48},{48,64},{64,80},{80,96},{96,112},{112,128},... | collective-permute-start | bytes 98312 | tf_op jit(solution)/shard_map/ppermute | solution.py:350
  58.8 5.2 %collective-permute-start.5 = (f32[64,128]{1,0:T(8,128)}, f32[64,128]{1,0:T(8,128)S(1)}, u32[]{:S(2)}, u32[]{:S(2)}) collective-permute-start(f32[64,128]{1,0:T(8,128)} %get-tuple-element.37), channel_id=1, source_target_pairs={{16,0},{32,16},{48,32},{64,48},{80,64},{96,80},{112,96},{128,112},... | collective-permute-start | bytes 98312 | tf_op jit(solution)/shard_map/ppermute | solution.py:350
  64.1 1.9 %collective-permute-start.6 = (f32[8,128]{1,0:T(8,128)}, f32[8,128]{1,0:T(8,128)S(1)}, u32[]{:S(2)}, u32[]{:S(2)}) collective-permute-start(f32[8,128]{1,0:T(8,128)} %get-tuple-element.38), channel_id=1, source_target_pairs={{0,1},{1,2},{2,3},{3,4},{4,5},{5,6},{6,7},{7,8},{8,9},{9,10},{10,1... | collective-permute-start | bytes 12296 | tf_op jit(solution)/shard_map/ppermute | solution.py:350
  66.0 6.0 %collective-permute-start.7 = (f32[8,128]{1,0:T(8,128)S(1)}, f32[8,128]{1,0:T(8,128)S(1)}, u32[]{:S(2)}, u32[]{:S(2)}) collective-permute-start(f32[8,128]{1,0:T(8,128)S(1)} %copy-done.19), channel_id=1, source_target_pairs={{1,0},{2,1},{3,2},{4,3},{5,4},{6,5},{7,6},{8,7},{9,8},{10,9},{11,1... | collective-permute-start | bytes 12296 | tf_op jit(solution)/shard_map/ppermute | solution.py:350
  72.1 1.3 %collective-permute-done.7.refs_4_ = f32[8,128]{1,0:T(8,128)S(1)} collective-permute-done((f32[8,128]{1,0:T(8,128)S(1)}, f32[8,128]{1,0:T(8,128)S(1)}, u32[]{:S(2)}, u32[]{:S(2)}) %collective-permute-start.7) | collective-permute-done | bytes 4128 | tf_op jit(solution)/shard_map/ppermute | solution.py:350
  73.4 0.6 copy-done.12
  74.0 3.6 %shard_map.81 = (f32[2,32,8,128]{3,2,1,0:T(8,128)}, f32[64,128]{1,0:T(8,128)}, f32[64,128]{1,0:T(8,128)}, f32[8,128]{1,0:T(8,128)}, f32[8,128]{1,0:T(8,128)}) custom-call(f32[2,32,8,128]{3,2,1,0:T(8,128)} %get-tuple-element.35.refs_0_, f32[64,128]{1,0:T(8,128)} %copy-done.5, f32[64,128]{1,0:T(8,128)} %copy-done.6, f32[8,128]{1,0:T(8,128)} %copy-done.11, ...), custom_call_target="tpu_custom_call" | custom-call | tf_op jit(solution)/shard_map/pallas_call | solution.py:334
  77.6 1.9 %collective-permute-start.8 = (f32[64,128]{1,0:T(8,128)}, f32[64,128]{1,0:T(8,128)S(1)}, u32[]{:S(2)}, u32[]{:S(2)}) collective-permute-start(f32[64,128]{1,0:T(8,128)} %get-tuple-element.41), channel_id=1, source_target_pairs={{0,16},{16,32},{32,48},{48,64},{64,80},{80,96},{96,112},{112,128},... | collective-permute-start | bytes 98312 | tf_op jit(solution)/shard_map/ppermute | solution.py:350
  79.5 6.0 %collective-permute-start.9 = (f32[64,128]{1,0:T(8,128)}, f32[64,128]{1,0:T(8,128)S(1)}, u32[]{:S(2)}, u32[]{:S(2)}) collective-permute-start(f32[64,128]{1,0:T(8,128)} %get-tuple-element.42), channel_id=1, source_target_pairs={{16,0},{32,16},{48,32},{64,48},{80,64},{96,80},{112,96},{128,112},... | collective-permute-start | bytes 98312 | tf_op jit(solution)/shard_map/ppermute | solution.py:350
  85.6 2.7 %collective-permute-start.10 = (f32[8,128]{1,0:T(8,128)}, f32[8,128]{1,0:T(8,128)S(1)}, u32[]{:S(2)}, u32[]{:S(2)}) collective-permute-start(f32[8,128]{1,0:T(8,128)} %get-tuple-element.43), channel_id=1, source_target_pairs={{0,1},{1,2},{2,3},{3,4},{4,5},{5,6},{6,7},{7,8},{8,9},{9,10},{10,1... | collective-permute-start | bytes 12296 | tf_op jit(solution)/shard_map/ppermute | solution.py:350
  88.3 5.2 %collective-permute-start.11 = (f32[8,128]{1,0:T(8,128)S(1)}, f32[8,128]{1,0:T(8,128)S(1)}, u32[]{:S(2)}, u32[]{:S(2)}) collective-permute-start(f32[8,128]{1,0:T(8,128)S(1)} %copy-done.18), channel_id=1, source_target_pairs={{1,0},{2,1},{3,2},{4,3},{5,4},{6,5},{7,6},{8,7},{9,8},{10,9},{11,1... | collective-permute-start | bytes 12296 | tf_op jit(solution)/shard_map/ppermute | solution.py:350
  93.5 2.9 %shard_map.80 = f32[2,32,8,128]{3,2,1,0:T(8,128)} custom-call(f32[2,32,8,128]{3,2,1,0:T(8,128)} %get-tuple-element.35.refs_0_, f32[64,128]{1,0:T(8,128)} %copy-done.5, f32[64,128]{1,0:T(8,128)} %copy-done.6, f32[8,128]{1,0:T(8,128)} %copy-done.11, f32[8,128]{1,0:T(8,128)} %copy-done.12, f32[4,8,128]{2,1,0:T(8,128)} %get-tuple-element.32.refs_5_.refs_10_, ...), custom_call_target="tpu_custom_call" | custom-call | tf_op jit(solution)/shard_map/pallas_call | solution.py:297
  96.5 0.5 copy-done.13
  97.1 3.4 %shard_map.82 = f32[2,32,8,128]{3,2,1,0:T(8,128)} custom-call(f32[2,32,8,128]{3,2,1,0:T(8,128)} %get-tuple-element.27.refs_0_, f32[64,128]{1,0:T(8,128)} %get-tuple-element.28.refs_1_, f32[64,128]{1,0:T(8,128)} %get-tuple-element.29.refs_2_, f32[8,128]{1,0:T(8,128)} %get-tuple-element.30.refs_3_, f32[8,128]{1,0:T(8,128)} %get-tuple-element.31.refs_4_, ...), custom_call_target="tpu_custom_call" | custom-call | tf_op jit(solution)/shard_map/pallas_call | solution.py:334
  (88 shorter events, 1.7 us)
Async XLA Ops:
  0.6 1.4 %copy-start.15 = (bf16[2,32,1,1]{1,0,3,2:T(2,128)(2,1)S(1)}, bf16[2,32,1,1]{1,0,3,2:T(2,128)(2,1)}, u32[]{:S(2)}) copy-start(bf16[2,32,1,1]{1,0,3,2:T(2,128)(2,1)} %param.13) | copy-start | bytes 388
  4.5 10.1 %collective-permute-start = (f32[136,128]{1,0:T(8,128)}, f32[136,128]{1,0:T(8,128)S(1)}, u32[]{:S(2)}, u32[]{:S(2)}) collective-permute-start(f32[136,128]{1,0:T(8,128)} %get-tuple-element.25), channel_id=1, source_target_pairs={{0,16},{16,32},{32,48},{48,64},{64,80},{80,96},{96,112},{112,128},... | collective-permute-start | bytes 208904 | tf_op jit(solution)/shard_map/ppermute | solution.py:350
  8.0 6.7 %collective-permute-start.1 = (f32[136,128]{1,0:T(8,128)}, f32[136,128]{1,0:T(8,128)S(1)}, u32[]{:S(2)}, u32[]{:S(2)}) collective-permute-start(f32[136,128]{1,0:T(8,128)} %get-tuple-element.26), channel_id=1, source_target_pairs={{16,0},{32,16},{48,32},{64,48},{80,64},{96,80},{112,96},{128,112},... | collective-permute-start | bytes 208904 | tf_op jit(solution)/shard_map/ppermute | solution.py:350
  12.5 0.7 copy-start
  14.6 0.6 copy-start.1
  14.7 0.9 copy-start.4
  14.7 0.7 copy-start.2
  16.3 14.1 %all-to-all-start = ((bf16[16,6,8,128]{3,2,1,0:T(8,128)(2,1)}), bf16[16,6,8,128]{3,2,1,0:T(8,128)(2,1)S(1)}, u32[]{:S(2)}, u32[]{:S(2)}) async-start(bf16[16,6,8,128]{3,2,1,0:T(8,128)(2,1)} %pad_maximum_fusion.1), calls=%async_computation | async-start | bytes 393216 | tf_op jit(solution)/shard_map/all_to_all | solution.py:376
  36.0 5.6 %copy-start.17 = (f32[8,128]{1,0:T(8,128)S(1)}, f32[8,128]{1,0:T(8,128)}, u32[]{:S(2)}) copy-start(f32[8,128]{1,0:T(8,128)} %get-tuple-element.33) | copy-start | bytes 12292
  36.0 7.6 %copy-start.16 = (f32[8,128]{1,0:T(8,128)S(1)}, f32[8,128]{1,0:T(8,128)}, u32[]{:S(2)}) copy-start(f32[8,128]{1,0:T(8,128)} %get-tuple-element.34) | copy-start | bytes 12292
  36.0 13.6 %all-to-all-start.1 = ((bf16[16,8,8,128]{3,2,1,0:T(8,128)(2,1)}), bf16[16,8,8,128]{3,2,1,0:T(8,128)(2,1)S(1)}, u32[]{:S(2)}, u32[]{:S(2)}) async-start(bf16[16,8,8,128]{3,2,1,0:T(8,128)(2,1)} %pad_maximum_fusion), calls=%async_computation.1 | async-start | bytes 524288 | tf_op jit(solution)/shard_map/all_to_all | solution.py:398
  41.5 11.0 %collective-permute-start.2 = (f32[8,128]{1,0:T(8,128)S(1)}, f32[8,128]{1,0:T(8,128)S(1)}, u32[]{:S(2)}, u32[]{:S(2)}) collective-permute-start(f32[8,128]{1,0:T(8,128)S(1)} %copy-done.17), channel_id=1, source_target_pairs={{0,1},{1,2},{2,3},{3,4},{4,5},{5,6},{6,7},{7,8},{8,9},{9,10},{10,1... | collective-permute-start | bytes 12296 | tf_op jit(solution)/shard_map/ppermute | solution.py:350
  43.6 8.9 %collective-permute-start.3 = (f32[8,128]{1,0:T(8,128)S(1)}, f32[8,128]{1,0:T(8,128)S(1)}, u32[]{:S(2)}, u32[]{:S(2)}) collective-permute-start(f32[8,128]{1,0:T(8,128)S(1)} %copy-done.16), channel_id=1, source_target_pairs={{1,0},{2,1},{3,2},{4,3},{5,4},{6,5},{7,6},{8,7},{9,8},{10,9},{11,1... | collective-permute-start | bytes 12296 | tf_op jit(solution)/shard_map/ppermute | solution.py:350
  49.5 1.1 %copy-start.3 = (bf16[16,8,8,128]{3,2,1,0:T(8,128)(2,1)}, bf16[16,8,8,128]{3,2,1,0:T(8,128)(2,1)S(1)}, u32[]{:S(2)}) copy-start(bf16[16,8,8,128]{3,2,1,0:T(8,128)(2,1)S(1)} %all-to-all-done.1.r_ref) | copy-start | bytes 786436
  52.5 0.6 copy-start.7
  52.5 0.6 copy-start.8
  56.1 9.9 %copy-start.19 = (f32[8,128]{1,0:T(8,128)S(1)}, f32[8,128]{1,0:T(8,128)}, u32[]{:S(2)}) copy-start(f32[8,128]{1,0:T(8,128)} %get-tuple-element.39) | copy-start | bytes 12292
  56.1 17.3 %collective-permute-start.4 = (f32[64,128]{1,0:T(8,128)}, f32[64,128]{1,0:T(8,128)S(1)}, u32[]{:S(2)}, u32[]{:S(2)}) collective-permute-start(f32[64,128]{1,0:T(8,128)} %get-tuple-element.36), channel_id=1, source_target_pairs={{0,16},{16,32},{32,48},{48,64},{64,80},{80,96},{96,112},{112,128},... | collective-permute-start | bytes 98312 | tf_op jit(solution)/shard_map/ppermute | solution.py:350
  58.8 14.6 %collective-permute-start.5 = (f32[64,128]{1,0:T(8,128)}, f32[64,128]{1,0:T(8,128)S(1)}, u32[]{:S(2)}, u32[]{:S(2)}) collective-permute-start(f32[64,128]{1,0:T(8,128)} %get-tuple-element.37), channel_id=1, source_target_pairs={{16,0},{32,16},{48,32},{64,48},{80,64},{96,80},{112,96},{128,112},... | collective-permute-start | bytes 98312 | tf_op jit(solution)/shard_map/ppermute | solution.py:350
  64.1 8.0 %collective-permute-start.6 = (f32[8,128]{1,0:T(8,128)}, f32[8,128]{1,0:T(8,128)S(1)}, u32[]{:S(2)}, u32[]{:S(2)}) collective-permute-start(f32[8,128]{1,0:T(8,128)} %get-tuple-element.38), channel_id=1, source_target_pairs={{0,1},{1,2},{2,3},{3,4},{4,5},{5,6},{6,7},{7,8},{8,9},{9,10},{10,1... | collective-permute-start | bytes 12296 | tf_op jit(solution)/shard_map/ppermute | solution.py:350
  66.0 7.4 %collective-permute-start.7 = (f32[8,128]{1,0:T(8,128)S(1)}, f32[8,128]{1,0:T(8,128)S(1)}, u32[]{:S(2)}, u32[]{:S(2)}) collective-permute-start(f32[8,128]{1,0:T(8,128)S(1)} %copy-done.19), channel_id=1, source_target_pairs={{1,0},{2,1},{3,2},{4,3},{5,4},{6,5},{7,6},{8,7},{9,8},{10,9},{11,1... | collective-permute-start | bytes 12296 | tf_op jit(solution)/shard_map/ppermute | solution.py:350
  72.1 1.3 %copy-start.11 = (f32[8,128]{1,0:T(8,128)}, f32[8,128]{1,0:T(8,128)S(1)}, u32[]{:S(2)}) copy-start(f32[8,128]{1,0:T(8,128)S(1)} %collective-permute-done.6.refs_3_) | copy-start | bytes 12292
  73.4 0.6 copy-start.12
  73.4 0.6 copy-start.5
  73.4 0.6 copy-start.6
  77.6 10.7 %copy-start.18 = (f32[8,128]{1,0:T(8,128)S(1)}, f32[8,128]{1,0:T(8,128)}, u32[]{:S(2)}) copy-start(f32[8,128]{1,0:T(8,128)} %get-tuple-element.44) | copy-start | bytes 12292
  77.6 18.9 %collective-permute-start.8 = (f32[64,128]{1,0:T(8,128)}, f32[64,128]{1,0:T(8,128)S(1)}, u32[]{:S(2)}, u32[]{:S(2)}) collective-permute-start(f32[64,128]{1,0:T(8,128)} %get-tuple-element.41), channel_id=1, source_target_pairs={{0,16},{16,32},{32,48},{48,64},{64,80},{80,96},{96,112},{112,128},... | collective-permute-start | bytes 98312 | tf_op jit(solution)/shard_map/ppermute | solution.py:350
  79.5 16.9 %collective-permute-start.9 = (f32[64,128]{1,0:T(8,128)}, f32[64,128]{1,0:T(8,128)S(1)}, u32[]{:S(2)}, u32[]{:S(2)}) collective-permute-start(f32[64,128]{1,0:T(8,128)} %get-tuple-element.42), channel_id=1, source_target_pairs={{16,0},{32,16},{48,32},{64,48},{80,64},{96,80},{112,96},{128,112},... | collective-permute-start | bytes 98312 | tf_op jit(solution)/shard_map/ppermute | solution.py:350
  85.6 10.9 %collective-permute-start.10 = (f32[8,128]{1,0:T(8,128)}, f32[8,128]{1,0:T(8,128)S(1)}, u32[]{:S(2)}, u32[]{:S(2)}) collective-permute-start(f32[8,128]{1,0:T(8,128)} %get-tuple-element.43), channel_id=1, source_target_pairs={{0,1},{1,2},{2,3},{3,4},{4,5},{5,6},{6,7},{7,8},{8,9},{9,10},{10,1... | collective-permute-start | bytes 12296 | tf_op jit(solution)/shard_map/ppermute | solution.py:350
  88.3 8.1 %collective-permute-start.11 = (f32[8,128]{1,0:T(8,128)S(1)}, f32[8,128]{1,0:T(8,128)S(1)}, u32[]{:S(2)}, u32[]{:S(2)}) collective-permute-start(f32[8,128]{1,0:T(8,128)S(1)} %copy-done.18), channel_id=1, source_target_pairs={{1,0},{2,1},{3,2},{4,3},{5,4},{6,5},{7,6},{8,7},{9,8},{10,9},{11,1... | collective-permute-start | bytes 12296 | tf_op jit(solution)/shard_map/ppermute | solution.py:350
  96.4 0.6 copy-start.13
  96.4 0.6 copy-start.14
  96.5 0.6 copy-start.9
  96.5 0.6 copy-start.10

commit v4 on v3

--- a/solution.py
+++ b/solution.py
@@ -196,12 +196,11 @@
     return -(-n // 8) * 8
 
 
-def prep_call(soil_class, soil_table, cot, slab, scales):
+def prep_call(soil_class, soil_table, cot):
     nf, nz, x, y = cot.shape
     nclass = soil_table.shape[0]
-    nplanes = nf * nz
-
-    def kernel(cls_ref, tab_ref, sc_ref, cot_ref, slab_ref, coef_ref, xf_ref, xl_ref, yf_ref, yl_ref):
+
+    def kernel(cls_ref, tab_ref, cot_ref, coef_ref, xf_ref, xl_ref, yf_ref, yl_ref):
         cls = cls_ref[...]
         coefs = []
         for k in range(NCOEF):
@@ -212,32 +211,17 @@
             coefs.append(cv)
         vals = [cot_ref[f, z] for f in range(nf) for z in range(nz)] + coefs
         _pack_edges(vals, xf_ref, xl_ref, yf_ref, yl_ref)
-        base = len(vals)
-        for k in range(nplanes):
-            v = slab_ref[k // nz, k % nz].astype(F32)
-            xf_ref[base + k : base + k + 1, :] = v[0:1, :]
-            xl_ref[base + k : base + k + 1, :] = v[x - 1 : x, :]
-        _, lane = _iotas((1, y))
-        row = jnp.zeros((1, y), F32)
-        for k in range(nplanes):
-            row = jnp.where(lane == k, sc_ref[k], row)
-        xf_ref[base + nplanes : base + nplanes + 1, :] = row
-        xl_ref[base + nplanes : base + nplanes + 1, :] = row
-
-    rows = _rows(2 * nplanes + NCOEF + 1)
+
+    rows = _rows(nf * nz + NCOEF)
     return pl.pallas_call(
         kernel,
-        out_shape=(jax.ShapeDtypeStruct((NCOEF, x, y), F32),)
-        + _edge_shapes(rows, x, y)[:2]
-        + _edge_shapes(8, x, y)[2:],
+        out_shape=(jax.ShapeDtypeStruct((NCOEF, x, y), F32),) + _edge_shapes(rows, x, y),
         in_specs=[
             pl.BlockSpec(memory_space=VMEM),
             pl.BlockSpec(memory_space=SMEM),
-            pl.BlockSpec(memory_space=SMEM),
-            pl.BlockSpec(memory_space=VMEM),
             pl.BlockSpec(memory_space=VMEM),
         ],
-    )(soil_class, soil_table, scales, cot, slab)
+    )(soil_class, soil_table, cot)
 
 
 def state0_call(pieces, scales, nf, per):
@@ -398,17 +382,28 @@
     return lax.all_to_all(forward, "gy", 0, 0, tiled=True)
 
 
+def slab_edges(stored_slab, block_scales):
+    nf, nz, x, y = stored_slab.shape
+    nplanes = nf * nz
+    sc = jnp.pad(block_scales.reshape(1, nplanes), ((0, 7), (0, y - nplanes)))
+    first = jnp.concatenate([stored_slab[:, :, 0, :].reshape(nplanes, y), sc], axis=0)
+    last = jnp.concatenate([stored_slab[:, :, x - 1, :].reshape(nplanes, y), sc], axis=0)
+    return first, last
+
+
 def on_device(stored_slab, block_scales, holder, soil_class, soil_table, cotangent):
     nf, nz, x, y = stored_slab.shape
     nplanes = nf * nz
 
-    coef, cxf, cxl, cyf, cyl = prep_call(
-        soil_class, soil_table, cotangent, stored_slab, block_scales.reshape(-1).astype(F32)
-    )
+    sfirst, slast = slab_edges(stored_slab, block_scales)
+    pieces = route_blocks(
+        stored_slab, block_scales, holder, _shift(slast, "gx", 1), _shift(sfirst, "gx", -1), 0
+    )
+
+    coef, cxf, cxl, cyf, cyl = prep_call(soil_class, soil_table, cotangent)
     c_halo = exchange(cxf, cxl, cyf, cyl)
     c_first = nplanes
 
-    pieces = route_blocks(stored_slab, block_scales, holder, c_halo[0], c_halo[1], nplanes + NCOEF)
     per = nplanes // pieces.shape[0]
     scales = jnp.concatenate(
         [

time: 101 us -> 110 us (1.089)
  starting transfers between devices: 60.8 us -> 68.8 us
    ppermute x12 -> x14, starting transfers between devices: 47.7 us -> 55.8 us  [_shift(): return lax.ppermute(v, axis, pairs)]
    unnamed x43 -> x45, local copies, waits for them, and re-layouts: 4.55 us -> 4.42 us
  transfers between devices with their start and end apart: 14 -> 16, of which waited for: 2 -> 2; matrix products, arithmetic and copies ran while one was open for 3% -> 3% of each run, Pallas kernels for 5% -> 6%
where the time goes in v4:
time: 110 us; the launch traced here: 109 us
  starting transfers between devices  68.8 us (63%)
  Pallas kernels  16.3 us (15%)
  local copies, waits for them, and re-layouts  12.5 us (11%)
  waiting for transfers between devices  7.91 us (7%)
  other arithmetic  1.96 us (2%)
  between operations  1.21 us (1%)
    ppermute x14, starting transfers between devices, _shift(): return lax.ppermute(v, axis, pairs)  55.8 us
    all_to_all x1, starting transfers between devices, route_blocks(): lax.all_to_all(jnp.concatenate([slab, halo, sc], axis=1), 'gy', 0, 0, til...  7.48 us
    pallas_call x2, Pallas kernels, adjoint_call(): pl.pallas_call(kernel, out_shape=out_shape, scratch_shapes=_halo_scratch(...  6.92 us
    all_to_all x1, waiting for transfers between devices, route_blocks(): lax.all_to_all(jnp.concatenate([slab, halo, sc], axis=1), 'gy', 0, 0, til...  6.59 us
    pallas_call x2, Pallas kernels, step_call(): pl.pallas_call(kernel, out_shape=out_shape, scratch_shapes=_halo_scratch(...  5.75 us
    all_to_all x1, starting transfers between devices, route_blocks(): return lax.all_to_all(forward, 'gy', 0, 0, tiled=True)  5.56 us
    unnamed x45, local copies, waits for them, and re-layouts  4.42 us
  transfers between devices with their start and end apart: 16, of which 2 were waited for; matrix products, arithmetic and copies ran while one was open for 3% of the time, Pallas kernels for 6%

profile of v4, /device:TPU:130, one launch (start us, length us, event | category | flops | bytes accessed | tf_op | source)
XLA Modules:
  0.0 108.7 jit_solution(18422160636878496447)
XLA Ops:
  0.6 1.0 fusion.20
  1.7 0.6 copy-done.16
  2.4 3.5 %collective-permute-start = (bf16[72,128]{1,0:T(8,128)(2,1)S(1)}, bf16[72,128]{1,0:T(8,128)(2,1)S(1)}, u32[]{:S(2)}, u32[]{:S(2)}) collective-permute-start(bf16[72,128]{1,0:T(8,128)(2,1)S(1)} %get-tuple-element.53), channel_id=1, source_target_pairs={{0,16},{16,32},{32,48},{48,64},{64,80},{80,96},{96,112},{112,128},... | collective-permute-start | bytes 55304 | tf_op jit(solution)/shard_map/ppermute | solution.py:334
  5.9 4.5 %collective-permute-start.1 = (bf16[72,128]{1,0:T(8,128)(2,1)S(1)}, bf16[72,128]{1,0:T(8,128)(2,1)S(1)}, u32[]{:S(2)}, u32[]{:S(2)}) collective-permute-start(bf16[72,128]{1,0:T(8,128)(2,1)S(1)} %get-tuple-element.54), channel_id=1, source_target_pairs={{16,0},{32,16},{48,32},{64,48},{80,64},{96,80},{112,96},{128,112},... | collective-permute-start | bytes 55304 | tf_op jit(solution)/shard_map/ppermute | solution.py:334
  10.4 0.6 copy-done
  11.1 0.7 gather_fusion.3
  11.8 0.7 gather_fusion.1
  12.9 0.4 copy-done.4
  13.3 0.7 pad_maximum_fusion.1
  14.0 7.5 %all-to-all-start = ((bf16[16,6,8,128]{3,2,1,0:T(8,128)(2,1)}), bf16[16,6,8,128]{3,2,1,0:T(8,128)(2,1)S(1)}, u32[]{:S(2)}, u32[]{:S(2)}) async-start(bf16[16,6,8,128]{3,2,1,0:T(8,128)(2,1)} %pad_maximum_fusion.1), calls=%async_computation | async-start | bytes 393216 | tf_op jit(solution)/shard_map/all_to_all | solution.py:360
  21.5 6.6 %all-to-all-done = bf16[16,6,8,128]{3,2,1,0:T(8,128)(2,1)S(1)} async-done(((bf16[16,6,8,128]{3,2,1,0:T(8,128)(2,1)}), bf16[16,6,8,128]{3,2,1,0:T(8,128)(2,1)S(1)}, u32[]{:S(2)}, u32[]{:S(2)}) %all-to-all-start) | async-done | bytes 196640 | tf_op jit(solution)/shard_map/all_to_all | solution.py:360
  28.1 0.1 fusion.19
  28.2 0.3 copy.67
  28.6 0.3 copy.65
  29.2 0.6 gather_fusion.4
  29.8 0.6 gather_fusion.6
  30.4 0.6 gather_fusion.5
  31.0 0.6 gather_fusion.2
  31.6 0.1 select_select_fusion
  31.7 0.1 select_select_fusion.1
  32.3 0.6 gather_fusion
  33.0 0.7 pad_maximum_fusion
  33.7 5.6 %all-to-all-start.1 = ((bf16[16,8,8,128]{3,2,1,0:T(8,128)(2,1)}), bf16[16,8,8,128]{3,2,1,0:T(8,128)(2,1)S(1)}, u32[]{:S(2)}, u32[]{:S(2)}) async-start(bf16[16,8,8,128]{3,2,1,0:T(8,128)(2,1)} %pad_maximum_fusion), calls=%async_computation.1 | async-start | bytes 524288 | tf_op jit(solution)/shard_map/all_to_all | solution.py:382
  39.3 0.7 copy.79.tab_ref
  39.9 1.8 %shard_map.78 = (f32[4,8,128]{2,1,0:T(8,128)}, f32[72,128]{1,0:T(8,128)}, f32[72,128]{1,0:T(8,128)}, f32[8,128]{1,0:T(8,128)}, f32[8,128]{1,0:T(8,128)}) custom-call(s32[8,128]{1,0:T(8,128)} %cls_ref.1, f32[12,4]{1,0:T(8,128)} %copy.79.tab_ref, f32[2,32,8,128]{3,2,1,0:T(8,128)} %refs_5_.1), custom_call_target="tpu_custom_call" | custom-call | tf_op jit(solution)/shard_map/pallas_call | solution.py:216
  41.7 2.0 %collective-permute-start.2 = (f32[72,128]{1,0:T(8,128)}, f32[72,128]{1,0:T(8,128)S(1)}, u32[]{:S(2)}, u32[]{:S(2)}) collective-permute-start(f32[72,128]{1,0:T(8,128)} %get-tuple-element.31), channel_id=1, source_target_pairs={{0,16},{16,32},{32,48},{48,64},{64,80},{80,96},{96,112},{112,128},... | collective-permute-start | bytes 110600 | tf_op jit(solution)/shard_map/ppermute | solution.py:334
  43.8 6.0 %collective-permute-start.3 = (f32[72,128]{1,0:T(8,128)}, f32[72,128]{1,0:T(8,128)S(1)}, u32[]{:S(2)}, u32[]{:S(2)}) collective-permute-start(f32[72,128]{1,0:T(8,128)} %get-tuple-element.32), channel_id=1, source_target_pairs={{16,0},{32,16},{48,32},{64,48},{80,64},{96,80},{112,96},{128,112},... | collective-permute-start | bytes 110600 | tf_op jit(solution)/shard_map/ppermute | solution.py:334
  49.8 1.9 %collective-permute-start.4 = (f32[8,128]{1,0:T(8,128)}, f32[8,128]{1,0:T(8,128)S(1)}, u32[]{:S(2)}, u32[]{:S(2)}) collective-permute-start(f32[8,128]{1,0:T(8,128)} %get-tuple-element.33), channel_id=1, source_target_pairs={{0,1},{1,2},{2,3},{3,4},{4,5},{5,6},{6,7},{7,8},{8,9},{9,10},{10,1... | collective-permute-start | bytes 12296 | tf_op jit(solution)/shard_map/ppermute | solution.py:334
  51.8 6.0 %collective-permute-start.5 = (f32[8,128]{1,0:T(8,128)S(1)}, f32[8,128]{1,0:T(8,128)S(1)}, u32[]{:S(2)}, u32[]{:S(2)}) collective-permute-start(f32[8,128]{1,0:T(8,128)S(1)} %copy-done.17), channel_id=1, source_target_pairs={{1,0},{2,1},{3,2},{4,3},{5,4},{6,5},{7,6},{8,7},{9,8},{10,9},{11,1... | collective-permute-start | bytes 12296 | tf_op jit(solution)/shard_map/ppermute | solution.py:334
  58.1 0.1 copy.78
  58.3 0.7 reshape.89.sc_ref
  59.0 1.9 %shard_map.77 = (f32[2,32,8,128]{3,2,1,0:T(8,128)}, f32[64,128]{1,0:T(8,128)}, f32[64,128]{1,0:T(8,128)}, f32[8,128]{1,0:T(8,128)}, f32[8,128]{1,0:T(8,128)}) custom-call(f32[320]{0:T(512)} %reshape.89.sc_ref, bf16[16,8,8,128]{3,2,1,0:T(8,128)(2,1)} %copy-done.1), custom_call_target="tpu_custom_call" | custom-call | tf_op jit(solution)/shard_map/pallas_call | solution.py:248
  60.9 0.5 copy-done.7
  61.5 2.9 %shard_map.79 = (f32[2,32,8,128]{3,2,1,0:T(8,128)}, f32[64,128]{1,0:T(8,128)}, f32[64,128]{1,0:T(8,128)}, f32[8,128]{1,0:T(8,128)}, f32[8,128]{1,0:T(8,128)}) custom-call(f32[2,32,8,128]{3,2,1,0:T(8,128)} %get-tuple-element.25.refs_0_, f32[64,128]{1,0:T(8,128)} %get-tuple-element.26.refs_1_, f32[64,128]{1,0:T(8,128)} %get-tuple-element.27.refs_2_, ...), custom_call_target="tpu_custom_call" | custom-call | tf_op jit(solution)/shard_map/pallas_call | solution.py:281
  64.4 1.9 %collective-permute-start.6 = (f32[64,128]{1,0:T(8,128)}, f32[64,128]{1,0:T(8,128)S(1)}, u32[]{:S(2)}, u32[]{:S(2)}) collective-permute-start(f32[64,128]{1,0:T(8,128)} %get-tuple-element.36), channel_id=1, source_target_pairs={{0,16},{16,32},{32,48},{48,64},{64,80},{80,96},{96,112},{112,128},... | collective-permute-start | bytes 98312 | tf_op jit(solution)/shard_map/ppermute | solution.py:334
  66.4 6.0 %collective-permute-start.7 = (f32[64,128]{1,0:T(8,128)}, f32[64,128]{1,0:T(8,128)S(1)}, u32[]{:S(2)}, u32[]{:S(2)}) collective-permute-start(f32[64,128]{1,0:T(8,128)} %get-tuple-element.37), channel_id=1, source_target_pairs={{16,0},{32,16},{48,32},{64,48},{80,64},{96,80},{112,96},{128,112},... | collective-permute-start | bytes 98312 | tf_op jit(solution)/shard_map/ppermute | solution.py:334
  72.4 1.9 %collective-permute-start.8 = (f32[8,128]{1,0:T(8,128)}, f32[8,128]{1,0:T(8,128)S(1)}, u32[]{:S(2)}, u32[]{:S(2)}) collective-permute-start(f32[8,128]{1,0:T(8,128)} %get-tuple-element.38), channel_id=1, source_target_pairs={{0,1},{1,2},{2,3},{3,4},{4,5},{5,6},{6,7},{7,8},{8,9},{9,10},{10,1... | collective-permute-start | bytes 12296 | tf_op jit(solution)/shard_map/ppermute | solution.py:334
  74.4 6.0 %collective-permute-start.9 = (f32[8,128]{1,0:T(8,128)S(1)}, f32[8,128]{1,0:T(8,128)S(1)}, u32[]{:S(2)}, u32[]{:S(2)}) collective-permute-start(f32[8,128]{1,0:T(8,128)S(1)} %copy-done.19), channel_id=1, source_target_pairs={{1,0},{2,1},{3,2},{4,3},{5,4},{6,5},{7,6},{8,7},{9,8},{10,9},{11,1... | collective-permute-start | bytes 12296 | tf_op jit(solution)/shard_map/ppermute | solution.py:334
  80.4 1.3 %collective-permute-done.9.refs_4_ = f32[8,128]{1,0:T(8,128)S(1)} collective-permute-done((f32[8,128]{1,0:T(8,128)S(1)}, f32[8,128]{1,0:T(8,128)S(1)}, u32[]{:S(2)}, u32[]{:S(2)}) %collective-permute-start.9) | collective-permute-done | bytes 4128 | tf_op jit(solution)/shard_map/ppermute | solution.py:334
  81.7 0.6 copy-done.12
  82.3 3.5 %shard_map.81 = (f32[2,32,8,128]{3,2,1,0:T(8,128)}, f32[64,128]{1,0:T(8,128)}, f32[64,128]{1,0:T(8,128)}, f32[8,128]{1,0:T(8,128)}, f32[8,128]{1,0:T(8,128)}) custom-call(f32[2,32,8,128]{3,2,1,0:T(8,128)} %get-tuple-element.35.refs_0_, f32[64,128]{1,0:T(8,128)} %copy-done.5, f32[64,128]{1,0:T(8,128)} %copy-done.6, f32[8,128]{1,0:T(8,128)} %copy-done.11, ...), custom_call_target="tpu_custom_call" | custom-call | tf_op jit(solution)/shard_map/pallas_call | solution.py:318
  85.9 1.9 %collective-permute-start.10 = (f32[64,128]{1,0:T(8,128)}, f32[64,128]{1,0:T(8,128)S(1)}, u32[]{:S(2)}, u32[]{:S(2)}) collective-permute-start(f32[64,128]{1,0:T(8,128)} %get-tuple-element.41), channel_id=1, source_target_pairs={{0,16},{16,32},{32,48},{48,64},{64,80},{80,96},{96,112},{112,128},... | collective-permute-start | bytes 98312 | tf_op jit(solution)/shard_map/ppermute | solution.py:334
  87.8 6.0 %collective-permute-start.11 = (f32[64,128]{1,0:T(8,128)}, f32[64,128]{1,0:T(8,128)S(1)}, u32[]{:S(2)}, u32[]{:S(2)}) collective-permute-start(f32[64,128]{1,0:T(8,128)} %get-tuple-element.42), channel_id=1, source_target_pairs={{16,0},{32,16},{48,32},{64,48},{80,64},{96,80},{112,96},{128,112},... | collective-permute-start | bytes 98312 | tf_op jit(solution)/shard_map/ppermute | solution.py:334
  93.9 2.6 %collective-permute-start.12 = (f32[8,128]{1,0:T(8,128)}, f32[8,128]{1,0:T(8,128)S(1)}, u32[]{:S(2)}, u32[]{:S(2)}) collective-permute-start(f32[8,128]{1,0:T(8,128)} %get-tuple-element.43), channel_id=1, source_target_pairs={{0,1},{1,2},{2,3},{3,4},{4,5},{5,6},{6,7},{7,8},{8,9},{9,10},{10,1... | collective-permute-start | bytes 12296 | tf_op jit(solution)/shard_map/ppermute | solution.py:334
  96.5 5.4 %collective-permute-start.13 = (f32[8,128]{1,0:T(8,128)S(1)}, f32[8,128]{1,0:T(8,128)S(1)}, u32[]{:S(2)}, u32[]{:S(2)}) collective-permute-start(f32[8,128]{1,0:T(8,128)S(1)} %copy-done.18), channel_id=1, source_target_pairs={{1,0},{2,1},{3,2},{4,3},{5,4},{6,5},{7,6},{8,7},{9,8},{10,9},{11,1... | collective-permute-start | bytes 12296 | tf_op jit(solution)/shard_map/ppermute | solution.py:334
  101.8 2.8 %shard_map.80 = f32[2,32,8,128]{3,2,1,0:T(8,128)} custom-call(f32[2,32,8,128]{3,2,1,0:T(8,128)} %get-tuple-element.35.refs_0_, f32[64,128]{1,0:T(8,128)} %copy-done.5, f32[64,128]{1,0:T(8,128)} %copy-done.6, f32[8,128]{1,0:T(8,128)} %copy-done.11, f32[8,128]{1,0:T(8,128)} %copy-done.12, f32[4,8,128]{2,1,0:T(8,128)} %get-tuple-element.30.refs_5_.refs_10_, ...), custom_call_target="tpu_custom_call" | custom-call | tf_op jit(solution)/shard_map/pallas_call | solution.py:281
  104.7 0.5 copy-done.13
  105.3 3.4 %shard_map.82 = f32[2,32,8,128]{3,2,1,0:T(8,128)} custom-call(f32[2,32,8,128]{3,2,1,0:T(8,128)} %get-tuple-element.25.refs_0_, f32[64,128]{1,0:T(8,128)} %get-tuple-element.26.refs_1_, f32[64,128]{1,0:T(8,128)} %get-tuple-element.27.refs_2_, f32[8,128]{1,0:T(8,128)} %get-tuple-element.28.refs_3_, f32[8,128]{1,0:T(8,128)} %get-tuple-element.29.refs_4_, ...), custom_call_target="tpu_custom_call" | custom-call | tf_op jit(solution)/shard_map/pallas_call | solution.py:318
  (93 shorter events, 2.1 us)
Async XLA Ops:
  1.7 0.7 copy-start.16
  2.4 10.1 %collective-permute-start = (bf16[72,128]{1,0:T(8,128)(2,1)S(1)}, bf16[72,128]{1,0:T(8,128)(2,1)S(1)}, u32[]{:S(2)}, u32[]{:S(2)}) collective-permute-start(bf16[72,128]{1,0:T(8,128)(2,1)S(1)} %get-tuple-element.53), channel_id=1, source_target_pairs={{0,16},{16,32},{32,48},{48,64},{64,80},{80,96},{96,112},{112,128},... | collective-permute-start | bytes 55304 | tf_op jit(solution)/shard_map/ppermute | solution.py:334
  5.9 6.8 %collective-permute-start.1 = (bf16[72,128]{1,0:T(8,128)(2,1)S(1)}, bf16[72,128]{1,0:T(8,128)(2,1)S(1)}, u32[]{:S(2)}, u32[]{:S(2)}) collective-permute-start(bf16[72,128]{1,0:T(8,128)(2,1)S(1)} %get-tuple-element.54), channel_id=1, source_target_pairs={{16,0},{32,16},{48,32},{64,48},{80,64},{96,80},{112,96},{128,112},... | collective-permute-start | bytes 55304 | tf_op jit(solution)/shard_map/ppermute | solution.py:334
  10.4 0.7 copy-start
  12.4 0.9 copy-start.4
  14.0 14.1 %all-to-all-start = ((bf16[16,6,8,128]{3,2,1,0:T(8,128)(2,1)}), bf16[16,6,8,128]{3,2,1,0:T(8,128)(2,1)S(1)}, u32[]{:S(2)}, u32[]{:S(2)}) async-start(bf16[16,6,8,128]{3,2,1,0:T(8,128)(2,1)} %pad_maximum_fusion.1), calls=%async_computation | async-start | bytes 393216 | tf_op jit(solution)/shard_map/all_to_all | solution.py:360
  33.7 5.6 %copy-start.15 = (f32[12,4]{0,1:T(4,128)S(1)}, f32[12,4]{0,1:T(4,128)}, u32[]{:S(2)}) copy-start(f32[12,4]{0,1:T(4,128)} %param.16) | copy-start | bytes 580
  33.7 24.1 %all-to-all-start.1 = ((bf16[16,8,8,128]{3,2,1,0:T(8,128)(2,1)}), bf16[16,8,8,128]{3,2,1,0:T(8,128)(2,1)S(1)}, u32[]{:S(2)}, u32[]{:S(2)}) async-start(bf16[16,8,8,128]{3,2,1,0:T(8,128)(2,1)} %pad_maximum_fusion), calls=%async_computation.1 | async-start | bytes 524288 | tf_op jit(solution)/shard_map/all_to_all | solution.py:382
  41.7 10.0 %copy-start.17 = (f32[8,128]{1,0:T(8,128)S(1)}, f32[8,128]{1,0:T(8,128)}, u32[]{:S(2)}) copy-start(f32[8,128]{1,0:T(8,128)} %get-tuple-element.34) | copy-start | bytes 12292
  41.7 19.1 %collective-permute-start.2 = (f32[72,128]{1,0:T(8,128)}, f32[72,128]{1,0:T(8,128)S(1)}, u32[]{:S(2)}, u32[]{:S(2)}) collective-permute-start(f32[72,128]{1,0:T(8,128)} %get-tuple-element.31), channel_id=1, source_target_pairs={{0,16},{16,32},{32,48},{48,64},{64,80},{80,96},{96,112},{112,128},... | collective-permute-start | bytes 110600 | tf_op jit(solution)/shard_map/ppermute | solution.py:334
  43.8 17.1 %collective-permute-start.3 = (f32[72,128]{1,0:T(8,128)}, f32[72,128]{1,0:T(8,128)S(1)}, u32[]{:S(2)}, u32[]{:S(2)}) collective-permute-start(f32[72,128]{1,0:T(8,128)} %get-tuple-element.32), channel_id=1, source_target_pairs={{16,0},{32,16},{48,32},{64,48},{80,64},{96,80},{112,96},{128,112},... | collective-permute-start | bytes 110600 | tf_op jit(solution)/shard_map/ppermute | solution.py:334
  49.8 11.0 %collective-permute-start.4 = (f32[8,128]{1,0:T(8,128)}, f32[8,128]{1,0:T(8,128)S(1)}, u32[]{:S(2)}, u32[]{:S(2)}) collective-permute-start(f32[8,128]{1,0:T(8,128)} %get-tuple-element.33), channel_id=1, source_target_pairs={{0,1},{1,2},{2,3},{3,4},{4,5},{5,6},{6,7},{7,8},{8,9},{9,10},{10,1... | collective-permute-start | bytes 12296 | tf_op jit(solution)/shard_map/ppermute | solution.py:334
  51.8 9.1 %collective-permute-start.5 = (f32[8,128]{1,0:T(8,128)S(1)}, f32[8,128]{1,0:T(8,128)S(1)}, u32[]{:S(2)}, u32[]{:S(2)}) collective-permute-start(f32[8,128]{1,0:T(8,128)S(1)} %copy-done.17), channel_id=1, source_target_pairs={{1,0},{2,1},{3,2},{4,3},{5,4},{6,5},{7,6},{8,7},{9,8},{10,9},{11,1... | collective-permute-start | bytes 12296 | tf_op jit(solution)/shard_map/ppermute | solution.py:334
  57.8 1.1 %copy-start.1 = (bf16[16,8,8,128]{3,2,1,0:T(8,128)(2,1)}, bf16[16,8,8,128]{3,2,1,0:T(8,128)(2,1)S(1)}, u32[]{:S(2)}) copy-start(bf16[16,8,8,128]{3,2,1,0:T(8,128)(2,1)S(1)} %all-to-all-done.1.r_ref) | copy-start | bytes 786436
  60.8 0.6 copy-start.7
  60.9 0.6 copy-start.8
  60.9 0.6 copy-start.2
  60.9 0.6 copy-start.3
  64.4 9.9 %copy-start.19 = (f32[8,128]{1,0:T(8,128)S(1)}, f32[8,128]{1,0:T(8,128)}, u32[]{:S(2)}) copy-start(f32[8,128]{1,0:T(8,128)} %get-tuple-element.39) | copy-start | bytes 12292
  64.4 17.3 %collective-permute-start.6 = (f32[64,128]{1,0:T(8,128)}, f32[64,128]{1,0:T(8,128)S(1)}, u32[]{:S(2)}, u32[]{:S(2)}) collective-permute-start(f32[64,128]{1,0:T(8,128)} %get-tuple-element.36), channel_id=1, source_target_pairs={{0,16},{16,32},{32,48},{48,64},{64,80},{80,96},{96,112},{112,128},... | collective-permute-start | bytes 98312 | tf_op jit(solution)/shard_map/ppermute | solution.py:334
  66.4 15.3 %collective-permute-start.7 = (f32[64,128]{1,0:T(8,128)}, f32[64,128]{1,0:T(8,128)S(1)}, u32[]{:S(2)}, u32[]{:S(2)}) collective-permute-start(f32[64,128]{1,0:T(8,128)} %get-tuple-element.37), channel_id=1, source_target_pairs={{16,0},{32,16},{48,32},{64,48},{80,64},{96,80},{112,96},{128,112},... | collective-permute-start | bytes 98312 | tf_op jit(solution)/shard_map/ppermute | solution.py:334
  72.4 8.0 %collective-permute-start.8 = (f32[8,128]{1,0:T(8,128)}, f32[8,128]{1,0:T(8,128)S(1)}, u32[]{:S(2)}, u32[]{:S(2)}) collective-permute-start(f32[8,128]{1,0:T(8,128)} %get-tuple-element.38), channel_id=1, source_target_pairs={{0,1},{1,2},{2,3},{3,4},{4,5},{5,6},{6,7},{7,8},{8,9},{9,10},{10,1... | collective-permute-start | bytes 12296 | tf_op jit(solution)/shard_map/ppermute | solution.py:334
  74.4 7.4 %collective-permute-start.9 = (f32[8,128]{1,0:T(8,128)S(1)}, f32[8,128]{1,0:T(8,128)S(1)}, u32[]{:S(2)}, u32[]{:S(2)}) collective-permute-start(f32[8,128]{1,0:T(8,128)S(1)} %copy-done.19), channel_id=1, source_target_pairs={{1,0},{2,1},{3,2},{4,3},{5,4},{6,5},{7,6},{8,7},{9,8},{10,9},{11,1... | collective-permute-start | bytes 12296 | tf_op jit(solution)/shard_map/ppermute | solution.py:334
  80.4 1.3 %copy-start.11 = (f32[8,128]{1,0:T(8,128)}, f32[8,128]{1,0:T(8,128)S(1)}, u32[]{:S(2)}) copy-start(f32[8,128]{1,0:T(8,128)S(1)} %collective-permute-done.8.refs_3_) | copy-start | bytes 12292
  81.7 0.6 copy-start.12
  81.7 0.6 copy-start.5
  81.7 0.6 copy-start.6
  85.9 10.6 %copy-start.18 = (f32[8,128]{1,0:T(8,128)S(1)}, f32[8,128]{1,0:T(8,128)}, u32[]{:S(2)}) copy-start(f32[8,128]{1,0:T(8,128)} %get-tuple-element.44) | copy-start | bytes 12292
  85.9 18.8 %collective-permute-start.10 = (f32[64,128]{1,0:T(8,128)}, f32[64,128]{1,0:T(8,128)S(1)}, u32[]{:S(2)}, u32[]{:S(2)}) collective-permute-start(f32[64,128]{1,0:T(8,128)} %get-tuple-element.41), channel_id=1, source_target_pairs={{0,16},{16,32},{32,48},{48,64},{64,80},{80,96},{96,112},{112,128},... | collective-permute-start | bytes 98312 | tf_op jit(solution)/shard_map/ppermute | solution.py:334
  87.8 16.9 %collective-permute-start.11 = (f32[64,128]{1,0:T(8,128)}, f32[64,128]{1,0:T(8,128)S(1)}, u32[]{:S(2)}, u32[]{:S(2)}) collective-permute-start(f32[64,128]{1,0:T(8,128)} %get-tuple-element.42), channel_id=1, source_target_pairs={{16,0},{32,16},{48,32},{64,48},{80,64},{96,80},{112,96},{128,112},... | collective-permute-start | bytes 98312 | tf_op jit(solution)/shard_map/ppermute | solution.py:334
  93.9 10.8 %collective-permute-start.12 = (f32[8,128]{1,0:T(8,128)}, f32[8,128]{1,0:T(8,128)S(1)}, u32[]{:S(2)}, u32[]{:S(2)}) collective-permute-start(f32[8,128]{1,0:T(8,128)} %get-tuple-element.43), channel_id=1, source_target_pairs={{0,1},{1,2},{2,3},{3,4},{4,5},{5,6},{6,7},{7,8},{8,9},{9,10},{10,1... | collective-permute-start | bytes 12296 | tf_op jit(solution)/shard_map/ppermute | solution.py:334
  96.5 8.2 %collective-permute-start.13 = (f32[8,128]{1,0:T(8,128)S(1)}, f32[8,128]{1,0:T(8,128)S(1)}, u32[]{:S(2)}, u32[]{:S(2)}) collective-permute-start(f32[8,128]{1,0:T(8,128)S(1)} %copy-done.18), channel_id=1, source_target_pairs={{1,0},{2,1},{3,2},{4,3},{5,4},{6,5},{7,6},{8,7},{9,8},{10,9},{11,1... | collective-permute-start | bytes 12296 | tf_op jit(solution)/shard_map/ppermute | solution.py:334
  104.7 0.6 copy-start.13
  104.7 0.6 copy-start.14
  104.7 0.6 copy-start.9
  104.7 0.6 copy-start.10

commit v5 on v3

--- a/solution.py
+++ b/solution.py
@@ -359,6 +359,40 @@
     )
 
 
+def forward_call(holder, held, per):
+    n, planes, x, y = held.shape
+
+    def kernel(hold_ref, h_ref, o_ref):
+        _, lane = _iotas((x, y))
+        for g in range(n):
+            h = hold_ref[g]
+            for i in range(planes):
+                o_ref[g, i] = h_ref[h, i]
+            cols = jnp.zeros((x, y), F32)
+            scl = jnp.zeros((x, y), F32)
+            if g > 0:
+                hl = hold_ref[g - 1]
+                for i in range(per):
+                    v = h_ref[hl, i].astype(F32)
+                    cols = jnp.where(lane == i, _roll(v, i - (y - 1), 1), cols)
+                scl = jnp.where(lane < per, h_ref[hl, per + 1].astype(F32), scl)
+            if g < n - 1:
+                hr = hold_ref[g + 1]
+                for i in range(per):
+                    v = h_ref[hr, i].astype(F32)
+                    cols = jnp.where(lane == per + i, _roll(v, per + i, 1), cols)
+                sv = _roll(h_ref[hr, per + 1].astype(F32), per, 1)
+                scl = jnp.where((lane >= per) & (lane < 2 * per), sv, scl)
+            o_ref[g, planes] = cols.astype(o_ref.dtype)
+            o_ref[g, planes + 1] = scl.astype(o_ref.dtype)
+
+    return pl.pallas_call(
+        kernel,
+        out_shape=jax.ShapeDtypeStruct((n, planes + 2, x, y), held.dtype),
+        in_specs=[pl.BlockSpec(memory_space=SMEM), pl.BlockSpec(memory_space=VMEM)],
+    )(holder, held)
+
+
 def route_blocks(stored_slab, block_scales, holder, xm_all, xp_all, first):
     nf, nz, x, y = stored_slab.shape
     n = lax.axis_size("gy")
@@ -375,26 +409,7 @@
     sc = jnp.pad(sc, ((0, 0), (0, x - 3), (0, y - per)))[:, None]
     held = lax.all_to_all(jnp.concatenate([slab, halo, sc], axis=1), "gy", 0, 0, tiled=True)
 
-    g = jnp.arange(n, dtype=jnp.int32)
-    left = jnp.take(holder, jnp.maximum(g - 1, 0))
-    right = jnp.take(holder, jnp.minimum(g + 1, n - 1))
-    has_l = (g > 0)[:, None, None]
-    has_r = (g < n - 1)[:, None, None]
-    zero = jnp.zeros((), bf)
-    cols_l = jnp.where(has_l, jnp.take(held[:, :per, :, y - 1], left, axis=0), zero)
-    cols_r = jnp.where(has_r, jnp.take(held[:, :per, :, 0], right, axis=0), zero)
-    scl_l = jnp.where(has_l, jnp.take(held[:, per + 1, 0:1, :per], left, axis=0), zero)
-    scl_r = jnp.where(has_r, jnp.take(held[:, per + 1, 0:1, :per], right, axis=0), zero)
-    cols = jnp.concatenate([cols_l, cols_r], axis=1).transpose(0, 2, 1)
-    scl = jnp.concatenate([scl_l, scl_r], axis=2)
-    yplane = jnp.concatenate(
-        [
-            jnp.pad(cols, ((0, 0), (0, 0), (0, y - 2 * per))),
-            jnp.pad(scl, ((0, 0), (0, x - 1), (0, y - 2 * per))),
-        ],
-        axis=1,
-    )
-    forward = jnp.concatenate([jnp.take(held, holder, axis=0), yplane.reshape(n, 2, x, y)], axis=1)
+    forward = forward_call(holder, held, per)
     return lax.all_to_all(forward, "gy", 0, 0, tiled=True)
 
 

time: 101 us -> 96.6 us (0.956)
  blocking collectives: 0 us -> 14 us
  starting transfers between devices: 60.8 us -> 53.3 us
  local copies, waits for them, and re-layouts: 12.1 us -> 5.65 us
  waiting for transfers between devices: 7.91 us -> 3.4 us
  Pallas kernels: 16.5 us -> 18.4 us
  other arithmetic: 1.99 us -> 0.14 us
    all_to_all x0 -> x1, blocking collectives: none -> 14 us  [route_blocks(): lax.all_to_all(jnp.concatenate([slab, halo, sc], axis=1), 'gy', 0, 0, til...]
    all_to_all x1 -> x0, starting transfers between devices: 7.48 us -> none  [route_blocks(): lax.all_to_all(jnp.concatenate([slab, halo, sc], axis=1), 'gy', 0, 0, til...]
    all_to_all x1 -> x0, waiting for transfers between devices: 6.59 us -> none  [route_blocks(): lax.all_to_all(jnp.concatenate([slab, halo, sc], axis=1), 'gy', 0, 0, til...]
    gather x9 -> x0, local copies, waits for them, and re-layouts: 4.41 us -> none  [the longest x2 0.67 us: route_blocks(): jnp.take(held[:, per + 1, 0:1, :per], left, axis=0)]
    ppermute x12, waiting for transfers between devices: 1.31 us -> 3.4 us  [_shift(): return lax.ppermute(v, axis, pairs)]
    pallas_call x0 -> x1, Pallas kernels: none -> 1.79 us  [forward_call(): pl.pallas_call(kernel, out_shape=jax.ShapeDtypeStruct((n, planes + 2, x,...]
    unnamed x43 -> x39, local copies, waits for them, and re-layouts: 4.55 us -> 3.67 us
  transfers between devices with their start and end apart: 14 -> 13, of which waited for: 2 -> 3; matrix products, arithmetic and copies ran while one was open for 3% -> 1% of each run, Pallas kernels for 5% -> 5%
where the time goes in v5:
time: 96.6 us; the launch traced here: 95.8 us
  starting transfers between devices  53.3 us (55%)
  Pallas kernels  18.4 us (19%)
  blocking collectives  14 us (14%)
  local copies, waits for them, and re-layouts  5.65 us (6%)
  waiting for transfers between devices  3.4 us (4%)
  between operations  0.99 us (1%)
    ppermute x12, starting transfers between devices, _shift(): return lax.ppermute(v, axis, pairs)  47.7 us
    all_to_all x1, blocking collectives, route_blocks(): lax.all_to_all(jnp.concatenate([slab, halo, sc], axis=1), 'gy', 0, 0, til...  14 us
    pallas_call x2, Pallas kernels, adjoint_call(): pl.pallas_call(kernel, out_shape=out_shape, scratch_shapes=_halo_scratch(...  7.04 us
    pallas_call x2, Pallas kernels, step_call(): pl.pallas_call(kernel, out_shape=out_shape, scratch_shapes=_halo_scratch(...  5.83 us
    all_to_all x1, starting transfers between devices, route_blocks(): return lax.all_to_all(forward, 'gy', 0, 0, tiled=True)  5.56 us
    unnamed x39, local copies, waits for them, and re-layouts  3.67 us
    ppermute x12, waiting for transfers between devices, _shift(): return lax.ppermute(v, axis, pairs)  3.4 us
  transfers between devices with their start and end apart: 13, of which 3 were waited for; matrix products, arithmetic and copies ran while one was open for 1% of the time, Pallas kernels for 5%

profile of v5, /device:TPU:130, one launch (start us, length us, event | category | flops | bytes accessed | tf_op | source)
XLA Modules:
  0.0 95.8 jit_solution(13094736051892539196)
XLA Ops:
  0.6 1.4 %copy.29.tab_ref = f32[12,4]{1,0:T(8,128)} copy(f32[12,4]{0,1:T(4,128)} %param.10) | data formatting | bytes 384 | tf_op args[4]
  2.0 0.6 reshape.59.sc_ref
  2.6 1.8 %shard_map.77 = (f32[4,8,128]{2,1,0:T(8,128)}, f32[136,128]{1,0:T(8,128)}, f32[136,128]{1,0:T(8,128)}, f32[8,128]{1,0:T(8,128)}, f32[8,128]{1,0:T(8,128)}) custom-call(s32[8,128]{1,0:T(8,128)} %cls_ref.1, f32[12,4]{1,0:T(8,128)} %copy.29.tab_ref, f32[64]{0:T(128)} %reshape.59.sc_ref, f32[2,32,8,128]{3,2,1,0:T(8,128)} %refs_5_.1, bf16[2,32,8,128]{3,2,1,0:T(8,128)(2,1)} %slab_ref.1), custom_call_target="tpu_custom_call" | custom-call | tf_op jit(solution)/shard_map/pallas_call | solution.py:228
  4.4 3.5 %collective-permute-start = (f32[136,128]{1,0:T(8,128)}, f32[136,128]{1,0:T(8,128)S(1)}, u32[]{:S(2)}, u32[]{:S(2)}) collective-permute-start(f32[136,128]{1,0:T(8,128)} %get-tuple-element.22), channel_id=1, source_target_pairs={{0,16},{16,32},{32,48},{48,64},{64,80},{80,96},{96,112},{112,128},... | collective-permute-start | bytes 208904 | tf_op jit(solution)/shard_map/ppermute | solution.py:350
  7.9 4.5 %collective-permute-start.1 = (f32[136,128]{1,0:T(8,128)}, f32[136,128]{1,0:T(8,128)S(1)}, u32[]{:S(2)}, u32[]{:S(2)}) collective-permute-start(f32[136,128]{1,0:T(8,128)} %get-tuple-element.23), channel_id=1, source_target_pairs={{16,0},{32,16},{48,32},{64,48},{80,64},{96,80},{112,96},{128,112},... | collective-permute-start | bytes 208904 | tf_op jit(solution)/shard_map/ppermute | solution.py:350
  12.4 0.1 reshape.61
  12.5 0.6 collective-permute-done.refs_6_.refs_11_
  13.1 1.5 %collective-permute-done.1.refs_7_.refs_12_ = f32[136,128]{1,0:T(8,128)S(1)} collective-permute-done((f32[136,128]{1,0:T(8,128)}, f32[136,128]{1,0:T(8,128)S(1)}, u32[]{:S(2)}, u32[]{:S(2)}) %collective-permute-start.1) | collective-permute-done | bytes 69664 | tf_op jit(solution)/shard_map/ppermute | solution.py:350
  14.7 0.1 convert_element_type.46
  14.8 0.5 copy-done.1
  15.2 0.1 convert_element_type.47
  15.4 0.1 fusion.9
  15.5 14.0 %all_to_all.10.h_ref = bf16[16,6,8,128]{3,2,1,0:T(8,128)(2,1)} all-to-all(bf16[16,6,8,128]{3,2,1,0:T(8,128)(2,1)S(1)} %pad_maximum_fusion), channel_id=1, replica_groups=mesh['gx'=16,'gy'=16] {'gy'}, dimensions={0} | all-to-all | bytes 393216 | tf_op jit(solution)/shard_map/all_to_all | solution.py:410
  29.4 1.8 %shard_map.78 = bf16[16,8,8,128]{3,2,1,0:T(8,128)(2,1)} custom-call(s32[16]{0:T(128)} %hold_ref.1, bf16[16,6,8,128]{3,2,1,0:T(8,128)(2,1)} %all_to_all.10.h_ref), custom_call_target="tpu_custom_call" | custom-call | tf_op jit(solution)/shard_map/pallas_call | solution.py:389
  31.2 5.6 %all-to-all-start.1 = ((bf16[16,8,8,128]{3,2,1,0:T(8,128)(2,1)}), bf16[16,8,8,128]{3,2,1,0:T(8,128)(2,1)S(1)}, u32[]{:S(2)}, u32[]{:S(2)}) async-start(bf16[16,8,8,128]{3,2,1,0:T(8,128)(2,1)} %shard_map.78), calls=%async_computation.1 | async-start | bytes 524288 | tf_op jit(solution)/shard_map/all_to_all | solution.py:413
  36.8 2.1 %collective-permute-start.2 = (f32[8,128]{1,0:T(8,128)S(1)}, f32[8,128]{1,0:T(8,128)S(1)}, u32[]{:S(2)}, u32[]{:S(2)}) collective-permute-start(f32[8,128]{1,0:T(8,128)S(1)} %copy-done.16), channel_id=1, source_target_pairs={{0,1},{1,2},{2,3},{3,4},{4,5},{5,6},{6,7},{7,8},{8,9},{9,10},{10,1... | collective-permute-start | bytes 12296 | tf_op jit(solution)/shard_map/ppermute | solution.py:350
  38.9 5.9 %collective-permute-start.3 = (f32[8,128]{1,0:T(8,128)S(1)}, f32[8,128]{1,0:T(8,128)S(1)}, u32[]{:S(2)}, u32[]{:S(2)}) collective-permute-start(f32[8,128]{1,0:T(8,128)S(1)} %copy-done.15), channel_id=1, source_target_pairs={{1,0},{2,1},{3,2},{4,3},{5,4},{6,5},{7,6},{8,7},{9,8},{10,9},{11,1... | collective-permute-start | bytes 12296 | tf_op jit(solution)/shard_map/ppermute | solution.py:350
  44.8 0.0 copy-start.2
  44.9 0.1 reshape.57
  45.0 0.1 copy.34
  45.1 0.1 copy.35
  45.2 0.1 reshape.58
  45.3 0.7 reshape.60.sc_ref
  45.9 1.9 %shard_map.79 = (f32[2,32,8,128]{3,2,1,0:T(8,128)}, f32[64,128]{1,0:T(8,128)}, f32[64,128]{1,0:T(8,128)}, f32[8,128]{1,0:T(8,128)}, f32[8,128]{1,0:T(8,128)}) custom-call(f32[320]{0:T(512)} %reshape.60.sc_ref, bf16[16,8,8,128]{3,2,1,0:T(8,128)(2,1)} %copy-done.2), custom_call_target="tpu_custom_call" | custom-call | tf_op jit(solution)/shard_map/pallas_call | solution.py:264
  47.8 0.0 collective-permute-done.2.refs_8_.refs_13_
  47.9 0.6 copy-done.6
  48.4 0.0 copy-done.7
  48.4 3.0 %shard_map.80 = (f32[2,32,8,128]{3,2,1,0:T(8,128)}, f32[64,128]{1,0:T(8,128)}, f32[64,128]{1,0:T(8,128)}, f32[8,128]{1,0:T(8,128)}, f32[8,128]{1,0:T(8,128)}) custom-call(f32[2,32,8,128]{3,2,1,0:T(8,128)} %get-tuple-element.24.refs_0_, f32[64,128]{1,0:T(8,128)} %get-tuple-element.25.refs_1_, f32[64,128]{1,0:T(8,128)} %get-tuple-element.26.refs_2_, ...), custom_call_target="tpu_custom_call" | custom-call | tf_op jit(solution)/shard_map/pallas_call | solution.py:297
  51.4 2.8 %collective-permute-start.4 = (f32[64,128]{1,0:T(8,128)}, f32[64,128]{1,0:T(8,128)S(1)}, u32[]{:S(2)}, u32[]{:S(2)}) collective-permute-start(f32[64,128]{1,0:T(8,128)} %get-tuple-element.33), channel_id=1, source_target_pairs={{0,16},{16,32},{32,48},{48,64},{64,80},{80,96},{96,112},{112,128},... | collective-permute-start | bytes 98312 | tf_op jit(solution)/shard_map/ppermute | solution.py:350
  54.2 5.1 %collective-permute-start.5 = (f32[64,128]{1,0:T(8,128)}, f32[64,128]{1,0:T(8,128)S(1)}, u32[]{:S(2)}, u32[]{:S(2)}) collective-permute-start(f32[64,128]{1,0:T(8,128)} %get-tuple-element.34), channel_id=1, source_target_pairs={{16,0},{32,16},{48,32},{64,48},{80,64},{96,80},{112,96},{128,112},... | collective-permute-start | bytes 98312 | tf_op jit(solution)/shard_map/ppermute | solution.py:350
  59.4 1.9 %collective-permute-start.6 = (f32[8,128]{1,0:T(8,128)}, f32[8,128]{1,0:T(8,128)S(1)}, u32[]{:S(2)}, u32[]{:S(2)}) collective-permute-start(f32[8,128]{1,0:T(8,128)} %get-tuple-element.35), channel_id=1, source_target_pairs={{0,1},{1,2},{2,3},{3,4},{4,5},{5,6},{6,7},{7,8},{8,9},{9,10},{10,1... | collective-permute-start | bytes 12296 | tf_op jit(solution)/shard_map/ppermute | solution.py:350
  61.3 6.0 %collective-permute-start.7 = (f32[8,128]{1,0:T(8,128)S(1)}, f32[8,128]{1,0:T(8,128)S(1)}, u32[]{:S(2)}, u32[]{:S(2)}) collective-permute-start(f32[8,128]{1,0:T(8,128)S(1)} %copy-done.18), channel_id=1, source_target_pairs={{1,0},{2,1},{3,2},{4,3},{5,4},{6,5},{7,6},{8,7},{9,8},{10,9},{11,1... | collective-permute-start | bytes 12296 | tf_op jit(solution)/shard_map/ppermute | solution.py:350
  67.4 1.3 %collective-permute-done.7.refs_4_ = f32[8,128]{1,0:T(8,128)S(1)} collective-permute-done((f32[8,128]{1,0:T(8,128)S(1)}, f32[8,128]{1,0:T(8,128)S(1)}, u32[]{:S(2)}, u32[]{:S(2)}) %collective-permute-start.7) | collective-permute-done | bytes 4128 | tf_op jit(solution)/shard_map/ppermute | solution.py:350
  68.7 0.0 collective-permute-done.4.refs_1_
  68.7 0.6 copy-done.11
  69.3 0.0 copy-done.4
  69.3 0.0 copy-done.5
  69.3 3.6 %shard_map.82 = (f32[2,32,8,128]{3,2,1,0:T(8,128)}, f32[64,128]{1,0:T(8,128)}, f32[64,128]{1,0:T(8,128)}, f32[8,128]{1,0:T(8,128)}, f32[8,128]{1,0:T(8,128)}) custom-call(f32[2,32,8,128]{3,2,1,0:T(8,128)} %get-tuple-element.32.refs_0_, f32[64,128]{1,0:T(8,128)} %copy-done.4, f32[64,128]{1,0:T(8,128)} %copy-done.5, f32[8,128]{1,0:T(8,128)} %copy-done.10, ...), custom_call_target="tpu_custom_call" | custom-call | tf_op jit(solution)/shard_map/pallas_call | solution.py:334
  72.9 1.9 %collective-permute-start.8 = (f32[64,128]{1,0:T(8,128)}, f32[64,128]{1,0:T(8,128)S(1)}, u32[]{:S(2)}, u32[]{:S(2)}) collective-permute-start(f32[64,128]{1,0:T(8,128)} %get-tuple-element.38), channel_id=1, source_target_pairs={{0,16},{16,32},{32,48},{48,64},{64,80},{80,96},{96,112},{112,128},... | collective-permute-start | bytes 98312 | tf_op jit(solution)/shard_map/ppermute | solution.py:350
  74.8 6.0 %collective-permute-start.9 = (f32[64,128]{1,0:T(8,128)}, f32[64,128]{1,0:T(8,128)S(1)}, u32[]{:S(2)}, u32[]{:S(2)}) collective-permute-start(f32[64,128]{1,0:T(8,128)} %get-tuple-element.39), channel_id=1, source_target_pairs={{16,0},{32,16},{48,32},{64,48},{80,64},{96,80},{112,96},{128,112},... | collective-permute-start | bytes 98312 | tf_op jit(solution)/shard_map/ppermute | solution.py:350
  80.9 2.9 %collective-permute-start.10 = (f32[8,128]{1,0:T(8,128)}, f32[8,128]{1,0:T(8,128)S(1)}, u32[]{:S(2)}, u32[]{:S(2)}) collective-permute-start(f32[8,128]{1,0:T(8,128)} %get-tuple-element.40), channel_id=1, source_target_pairs={{0,1},{1,2},{2,3},{3,4},{4,5},{5,6},{6,7},{7,8},{8,9},{9,10},{10,1... | collective-permute-start | bytes 12296 | tf_op jit(solution)/shard_map/ppermute | solution.py:350
  83.8 5.1 %collective-permute-start.11 = (f32[8,128]{1,0:T(8,128)S(1)}, f32[8,128]{1,0:T(8,128)S(1)}, u32[]{:S(2)}, u32[]{:S(2)}) collective-permute-start(f32[8,128]{1,0:T(8,128)S(1)} %copy-done.17), channel_id=1, source_target_pairs={{1,0},{2,1},{3,2},{4,3},{5,4},{6,5},{7,6},{8,7},{9,8},{10,9},{11,1... | collective-permute-start | bytes 12296 | tf_op jit(solution)/shard_map/ppermute | solution.py:350
  88.9 2.9 %shard_map.81 = f32[2,32,8,128]{3,2,1,0:T(8,128)} custom-call(f32[2,32,8,128]{3,2,1,0:T(8,128)} %get-tuple-element.32.refs_0_, f32[64,128]{1,0:T(8,128)} %copy-done.4, f32[64,128]{1,0:T(8,128)} %copy-done.5, f32[8,128]{1,0:T(8,128)} %copy-done.10, f32[8,128]{1,0:T(8,128)} %copy-done.11, f32[4,8,128]{2,1,0:T(8,128)} %get-tuple-element.29.refs_5_.refs_10_, ...), custom_call_target="tpu_custom_call" | custom-call | tf_op jit(solution)/shard_map/pallas_call | solution.py:297
  91.8 0.5 copy-done.12
  92.3 0.0 copy-done.13
  92.4 0.0 copy-done.8
  92.4 0.0 copy-done.9
  92.4 3.4 %shard_map.83 = f32[2,32,8,128]{3,2,1,0:T(8,128)} custom-call(f32[2,32,8,128]{3,2,1,0:T(8,128)} %get-tuple-element.24.refs_0_, f32[64,128]{1,0:T(8,128)} %get-tuple-element.25.refs_1_, f32[64,128]{1,0:T(8,128)} %get-tuple-element.26.refs_2_, f32[8,128]{1,0:T(8,128)} %get-tuple-element.27.refs_3_, f32[8,128]{1,0:T(8,128)} %get-tuple-element.28.refs_4_, ...), custom_call_target="tpu_custom_call" | custom-call | tf_op jit(solution)/shard_map/pallas_call | solution.py:334
  (47 shorter events, 0.2 us)
Async XLA Ops:
  0.6 1.4 %copy-start.14 = (bf16[2,32,1,1]{1,0,3,2:T(2,128)(2,1)S(1)}, bf16[2,32,1,1]{1,0,3,2:T(2,128)(2,1)}, u32[]{:S(2)}) copy-start(bf16[2,32,1,1]{1,0,3,2:T(2,128)(2,1)} %param.7) | copy-start | bytes 388
  4.4 8.6 %collective-permute-start = (f32[136,128]{1,0:T(8,128)}, f32[136,128]{1,0:T(8,128)S(1)}, u32[]{:S(2)}, u32[]{:S(2)}) collective-permute-start(f32[136,128]{1,0:T(8,128)} %get-tuple-element.22), channel_id=1, source_target_pairs={{0,16},{16,32},{32,48},{48,64},{64,80},{80,96},{96,112},{112,128},... | collective-permute-start | bytes 208904 | tf_op jit(solution)/shard_map/ppermute | solution.py:350
  7.9 6.7 %collective-permute-start.1 = (f32[136,128]{1,0:T(8,128)}, f32[136,128]{1,0:T(8,128)S(1)}, u32[]{:S(2)}, u32[]{:S(2)}) collective-permute-start(f32[136,128]{1,0:T(8,128)} %get-tuple-element.23), channel_id=1, source_target_pairs={{16,0},{32,16},{48,32},{64,48},{80,64},{96,80},{112,96},{128,112},... | collective-permute-start | bytes 208904 | tf_op jit(solution)/shard_map/ppermute | solution.py:350
  13.0 1.6 %copy-start = (f32[136,128]{1,0:T(8,128)}, f32[136,128]{1,0:T(8,128)S(1)}, u32[]{:S(2)}) copy-start(f32[136,128]{1,0:T(8,128)S(1)} %collective-permute-done.refs_6_.refs_11_) | copy-start | bytes 208900
  13.1 2.3 %copy-start.3 = (bf16[2,32,8,128]{3,2,1,0:T(8,128)(2,1)S(1)}, bf16[2,32,8,128]{3,2,1,0:T(8,128)(2,1)}, u32[]{:S(2)}) copy-start(bf16[2,32,8,128]{3,2,1,0:T(8,128)(2,1)} %slab_ref.1) | copy-start | bytes 393220
  14.6 0.6 copy-start.1
  31.2 5.6 %copy-start.16 = (f32[8,128]{1,0:T(8,128)S(1)}, f32[8,128]{1,0:T(8,128)}, u32[]{:S(2)}) copy-start(f32[8,128]{1,0:T(8,128)} %get-tuple-element.30) | copy-start | bytes 12292
  31.2 7.6 %copy-start.15 = (f32[8,128]{1,0:T(8,128)S(1)}, f32[8,128]{1,0:T(8,128)}, u32[]{:S(2)}) copy-start(f32[8,128]{1,0:T(8,128)} %get-tuple-element.31) | copy-start | bytes 12292
  31.2 13.6 %all-to-all-start.1 = ((bf16[16,8,8,128]{3,2,1,0:T(8,128)(2,1)}), bf16[16,8,8,128]{3,2,1,0:T(8,128)(2,1)S(1)}, u32[]{:S(2)}, u32[]{:S(2)}) async-start(bf16[16,8,8,128]{3,2,1,0:T(8,128)(2,1)} %shard_map.78), calls=%async_computation.1 | async-start | bytes 524288 | tf_op jit(solution)/shard_map/all_to_all | solution.py:413
  36.8 11.0 %collective-permute-start.2 = (f32[8,128]{1,0:T(8,128)S(1)}, f32[8,128]{1,0:T(8,128)S(1)}, u32[]{:S(2)}, u32[]{:S(2)}) collective-permute-start(f32[8,128]{1,0:T(8,128)S(1)} %copy-done.16), channel_id=1, source_target_pairs={{0,1},{1,2},{2,3},{3,4},{4,5},{5,6},{6,7},{7,8},{8,9},{9,10},{10,1... | collective-permute-start | bytes 12296 | tf_op jit(solution)/shard_map/ppermute | solution.py:350
  38.9 9.0 %collective-permute-start.3 = (f32[8,128]{1,0:T(8,128)S(1)}, f32[8,128]{1,0:T(8,128)S(1)}, u32[]{:S(2)}, u32[]{:S(2)}) collective-permute-start(f32[8,128]{1,0:T(8,128)S(1)} %copy-done.15), channel_id=1, source_target_pairs={{1,0},{2,1},{3,2},{4,3},{5,4},{6,5},{7,6},{8,7},{9,8},{10,9},{11,1... | collective-permute-start | bytes 12296 | tf_op jit(solution)/shard_map/ppermute | solution.py:350
  44.8 1.1 %copy-start.2 = (bf16[16,8,8,128]{3,2,1,0:T(8,128)(2,1)}, bf16[16,8,8,128]{3,2,1,0:T(8,128)(2,1)S(1)}, u32[]{:S(2)}) copy-start(bf16[16,8,8,128]{3,2,1,0:T(8,128)(2,1)S(1)} %all-to-all-done.1.r_ref) | copy-start | bytes 786436
  47.8 0.6 copy-start.6
  47.8 0.6 copy-start.7
  51.4 9.9 %copy-start.18 = (f32[8,128]{1,0:T(8,128)S(1)}, f32[8,128]{1,0:T(8,128)}, u32[]{:S(2)}) copy-start(f32[8,128]{1,0:T(8,128)} %get-tuple-element.36) | copy-start | bytes 12292
  51.4 17.3 %collective-permute-start.4 = (f32[64,128]{1,0:T(8,128)}, f32[64,128]{1,0:T(8,128)S(1)}, u32[]{:S(2)}, u32[]{:S(2)}) collective-permute-start(f32[64,128]{1,0:T(8,128)} %get-tuple-element.33), channel_id=1, source_target_pairs={{0,16},{16,32},{32,48},{48,64},{64,80},{80,96},{96,112},{112,128},... | collective-permute-start | bytes 98312 | tf_op jit(solution)/shard_map/ppermute | solution.py:350
  54.2 14.5 %collective-permute-start.5 = (f32[64,128]{1,0:T(8,128)}, f32[64,128]{1,0:T(8,128)S(1)}, u32[]{:S(2)}, u32[]{:S(2)}) collective-permute-start(f32[64,128]{1,0:T(8,128)} %get-tuple-element.34), channel_id=1, source_target_pairs={{16,0},{32,16},{48,32},{64,48},{80,64},{96,80},{112,96},{128,112},... | collective-permute-start | bytes 98312 | tf_op jit(solution)/shard_map/ppermute | solution.py:350
  59.4 8.0 %collective-permute-start.6 = (f32[8,128]{1,0:T(8,128)}, f32[8,128]{1,0:T(8,128)S(1)}, u32[]{:S(2)}, u32[]{:S(2)}) collective-permute-start(f32[8,128]{1,0:T(8,128)} %get-tuple-element.35), channel_id=1, source_target_pairs={{0,1},{1,2},{2,3},{3,4},{4,5},{5,6},{6,7},{7,8},{8,9},{9,10},{10,1... | collective-permute-start | bytes 12296 | tf_op jit(solution)/shard_map/ppermute | solution.py:350
  61.3 7.4 %collective-permute-start.7 = (f32[8,128]{1,0:T(8,128)S(1)}, f32[8,128]{1,0:T(8,128)S(1)}, u32[]{:S(2)}, u32[]{:S(2)}) collective-permute-start(f32[8,128]{1,0:T(8,128)S(1)} %copy-done.18), channel_id=1, source_target_pairs={{1,0},{2,1},{3,2},{4,3},{5,4},{6,5},{7,6},{8,7},{9,8},{10,9},{11,1... | collective-permute-start | bytes 12296 | tf_op jit(solution)/shard_map/ppermute | solution.py:350
  67.4 1.3 %copy-start.10 = (f32[8,128]{1,0:T(8,128)}, f32[8,128]{1,0:T(8,128)S(1)}, u32[]{:S(2)}) copy-start(f32[8,128]{1,0:T(8,128)S(1)} %collective-permute-done.6.refs_3_) | copy-start | bytes 12292
  68.7 0.6 copy-start.11
  68.7 0.6 copy-start.4
  68.7 0.6 copy-start.5
  72.9 10.8 %copy-start.17 = (f32[8,128]{1,0:T(8,128)S(1)}, f32[8,128]{1,0:T(8,128)}, u32[]{:S(2)}) copy-start(f32[8,128]{1,0:T(8,128)} %get-tuple-element.41) | copy-start | bytes 12292
  72.9 18.9 %collective-permute-start.8 = (f32[64,128]{1,0:T(8,128)}, f32[64,128]{1,0:T(8,128)S(1)}, u32[]{:S(2)}, u32[]{:S(2)}) collective-permute-start(f32[64,128]{1,0:T(8,128)} %get-tuple-element.38), channel_id=1, source_target_pairs={{0,16},{16,32},{32,48},{48,64},{64,80},{80,96},{96,112},{112,128},... | collective-permute-start | bytes 98312 | tf_op jit(solution)/shard_map/ppermute | solution.py:350
  74.8 16.9 %collective-permute-start.9 = (f32[64,128]{1,0:T(8,128)}, f32[64,128]{1,0:T(8,128)S(1)}, u32[]{:S(2)}, u32[]{:S(2)}) collective-permute-start(f32[64,128]{1,0:T(8,128)} %get-tuple-element.39), channel_id=1, source_target_pairs={{16,0},{32,16},{48,32},{64,48},{80,64},{96,80},{112,96},{128,112},... | collective-permute-start | bytes 98312 | tf_op jit(solution)/shard_map/ppermute | solution.py:350
  80.9 10.9 %collective-permute-start.10 = (f32[8,128]{1,0:T(8,128)}, f32[8,128]{1,0:T(8,128)S(1)}, u32[]{:S(2)}, u32[]{:S(2)}) collective-permute-start(f32[8,128]{1,0:T(8,128)} %get-tuple-element.40), channel_id=1, source_target_pairs={{0,1},{1,2},{2,3},{3,4},{4,5},{5,6},{6,7},{7,8},{8,9},{9,10},{10,1... | collective-permute-start | bytes 12296 | tf_op jit(solution)/shard_map/ppermute | solution.py:350
  83.8 8.0 %collective-permute-start.11 = (f32[8,128]{1,0:T(8,128)S(1)}, f32[8,128]{1,0:T(8,128)S(1)}, u32[]{:S(2)}, u32[]{:S(2)}) collective-permute-start(f32[8,128]{1,0:T(8,128)S(1)} %copy-done.17), channel_id=1, source_target_pairs={{1,0},{2,1},{3,2},{4,3},{5,4},{6,5},{7,6},{8,7},{9,8},{10,9},{11,1... | collective-permute-start | bytes 12296 | tf_op jit(solution)/shard_map/ppermute | solution.py:350
  91.7 0.6 copy-start.12
  91.8 0.6 copy-start.13
  91.8 0.6 copy-start.8
  91.8 0.6 copy-start.9

commit v6 on v5

--- a/solution.py
+++ b/solution.py
@@ -7,7 +7,7 @@
 
 F32 = jnp.float32
 NCOEF = 4
-UNROLL = 4
+UNROLL = 8
 VMEM = pltpu.MemorySpace.VMEM
 SMEM = pltpu.MemorySpace.SMEM
 
@@ -240,32 +240,52 @@
     )(soil_class, soil_table, scales, cot, slab)
 
 
-def state0_call(pieces, scales, nf, per):
+def _state0_body(sc_ref, r_ref, s_ref, xm_ref, xp_ref, ym_ref, yp_ref, per):
+    nz, x, y = s_ref.shape[1], s_ref.shape[2], s_ref.shape[3]
+    nplanes = s_ref.shape[0] * nz
+    _, lane = _iotas((x, y))
+    ym = jnp.zeros((x, y), F32)
+    yp = jnp.zeros((x, y), F32)
+    for k in range(nplanes):
+        p, i = k // per, k % per
+        s_ref[k // nz, k % nz] = r_ref[p, i].astype(F32) * sc_ref[k]
+        hx = r_ref[p, per].astype(F32)
+        xm_ref[k : k + 1, :] = hx[i : i + 1, :] * sc_ref[nplanes + k]
+        xp_ref[k : k + 1, :] = hx[per + i : per + i + 1, :] * sc_ref[2 * nplanes + k]
+        hy = r_ref[p, per + 2].astype(F32)
+        ym = jnp.where(lane == k, _roll(hy, k - i, 1) * sc_ref[3 * nplanes + k], ym)
+        yp = jnp.where(lane == k, _roll(hy, k - (per + i), 1) * sc_ref[4 * nplanes + k], yp)
+    ym_ref[...] = ym
+    yp_ref[...] = yp
+
+
+def state0_step_call(pieces, scales, nf, per, coef, c_halo, c_first):
     npiece, _, x, y = pieces.shape
     nplanes = npiece * per
     nz = nplanes // nf
 
-    def kernel(sc_ref, r_ref, s_ref, xm_ref, xp_ref, ym_ref, yp_ref):
-        _, lane = _iotas((x, y))
-        ym = jnp.zeros((x, y), F32)
-        yp = jnp.zeros((x, y), F32)
-        for k in range(nplanes):
-            p, i = k // per, k % per
-            s_ref[k // nz, k % nz] = r_ref[p, i].astype(F32) * sc_ref[k]
-            hx = r_ref[p, per].astype(F32)
-            xm_ref[k : k + 1, :] = hx[i : i + 1, :] * sc_ref[nplanes + k]
-            xp_ref[k : k + 1, :] = hx[per + i : per + i + 1, :] * sc_ref[2 * nplanes + k]
-            hy = r_ref[p, per + 2].astype(F32)
-            ym = jnp.where(lane == k, _roll(hy, k - i, 1) * sc_ref[3 * nplanes + k], ym)
-            yp = jnp.where(lane == k, _roll(hy, k - (per + i), 1) * sc_ref[4 * nplanes + k], yp)
-        ym_ref[...] = ym
-        yp_ref[...] = yp
-
+    def kernel(sc_ref, r_ref, c_ref, cxm, cxp, cym, cyp, *refs):
+        s0_ref, xm_ref, xp_ref, ym_ref, yp_ref = refs[:5]
+        s1_ref, xf_ref, xl_ref, yf_ref, yl_ref = refs[5:10]
+        scratch = refs[10:]
+        sh_all = scratch[0:4]
+        cs = scratch[4]
+        _state0_body(sc_ref, r_ref, s0_ref, xm_ref, xp_ref, ym_ref, yp_ref, per)
+        _expand_halo(xm_ref, xp_ref, ym_ref, yp_ref, 0, nf, nz, sh_all)
+        _coef_table(c_ref, cxm, cxp, cym, cyp, c_first, cs)
+        masks = _iotas((x, y))
+        sh = [tuple(h.at[f] for h in sh_all) for f in range(nf)]
+        _step_body(s0_ref, sh, cs, s1_ref, nz, masks)
+        vals = [s1_ref[f, z] for f in range(nf) for z in range(nz)]
+        _pack_edges(vals, xf_ref, xl_ref, yf_ref, yl_ref)
+
+    state = jax.ShapeDtypeStruct((nf, nz, x, y), F32)
     return pl.pallas_call(
         kernel,
-        out_shape=(jax.ShapeDtypeStruct((nf, nz, x, y), F32),) + _edge_shapes(nplanes, x, y),
-        in_specs=[pl.BlockSpec(memory_space=SMEM), pl.BlockSpec(memory_space=VMEM)],
-    )(scales, pieces)
+        out_shape=(state,) + _edge_shapes(nplanes, x, y) + (state,) + _edge_shapes(_rows(nplanes), x, y),
+        in_specs=[pl.BlockSpec(memory_space=SMEM)] + [pl.BlockSpec(memory_space=VMEM)] * 6,
+        scratch_shapes=_halo_scratch(nf, nz, x, y) + [pltpu.VMEM((5 * NCOEF, x, y), F32)],
+    )(scales, pieces, coef, *c_halo)
 
 
 def step_call(s, s_halo, coef, c_halo, c_first, with_edges):
@@ -431,9 +451,8 @@
             pieces[:, per + 3, 0, : 2 * per].reshape(-1, 2, per).transpose(1, 0, 2).reshape(2, nplanes),
         ]
     ).astype(F32).reshape(-1)
-    s0, *s0_halo = state0_call(pieces, scales, nf, per)
-
-    s1, *s1_edges = step_call(s0, s0_halo, coef, c_halo, c_first, True)
+    res = state0_step_call(pieces, scales, nf, per, coef, c_halo, c_first)
+    s0, s0_halo, s1, s1_edges = res[0], res[1:5], res[5], res[6:10]
     s1_halo = exchange(*s1_edges)
 
     a1, *a1_edges = adjoint_call(

time: 96.6 us -> 94.8 us (0.981)
  Pallas kernels: 18.4 us -> 16.3 us
    pallas_call x2 -> x1, Pallas kernels: 5.83 us -> 2.73 us  [step_call(): pl.pallas_call(kernel, out_shape=out_shape, scratch_shapes=_halo_scratch(...]
    pallas_call x1, Pallas kernels: 1.89 us -> 3.06 us  [state0_step_call(): pl.pallas_call(kernel, out_shape=(state,) + _edge_shapes(nplanes, x, y) +...]
  transfers between devices with their start and end apart: 13 -> 13, of which waited for: 3 -> 4; matrix products, arithmetic and copies ran while one was open for 1% -> 1% of each run, Pallas kernels for 5% -> 3%
where the time goes in v6:
time: 94.8 us; the launch traced here: 94 us
  starting transfers between devices  53.3 us (56%)
  Pallas kernels  16.3 us (17%)
  blocking collectives  14 us (15%)
  local copies, waits for them, and re-layouts  5.73 us (6%)
  waiting for transfers between devices  3.55 us (4%)
  between operations  0.99 us (1%)
    ppermute x12, starting transfers between devices, _shift(): return lax.ppermute(v, axis, pairs)  47.7 us
    all_to_all x1, blocking collectives, route_blocks(): lax.all_to_all(jnp.concatenate([slab, halo, sc], axis=1), 'gy', 0, 0, til...  14 us
    pallas_call x2, Pallas kernels, adjoint_call(): pl.pallas_call(kernel, out_shape=out_shape, scratch_shapes=_halo_scratch(...  6.92 us
    all_to_all x1, starting transfers between devices, route_blocks(): return lax.all_to_all(forward, 'gy', 0, 0, tiled=True)  5.56 us
    unnamed x39, local copies, waits for them, and re-layouts  3.67 us
    ppermute x12, waiting for transfers between devices, _shift(): return lax.ppermute(v, axis, pairs)  3.55 us
    pallas_call x1, Pallas kernels, state0_step_call(): pl.pallas_call(kernel, out_shape=(state,) + _edge_shapes(nplanes, x, y) +...  3.06 us
    pallas_call x1, Pallas kernels, step_call(): pl.pallas_call(kernel, out_shape=out_shape, scratch_shapes=_halo_scratch(...  2.73 us
  transfers between devices with their start and end apart: 13, of which 4 were waited for; matrix products, arithmetic and copies ran while one was open for 1% of the time, Pallas kernels for 3%

profile of v6, /device:TPU:130, one launch (start us, length us, event | category | flops | bytes accessed | tf_op | source)
XLA Modules:
  0.0 94.0 jit_solution(820163061145747647)
XLA Ops:
  0.6 1.4 %copy.29.tab_ref = f32[12,4]{1,0:T(8,128)} copy(f32[12,4]{0,1:T(4,128)} %param.10) | data formatting | bytes 384 | tf_op args[4]
  2.0 0.7 reshape.59.sc_ref
  2.7 1.8 %shard_map.77 = (f32[4,8,128]{2,1,0:T(8,128)}, f32[136,128]{1,0:T(8,128)}, f32[136,128]{1,0:T(8,128)}, f32[8,128]{1,0:T(8,128)}, f32[8,128]{1,0:T(8,128)}) custom-call(s32[8,128]{1,0:T(8,128)} %cls_ref.1, f32[12,4]{1,0:T(8,128)} %copy.29.tab_ref, f32[64]{0:T(128)} %reshape.59.sc_ref, f32[2,32,8,128]{3,2,1,0:T(8,128)} %refs_5_.1, bf16[2,32,8,128]{3,2,1,0:T(8,128)(2,1)} %slab_ref.1), custom_call_target="tpu_custom_call" | custom-call | tf_op jit(solution)/shard_map/pallas_call | solution.py:228
  4.5 3.5 %collective-permute-start = (f32[136,128]{1,0:T(8,128)}, f32[136,128]{1,0:T(8,128)S(1)}, u32[]{:S(2)}, u32[]{:S(2)}) collective-permute-start(f32[136,128]{1,0:T(8,128)} %get-tuple-element.22), channel_id=1, source_target_pairs={{0,16},{16,32},{32,48},{48,64},{64,80},{80,96},{96,112},{112,128},... | collective-permute-start | bytes 208904 | tf_op jit(solution)/shard_map/ppermute | solution.py:370
  8.0 4.5 %collective-permute-start.1 = (f32[136,128]{1,0:T(8,128)}, f32[136,128]{1,0:T(8,128)S(1)}, u32[]{:S(2)}, u32[]{:S(2)}) collective-permute-start(f32[136,128]{1,0:T(8,128)} %get-tuple-element.23), channel_id=1, source_target_pairs={{16,0},{32,16},{48,32},{64,48},{80,64},{96,80},{112,96},{128,112},... | collective-permute-start | bytes 208904 | tf_op jit(solution)/shard_map/ppermute | solution.py:370
  12.4 0.1 reshape.61
  12.5 0.6 collective-permute-done.cxm.refs_6_.refs_11_
  13.2 1.5 %collective-permute-done.1.cxp.refs_7_.refs_12_ = f32[136,128]{1,0:T(8,128)S(1)} collective-permute-done((f32[136,128]{1,0:T(8,128)}, f32[136,128]{1,0:T(8,128)S(1)}, u32[]{:S(2)}, u32[]{:S(2)}) %collective-permute-start.1) | collective-permute-done | bytes 69664 | tf_op jit(solution)/shard_map/ppermute | solution.py:370
  14.7 0.1 convert_element_type.46
  14.8 0.5 copy-done.1
  15.3 0.1 convert_element_type.47
  15.4 0.1 fusion.9
  15.5 14.0 %all_to_all.10.h_ref = bf16[16,6,8,128]{3,2,1,0:T(8,128)(2,1)} all-to-all(bf16[16,6,8,128]{3,2,1,0:T(8,128)(2,1)S(1)} %pad_maximum_fusion), channel_id=1, replica_groups=mesh['gx'=16,'gy'=16] {'gy'}, dimensions={0} | all-to-all | bytes 393216 | tf_op jit(solution)/shard_map/all_to_all | solution.py:430
  29.5 1.8 %shard_map.78 = bf16[16,8,8,128]{3,2,1,0:T(8,128)(2,1)} custom-call(s32[16]{0:T(128)} %hold_ref.1, bf16[16,6,8,128]{3,2,1,0:T(8,128)(2,1)} %all_to_all.10.h_ref), custom_call_target="tpu_custom_call" | custom-call | tf_op jit(solution)/shard_map/pallas_call | solution.py:409
  31.3 5.6 %all-to-all-start.1 = ((bf16[16,8,8,128]{3,2,1,0:T(8,128)(2,1)}), bf16[16,8,8,128]{3,2,1,0:T(8,128)(2,1)S(1)}, u32[]{:S(2)}, u32[]{:S(2)}) async-start(bf16[16,8,8,128]{3,2,1,0:T(8,128)(2,1)} %shard_map.78), calls=%async_computation.1 | async-start | bytes 524288 | tf_op jit(solution)/shard_map/all_to_all | solution.py:433
  36.9 2.1 %collective-permute-start.2 = (f32[8,128]{1,0:T(8,128)S(1)}, f32[8,128]{1,0:T(8,128)S(1)}, u32[]{:S(2)}, u32[]{:S(2)}) collective-permute-start(f32[8,128]{1,0:T(8,128)S(1)} %copy-done.16), channel_id=1, source_target_pairs={{0,1},{1,2},{2,3},{3,4},{4,5},{5,6},{6,7},{7,8},{8,9},{9,10},{10,1... | collective-permute-start | bytes 12296 | tf_op jit(solution)/shard_map/ppermute | solution.py:370
  38.9 5.9 %collective-permute-start.3 = (f32[8,128]{1,0:T(8,128)S(1)}, f32[8,128]{1,0:T(8,128)S(1)}, u32[]{:S(2)}, u32[]{:S(2)}) collective-permute-start(f32[8,128]{1,0:T(8,128)S(1)} %copy-done.15), channel_id=1, source_target_pairs={{1,0},{2,1},{3,2},{4,3},{5,4},{6,5},{7,6},{8,7},{9,8},{10,9},{11,1... | collective-permute-start | bytes 12296 | tf_op jit(solution)/shard_map/ppermute | solution.py:370
  44.9 0.0 copy-start.2
  44.9 0.1 reshape.57
  45.0 0.1 copy.34
  45.1 0.1 copy.35
  45.2 0.1 reshape.58
  45.3 0.7 reshape.60.sc_ref
  46.0 0.2 collective-permute-done.3.cyp.refs_9_.refs_14_
  46.2 0.4 copy-done.6
  46.6 0.2 copy-done.7
  46.8 3.1 %shard_map.79 = (f32[2,32,8,128]{3,2,1,0:T(8,128)}, f32[64,128]{1,0:T(8,128)}, f32[64,128]{1,0:T(8,128)}, f32[8,128]{1,0:T(8,128)}, f32[8,128]{1,0:T(8,128)}, /*...) custom-call(f32[320]{0:T(512)} %reshape.60.sc_ref, ...), custom_call_target="tpu_custom_call" | custom-call | tf_op jit(solution)/shard_map/pallas_call | solution.py:283
  49.8 2.8 %collective-permute-start.4 = (f32[64,128]{1,0:T(8,128)}, f32[64,128]{1,0:T(8,128)S(1)}, u32[]{:S(2)}, u32[]{:S(2)}) collective-permute-start(f32[64,128]{1,0:T(8,128)} %get-tuple-element.28), channel_id=1, source_target_pairs={{0,16},{16,32},{32,48},{48,64},{64,80},{80,96},{96,112},{112,128},... | collective-permute-start | bytes 98312 | tf_op jit(solution)/shard_map/ppermute | solution.py:370
  52.7 5.1 %collective-permute-start.5 = (f32[64,128]{1,0:T(8,128)}, f32[64,128]{1,0:T(8,128)S(1)}, u32[]{:S(2)}, u32[]{:S(2)}) collective-permute-start(f32[64,128]{1,0:T(8,128)} %get-tuple-element.29), channel_id=1, source_target_pairs={{16,0},{32,16},{48,32},{64,48},{80,64},{96,80},{112,96},{128,112},... | collective-permute-start | bytes 98312 | tf_op jit(solution)/shard_map/ppermute | solution.py:370
  57.8 3.5 %collective-permute-start.6 = (f32[8,128]{1,0:T(8,128)}, f32[8,128]{1,0:T(8,128)S(1)}, u32[]{:S(2)}, u32[]{:S(2)}) collective-permute-start(f32[8,128]{1,0:T(8,128)} %get-tuple-element.30), channel_id=1, source_target_pairs={{0,1},{1,2},{2,3},{3,4},{4,5},{5,6},{6,7},{7,8},{8,9},{9,10},{10,1... | collective-permute-start | bytes 12296 | tf_op jit(solution)/shard_map/ppermute | solution.py:370
  61.3 4.5 %collective-permute-start.7 = (f32[8,128]{1,0:T(8,128)S(1)}, f32[8,128]{1,0:T(8,128)S(1)}, u32[]{:S(2)}, u32[]{:S(2)}) collective-permute-start(f32[8,128]{1,0:T(8,128)S(1)} %copy-done.17), channel_id=1, source_target_pairs={{1,0},{2,1},{3,2},{4,3},{5,4},{6,5},{7,6},{8,7},{9,8},{10,9},{11,1... | collective-permute-start | bytes 12296 | tf_op jit(solution)/shard_map/ppermute | solution.py:370
  65.8 1.3 %collective-permute-done.7.refs_4_ = f32[8,128]{1,0:T(8,128)S(1)} collective-permute-done((f32[8,128]{1,0:T(8,128)S(1)}, f32[8,128]{1,0:T(8,128)S(1)}, u32[]{:S(2)}, u32[]{:S(2)}) %collective-permute-start.7) | collective-permute-done | bytes 4128 | tf_op jit(solution)/shard_map/ppermute | solution.py:370
  67.1 0.0 collective-permute-done.5.refs_2_
  67.1 0.6 copy-done.11
  67.7 0.0 copy-done.4
  67.7 0.0 copy-done.5
  67.7 3.5 %shard_map.81 = (f32[2,32,8,128]{3,2,1,0:T(8,128)}, f32[64,128]{1,0:T(8,128)}, f32[64,128]{1,0:T(8,128)}, f32[8,128]{1,0:T(8,128)}, f32[8,128]{1,0:T(8,128)}) custom-call(f32[2,32,8,128]{3,2,1,0:T(8,128)} %get-tuple-element.27.refs_0_, f32[64,128]{1,0:T(8,128)} %copy-done.4, f32[64,128]{1,0:T(8,128)} %copy-done.5, f32[8,128]{1,0:T(8,128)} %copy-done.10, ...), custom_call_target="tpu_custom_call" | custom-call | tf_op jit(solution)/shard_map/pallas_call | solution.py:354
  71.3 1.9 %collective-permute-start.8 = (f32[64,128]{1,0:T(8,128)}, f32[64,128]{1,0:T(8,128)S(1)}, u32[]{:S(2)}, u32[]{:S(2)}) collective-permute-start(f32[64,128]{1,0:T(8,128)} %get-tuple-element.38), channel_id=1, source_target_pairs={{0,16},{16,32},{32,48},{48,64},{64,80},{80,96},{96,112},{112,128},... | collective-permute-start | bytes 98312 | tf_op jit(solution)/shard_map/ppermute | solution.py:370
  73.2 6.0 %collective-permute-start.9 = (f32[64,128]{1,0:T(8,128)}, f32[64,128]{1,0:T(8,128)S(1)}, u32[]{:S(2)}, u32[]{:S(2)}) collective-permute-start(f32[64,128]{1,0:T(8,128)} %get-tuple-element.39), channel_id=1, source_target_pairs={{16,0},{32,16},{48,32},{64,48},{80,64},{96,80},{112,96},{128,112},... | collective-permute-start | bytes 98312 | tf_op jit(solution)/shard_map/ppermute | solution.py:370
  79.2 2.9 %collective-permute-start.10 = (f32[8,128]{1,0:T(8,128)}, f32[8,128]{1,0:T(8,128)S(1)}, u32[]{:S(2)}, u32[]{:S(2)}) collective-permute-start(f32[8,128]{1,0:T(8,128)} %get-tuple-element.40), channel_id=1, source_target_pairs={{0,1},{1,2},{2,3},{3,4},{4,5},{5,6},{6,7},{7,8},{8,9},{9,10},{10,1... | collective-permute-start | bytes 12296 | tf_op jit(solution)/shard_map/ppermute | solution.py:370
  82.1 5.1 %collective-permute-start.11 = (f32[8,128]{1,0:T(8,128)S(1)}, f32[8,128]{1,0:T(8,128)S(1)}, u32[]{:S(2)}, u32[]{:S(2)}) collective-permute-start(f32[8,128]{1,0:T(8,128)S(1)} %copy-done.18), channel_id=1, source_target_pairs={{1,0},{2,1},{3,2},{4,3},{5,4},{6,5},{7,6},{8,7},{9,8},{10,9},{11,1... | collective-permute-start | bytes 12296 | tf_op jit(solution)/shard_map/ppermute | solution.py:370
  87.2 2.7 %shard_map.80 = f32[2,32,8,128]{3,2,1,0:T(8,128)} custom-call(f32[2,32,8,128]{3,2,1,0:T(8,128)} %get-tuple-element.27.refs_0_, f32[64,128]{1,0:T(8,128)} %copy-done.4, f32[64,128]{1,0:T(8,128)} %copy-done.5, f32[8,128]{1,0:T(8,128)} %copy-done.10, f32[8,128]{1,0:T(8,128)} %copy-done.11, f32[4,8,128]{2,1,0:T(8,128)} %get-tuple-element.24.c_ref.refs_5_.refs_10_, ...), custom_call_target="tpu_custom_call" | custom-call | tf_op jit(solution)/shard_map/pallas_call | solution.py:317
  90.0 0.0 collective-permute-done.10.refs_8_
  90.0 0.5 copy-done.12
  90.6 0.0 copy-done.13
  90.6 0.0 copy-done.8
  90.6 0.0 copy-done.9
  90.6 3.4 %shard_map.82 = f32[2,32,8,128]{3,2,1,0:T(8,128)} custom-call(f32[2,32,8,128]{3,2,1,0:T(8,128)} %get-tuple-element.32.refs_0_, f32[64,128]{1,0:T(8,128)} %get-tuple-element.33.refs_1_, f32[64,128]{1,0:T(8,128)} %get-tuple-element.34.refs_2_, f32[8,128]{1,0:T(8,128)} %get-tuple-element.35.refs_3_, f32[8,128]{1,0:T(8,128)} %get-tuple-element.36.refs_4_, ...), custom_call_target="tpu_custom_call" | custom-call | tf_op jit(solution)/shard_map/pallas_call | solution.py:354
  (46 shorter events, 0.2 us)
Async XLA Ops:
  0.6 1.4 %copy-start.14 = (bf16[2,32,1,1]{1,0,3,2:T(2,128)(2,1)S(1)}, bf16[2,32,1,1]{1,0,3,2:T(2,128)(2,1)}, u32[]{:S(2)}) copy-start(bf16[2,32,1,1]{1,0,3,2:T(2,128)(2,1)} %param.7) | copy-start | bytes 388
  4.5 8.6 %collective-permute-start = (f32[136,128]{1,0:T(8,128)}, f32[136,128]{1,0:T(8,128)S(1)}, u32[]{:S(2)}, u32[]{:S(2)}) collective-permute-start(f32[136,128]{1,0:T(8,128)} %get-tuple-element.22), channel_id=1, source_target_pairs={{0,16},{16,32},{32,48},{48,64},{64,80},{80,96},{96,112},{112,128},... | collective-permute-start | bytes 208904 | tf_op jit(solution)/shard_map/ppermute | solution.py:370
  8.0 6.7 %collective-permute-start.1 = (f32[136,128]{1,0:T(8,128)}, f32[136,128]{1,0:T(8,128)S(1)}, u32[]{:S(2)}, u32[]{:S(2)}) collective-permute-start(f32[136,128]{1,0:T(8,128)} %get-tuple-element.23), channel_id=1, source_target_pairs={{16,0},{32,16},{48,32},{64,48},{80,64},{96,80},{112,96},{128,112},... | collective-permute-start | bytes 208904 | tf_op jit(solution)/shard_map/ppermute | solution.py:370
  13.1 1.6 %copy-start = (f32[136,128]{1,0:T(8,128)}, f32[136,128]{1,0:T(8,128)S(1)}, u32[]{:S(2)}) copy-start(f32[136,128]{1,0:T(8,128)S(1)} %collective-permute-done.cxm.refs_6_.refs_11_) | copy-start | bytes 208900
  13.2 2.3 %copy-start.3 = (bf16[2,32,8,128]{3,2,1,0:T(8,128)(2,1)S(1)}, bf16[2,32,8,128]{3,2,1,0:T(8,128)(2,1)}, u32[]{:S(2)}) copy-start(bf16[2,32,8,128]{3,2,1,0:T(8,128)(2,1)} %slab_ref.1) | copy-start | bytes 393220
  14.7 0.6 copy-start.1
  31.3 5.6 %copy-start.16 = (f32[8,128]{1,0:T(8,128)S(1)}, f32[8,128]{1,0:T(8,128)}, u32[]{:S(2)}) copy-start(f32[8,128]{1,0:T(8,128)} %get-tuple-element.25) | copy-start | bytes 12292
  31.3 7.6 %copy-start.15 = (f32[8,128]{1,0:T(8,128)S(1)}, f32[8,128]{1,0:T(8,128)}, u32[]{:S(2)}) copy-start(f32[8,128]{1,0:T(8,128)} %get-tuple-element.26) | copy-start | bytes 12292
  31.3 13.6 %all-to-all-start.1 = ((bf16[16,8,8,128]{3,2,1,0:T(8,128)(2,1)}), bf16[16,8,8,128]{3,2,1,0:T(8,128)(2,1)S(1)}, u32[]{:S(2)}, u32[]{:S(2)}) async-start(bf16[16,8,8,128]{3,2,1,0:T(8,128)(2,1)} %shard_map.78), calls=%async_computation.1 | async-start | bytes 524288 | tf_op jit(solution)/shard_map/all_to_all | solution.py:433
  36.9 9.1 %collective-permute-start.2 = (f32[8,128]{1,0:T(8,128)S(1)}, f32[8,128]{1,0:T(8,128)S(1)}, u32[]{:S(2)}, u32[]{:S(2)}) collective-permute-start(f32[8,128]{1,0:T(8,128)S(1)} %copy-done.16), channel_id=1, source_target_pairs={{0,1},{1,2},{2,3},{3,4},{4,5},{5,6},{6,7},{7,8},{8,9},{9,10},{10,1... | collective-permute-start | bytes 12296 | tf_op jit(solution)/shard_map/ppermute | solution.py:370
  38.9 7.2 %collective-permute-start.3 = (f32[8,128]{1,0:T(8,128)S(1)}, f32[8,128]{1,0:T(8,128)S(1)}, u32[]{:S(2)}, u32[]{:S(2)}) collective-permute-start(f32[8,128]{1,0:T(8,128)S(1)} %copy-done.15), channel_id=1, source_target_pairs={{1,0},{2,1},{3,2},{4,3},{5,4},{6,5},{7,6},{8,7},{9,8},{10,9},{11,1... | collective-permute-start | bytes 12296 | tf_op jit(solution)/shard_map/ppermute | solution.py:370
  44.9 1.3 %copy-start.2 = (bf16[16,8,8,128]{3,2,1,0:T(8,128)(2,1)}, bf16[16,8,8,128]{3,2,1,0:T(8,128)(2,1)S(1)}, u32[]{:S(2)}) copy-start(bf16[16,8,8,128]{3,2,1,0:T(8,128)(2,1)S(1)} %all-to-all-done.1.r_ref) | copy-start | bytes 786436
  46.0 0.6 copy-start.6
  46.2 0.6 copy-start.7
  49.8 11.5 %copy-start.17 = (f32[8,128]{1,0:T(8,128)S(1)}, f32[8,128]{1,0:T(8,128)}, u32[]{:S(2)}) copy-start(f32[8,128]{1,0:T(8,128)} %get-tuple-element.31) | copy-start | bytes 12292
  49.8 17.3 %collective-permute-start.4 = (f32[64,128]{1,0:T(8,128)}, f32[64,128]{1,0:T(8,128)S(1)}, u32[]{:S(2)}, u32[]{:S(2)}) collective-permute-start(f32[64,128]{1,0:T(8,128)} %get-tuple-element.28), channel_id=1, source_target_pairs={{0,16},{16,32},{32,48},{48,64},{64,80},{80,96},{96,112},{112,128},... | collective-permute-start | bytes 98312 | tf_op jit(solution)/shard_map/ppermute | solution.py:370
  52.7 14.5 %collective-permute-start.5 = (f32[64,128]{1,0:T(8,128)}, f32[64,128]{1,0:T(8,128)S(1)}, u32[]{:S(2)}, u32[]{:S(2)}) collective-permute-start(f32[64,128]{1,0:T(8,128)} %get-tuple-element.29), channel_id=1, source_target_pairs={{16,0},{32,16},{48,32},{64,48},{80,64},{96,80},{112,96},{128,112},... | collective-permute-start | bytes 98312 | tf_op jit(solution)/shard_map/ppermute | solution.py:370
  57.8 8.0 %collective-permute-start.6 = (f32[8,128]{1,0:T(8,128)}, f32[8,128]{1,0:T(8,128)S(1)}, u32[]{:S(2)}, u32[]{:S(2)}) collective-permute-start(f32[8,128]{1,0:T(8,128)} %get-tuple-element.30), channel_id=1, source_target_pairs={{0,1},{1,2},{2,3},{3,4},{4,5},{5,6},{6,7},{7,8},{8,9},{9,10},{10,1... | collective-permute-start | bytes 12296 | tf_op jit(solution)/shard_map/ppermute | solution.py:370
  61.3 5.8 %collective-permute-start.7 = (f32[8,128]{1,0:T(8,128)S(1)}, f32[8,128]{1,0:T(8,128)S(1)}, u32[]{:S(2)}, u32[]{:S(2)}) collective-permute-start(f32[8,128]{1,0:T(8,128)S(1)} %copy-done.17), channel_id=1, source_target_pairs={{1,0},{2,1},{3,2},{4,3},{5,4},{6,5},{7,6},{8,7},{9,8},{10,9},{11,1... | collective-permute-start | bytes 12296 | tf_op jit(solution)/shard_map/ppermute | solution.py:370
  65.8 1.3 %copy-start.10 = (f32[8,128]{1,0:T(8,128)}, f32[8,128]{1,0:T(8,128)S(1)}, u32[]{:S(2)}) copy-start(f32[8,128]{1,0:T(8,128)S(1)} %collective-permute-done.6.refs_3_) | copy-start | bytes 12292
  67.1 0.6 copy-start.11
  67.1 0.6 copy-start.4
  67.1 0.6 copy-start.5
  71.3 10.8 %copy-start.18 = (f32[8,128]{1,0:T(8,128)S(1)}, f32[8,128]{1,0:T(8,128)}, u32[]{:S(2)}) copy-start(f32[8,128]{1,0:T(8,128)} %get-tuple-element.41) | copy-start | bytes 12292
  71.3 18.7 %collective-permute-start.8 = (f32[64,128]{1,0:T(8,128)}, f32[64,128]{1,0:T(8,128)S(1)}, u32[]{:S(2)}, u32[]{:S(2)}) collective-permute-start(f32[64,128]{1,0:T(8,128)} %get-tuple-element.38), channel_id=1, source_target_pairs={{0,16},{16,32},{32,48},{48,64},{64,80},{80,96},{96,112},{112,128},... | collective-permute-start | bytes 98312 | tf_op jit(solution)/shard_map/ppermute | solution.py:370
  73.2 16.8 %collective-permute-start.9 = (f32[64,128]{1,0:T(8,128)}, f32[64,128]{1,0:T(8,128)S(1)}, u32[]{:S(2)}, u32[]{:S(2)}) collective-permute-start(f32[64,128]{1,0:T(8,128)} %get-tuple-element.39), channel_id=1, source_target_pairs={{16,0},{32,16},{48,32},{64,48},{80,64},{96,80},{112,96},{128,112},... | collective-permute-start | bytes 98312 | tf_op jit(solution)/shard_map/ppermute | solution.py:370
  79.2 10.7 %collective-permute-start.10 = (f32[8,128]{1,0:T(8,128)}, f32[8,128]{1,0:T(8,128)S(1)}, u32[]{:S(2)}, u32[]{:S(2)}) collective-permute-start(f32[8,128]{1,0:T(8,128)} %get-tuple-element.40), channel_id=1, source_target_pairs={{0,1},{1,2},{2,3},{3,4},{4,5},{5,6},{6,7},{7,8},{8,9},{9,10},{10,1... | collective-permute-start | bytes 12296 | tf_op jit(solution)/shard_map/ppermute | solution.py:370
  82.1 7.9 %collective-permute-start.11 = (f32[8,128]{1,0:T(8,128)S(1)}, f32[8,128]{1,0:T(8,128)S(1)}, u32[]{:S(2)}, u32[]{:S(2)}) collective-permute-start(f32[8,128]{1,0:T(8,128)S(1)} %copy-done.18), channel_id=1, source_target_pairs={{1,0},{2,1},{3,2},{4,3},{5,4},{6,5},{7,6},{8,7},{9,8},{10,9},{11,1... | collective-permute-start | bytes 12296 | tf_op jit(solution)/shard_map/ppermute | solution.py:370
  90.0 0.6 copy-start.12
  90.0 0.6 copy-start.13
  90.0 0.6 copy-start.8
  90.0 0.6 copy-start.9

commit v7 on v6

--- a/solution.py
+++ b/solution.py
@@ -196,12 +196,11 @@
     return -(-n // 8) * 8
 
 
-def prep_call(soil_class, soil_table, cot, slab, scales):
+def prep_call(soil_class, soil_table, cot):
     nf, nz, x, y = cot.shape
     nclass = soil_table.shape[0]
-    nplanes = nf * nz
-
-    def kernel(cls_ref, tab_ref, sc_ref, cot_ref, slab_ref, coef_ref, xf_ref, xl_ref, yf_ref, yl_ref):
+
+    def kernel(cls_ref, tab_ref, cot_ref, coef_ref, xf_ref, xl_ref, yf_ref, yl_ref):
         cls = cls_ref[...]
         coefs = []
         for k in range(NCOEF):
@@ -212,32 +211,17 @@
             coefs.append(cv)
         vals = [cot_ref[f, z] for f in range(nf) for z in range(nz)] + coefs
         _pack_edges(vals, xf_ref, xl_ref, yf_ref, yl_ref)
-        base = len(vals)
-        for k in range(nplanes):
-            v = slab_ref[k // nz, k % nz].astype(F32)
-            xf_ref[base + k : base + k + 1, :] = v[0:1, :]
-            xl_ref[base + k : base + k + 1, :] = v[x - 1 : x, :]
-        _, lane = _iotas((1, y))
-        row = jnp.zeros((1, y), F32)
-        for k in range(nplanes):
-            row = jnp.where(lane == k, sc_ref[k], row)
-        xf_ref[base + nplanes : base + nplanes + 1, :] = row
-        xl_ref[base + nplanes : base + nplanes + 1, :] = row
-
-    rows = _rows(2 * nplanes + NCOEF + 1)
+
+    rows = _rows(nf * nz + NCOEF)
     return pl.pallas_call(
         kernel,
-        out_shape=(jax.ShapeDtypeStruct((NCOEF, x, y), F32),)
-        + _edge_shapes(rows, x, y)[:2]
-        + _edge_shapes(8, x, y)[2:],
+        out_shape=(jax.ShapeDtypeStruct((NCOEF, x, y), F32),) + _edge_shapes(rows, x, y),
         in_specs=[
             pl.BlockSpec(memory_space=VMEM),
             pl.BlockSpec(memory_space=SMEM),
-            pl.BlockSpec(memory_space=SMEM),
-            pl.BlockSpec(memory_space=VMEM),
             pl.BlockSpec(memory_space=VMEM),
         ],
-    )(soil_class, soil_table, scales, cot, slab)
+    )(soil_class, soil_table, cot)
 
 
 def _state0_body(sc_ref, r_ref, s_ref, xm_ref, xp_ref, ym_ref, yp_ref, per):
@@ -379,15 +363,21 @@
     )
 
 
-def forward_call(holder, held, per):
+def forward_call(holder, held, xm_rows, xp_rows, per):
     n, planes, x, y = held.shape
 
-    def kernel(hold_ref, h_ref, o_ref):
-        _, lane = _iotas((x, y))
+    def kernel(hold_ref, h_ref, m_ref, p_ref, o_ref):
+        row, lane = _iotas((x, y))
         for g in range(n):
             h = hold_ref[g]
-            for i in range(planes):
+            for i in range(per):
                 o_ref[g, i] = h_ref[h, i]
+            hm = m_ref[h].astype(F32)
+            hp = p_ref[h].astype(F32)
+            o_ref[g, per] = jnp.where(row < per, hm, _roll(hp, per, 0)).astype(o_ref.dtype)
+            own = h_ref[h, per].astype(F32)
+            sc = jnp.where(row == 0, own, jnp.where(row == 1, _roll(hm, 1 - per, 0), _roll(hp, 2 - per, 0)))
+            o_ref[g, per + 1] = jnp.where(row < 3, sc, 0.0).astype(o_ref.dtype)
             cols = jnp.zeros((x, y), F32)
             scl = jnp.zeros((x, y), F32)
             if g > 0:
@@ -395,41 +385,36 @@
                 for i in range(per):
                     v = h_ref[hl, i].astype(F32)
                     cols = jnp.where(lane == i, _roll(v, i - (y - 1), 1), cols)
-                scl = jnp.where(lane < per, h_ref[hl, per + 1].astype(F32), scl)
+                scl = jnp.where(lane < per, h_ref[hl, per].astype(F32), scl)
             if g < n - 1:
                 hr = hold_ref[g + 1]
                 for i in range(per):
                     v = h_ref[hr, i].astype(F32)
                     cols = jnp.where(lane == per + i, _roll(v, per + i, 1), cols)
-                sv = _roll(h_ref[hr, per + 1].astype(F32), per, 1)
+                sv = _roll(h_ref[hr, per].astype(F32), per, 1)
                 scl = jnp.where((lane >= per) & (lane < 2 * per), sv, scl)
-            o_ref[g, planes] = cols.astype(o_ref.dtype)
-            o_ref[g, planes + 1] = scl.astype(o_ref.dtype)
+            o_ref[g, per + 2] = cols.astype(o_ref.dtype)
+            o_ref[g, per + 3] = scl.astype(o_ref.dtype)
 
     return pl.pallas_call(
         kernel,
-        out_shape=jax.ShapeDtypeStruct((n, planes + 2, x, y), held.dtype),
-        in_specs=[pl.BlockSpec(memory_space=SMEM), pl.BlockSpec(memory_space=VMEM)],
-    )(holder, held)
-
-
-def route_blocks(stored_slab, block_scales, holder, xm_all, xp_all, first):
+        out_shape=jax.ShapeDtypeStruct((n, per + 4, x, y), held.dtype),
+        in_specs=[pl.BlockSpec(memory_space=SMEM)] + [pl.BlockSpec(memory_space=VMEM)] * 3,
+    )(holder, held, xm_rows, xp_rows)
+
+
+def route_blocks(stored_slab, block_scales, holder):
     nf, nz, x, y = stored_slab.shape
     n = lax.axis_size("gy")
     nplanes = nf * nz
     per = nplanes // n
-    bf = stored_slab.dtype
     slab = stored_slab.reshape(n, per, x, y)
-    rows_m = xm_all[first : first + nplanes].astype(bf).reshape(n, per, y)
-    rows_p = xp_all[first : first + nplanes].astype(bf).reshape(n, per, y)
-    halo = jnp.concatenate([rows_m, rows_p], axis=1)[:, None]
-    sc_m = xm_all[first + nplanes, :nplanes].astype(bf).reshape(n, 1, per)
-    sc_p = xp_all[first + nplanes, :nplanes].astype(bf).reshape(n, 1, per)
-    sc = jnp.concatenate([block_scales.reshape(n, 1, per), sc_m, sc_p], axis=1)
-    sc = jnp.pad(sc, ((0, 0), (0, x - 3), (0, y - per)))[:, None]
-    held = lax.all_to_all(jnp.concatenate([slab, halo, sc], axis=1), "gy", 0, 0, tiled=True)
-
-    forward = forward_call(holder, held, per)
+    sc = jnp.pad(block_scales.reshape(n, 1, 1, per), ((0, 0), (0, 0), (0, x - 1), (0, y - per)))
+    held = lax.all_to_all(jnp.concatenate([slab, sc], axis=1), "gy", 0, 0, tiled=True)
+    pad = ((0, 0), (0, x - per - 1), (0, 0))
+    first = jnp.pad(jnp.concatenate([held[:, :per, 0, :], held[:, per:, 0, :]], axis=1), pad)
+    last = jnp.pad(jnp.concatenate([held[:, :per, x - 1, :], held[:, per:, 0, :]], axis=1), pad)
+    forward = forward_call(holder, held, _shift(last, "gx", 1), _shift(first, "gx", -1), per)
     return lax.all_to_all(forward, "gy", 0, 0, tiled=True)
 
 
@@ -437,13 +422,11 @@
     nf, nz, x, y = stored_slab.shape
     nplanes = nf * nz
 
-    coef, cxf, cxl, cyf, cyl = prep_call(
-        soil_class, soil_table, cotangent, stored_slab, block_scales.reshape(-1).astype(F32)
-    )
+    pieces = route_blocks(stored_slab, block_scales, holder)
+
+    coef, cxf, cxl, cyf, cyl = prep_call(soil_class, soil_table, cotangent)
     c_halo = exchange(cxf, cxl, cyf, cyl)
     c_first = nplanes
-
-    pieces = route_blocks(stored_slab, block_scales, holder, c_halo[0], c_halo[1], nplanes + NCOEF)
     per = nplanes // pieces.shape[0]
     scales = jnp.concatenate(
         [

time: 94.8 us -> 103 us (1.086)
  starting transfers between devices: 53.3 us -> 61.6 us
    ppermute x12 -> x14, starting transfers between devices: 47.7 us -> 56.1 us  [_shift(): return lax.ppermute(v, axis, pairs)]
    ppermute x12 -> x14, waiting for transfers between devices: 3.55 us -> 3.02 us  [_shift(): return lax.ppermute(v, axis, pairs)]
    unnamed x39 -> x42, local copies, waits for them, and re-layouts: 3.67 us -> 3.63 us
  transfers between devices with their start and end apart: 13 -> 15, of which waited for: 4 -> 3; matrix products, arithmetic and copies ran while one was open for 1% -> 2% of each run, Pallas kernels for 3% -> 4%
where the time goes in v7:
time: 103 us; the launch traced here: 102 us
  starting transfers between devices  61.6 us (60%)
  Pallas kernels  16.1 us (16%)
  blocking collectives  13.6 us (13%)
  local copies, waits for them, and re-layouts  5.56 us (5%)
  waiting for transfers between devices  3.02 us (3%)
  between operations  1.03 us (1%)
    ppermute x14, starting transfers between devices, _shift(): return lax.ppermute(v, axis, pairs)  56.1 us
    all_to_all x1, blocking collectives, route_blocks(): lax.all_to_all(jnp.concatenate([slab, sc], axis=1), 'gy', 0, 0, tiled=True)  13.6 us
    pallas_call x2, Pallas kernels, adjoint_call(): pl.pallas_call(kernel, out_shape=out_shape, scratch_shapes=_halo_scratch(...  6.8 us
    all_to_all x1, starting transfers between devices, route_blocks(): return lax.all_to_all(forward, 'gy', 0, 0, tiled=True)  5.49 us
    unnamed x42, local copies, waits for them, and re-layouts  3.63 us
    pallas_call x1, Pallas kernels, state0_step_call(): pl.pallas_call(kernel, out_shape=(state,) + _edge_shapes(nplanes, x, y) +...  3.06 us
    ppermute x14, waiting for transfers between devices, _shift(): return lax.ppermute(v, axis, pairs)  3.02 us
    pallas_call x1, Pallas kernels, step_call(): pl.pallas_call(kernel, out_shape=out_shape, scratch_shapes=_halo_scratch(...  2.69 us
  transfers between devices with their start and end apart: 15, of which 3 were waited for; matrix products, arithmetic and copies ran while one was open for 2% of the time, Pallas kernels for 4%

profile of v7, /device:TPU:130, one launch (start us, length us, event | category | flops | bytes accessed | tf_op | source)
XLA Modules:
  0.0 102.0 jit_solution(6214165450223419043)
XLA Ops:
  0.6 0.7 reshape.25
  1.4 0.9 fusion.1
  2.3 13.6 %all_to_all.10.h_ref = bf16[16,5,8,128]{3,2,1,0:T(8,128)(2,1)S(1)} all-to-all(bf16[16,5,8,128]{3,2,1,0:T(8,128)(2,1)S(1)} %fusion.1), channel_id=1, replica_groups=mesh['gx'=16,'gy'=16] {'gy'}, dimensions={0} | all-to-all | bytes 327680 | tf_op jit(solution)/shard_map/all_to_all | solution.py:413
  16.1 0.5 copy-done.1
  16.6 2.6 %collective-permute-start = (bf16[16,8,128]{2,1,0:T(8,128)(2,1)S(1)}, bf16[16,8,128]{2,1,0:T(8,128)(2,1)S(1)}, u32[]{:S(2)}, u32[]{:S(2)}) collective-permute-start(bf16[16,8,128]{2,1,0:T(8,128)(2,1)S(1)} %pad.12), channel_id=1, source_target_pairs={{0,16},{16,32},{32,48},{48,64},{64,80},{80,96},{96,112},{112,128},... | collective-permute-start | bytes 98312 | tf_op jit(solution)/shard_map/ppermute | solution.py:354
  19.2 5.4 %collective-permute-start.1 = (bf16[16,8,128]{2,1,0:T(8,128)(2,1)S(1)}, bf16[16,8,128]{2,1,0:T(8,128)(2,1)S(1)}, u32[]{:S(2)}, u32[]{:S(2)}) collective-permute-start(bf16[16,8,128]{2,1,0:T(8,128)(2,1)S(1)} %pad.13), channel_id=1, source_target_pairs={{16,0},{32,16},{48,32},{64,48},{80,64},{96,80},{112,96},{128,112},... | collective-permute-start | bytes 98312 | tf_op jit(solution)/shard_map/ppermute | solution.py:354
  24.6 1.6 %collective-permute-done.1.p_ref = bf16[16,8,128]{2,1,0:T(8,128)(2,1)S(1)} collective-permute-done((bf16[16,8,128]{2,1,0:T(8,128)(2,1)S(1)}, bf16[16,8,128]{2,1,0:T(8,128)(2,1)S(1)}, u32[]{:S(2)}, u32[]{:S(2)}) %collective-permute-start.1) | collective-permute-done | bytes 32800 | tf_op jit(solution)/shard_map/ppermute | solution.py:354
  26.2 0.6 copy-done.11
  26.8 1.8 %shard_map.77 = bf16[16,8,8,128]{3,2,1,0:T(8,128)(2,1)} custom-call(s32[16]{0:T(128)} %hold_ref.1, bf16[16,5,8,128]{3,2,1,0:T(8,128)(2,1)} %copy-done.1, bf16[16,8,128]{2,1,0:T(8,128)(2,1)} %copy-done.10, bf16[16,8,128]{2,1,0:T(8,128)(2,1)} %copy-done.11), custom_call_target="tpu_custom_call" | custom-call | tf_op jit(solution)/shard_map/pallas_call | solution.py:399
  28.6 5.5 %all-to-all-start.1 = ((bf16[16,8,8,128]{3,2,1,0:T(8,128)(2,1)}), bf16[16,8,8,128]{3,2,1,0:T(8,128)(2,1)S(1)}, u32[]{:S(2)}, u32[]{:S(2)}) async-start(bf16[16,8,8,128]{3,2,1,0:T(8,128)(2,1)} %shard_map.77), calls=%async_computation.1 | async-start | bytes 524288 | tf_op jit(solution)/shard_map/all_to_all | solution.py:418
  34.1 0.7 copy.33.tab_ref
  34.8 1.8 %shard_map.78 = (f32[4,8,128]{2,1,0:T(8,128)}, f32[72,128]{1,0:T(8,128)}, f32[72,128]{1,0:T(8,128)}, f32[8,128]{1,0:T(8,128)}, f32[8,128]{1,0:T(8,128)}) custom-call(s32[8,128]{1,0:T(8,128)} %cls_ref.1, f32[12,4]{1,0:T(8,128)} %copy.33.tab_ref, f32[2,32,8,128]{3,2,1,0:T(8,128)} %refs_5_.1), custom_call_target="tpu_custom_call" | custom-call | tf_op jit(solution)/shard_map/pallas_call | solution.py:216
  36.5 3.6 %collective-permute-start.2 = (f32[72,128]{1,0:T(8,128)}, f32[72,128]{1,0:T(8,128)S(1)}, u32[]{:S(2)}, u32[]{:S(2)}) collective-permute-start(f32[72,128]{1,0:T(8,128)} %get-tuple-element.23), channel_id=1, source_target_pairs={{0,16},{16,32},{32,48},{48,64},{64,80},{80,96},{96,112},{112,128},... | collective-permute-start | bytes 110600 | tf_op jit(solution)/shard_map/ppermute | solution.py:354
  40.1 4.8 %collective-permute-start.3 = (f32[72,128]{1,0:T(8,128)}, f32[72,128]{1,0:T(8,128)S(1)}, u32[]{:S(2)}, u32[]{:S(2)}) collective-permute-start(f32[72,128]{1,0:T(8,128)} %get-tuple-element.24), channel_id=1, source_target_pairs={{16,0},{32,16},{48,32},{64,48},{80,64},{96,80},{112,96},{128,112},... | collective-permute-start | bytes 110600 | tf_op jit(solution)/shard_map/ppermute | solution.py:354
  44.9 1.9 %collective-permute-start.4 = (f32[8,128]{1,0:T(8,128)}, f32[8,128]{1,0:T(8,128)S(1)}, u32[]{:S(2)}, u32[]{:S(2)}) collective-permute-start(f32[8,128]{1,0:T(8,128)} %get-tuple-element.25), channel_id=1, source_target_pairs={{0,1},{1,2},{2,3},{3,4},{4,5},{5,6},{6,7},{7,8},{8,9},{9,10},{10,1... | collective-permute-start | bytes 12296 | tf_op jit(solution)/shard_map/ppermute | solution.py:354
  46.9 6.0 %collective-permute-start.5 = (f32[8,128]{1,0:T(8,128)S(1)}, f32[8,128]{1,0:T(8,128)S(1)}, u32[]{:S(2)}, u32[]{:S(2)}) collective-permute-start(f32[8,128]{1,0:T(8,128)S(1)} %copy-done.17), channel_id=1, source_target_pairs={{1,0},{2,1},{3,2},{4,3},{5,4},{6,5},{7,6},{8,7},{9,8},{10,9},{11,1... | collective-permute-start | bytes 12296 | tf_op jit(solution)/shard_map/ppermute | solution.py:354
  52.9 0.0 all-to-all-done.1.r_ref
  52.9 0.0 copy-start
  53.0 0.1 reshape.22
  53.1 0.1 copy.31
  53.2 0.1 copy.32
  53.3 0.1 reshape.23
  53.4 0.7 reshape.24.sc_ref
  54.1 0.0 collective-permute-done.4.cym.refs_8_.refs_13_
  54.1 0.2 collective-permute-done.5.cyp.refs_9_.refs_14_
  54.3 0.4 copy-done.6
  54.7 0.2 copy-done.7
  54.8 0.0 copy-done.2
  54.8 0.0 copy-done.3
  54.9 3.1 %shard_map.79 = (f32[2,32,8,128]{3,2,1,0:T(8,128)}, f32[64,128]{1,0:T(8,128)}, f32[64,128]{1,0:T(8,128)}, f32[8,128]{1,0:T(8,128)}, f32[8,128]{1,0:T(8,128)}, /*...) custom-call(f32[320]{0:T(512)} %reshape.24.sc_ref, ...), custom_call_target="tpu_custom_call" | custom-call | tf_op jit(solution)/shard_map/pallas_call | solution.py:267
  57.9 1.9 %collective-permute-start.6 = (f32[64,128]{1,0:T(8,128)}, f32[64,128]{1,0:T(8,128)S(1)}, u32[]{:S(2)}, u32[]{:S(2)}) collective-permute-start(f32[64,128]{1,0:T(8,128)} %get-tuple-element.28), channel_id=1, source_target_pairs={{0,16},{16,32},{32,48},{48,64},{64,80},{80,96},{96,112},{112,128},... | collective-permute-start | bytes 98312 | tf_op jit(solution)/shard_map/ppermute | solution.py:354
  59.9 6.0 %collective-permute-start.7 = (f32[64,128]{1,0:T(8,128)}, f32[64,128]{1,0:T(8,128)S(1)}, u32[]{:S(2)}, u32[]{:S(2)}) collective-permute-start(f32[64,128]{1,0:T(8,128)} %get-tuple-element.29), channel_id=1, source_target_pairs={{16,0},{32,16},{48,32},{64,48},{80,64},{96,80},{112,96},{128,112},... | collective-permute-start | bytes 98312 | tf_op jit(solution)/shard_map/ppermute | solution.py:354
  65.9 4.1 %collective-permute-start.8 = (f32[8,128]{1,0:T(8,128)}, f32[8,128]{1,0:T(8,128)S(1)}, u32[]{:S(2)}, u32[]{:S(2)}) collective-permute-start(f32[8,128]{1,0:T(8,128)} %get-tuple-element.30), channel_id=1, source_target_pairs={{0,1},{1,2},{2,3},{3,4},{4,5},{5,6},{6,7},{7,8},{8,9},{9,10},{10,1... | collective-permute-start | bytes 12296 | tf_op jit(solution)/shard_map/ppermute | solution.py:354
  70.0 3.9 %collective-permute-start.9 = (f32[8,128]{1,0:T(8,128)S(1)}, f32[8,128]{1,0:T(8,128)S(1)}, u32[]{:S(2)}, u32[]{:S(2)}) collective-permute-start(f32[8,128]{1,0:T(8,128)S(1)} %copy-done.18), channel_id=1, source_target_pairs={{1,0},{2,1},{3,2},{4,3},{5,4},{6,5},{7,6},{8,7},{9,8},{10,9},{11,1... | collective-permute-start | bytes 12296 | tf_op jit(solution)/shard_map/ppermute | solution.py:354
  73.9 1.3 %collective-permute-done.9.refs_4_ = f32[8,128]{1,0:T(8,128)S(1)} collective-permute-done((f32[8,128]{1,0:T(8,128)S(1)}, f32[8,128]{1,0:T(8,128)S(1)}, u32[]{:S(2)}, u32[]{:S(2)}) %collective-permute-start.9) | collective-permute-done | bytes 4128 | tf_op jit(solution)/shard_map/ppermute | solution.py:354
  75.2 0.6 copy-done.13
  75.8 0.0 copy-done.4
  75.8 3.5 %shard_map.81 = (f32[2,32,8,128]{3,2,1,0:T(8,128)}, f32[64,128]{1,0:T(8,128)}, f32[64,128]{1,0:T(8,128)}, f32[8,128]{1,0:T(8,128)}, f32[8,128]{1,0:T(8,128)}) custom-call(f32[2,32,8,128]{3,2,1,0:T(8,128)} %get-tuple-element.27.refs_0_, f32[64,128]{1,0:T(8,128)} %copy-done.4, f32[64,128]{1,0:T(8,128)} %copy-done.5, f32[8,128]{1,0:T(8,128)} %copy-done.12, ...), custom_call_target="tpu_custom_call" | custom-call | tf_op jit(solution)/shard_map/pallas_call | solution.py:338
  79.3 1.9 %collective-permute-start.10 = (f32[64,128]{1,0:T(8,128)}, f32[64,128]{1,0:T(8,128)S(1)}, u32[]{:S(2)}, u32[]{:S(2)}) collective-permute-start(f32[64,128]{1,0:T(8,128)} %get-tuple-element.38), channel_id=1, source_target_pairs={{0,16},{16,32},{32,48},{48,64},{64,80},{80,96},{96,112},{112,128},... | collective-permute-start | bytes 98312 | tf_op jit(solution)/shard_map/ppermute | solution.py:354
  81.2 6.0 %collective-permute-start.11 = (f32[64,128]{1,0:T(8,128)}, f32[64,128]{1,0:T(8,128)S(1)}, u32[]{:S(2)}, u32[]{:S(2)}) collective-permute-start(f32[64,128]{1,0:T(8,128)} %get-tuple-element.39), channel_id=1, source_target_pairs={{16,0},{32,16},{48,32},{64,48},{80,64},{96,80},{112,96},{128,112},... | collective-permute-start | bytes 98312 | tf_op jit(solution)/shard_map/ppermute | solution.py:354
  87.3 3.2 %collective-permute-start.12 = (f32[8,128]{1,0:T(8,128)}, f32[8,128]{1,0:T(8,128)S(1)}, u32[]{:S(2)}, u32[]{:S(2)}) collective-permute-start(f32[8,128]{1,0:T(8,128)} %get-tuple-element.40), channel_id=1, source_target_pairs={{0,1},{1,2},{2,3},{3,4},{4,5},{5,6},{6,7},{7,8},{8,9},{9,10},{10,1... | collective-permute-start | bytes 12296 | tf_op jit(solution)/shard_map/ppermute | solution.py:354
  90.5 4.8 %collective-permute-start.13 = (f32[8,128]{1,0:T(8,128)S(1)}, f32[8,128]{1,0:T(8,128)S(1)}, u32[]{:S(2)}, u32[]{:S(2)}) collective-permute-start(f32[8,128]{1,0:T(8,128)S(1)} %copy-done.19), channel_id=1, source_target_pairs={{1,0},{2,1},{3,2},{4,3},{5,4},{6,5},{7,6},{8,7},{9,8},{10,9},{11,1... | collective-permute-start | bytes 12296 | tf_op jit(solution)/shard_map/ppermute | solution.py:354
  95.3 2.7 %shard_map.80 = f32[2,32,8,128]{3,2,1,0:T(8,128)} custom-call(f32[2,32,8,128]{3,2,1,0:T(8,128)} %get-tuple-element.27.refs_0_, f32[64,128]{1,0:T(8,128)} %copy-done.4, f32[64,128]{1,0:T(8,128)} %copy-done.5, f32[8,128]{1,0:T(8,128)} %copy-done.12, f32[8,128]{1,0:T(8,128)} %copy-done.13, f32[4,8,128]{2,1,0:T(8,128)} %get-tuple-element.22.c_ref.refs_5_.refs_10_, ...), custom_call_target="tpu_custom_call" | custom-call | tf_op jit(solution)/shard_map/pallas_call | solution.py:301
  98.0 0.5 copy-done.14
  98.6 0.0 copy-done.15
  98.6 0.0 copy-done.8
  98.6 0.0 copy-done.9
  98.6 3.3 %shard_map.82 = f32[2,32,8,128]{3,2,1,0:T(8,128)} custom-call(f32[2,32,8,128]{3,2,1,0:T(8,128)} %get-tuple-element.32.refs_0_, f32[64,128]{1,0:T(8,128)} %get-tuple-element.33.refs_1_, f32[64,128]{1,0:T(8,128)} %get-tuple-element.34.refs_2_, f32[8,128]{1,0:T(8,128)} %get-tuple-element.35.refs_3_, f32[8,128]{1,0:T(8,128)} %get-tuple-element.36.refs_4_, ...), custom_call_target="tpu_custom_call" | custom-call | tf_op jit(solution)/shard_map/pallas_call | solution.py:338
  (49 shorter events, 0.3 us)
Async XLA Ops:
  15.9 0.7 copy-start.1
  16.6 8.0 %collective-permute-start = (bf16[16,8,128]{2,1,0:T(8,128)(2,1)S(1)}, bf16[16,8,128]{2,1,0:T(8,128)(2,1)S(1)}, u32[]{:S(2)}, u32[]{:S(2)}) collective-permute-start(bf16[16,8,128]{2,1,0:T(8,128)(2,1)S(1)} %pad.12), channel_id=1, source_target_pairs={{0,16},{16,32},{32,48},{48,64},{64,80},{80,96},{96,112},{112,128},... | collective-permute-start | bytes 98312 | tf_op jit(solution)/shard_map/ppermute | solution.py:354
  19.2 7.0 %collective-permute-start.1 = (bf16[16,8,128]{2,1,0:T(8,128)(2,1)S(1)}, bf16[16,8,128]{2,1,0:T(8,128)(2,1)S(1)}, u32[]{:S(2)}, u32[]{:S(2)}) collective-permute-start(bf16[16,8,128]{2,1,0:T(8,128)(2,1)S(1)} %pad.13), channel_id=1, source_target_pairs={{16,0},{32,16},{48,32},{64,48},{80,64},{96,80},{112,96},{128,112},... | collective-permute-start | bytes 98312 | tf_op jit(solution)/shard_map/ppermute | solution.py:354
  24.6 1.6 %copy-start.10 = (bf16[16,8,128]{2,1,0:T(8,128)(2,1)}, bf16[16,8,128]{2,1,0:T(8,128)(2,1)S(1)}, u32[]{:S(2)}) copy-start(bf16[16,8,128]{2,1,0:T(8,128)(2,1)S(1)} %collective-permute-done.m_ref) | copy-start | bytes 98308
  26.2 0.6 copy-start.11
  28.6 5.5 %copy-start.16 = (f32[12,4]{0,1:T(4,128)S(1)}, f32[12,4]{0,1:T(4,128)}, u32[]{:S(2)}) copy-start(f32[12,4]{0,1:T(4,128)} %param.10) | copy-start | bytes 580
  28.6 24.3 %all-to-all-start.1 = ((bf16[16,8,8,128]{3,2,1,0:T(8,128)(2,1)}), bf16[16,8,8,128]{3,2,1,0:T(8,128)(2,1)S(1)}, u32[]{:S(2)}, u32[]{:S(2)}) async-start(bf16[16,8,8,128]{3,2,1,0:T(8,128)(2,1)} %shard_map.77), calls=%async_computation.1 | async-start | bytes 524288 | tf_op jit(solution)/shard_map/all_to_all | solution.py:418
  36.5 10.3 %copy-start.17 = (f32[8,128]{1,0:T(8,128)S(1)}, f32[8,128]{1,0:T(8,128)}, u32[]{:S(2)}) copy-start(f32[8,128]{1,0:T(8,128)} %get-tuple-element.26) | copy-start | bytes 12292
  36.5 17.7 %collective-permute-start.2 = (f32[72,128]{1,0:T(8,128)}, f32[72,128]{1,0:T(8,128)S(1)}, u32[]{:S(2)}, u32[]{:S(2)}) collective-permute-start(f32[72,128]{1,0:T(8,128)} %get-tuple-element.23), channel_id=1, source_target_pairs={{0,16},{16,32},{32,48},{48,64},{64,80},{80,96},{96,112},{112,128},... | collective-permute-start | bytes 110600 | tf_op jit(solution)/shard_map/ppermute | solution.py:354
  40.1 14.1 %collective-permute-start.3 = (f32[72,128]{1,0:T(8,128)}, f32[72,128]{1,0:T(8,128)S(1)}, u32[]{:S(2)}, u32[]{:S(2)}) collective-permute-start(f32[72,128]{1,0:T(8,128)} %get-tuple-element.24), channel_id=1, source_target_pairs={{16,0},{32,16},{48,32},{64,48},{80,64},{96,80},{112,96},{128,112},... | collective-permute-start | bytes 110600 | tf_op jit(solution)/shard_map/ppermute | solution.py:354
  44.9 9.1 %collective-permute-start.4 = (f32[8,128]{1,0:T(8,128)}, f32[8,128]{1,0:T(8,128)S(1)}, u32[]{:S(2)}, u32[]{:S(2)}) collective-permute-start(f32[8,128]{1,0:T(8,128)} %get-tuple-element.25), channel_id=1, source_target_pairs={{0,1},{1,2},{2,3},{3,4},{4,5},{5,6},{6,7},{7,8},{8,9},{9,10},{10,1... | collective-permute-start | bytes 12296 | tf_op jit(solution)/shard_map/ppermute | solution.py:354
  46.9 7.4 %collective-permute-start.5 = (f32[8,128]{1,0:T(8,128)S(1)}, f32[8,128]{1,0:T(8,128)S(1)}, u32[]{:S(2)}, u32[]{:S(2)}) collective-permute-start(f32[8,128]{1,0:T(8,128)S(1)} %copy-done.17), channel_id=1, source_target_pairs={{1,0},{2,1},{3,2},{4,3},{5,4},{6,5},{7,6},{8,7},{9,8},{10,9},{11,1... | collective-permute-start | bytes 12296 | tf_op jit(solution)/shard_map/ppermute | solution.py:354
  52.9 1.3 %copy-start = (bf16[16,8,8,128]{3,2,1,0:T(8,128)(2,1)}, bf16[16,8,8,128]{3,2,1,0:T(8,128)(2,1)S(1)}, u32[]{:S(2)}) copy-start(bf16[16,8,8,128]{3,2,1,0:T(8,128)(2,1)S(1)} %all-to-all-done.1.r_ref) | copy-start | bytes 786436
  54.1 0.6 copy-start.6
  54.2 0.6 copy-start.7
  54.2 0.6 copy-start.2
  54.2 0.6 copy-start.3
  57.9 12.1 %copy-start.18 = (f32[8,128]{1,0:T(8,128)S(1)}, f32[8,128]{1,0:T(8,128)}, u32[]{:S(2)}) copy-start(f32[8,128]{1,0:T(8,128)} %get-tuple-element.31) | copy-start | bytes 12292
  57.9 17.3 %collective-permute-start.6 = (f32[64,128]{1,0:T(8,128)}, f32[64,128]{1,0:T(8,128)S(1)}, u32[]{:S(2)}, u32[]{:S(2)}) collective-permute-start(f32[64,128]{1,0:T(8,128)} %get-tuple-element.28), channel_id=1, source_target_pairs={{0,16},{16,32},{32,48},{48,64},{64,80},{80,96},{96,112},{112,128},... | collective-permute-start | bytes 98312 | tf_op jit(solution)/shard_map/ppermute | solution.py:354
  59.9 15.3 %collective-permute-start.7 = (f32[64,128]{1,0:T(8,128)}, f32[64,128]{1,0:T(8,128)S(1)}, u32[]{:S(2)}, u32[]{:S(2)}) collective-permute-start(f32[64,128]{1,0:T(8,128)} %get-tuple-element.29), channel_id=1, source_target_pairs={{16,0},{32,16},{48,32},{64,48},{80,64},{96,80},{112,96},{128,112},... | collective-permute-start | bytes 98312 | tf_op jit(solution)/shard_map/ppermute | solution.py:354
  65.9 8.0 %collective-permute-start.8 = (f32[8,128]{1,0:T(8,128)}, f32[8,128]{1,0:T(8,128)S(1)}, u32[]{:S(2)}, u32[]{:S(2)}) collective-permute-start(f32[8,128]{1,0:T(8,128)} %get-tuple-element.30), channel_id=1, source_target_pairs={{0,1},{1,2},{2,3},{3,4},{4,5},{5,6},{6,7},{7,8},{8,9},{9,10},{10,1... | collective-permute-start | bytes 12296 | tf_op jit(solution)/shard_map/ppermute | solution.py:354
  70.0 5.2 %collective-permute-start.9 = (f32[8,128]{1,0:T(8,128)S(1)}, f32[8,128]{1,0:T(8,128)S(1)}, u32[]{:S(2)}, u32[]{:S(2)}) collective-permute-start(f32[8,128]{1,0:T(8,128)S(1)} %copy-done.18), channel_id=1, source_target_pairs={{1,0},{2,1},{3,2},{4,3},{5,4},{6,5},{7,6},{8,7},{9,8},{10,9},{11,1... | collective-permute-start | bytes 12296 | tf_op jit(solution)/shard_map/ppermute | solution.py:354
  73.9 1.3 %copy-start.12 = (f32[8,128]{1,0:T(8,128)}, f32[8,128]{1,0:T(8,128)S(1)}, u32[]{:S(2)}) copy-start(f32[8,128]{1,0:T(8,128)S(1)} %collective-permute-done.8.refs_3_) | copy-start | bytes 12292
  75.2 0.6 copy-start.13
  75.2 0.6 copy-start.4
  75.2 0.6 copy-start.5
  79.3 11.2 %copy-start.19 = (f32[8,128]{1,0:T(8,128)S(1)}, f32[8,128]{1,0:T(8,128)}, u32[]{:S(2)}) copy-start(f32[8,128]{1,0:T(8,128)} %get-tuple-element.41) | copy-start | bytes 12292
  79.3 18.7 %collective-permute-start.10 = (f32[64,128]{1,0:T(8,128)}, f32[64,128]{1,0:T(8,128)S(1)}, u32[]{:S(2)}, u32[]{:S(2)}) collective-permute-start(f32[64,128]{1,0:T(8,128)} %get-tuple-element.38), channel_id=1, source_target_pairs={{0,16},{16,32},{32,48},{48,64},{64,80},{80,96},{96,112},{112,128},... | collective-permute-start | bytes 98312 | tf_op jit(solution)/shard_map/ppermute | solution.py:354
  81.2 16.8 %collective-permute-start.11 = (f32[64,128]{1,0:T(8,128)}, f32[64,128]{1,0:T(8,128)S(1)}, u32[]{:S(2)}, u32[]{:S(2)}) collective-permute-start(f32[64,128]{1,0:T(8,128)} %get-tuple-element.39), channel_id=1, source_target_pairs={{16,0},{32,16},{48,32},{64,48},{80,64},{96,80},{112,96},{128,112},... | collective-permute-start | bytes 98312 | tf_op jit(solution)/shard_map/ppermute | solution.py:354
  87.3 10.7 %collective-permute-start.12 = (f32[8,128]{1,0:T(8,128)}, f32[8,128]{1,0:T(8,128)S(1)}, u32[]{:S(2)}, u32[]{:S(2)}) collective-permute-start(f32[8,128]{1,0:T(8,128)} %get-tuple-element.40), channel_id=1, source_target_pairs={{0,1},{1,2},{2,3},{3,4},{4,5},{5,6},{6,7},{7,8},{8,9},{9,10},{10,1... | collective-permute-start | bytes 12296 | tf_op jit(solution)/shard_map/ppermute | solution.py:354
  90.5 7.5 %collective-permute-start.13 = (f32[8,128]{1,0:T(8,128)S(1)}, f32[8,128]{1,0:T(8,128)S(1)}, u32[]{:S(2)}, u32[]{:S(2)}) collective-permute-start(f32[8,128]{1,0:T(8,128)S(1)} %copy-done.19), channel_id=1, source_target_pairs={{1,0},{2,1},{3,2},{4,3},{5,4},{6,5},{7,6},{8,7},{9,8},{10,9},{11,1... | collective-permute-start | bytes 12296 | tf_op jit(solution)/shard_map/ppermute | solution.py:354
  98.0 0.6 copy-start.14
  98.0 0.6 copy-start.15
  98.0 0.6 copy-start.8
  98.0 0.6 copy-start.9

commit v8 on v6

--- a/solution.py
+++ b/solution.py
@@ -1,5 +1,6 @@
 import jax
 import jax.numpy as jnp
+from jax.sharding import Mesh
 from jax import lax
 from jax.experimental import pallas as pl
 from jax.experimental.pallas import tpu as pltpu
@@ -8,6 +9,7 @@
 F32 = jnp.float32
 NCOEF = 4
 UNROLL = 8
+GY = ("ga", "gb")
 VMEM = pltpu.MemorySpace.VMEM
 SMEM = pltpu.MemorySpace.SMEM
 
@@ -374,8 +376,8 @@
     return (
         _shift(xl, "gx", 1),
         _shift(xf, "gx", -1),
-        _shift(yl, "gy", 1),
-        _shift(yf, "gy", -1),
+        _shift(yl, GY, 1),
+        _shift(yf, GY, -1),
     )
 
 
@@ -413,9 +415,18 @@
     )(holder, held)
 
 
+def _all_to_all(v):
+    na, nb = lax.axis_size("ga"), lax.axis_size("gb")
+    rest = v.shape[1:]
+    v = v.reshape((na, nb) + rest)
+    v = lax.all_to_all(v, "gb", 1, 1, tiled=True)
+    v = lax.all_to_all(v, "ga", 0, 0, tiled=True)
+    return v.reshape((na * nb,) + rest)
+
+
 def route_blocks(stored_slab, block_scales, holder, xm_all, xp_all, first):
     nf, nz, x, y = stored_slab.shape
-    n = lax.axis_size("gy")
+    n = lax.axis_size(GY)
     nplanes = nf * nz
     per = nplanes // n
     bf = stored_slab.dtype
@@ -427,10 +438,10 @@
     sc_p = xp_all[first + nplanes, :nplanes].astype(bf).reshape(n, 1, per)
     sc = jnp.concatenate([block_scales.reshape(n, 1, per), sc_m, sc_p], axis=1)
     sc = jnp.pad(sc, ((0, 0), (0, x - 3), (0, y - per)))[:, None]
-    held = lax.all_to_all(jnp.concatenate([slab, halo, sc], axis=1), "gy", 0, 0, tiled=True)
+    held = _all_to_all(jnp.concatenate([slab, halo, sc], axis=1))
 
     forward = forward_call(holder, held, per)
-    return lax.all_to_all(forward, "gy", 0, 0, tiled=True)
+    return _all_to_all(forward)
 
 
 def on_device(stored_slab, block_scales, holder, soil_class, soil_table, cotangent):
@@ -466,18 +477,21 @@
 
 
 def solution(mesh):
+    ngx, ngy = mesh.shape["gx"], mesh.shape["gy"]
+    nb = 4 if ngy % 4 == 0 else 1
+    split = Mesh(mesh.devices.reshape(ngx, ngy // nb, nb), ("gx",) + GY)
     placed = (
-        P(None, None, "gx", "gy"),
-        P(None, None, "gx", "gy"),
+        P(None, None, "gx", GY),
+        P(None, None, "gx", GY),
         P(),
-        P("gx", "gy"),
+        P("gx", GY),
         P(),
-        P(None, None, "gx", "gy"),
+        P(None, None, "gx", GY),
     )
     return jax.shard_map(
         on_device,
-        mesh=mesh,
+        mesh=split,
         in_specs=placed,
-        out_specs=(P(None, None, "gx", "gy"), P(None, None, "gx", "gy")),
+        out_specs=(P(None, None, "gx", GY), P(None, None, "gx", GY)),
         check_vma=False,
     )

time: 94.8 us -> 113 us (1.19)
  blocking collectives: 14 us -> 30.6 us
  local copies, waits for them, and re-layouts: 5.73 us -> 7.46 us
    all_to_all x1 -> x3, blocking collectives: 14 us -> 30.6 us  [the longest x2 21 us: _all_to_all(): v = lax.all_to_all(v, 'gb', 1, 1, tiled=True)]
  transfers between devices with their start and end apart: 13 -> 13, of which waited for: 4 -> 4; matrix products, arithmetic and copies ran while one was open for 1% -> 1% of each run, Pallas kernels for 3% -> 2%
where the time goes in v8:
time: 113 us; the launch traced here: 112 us
  starting transfers between devices  52.7 us (47%)
  blocking collectives  30.6 us (27%)
  Pallas kernels  16.3 us (14%)
  local copies, waits for them, and re-layouts  7.46 us (7%)
  waiting for transfers between devices  3.55 us (3%)
    ppermute x12, starting transfers between devices, _shift(): return lax.ppermute(v, axis, pairs)  47.7 us
    all_to_all x2, blocking collectives, _all_to_all(): v = lax.all_to_all(v, 'gb', 1, 1, tiled=True)  21 us
    all_to_all x1, blocking collectives, _all_to_all(): v = lax.all_to_all(v, 'ga', 0, 0, tiled=True)  9.6 us
    pallas_call x2, Pallas kernels, adjoint_call(): pl.pallas_call(kernel, out_shape=out_shape, scratch_shapes=_halo_scratch(...  6.92 us
    all_to_all x1, starting transfers between devices, _all_to_all(): v = lax.all_to_all(v, 'ga', 0, 0, tiled=True)  4.97 us
    unnamed x39, local copies, waits for them, and re-layouts  3.68 us
    ppermute x12, waiting for transfers between devices, _shift(): return lax.ppermute(v, axis, pairs)  3.55 us
    pallas_call x1, Pallas kernels, state0_step_call(): pl.pallas_call(kernel, out_shape=(state,) + _edge_shapes(nplanes, x, y) +...  3.06 us
  transfers between devices with their start and end apart: 13, of which 4 were waited for; matrix products, arithmetic and copies ran while one was open for 1% of the time, Pallas kernels for 2%

profile of v8, /device:TPU:130, one launch (start us, length us, event | category | flops | bytes accessed | tf_op | source)
XLA Modules:
  0.0 111.7 jit_solution(11847659034264730613)
XLA Ops:
  0.6 1.4 %copy.61.tab_ref = f32[12,4]{1,0:T(8,128)} copy(f32[12,4]{0,1:T(4,128)} %param.10) | data formatting | bytes 384 | tf_op args[4]
  2.0 0.7 reshape.73.sc_ref
  2.7 1.8 %shard_map.77 = (f32[4,8,128]{2,1,0:T(8,128)}, f32[136,128]{1,0:T(8,128)}, f32[136,128]{1,0:T(8,128)}, f32[8,128]{1,0:T(8,128)}, f32[8,128]{1,0:T(8,128)}) custom-call(s32[8,128]{1,0:T(8,128)} %cls_ref.1, f32[12,4]{1,0:T(8,128)} %copy.61.tab_ref, f32[64]{0:T(128)} %reshape.73.sc_ref, f32[2,32,8,128]{3,2,1,0:T(8,128)} %refs_5_.1, bf16[2,32,8,128]{3,2,1,0:T(8,128)(2,1)} %slab_ref.1), custom_call_target="tpu_custom_call" | custom-call | tf_op jit(solution)/shard_map/pallas_call | solution.py:230
  4.5 3.5 %collective-permute-start = (f32[136,128]{1,0:T(8,128)}, f32[136,128]{1,0:T(8,128)S(1)}, u32[]{:S(2)}, u32[]{:S(2)}) collective-permute-start(f32[136,128]{1,0:T(8,128)} %get-tuple-element.22), channel_id=1, source_target_pairs={{0,16},{16,32},{32,48},{48,64},{64,80},{80,96},{96,112},{112,128},... | collective-permute-start | bytes 208904 | tf_op jit(solution)/shard_map/ppermute | solution.py:372
  8.0 4.5 %collective-permute-start.1 = (f32[136,128]{1,0:T(8,128)}, f32[136,128]{1,0:T(8,128)S(1)}, u32[]{:S(2)}, u32[]{:S(2)}) collective-permute-start(f32[136,128]{1,0:T(8,128)} %get-tuple-element.23), channel_id=1, source_target_pairs={{16,0},{32,16},{48,32},{64,48},{80,64},{96,80},{112,96},{128,112},... | collective-permute-start | bytes 208904 | tf_op jit(solution)/shard_map/ppermute | solution.py:372
  12.4 0.1 reshape.67
  12.5 0.6 collective-permute-done.cxm.refs_6_.refs_11_
  13.2 1.5 %collective-permute-done.1.cxp.refs_7_.refs_12_ = f32[136,128]{1,0:T(8,128)S(1)} collective-permute-done((f32[136,128]{1,0:T(8,128)}, f32[136,128]{1,0:T(8,128)S(1)}, u32[]{:S(2)}, u32[]{:S(2)}) %collective-permute-start.1) | collective-permute-done | bytes 69664 | tf_op jit(solution)/shard_map/ppermute | solution.py:372
  14.7 0.1 convert_element_type.40
  14.8 0.5 copy-done.1
  15.3 0.1 convert_element_type.41
  15.5 11.1 %all_to_all.20 = bf16[4,4,6,8,128]{4,3,2,0,1:T(8,128)(2,1)S(1)} all-to-all(bf16[4,4,6,8,128]{4,3,2,0,1:T(8,128)(2,1)S(1)} %copy.66), channel_id=1, replica_groups=mesh['gx'=16,'ga'=4,'gb'=4] {'gb'}, dimensions={1} | all-to-all | bytes 393216 | tf_op jit(solution)/shard_map/all_to_all | solution.py:422
  26.6 9.6 %all_to_all.21 = bf16[4,4,6,8,128]{4,3,2,1,0:T(8,128)(2,1)} all-to-all(bf16[4,4,6,8,128]{4,3,2,1,0:T(8,128)(2,1)S(1)} %copy.67), channel_id=1, replica_groups=mesh['gx'=16,'ga'=4,'gb'=4] {'ga'}, dimensions={0} | all-to-all | bytes 393216 | tf_op jit(solution)/shard_map/all_to_all | solution.py:423
  36.2 1.8 %shard_map.78 = bf16[16,8,8,128]{3,2,1,0:T(8,128)(2,1)} custom-call(s32[16]{0:T(128)} %hold_ref.1, bf16[16,6,8,128]{3,2,1,0:T(8,128)(2,1)} %bitcast.26), custom_call_target="tpu_custom_call" | custom-call | tf_op jit(solution)/shard_map/pallas_call | solution.py:411
  38.0 1.0 copy.68
  39.0 9.9 %all_to_all.22 = bf16[4,4,8,8,128]{4,3,2,0,1:T(8,128)(2,1)S(1)} all-to-all(bf16[4,4,8,8,128]{4,3,2,0,1:T(8,128)(2,1)S(1)} %copy.68), channel_id=1, replica_groups=mesh['gx'=16,'ga'=4,'gb'=4] {'gb'}, dimensions={1} | all-to-all | bytes 524288 | tf_op jit(solution)/shard_map/all_to_all | solution.py:422
  48.9 0.7 copy.69
  49.6 5.0 %all-to-all-start.3 = ((bf16[4,4,8,8,128]{4,3,2,1,0:T(8,128)(2,1)}), bf16[4,4,8,8,128]{4,3,2,1,0:T(8,128)(2,1)S(1)}, u32[]{:S(2)}, u32[]{:S(2)}) async-start(bf16[4,4,8,8,128]{4,3,2,1,0:T(8,128)(2,1)} %copy.69), calls=%async_computation.3 | async-start | bytes 524288 | tf_op jit(solution)/shard_map/all_to_all | solution.py:423
  54.6 1.9 %collective-permute-start.2 = (f32[8,128]{1,0:T(8,128)S(1)}, f32[8,128]{1,0:T(8,128)S(1)}, u32[]{:S(2)}, u32[]{:S(2)}) collective-permute-start(f32[8,128]{1,0:T(8,128)S(1)} %copy-done.16), channel_id=1, source_target_pairs={{0,1},{1,2},{2,3},{3,4},{4,5},{5,6},{6,7},{7,8},{8,9},{9,10},{10,1... | collective-permute-start | bytes 12296 | tf_op jit(solution)/shard_map/ppermute | solution.py:372
  56.5 6.0 %collective-permute-start.3 = (f32[8,128]{1,0:T(8,128)S(1)}, f32[8,128]{1,0:T(8,128)S(1)}, u32[]{:S(2)}, u32[]{:S(2)}) collective-permute-start(f32[8,128]{1,0:T(8,128)S(1)} %copy-done.15), channel_id=1, source_target_pairs={{1,0},{2,1},{3,2},{4,3},{5,4},{6,5},{7,6},{8,7},{9,8},{10,9},{11,1... | collective-permute-start | bytes 12296 | tf_op jit(solution)/shard_map/ppermute | solution.py:372
  62.6 0.0 copy-start.2
  62.7 0.1 reshape.71
  62.8 0.1 copy.71
  62.8 0.1 copy.72
  63.0 0.1 reshape.72
  63.1 0.7 reshape.74.sc_ref
  63.8 0.1 collective-permute-done.3.cyp.refs_9_.refs_14_
  63.9 0.4 copy-done.6
  64.3 0.2 copy-done.7
  64.5 3.1 %shard_map.79 = (f32[2,32,8,128]{3,2,1,0:T(8,128)}, f32[64,128]{1,0:T(8,128)}, f32[64,128]{1,0:T(8,128)}, f32[8,128]{1,0:T(8,128)}, f32[8,128]{1,0:T(8,128)}, /*...) custom-call(f32[320]{0:T(512)} %reshape.74.sc_ref, ...), custom_call_target="tpu_custom_call" | custom-call | tf_op jit(solution)/shard_map/pallas_call | solution.py:285
  67.6 2.8 %collective-permute-start.4 = (f32[64,128]{1,0:T(8,128)}, f32[64,128]{1,0:T(8,128)S(1)}, u32[]{:S(2)}, u32[]{:S(2)}) collective-permute-start(f32[64,128]{1,0:T(8,128)} %get-tuple-element.28), channel_id=1, source_target_pairs={{0,16},{16,32},{32,48},{48,64},{64,80},{80,96},{96,112},{112,128},... | collective-permute-start | bytes 98312 | tf_op jit(solution)/shard_map/ppermute | solution.py:372
  70.4 5.1 %collective-permute-start.5 = (f32[64,128]{1,0:T(8,128)}, f32[64,128]{1,0:T(8,128)S(1)}, u32[]{:S(2)}, u32[]{:S(2)}) collective-permute-start(f32[64,128]{1,0:T(8,128)} %get-tuple-element.29), channel_id=1, source_target_pairs={{16,0},{32,16},{48,32},{64,48},{80,64},{96,80},{112,96},{128,112},... | collective-permute-start | bytes 98312 | tf_op jit(solution)/shard_map/ppermute | solution.py:372
  75.5 1.9 %collective-permute-start.6 = (f32[8,128]{1,0:T(8,128)}, f32[8,128]{1,0:T(8,128)S(1)}, u32[]{:S(2)}, u32[]{:S(2)}) collective-permute-start(f32[8,128]{1,0:T(8,128)} %get-tuple-element.30), channel_id=1, source_target_pairs={{0,1},{1,2},{2,3},{3,4},{4,5},{5,6},{6,7},{7,8},{8,9},{9,10},{10,1... | collective-permute-start | bytes 12296 | tf_op jit(solution)/shard_map/ppermute | solution.py:372
  77.5 6.0 %collective-permute-start.7 = (f32[8,128]{1,0:T(8,128)S(1)}, f32[8,128]{1,0:T(8,128)S(1)}, u32[]{:S(2)}, u32[]{:S(2)}) collective-permute-start(f32[8,128]{1,0:T(8,128)S(1)} %copy-done.17), channel_id=1, source_target_pairs={{1,0},{2,1},{3,2},{4,3},{5,4},{6,5},{7,6},{8,7},{9,8},{10,9},{11,1... | collective-permute-start | bytes 12296 | tf_op jit(solution)/shard_map/ppermute | solution.py:372
  83.5 1.3 %collective-permute-done.7.refs_4_ = f32[8,128]{1,0:T(8,128)S(1)} collective-permute-done((f32[8,128]{1,0:T(8,128)S(1)}, f32[8,128]{1,0:T(8,128)S(1)}, u32[]{:S(2)}, u32[]{:S(2)}) %collective-permute-start.7) | collective-permute-done | bytes 4128 | tf_op jit(solution)/shard_map/ppermute | solution.py:372
  84.9 0.6 copy-done.11
  85.4 0.0 copy-done.4
  85.5 3.5 %shard_map.81 = (f32[2,32,8,128]{3,2,1,0:T(8,128)}, f32[64,128]{1,0:T(8,128)}, f32[64,128]{1,0:T(8,128)}, f32[8,128]{1,0:T(8,128)}, f32[8,128]{1,0:T(8,128)}) custom-call(f32[2,32,8,128]{3,2,1,0:T(8,128)} %get-tuple-element.27.refs_0_, f32[64,128]{1,0:T(8,128)} %copy-done.4, f32[64,128]{1,0:T(8,128)} %copy-done.5, f32[8,128]{1,0:T(8,128)} %copy-done.10, ...), custom_call_target="tpu_custom_call" | custom-call | tf_op jit(solution)/shard_map/pallas_call | solution.py:356
  89.0 1.9 %collective-permute-start.8 = (f32[64,128]{1,0:T(8,128)}, f32[64,128]{1,0:T(8,128)S(1)}, u32[]{:S(2)}, u32[]{:S(2)}) collective-permute-start(f32[64,128]{1,0:T(8,128)} %get-tuple-element.38), channel_id=1, source_target_pairs={{0,16},{16,32},{32,48},{48,64},{64,80},{80,96},{96,112},{112,128},... | collective-permute-start | bytes 98312 | tf_op jit(solution)/shard_map/ppermute | solution.py:372
  90.9 6.0 %collective-permute-start.9 = (f32[64,128]{1,0:T(8,128)}, f32[64,128]{1,0:T(8,128)S(1)}, u32[]{:S(2)}, u32[]{:S(2)}) collective-permute-start(f32[64,128]{1,0:T(8,128)} %get-tuple-element.39), channel_id=1, source_target_pairs={{16,0},{32,16},{48,32},{64,48},{80,64},{96,80},{112,96},{128,112},... | collective-permute-start | bytes 98312 | tf_op jit(solution)/shard_map/ppermute | solution.py:372
  97.0 1.9 %collective-permute-start.10 = (f32[8,128]{1,0:T(8,128)}, f32[8,128]{1,0:T(8,128)S(1)}, u32[]{:S(2)}, u32[]{:S(2)}) collective-permute-start(f32[8,128]{1,0:T(8,128)} %get-tuple-element.40), channel_id=1, source_target_pairs={{0,1},{1,2},{2,3},{3,4},{4,5},{5,6},{6,7},{7,8},{8,9},{9,10},{10,1... | collective-permute-start | bytes 12296 | tf_op jit(solution)/shard_map/ppermute | solution.py:372
  98.9 6.0 %collective-permute-start.11 = (f32[8,128]{1,0:T(8,128)S(1)}, f32[8,128]{1,0:T(8,128)S(1)}, u32[]{:S(2)}, u32[]{:S(2)}) collective-permute-start(f32[8,128]{1,0:T(8,128)S(1)} %copy-done.18), channel_id=1, source_target_pairs={{1,0},{2,1},{3,2},{4,3},{5,4},{6,5},{7,6},{8,7},{9,8},{10,9},{11,1... | collective-permute-start | bytes 12296 | tf_op jit(solution)/shard_map/ppermute | solution.py:372
  105.0 2.7 %shard_map.80 = f32[2,32,8,128]{3,2,1,0:T(8,128)} custom-call(f32[2,32,8,128]{3,2,1,0:T(8,128)} %get-tuple-element.27.refs_0_, f32[64,128]{1,0:T(8,128)} %copy-done.4, f32[64,128]{1,0:T(8,128)} %copy-done.5, f32[8,128]{1,0:T(8,128)} %copy-done.10, f32[8,128]{1,0:T(8,128)} %copy-done.11, f32[4,8,128]{2,1,0:T(8,128)} %get-tuple-element.24.c_ref.refs_5_.refs_10_, ...), custom_call_target="tpu_custom_call" | custom-call | tf_op jit(solution)/shard_map/pallas_call | solution.py:319
  107.8 0.5 copy-done.12
  108.3 0.0 copy-done.13
  108.3 0.0 copy-done.8
  108.3 0.0 copy-done.9
  108.4 3.4 %shard_map.82 = f32[2,32,8,128]{3,2,1,0:T(8,128)} custom-call(f32[2,32,8,128]{3,2,1,0:T(8,128)} %get-tuple-element.32.refs_0_, f32[64,128]{1,0:T(8,128)} %get-tuple-element.33.refs_1_, f32[64,128]{1,0:T(8,128)} %get-tuple-element.34.refs_2_, f32[8,128]{1,0:T(8,128)} %get-tuple-element.35.refs_3_, f32[8,128]{1,0:T(8,128)} %get-tuple-element.36.refs_4_, ...), custom_call_target="tpu_custom_call" | custom-call | tf_op jit(solution)/shard_map/pallas_call | solution.py:356
  (52 shorter events, 0.3 us)
Async XLA Ops:
  0.6 1.4 %copy-start.14 = (bf16[2,32,1,1]{1,0,3,2:T(2,128)(2,1)S(1)}, bf16[2,32,1,1]{1,0,3,2:T(2,128)(2,1)}, u32[]{:S(2)}) copy-start(bf16[2,32,1,1]{1,0,3,2:T(2,128)(2,1)} %param.7) | copy-start | bytes 388
  4.5 8.6 %collective-permute-start = (f32[136,128]{1,0:T(8,128)}, f32[136,128]{1,0:T(8,128)S(1)}, u32[]{:S(2)}, u32[]{:S(2)}) collective-permute-start(f32[136,128]{1,0:T(8,128)} %get-tuple-element.22), channel_id=1, source_target_pairs={{0,16},{16,32},{32,48},{48,64},{64,80},{80,96},{96,112},{112,128},... | collective-permute-start | bytes 208904 | tf_op jit(solution)/shard_map/ppermute | solution.py:372
  8.0 6.7 %collective-permute-start.1 = (f32[136,128]{1,0:T(8,128)}, f32[136,128]{1,0:T(8,128)S(1)}, u32[]{:S(2)}, u32[]{:S(2)}) collective-permute-start(f32[136,128]{1,0:T(8,128)} %get-tuple-element.23), channel_id=1, source_target_pairs={{16,0},{32,16},{48,32},{64,48},{80,64},{96,80},{112,96},{128,112},... | collective-permute-start | bytes 208904 | tf_op jit(solution)/shard_map/ppermute | solution.py:372
  13.1 1.6 %copy-start = (f32[136,128]{1,0:T(8,128)}, f32[136,128]{1,0:T(8,128)S(1)}, u32[]{:S(2)}) copy-start(f32[136,128]{1,0:T(8,128)S(1)} %collective-permute-done.cxm.refs_6_.refs_11_) | copy-start | bytes 208900
  13.2 2.3 %copy-start.3 = (bf16[2,32,8,128]{3,2,1,0:T(8,128)(2,1)S(1)}, bf16[2,32,8,128]{3,2,1,0:T(8,128)(2,1)}, u32[]{:S(2)}) copy-start(bf16[2,32,8,128]{3,2,1,0:T(8,128)(2,1)} %slab_ref.1) | copy-start | bytes 393220
  14.7 0.6 copy-start.1
  49.6 5.0 %copy-start.16 = (f32[8,128]{1,0:T(8,128)S(1)}, f32[8,128]{1,0:T(8,128)}, u32[]{:S(2)}) copy-start(f32[8,128]{1,0:T(8,128)} %get-tuple-element.25) | copy-start | bytes 12292
  49.6 6.9 %copy-start.15 = (f32[8,128]{1,0:T(8,128)S(1)}, f32[8,128]{1,0:T(8,128)}, u32[]{:S(2)}) copy-start(f32[8,128]{1,0:T(8,128)} %get-tuple-element.26) | copy-start | bytes 12292
  49.6 13.0 %all-to-all-start.3 = ((bf16[4,4,8,8,128]{4,3,2,1,0:T(8,128)(2,1)}), bf16[4,4,8,8,128]{4,3,2,1,0:T(8,128)(2,1)S(1)}, u32[]{:S(2)}, u32[]{:S(2)}) async-start(bf16[4,4,8,8,128]{4,3,2,1,0:T(8,128)(2,1)} %copy.69), calls=%async_computation.3 | async-start | bytes 524288 | tf_op jit(solution)/shard_map/all_to_all | solution.py:423
  54.6 9.1 %collective-permute-start.2 = (f32[8,128]{1,0:T(8,128)S(1)}, f32[8,128]{1,0:T(8,128)S(1)}, u32[]{:S(2)}, u32[]{:S(2)}) collective-permute-start(f32[8,128]{1,0:T(8,128)S(1)} %copy-done.16), channel_id=1, source_target_pairs={{0,1},{1,2},{2,3},{3,4},{4,5},{5,6},{6,7},{7,8},{8,9},{9,10},{10,1... | collective-permute-start | bytes 12296 | tf_op jit(solution)/shard_map/ppermute | solution.py:372
  56.5 7.4 %collective-permute-start.3 = (f32[8,128]{1,0:T(8,128)S(1)}, f32[8,128]{1,0:T(8,128)S(1)}, u32[]{:S(2)}, u32[]{:S(2)}) collective-permute-start(f32[8,128]{1,0:T(8,128)S(1)} %copy-done.15), channel_id=1, source_target_pairs={{1,0},{2,1},{3,2},{4,3},{5,4},{6,5},{7,6},{8,7},{9,8},{10,9},{11,1... | collective-permute-start | bytes 12296 | tf_op jit(solution)/shard_map/ppermute | solution.py:372
  62.6 1.3 %copy-start.2 = (bf16[4,4,8,8,128]{4,3,2,1,0:T(8,128)(2,1)}, bf16[4,4,8,8,128]{4,3,2,1,0:T(8,128)(2,1)S(1)}, u32[]{:S(2)}) copy-start(bf16[4,4,8,8,128]{4,3,2,1,0:T(8,128)(2,1)S(1)} %all-to-all-done.3) | copy-start | bytes 786436
  63.7 0.6 copy-start.6
  63.9 0.6 copy-start.7
  67.6 9.9 %copy-start.17 = (f32[8,128]{1,0:T(8,128)S(1)}, f32[8,128]{1,0:T(8,128)}, u32[]{:S(2)}) copy-start(f32[8,128]{1,0:T(8,128)} %get-tuple-element.31) | copy-start | bytes 12292
  67.6 17.3 %collective-permute-start.4 = (f32[64,128]{1,0:T(8,128)}, f32[64,128]{1,0:T(8,128)S(1)}, u32[]{:S(2)}, u32[]{:S(2)}) collective-permute-start(f32[64,128]{1,0:T(8,128)} %get-tuple-element.28), channel_id=1, source_target_pairs={{0,16},{16,32},{32,48},{48,64},{64,80},{80,96},{96,112},{112,128},... | collective-permute-start | bytes 98312 | tf_op jit(solution)/shard_map/ppermute | solution.py:372
  70.4 14.5 %collective-permute-start.5 = (f32[64,128]{1,0:T(8,128)}, f32[64,128]{1,0:T(8,128)S(1)}, u32[]{:S(2)}, u32[]{:S(2)}) collective-permute-start(f32[64,128]{1,0:T(8,128)} %get-tuple-element.29), channel_id=1, source_target_pairs={{16,0},{32,16},{48,32},{64,48},{80,64},{96,80},{112,96},{128,112},... | collective-permute-start | bytes 98312 | tf_op jit(solution)/shard_map/ppermute | solution.py:372
  75.5 8.0 %collective-permute-start.6 = (f32[8,128]{1,0:T(8,128)}, f32[8,128]{1,0:T(8,128)S(1)}, u32[]{:S(2)}, u32[]{:S(2)}) collective-permute-start(f32[8,128]{1,0:T(8,128)} %get-tuple-element.30), channel_id=1, source_target_pairs={{0,1},{1,2},{2,3},{3,4},{4,5},{5,6},{6,7},{7,8},{8,9},{9,10},{10,1... | collective-permute-start | bytes 12296 | tf_op jit(solution)/shard_map/ppermute | solution.py:372
  77.5 7.4 %collective-permute-start.7 = (f32[8,128]{1,0:T(8,128)S(1)}, f32[8,128]{1,0:T(8,128)S(1)}, u32[]{:S(2)}, u32[]{:S(2)}) collective-permute-start(f32[8,128]{1,0:T(8,128)S(1)} %copy-done.17), channel_id=1, source_target_pairs={{1,0},{2,1},{3,2},{4,3},{5,4},{6,5},{7,6},{8,7},{9,8},{10,9},{11,1... | collective-permute-start | bytes 12296 | tf_op jit(solution)/shard_map/ppermute | solution.py:372
  83.5 1.3 %copy-start.10 = (f32[8,128]{1,0:T(8,128)}, f32[8,128]{1,0:T(8,128)S(1)}, u32[]{:S(2)}) copy-start(f32[8,128]{1,0:T(8,128)S(1)} %collective-permute-done.6.refs_3_) | copy-start | bytes 12292
  84.8 0.6 copy-start.11
  84.8 0.6 copy-start.4
  84.8 0.6 copy-start.5
  89.0 9.9 %copy-start.18 = (f32[8,128]{1,0:T(8,128)S(1)}, f32[8,128]{1,0:T(8,128)}, u32[]{:S(2)}) copy-start(f32[8,128]{1,0:T(8,128)} %get-tuple-element.41) | copy-start | bytes 12292
  89.0 18.7 %collective-permute-start.8 = (f32[64,128]{1,0:T(8,128)}, f32[64,128]{1,0:T(8,128)S(1)}, u32[]{:S(2)}, u32[]{:S(2)}) collective-permute-start(f32[64,128]{1,0:T(8,128)} %get-tuple-element.38), channel_id=1, source_target_pairs={{0,16},{16,32},{32,48},{48,64},{64,80},{80,96},{96,112},{112,128},... | collective-permute-start | bytes 98312 | tf_op jit(solution)/shard_map/ppermute | solution.py:372
  90.9 16.8 %collective-permute-start.9 = (f32[64,128]{1,0:T(8,128)}, f32[64,128]{1,0:T(8,128)S(1)}, u32[]{:S(2)}, u32[]{:S(2)}) collective-permute-start(f32[64,128]{1,0:T(8,128)} %get-tuple-element.39), channel_id=1, source_target_pairs={{16,0},{32,16},{48,32},{64,48},{80,64},{96,80},{112,96},{128,112},... | collective-permute-start | bytes 98312 | tf_op jit(solution)/shard_map/ppermute | solution.py:372
  97.0 10.7 %collective-permute-start.10 = (f32[8,128]{1,0:T(8,128)}, f32[8,128]{1,0:T(8,128)S(1)}, u32[]{:S(2)}, u32[]{:S(2)}) collective-permute-start(f32[8,128]{1,0:T(8,128)} %get-tuple-element.40), channel_id=1, source_target_pairs={{0,1},{1,2},{2,3},{3,4},{4,5},{5,6},{6,7},{7,8},{8,9},{9,10},{10,1... | collective-permute-start | bytes 12296 | tf_op jit(solution)/shard_map/ppermute | solution.py:372
  98.9 8.8 %collective-permute-start.11 = (f32[8,128]{1,0:T(8,128)S(1)}, f32[8,128]{1,0:T(8,128)S(1)}, u32[]{:S(2)}, u32[]{:S(2)}) collective-permute-start(f32[8,128]{1,0:T(8,128)S(1)} %copy-done.18), channel_id=1, source_target_pairs={{1,0},{2,1},{3,2},{4,3},{5,4},{6,5},{7,6},{8,7},{9,8},{10,9},{11,1... | collective-permute-start | bytes 12296 | tf_op jit(solution)/shard_map/ppermute | solution.py:372
  107.7 0.6 copy-start.12
  107.7 0.6 copy-start.13
  107.7 0.6 copy-start.8
  107.7 0.6 copy-start.9

commit v9 on v6

--- a/solution.py
+++ b/solution.py
@@ -7,7 +7,7 @@
 
 F32 = jnp.float32
 NCOEF = 4
-UNROLL = 8
+UNROLL = 32
 VMEM = pltpu.MemorySpace.VMEM
 SMEM = pltpu.MemorySpace.SMEM
 

time: 94.8 us -> 94.1 us (level)
  no operation moved by 1% of the time
where the time goes in v9:
time: 94.1 us; the launch traced here: 93.1 us
  starting transfers between devices  53.3 us (57%)
  Pallas kernels  15.5 us (16%)
  blocking collectives  14 us (15%)
  local copies, waits for them, and re-layouts  5.73 us (6%)
  waiting for transfers between devices  3.55 us (4%)
  between operations  0.98 us (1%)
    ppermute x12, starting transfers between devices, _shift(): return lax.ppermute(v, axis, pairs)  47.7 us
    all_to_all x1, blocking collectives, route_blocks(): lax.all_to_all(jnp.concatenate([slab, halo, sc], axis=1), 'gy', 0, 0, til...  14 us
    pallas_call x2, Pallas kernels, adjoint_call(): pl.pallas_call(kernel, out_shape=out_shape, scratch_shapes=_halo_scratch(...  6.4 us
    all_to_all x1, starting transfers between devices, route_blocks(): return lax.all_to_all(forward, 'gy', 0, 0, tiled=True)  5.56 us
    unnamed x39, local copies, waits for them, and re-layouts  3.67 us
    ppermute x12, waiting for transfers between devices, _shift(): return lax.ppermute(v, axis, pairs)  3.55 us
    pallas_call x1, Pallas kernels, state0_step_call(): pl.pallas_call(kernel, out_shape=(state,) + _edge_shapes(nplanes, x, y) +...  2.93 us
    pallas_call x1, Pallas kernels, step_call(): pl.pallas_call(kernel, out_shape=out_shape, scratch_shapes=_halo_scratch(...  2.52 us
  transfers between devices with their start and end apart: 13, of which 4 were waited for; matrix products, arithmetic and copies ran while one was open for 1% of the time, Pallas kernels for 3%

profile of v9, /device:TPU:130, one launch (start us, length us, event | category | flops | bytes accessed | tf_op | source)
XLA Modules:
  0.0 93.1 jit_solution(1383638958191472060)
XLA Ops:
  0.6 1.4 %copy.29.tab_ref = f32[12,4]{1,0:T(8,128)} copy(f32[12,4]{0,1:T(4,128)} %param.10) | data formatting | bytes 384 | tf_op args[4]
  2.0 0.7 reshape.59.sc_ref
  2.7 1.8 %shard_map.77 = (f32[4,8,128]{2,1,0:T(8,128)}, f32[136,128]{1,0:T(8,128)}, f32[136,128]{1,0:T(8,128)}, f32[8,128]{1,0:T(8,128)}, f32[8,128]{1,0:T(8,128)}) custom-call(s32[8,128]{1,0:T(8,128)} %cls_ref.1, f32[12,4]{1,0:T(8,128)} %copy.29.tab_ref, f32[64]{0:T(128)} %reshape.59.sc_ref, f32[2,32,8,128]{3,2,1,0:T(8,128)} %refs_5_.1, bf16[2,32,8,128]{3,2,1,0:T(8,128)(2,1)} %slab_ref.1), custom_call_target="tpu_custom_call" | custom-call | tf_op jit(solution)/shard_map/pallas_call | solution.py:228
  4.5 3.5 %collective-permute-start = (f32[136,128]{1,0:T(8,128)}, f32[136,128]{1,0:T(8,128)S(1)}, u32[]{:S(2)}, u32[]{:S(2)}) collective-permute-start(f32[136,128]{1,0:T(8,128)} %get-tuple-element.22), channel_id=1, source_target_pairs={{0,16},{16,32},{32,48},{48,64},{64,80},{80,96},{96,112},{112,128},... | collective-permute-start | bytes 208904 | tf_op jit(solution)/shard_map/ppermute | solution.py:370
  8.0 4.5 %collective-permute-start.1 = (f32[136,128]{1,0:T(8,128)}, f32[136,128]{1,0:T(8,128)S(1)}, u32[]{:S(2)}, u32[]{:S(2)}) collective-permute-start(f32[136,128]{1,0:T(8,128)} %get-tuple-element.23), channel_id=1, source_target_pairs={{16,0},{32,16},{48,32},{64,48},{80,64},{96,80},{112,96},{128,112},... | collective-permute-start | bytes 208904 | tf_op jit(solution)/shard_map/ppermute | solution.py:370
  12.4 0.1 reshape.61
  12.5 0.6 collective-permute-done.cxm.refs_6_.refs_11_
  13.2 1.5 %collective-permute-done.1.cxp.refs_7_.refs_12_ = f32[136,128]{1,0:T(8,128)S(1)} collective-permute-done((f32[136,128]{1,0:T(8,128)}, f32[136,128]{1,0:T(8,128)S(1)}, u32[]{:S(2)}, u32[]{:S(2)}) %collective-permute-start.1) | collective-permute-done | bytes 69664 | tf_op jit(solution)/shard_map/ppermute | solution.py:370
  14.7 0.1 convert_element_type.46
  14.8 0.5 copy-done.1
  15.3 0.1 convert_element_type.47
  15.4 0.1 fusion.9
  15.5 14.0 %all_to_all.10.h_ref = bf16[16,6,8,128]{3,2,1,0:T(8,128)(2,1)} all-to-all(bf16[16,6,8,128]{3,2,1,0:T(8,128)(2,1)S(1)} %pad_maximum_fusion), channel_id=1, replica_groups=mesh['gx'=16,'gy'=16] {'gy'}, dimensions={0} | all-to-all | bytes 393216 | tf_op jit(solution)/shard_map/all_to_all | solution.py:430
  29.5 1.8 %shard_map.78 = bf16[16,8,8,128]{3,2,1,0:T(8,128)(2,1)} custom-call(s32[16]{0:T(128)} %hold_ref.1, bf16[16,6,8,128]{3,2,1,0:T(8,128)(2,1)} %all_to_all.10.h_ref), custom_call_target="tpu_custom_call" | custom-call | tf_op jit(solution)/shard_map/pallas_call | solution.py:409
  31.3 5.6 %all-to-all-start.1 = ((bf16[16,8,8,128]{3,2,1,0:T(8,128)(2,1)}), bf16[16,8,8,128]{3,2,1,0:T(8,128)(2,1)S(1)}, u32[]{:S(2)}, u32[]{:S(2)}) async-start(bf16[16,8,8,128]{3,2,1,0:T(8,128)(2,1)} %shard_map.78), calls=%async_computation.1 | async-start | bytes 524288 | tf_op jit(solution)/shard_map/all_to_all | solution.py:433
  36.9 2.1 %collective-permute-start.2 = (f32[8,128]{1,0:T(8,128)S(1)}, f32[8,128]{1,0:T(8,128)S(1)}, u32[]{:S(2)}, u32[]{:S(2)}) collective-permute-start(f32[8,128]{1,0:T(8,128)S(1)} %copy-done.16), channel_id=1, source_target_pairs={{0,1},{1,2},{2,3},{3,4},{4,5},{5,6},{6,7},{7,8},{8,9},{9,10},{10,1... | collective-permute-start | bytes 12296 | tf_op jit(solution)/shard_map/ppermute | solution.py:370
  38.9 5.9 %collective-permute-start.3 = (f32[8,128]{1,0:T(8,128)S(1)}, f32[8,128]{1,0:T(8,128)S(1)}, u32[]{:S(2)}, u32[]{:S(2)}) collective-permute-start(f32[8,128]{1,0:T(8,128)S(1)} %copy-done.15), channel_id=1, source_target_pairs={{1,0},{2,1},{3,2},{4,3},{5,4},{6,5},{7,6},{8,7},{9,8},{10,9},{11,1... | collective-permute-start | bytes 12296 | tf_op jit(solution)/shard_map/ppermute | solution.py:370
  44.9 0.0 all-to-all-done.1.r_ref
  44.9 0.0 copy-start.2
  44.9 0.1 reshape.57
  45.0 0.1 copy.34
  45.1 0.1 copy.35
  45.2 0.1 reshape.58
  45.3 0.7 reshape.60.sc_ref
  46.0 0.0 collective-permute-done.2.cym.refs_8_.refs_13_
  46.0 0.2 collective-permute-done.3.cyp.refs_9_.refs_14_
  46.2 0.4 copy-done.6
  46.6 0.2 copy-done.7
  46.8 2.9 %shard_map.79 = (f32[2,32,8,128]{3,2,1,0:T(8,128)}, f32[64,128]{1,0:T(8,128)}, f32[64,128]{1,0:T(8,128)}, f32[8,128]{1,0:T(8,128)}, f32[8,128]{1,0:T(8,128)}, /*...) custom-call(f32[320]{0:T(512)} %reshape.60.sc_ref, ...), custom_call_target="tpu_custom_call" | custom-call | tf_op jit(solution)/shard_map/pallas_call | solution.py:283
  49.7 2.8 %collective-permute-start.4 = (f32[64,128]{1,0:T(8,128)}, f32[64,128]{1,0:T(8,128)S(1)}, u32[]{:S(2)}, u32[]{:S(2)}) collective-permute-start(f32[64,128]{1,0:T(8,128)} %get-tuple-element.28), channel_id=1, source_target_pairs={{0,16},{16,32},{32,48},{48,64},{64,80},{80,96},{96,112},{112,128},... | collective-permute-start | bytes 98312 | tf_op jit(solution)/shard_map/ppermute | solution.py:370
  52.5 5.1 %collective-permute-start.5 = (f32[64,128]{1,0:T(8,128)}, f32[64,128]{1,0:T(8,128)S(1)}, u32[]{:S(2)}, u32[]{:S(2)}) collective-permute-start(f32[64,128]{1,0:T(8,128)} %get-tuple-element.29), channel_id=1, source_target_pairs={{16,0},{32,16},{48,32},{64,48},{80,64},{96,80},{112,96},{128,112},... | collective-permute-start | bytes 98312 | tf_op jit(solution)/shard_map/ppermute | solution.py:370
  57.7 3.5 %collective-permute-start.6 = (f32[8,128]{1,0:T(8,128)}, f32[8,128]{1,0:T(8,128)S(1)}, u32[]{:S(2)}, u32[]{:S(2)}) collective-permute-start(f32[8,128]{1,0:T(8,128)} %get-tuple-element.30), channel_id=1, source_target_pairs={{0,1},{1,2},{2,3},{3,4},{4,5},{5,6},{6,7},{7,8},{8,9},{9,10},{10,1... | collective-permute-start | bytes 12296 | tf_op jit(solution)/shard_map/ppermute | solution.py:370
  61.2 4.5 %collective-permute-start.7 = (f32[8,128]{1,0:T(8,128)S(1)}, f32[8,128]{1,0:T(8,128)S(1)}, u32[]{:S(2)}, u32[]{:S(2)}) collective-permute-start(f32[8,128]{1,0:T(8,128)S(1)} %copy-done.17), channel_id=1, source_target_pairs={{1,0},{2,1},{3,2},{4,3},{5,4},{6,5},{7,6},{8,7},{9,8},{10,9},{11,1... | collective-permute-start | bytes 12296 | tf_op jit(solution)/shard_map/ppermute | solution.py:370
  65.7 1.3 %collective-permute-done.7.refs_4_ = f32[8,128]{1,0:T(8,128)S(1)} collective-permute-done((f32[8,128]{1,0:T(8,128)S(1)}, f32[8,128]{1,0:T(8,128)S(1)}, u32[]{:S(2)}, u32[]{:S(2)}) %collective-permute-start.7) | collective-permute-done | bytes 4128 | tf_op jit(solution)/shard_map/ppermute | solution.py:370
  67.0 0.0 collective-permute-done.4.refs_1_
  67.0 0.6 copy-done.11
  67.6 0.0 copy-done.4
  67.6 3.3 %shard_map.81 = (f32[2,32,8,128]{3,2,1,0:T(8,128)}, f32[64,128]{1,0:T(8,128)}, f32[64,128]{1,0:T(8,128)}, f32[8,128]{1,0:T(8,128)}, f32[8,128]{1,0:T(8,128)}) custom-call(f32[2,32,8,128]{3,2,1,0:T(8,128)} %get-tuple-element.27.refs_0_, f32[64,128]{1,0:T(8,128)} %copy-done.4, f32[64,128]{1,0:T(8,128)} %copy-done.5, f32[8,128]{1,0:T(8,128)} %copy-done.10, ...), custom_call_target="tpu_custom_call" | custom-call | tf_op jit(solution)/shard_map/pallas_call | solution.py:354
  70.9 1.9 %collective-permute-start.8 = (f32[64,128]{1,0:T(8,128)}, f32[64,128]{1,0:T(8,128)S(1)}, u32[]{:S(2)}, u32[]{:S(2)}) collective-permute-start(f32[64,128]{1,0:T(8,128)} %get-tuple-element.38), channel_id=1, source_target_pairs={{0,16},{16,32},{32,48},{48,64},{64,80},{80,96},{96,112},{112,128},... | collective-permute-start | bytes 98312 | tf_op jit(solution)/shard_map/ppermute | solution.py:370
  72.8 6.0 %collective-permute-start.9 = (f32[64,128]{1,0:T(8,128)}, f32[64,128]{1,0:T(8,128)S(1)}, u32[]{:S(2)}, u32[]{:S(2)}) collective-permute-start(f32[64,128]{1,0:T(8,128)} %get-tuple-element.39), channel_id=1, source_target_pairs={{16,0},{32,16},{48,32},{64,48},{80,64},{96,80},{112,96},{128,112},... | collective-permute-start | bytes 98312 | tf_op jit(solution)/shard_map/ppermute | solution.py:370
  78.8 2.9 %collective-permute-start.10 = (f32[8,128]{1,0:T(8,128)}, f32[8,128]{1,0:T(8,128)S(1)}, u32[]{:S(2)}, u32[]{:S(2)}) collective-permute-start(f32[8,128]{1,0:T(8,128)} %get-tuple-element.40), channel_id=1, source_target_pairs={{0,1},{1,2},{2,3},{3,4},{4,5},{5,6},{6,7},{7,8},{8,9},{9,10},{10,1... | collective-permute-start | bytes 12296 | tf_op jit(solution)/shard_map/ppermute | solution.py:370
  81.7 5.1 %collective-permute-start.11 = (f32[8,128]{1,0:T(8,128)S(1)}, f32[8,128]{1,0:T(8,128)S(1)}, u32[]{:S(2)}, u32[]{:S(2)}) collective-permute-start(f32[8,128]{1,0:T(8,128)S(1)} %copy-done.18), channel_id=1, source_target_pairs={{1,0},{2,1},{3,2},{4,3},{5,4},{6,5},{7,6},{8,7},{9,8},{10,9},{11,1... | collective-permute-start | bytes 12296 | tf_op jit(solution)/shard_map/ppermute | solution.py:370
  86.8 2.5 %shard_map.80 = f32[2,32,8,128]{3,2,1,0:T(8,128)} custom-call(f32[2,32,8,128]{3,2,1,0:T(8,128)} %get-tuple-element.27.refs_0_, f32[64,128]{1,0:T(8,128)} %copy-done.4, f32[64,128]{1,0:T(8,128)} %copy-done.5, f32[8,128]{1,0:T(8,128)} %copy-done.10, f32[8,128]{1,0:T(8,128)} %copy-done.11, f32[4,8,128]{2,1,0:T(8,128)} %get-tuple-element.24.c_ref.refs_5_.refs_10_, ...), custom_call_target="tpu_custom_call" | custom-call | tf_op jit(solution)/shard_map/pallas_call | solution.py:317
  89.4 0.5 copy-done.12
  89.9 0.0 copy-done.13
  90.0 0.0 copy-done.8
  90.0 0.0 copy-done.9
  90.0 3.1 %shard_map.82 = f32[2,32,8,128]{3,2,1,0:T(8,128)} custom-call(f32[2,32,8,128]{3,2,1,0:T(8,128)} %get-tuple-element.32.refs_0_, f32[64,128]{1,0:T(8,128)} %get-tuple-element.33.refs_1_, f32[64,128]{1,0:T(8,128)} %get-tuple-element.34.refs_2_, f32[8,128]{1,0:T(8,128)} %get-tuple-element.35.refs_3_, f32[8,128]{1,0:T(8,128)} %get-tuple-element.36.refs_4_, ...), custom_call_target="tpu_custom_call" | custom-call | tf_op jit(solution)/shard_map/pallas_call | solution.py:354
  (46 shorter events, 0.2 us)
Async XLA Ops:
  0.6 1.4 %copy-start.14 = (bf16[2,32,1,1]{1,0,3,2:T(2,128)(2,1)S(1)}, bf16[2,32,1,1]{1,0,3,2:T(2,128)(2,1)}, u32[]{:S(2)}) copy-start(bf16[2,32,1,1]{1,0,3,2:T(2,128)(2,1)} %param.7) | copy-start | bytes 388
  4.5 8.6 %collective-permute-start = (f32[136,128]{1,0:T(8,128)}, f32[136,128]{1,0:T(8,128)S(1)}, u32[]{:S(2)}, u32[]{:S(2)}) collective-permute-start(f32[136,128]{1,0:T(8,128)} %get-tuple-element.22), channel_id=1, source_target_pairs={{0,16},{16,32},{32,48},{48,64},{64,80},{80,96},{96,112},{112,128},... | collective-permute-start | bytes 208904 | tf_op jit(solution)/shard_map/ppermute | solution.py:370
  8.0 6.7 %collective-permute-start.1 = (f32[136,128]{1,0:T(8,128)}, f32[136,128]{1,0:T(8,128)S(1)}, u32[]{:S(2)}, u32[]{:S(2)}) collective-permute-start(f32[136,128]{1,0:T(8,128)} %get-tuple-element.23), channel_id=1, source_target_pairs={{16,0},{32,16},{48,32},{64,48},{80,64},{96,80},{112,96},{128,112},... | collective-permute-start | bytes 208904 | tf_op jit(solution)/shard_map/ppermute | solution.py:370
  13.1 1.6 %copy-start = (f32[136,128]{1,0:T(8,128)}, f32[136,128]{1,0:T(8,128)S(1)}, u32[]{:S(2)}) copy-start(f32[136,128]{1,0:T(8,128)S(1)} %collective-permute-done.cxm.refs_6_.refs_11_) | copy-start | bytes 208900
  13.2 2.3 %copy-start.3 = (bf16[2,32,8,128]{3,2,1,0:T(8,128)(2,1)S(1)}, bf16[2,32,8,128]{3,2,1,0:T(8,128)(2,1)}, u32[]{:S(2)}) copy-start(bf16[2,32,8,128]{3,2,1,0:T(8,128)(2,1)} %slab_ref.1) | copy-start | bytes 393220
  14.7 0.6 copy-start.1
  31.3 5.6 %copy-start.16 = (f32[8,128]{1,0:T(8,128)S(1)}, f32[8,128]{1,0:T(8,128)}, u32[]{:S(2)}) copy-start(f32[8,128]{1,0:T(8,128)} %get-tuple-element.25) | copy-start | bytes 12292
  31.3 7.6 %copy-start.15 = (f32[8,128]{1,0:T(8,128)S(1)}, f32[8,128]{1,0:T(8,128)}, u32[]{:S(2)}) copy-start(f32[8,128]{1,0:T(8,128)} %get-tuple-element.26) | copy-start | bytes 12292
  31.3 13.6 %all-to-all-start.1 = ((bf16[16,8,8,128]{3,2,1,0:T(8,128)(2,1)}), bf16[16,8,8,128]{3,2,1,0:T(8,128)(2,1)S(1)}, u32[]{:S(2)}, u32[]{:S(2)}) async-start(bf16[16,8,8,128]{3,2,1,0:T(8,128)(2,1)} %shard_map.78), calls=%async_computation.1 | async-start | bytes 524288 | tf_op jit(solution)/shard_map/all_to_all | solution.py:433
  36.9 9.1 %collective-permute-start.2 = (f32[8,128]{1,0:T(8,128)S(1)}, f32[8,128]{1,0:T(8,128)S(1)}, u32[]{:S(2)}, u32[]{:S(2)}) collective-permute-start(f32[8,128]{1,0:T(8,128)S(1)} %copy-done.16), channel_id=1, source_target_pairs={{0,1},{1,2},{2,3},{3,4},{4,5},{5,6},{6,7},{7,8},{8,9},{9,10},{10,1... | collective-permute-start | bytes 12296 | tf_op jit(solution)/shard_map/ppermute | solution.py:370
  38.9 7.2 %collective-permute-start.3 = (f32[8,128]{1,0:T(8,128)S(1)}, f32[8,128]{1,0:T(8,128)S(1)}, u32[]{:S(2)}, u32[]{:S(2)}) collective-permute-start(f32[8,128]{1,0:T(8,128)S(1)} %copy-done.15), channel_id=1, source_target_pairs={{1,0},{2,1},{3,2},{4,3},{5,4},{6,5},{7,6},{8,7},{9,8},{10,9},{11,1... | collective-permute-start | bytes 12296 | tf_op jit(solution)/shard_map/ppermute | solution.py:370
  44.9 1.3 %copy-start.2 = (bf16[16,8,8,128]{3,2,1,0:T(8,128)(2,1)}, bf16[16,8,8,128]{3,2,1,0:T(8,128)(2,1)S(1)}, u32[]{:S(2)}) copy-start(bf16[16,8,8,128]{3,2,1,0:T(8,128)(2,1)S(1)} %all-to-all-done.1.r_ref) | copy-start | bytes 786436
  46.0 0.6 copy-start.6
  46.2 0.6 copy-start.7
  49.7 11.5 %copy-start.17 = (f32[8,128]{1,0:T(8,128)S(1)}, f32[8,128]{1,0:T(8,128)}, u32[]{:S(2)}) copy-start(f32[8,128]{1,0:T(8,128)} %get-tuple-element.31) | copy-start | bytes 12292
  49.7 17.3 %collective-permute-start.4 = (f32[64,128]{1,0:T(8,128)}, f32[64,128]{1,0:T(8,128)S(1)}, u32[]{:S(2)}, u32[]{:S(2)}) collective-permute-start(f32[64,128]{1,0:T(8,128)} %get-tuple-element.28), channel_id=1, source_target_pairs={{0,16},{16,32},{32,48},{48,64},{64,80},{80,96},{96,112},{112,128},... | collective-permute-start | bytes 98312 | tf_op jit(solution)/shard_map/ppermute | solution.py:370
  52.5 14.5 %collective-permute-start.5 = (f32[64,128]{1,0:T(8,128)}, f32[64,128]{1,0:T(8,128)S(1)}, u32[]{:S(2)}, u32[]{:S(2)}) collective-permute-start(f32[64,128]{1,0:T(8,128)} %get-tuple-element.29), channel_id=1, source_target_pairs={{16,0},{32,16},{48,32},{64,48},{80,64},{96,80},{112,96},{128,112},... | collective-permute-start | bytes 98312 | tf_op jit(solution)/shard_map/ppermute | solution.py:370
  57.7 8.0 %collective-permute-start.6 = (f32[8,128]{1,0:T(8,128)}, f32[8,128]{1,0:T(8,128)S(1)}, u32[]{:S(2)}, u32[]{:S(2)}) collective-permute-start(f32[8,128]{1,0:T(8,128)} %get-tuple-element.30), channel_id=1, source_target_pairs={{0,1},{1,2},{2,3},{3,4},{4,5},{5,6},{6,7},{7,8},{8,9},{9,10},{10,1... | collective-permute-start | bytes 12296 | tf_op jit(solution)/shard_map/ppermute | solution.py:370
  61.2 5.8 %collective-permute-start.7 = (f32[8,128]{1,0:T(8,128)S(1)}, f32[8,128]{1,0:T(8,128)S(1)}, u32[]{:S(2)}, u32[]{:S(2)}) collective-permute-start(f32[8,128]{1,0:T(8,128)S(1)} %copy-done.17), channel_id=1, source_target_pairs={{1,0},{2,1},{3,2},{4,3},{5,4},{6,5},{7,6},{8,7},{9,8},{10,9},{11,1... | collective-permute-start | bytes 12296 | tf_op jit(solution)/shard_map/ppermute | solution.py:370
  65.7 1.3 %copy-start.10 = (f32[8,128]{1,0:T(8,128)}, f32[8,128]{1,0:T(8,128)S(1)}, u32[]{:S(2)}) copy-start(f32[8,128]{1,0:T(8,128)S(1)} %collective-permute-done.6.refs_3_) | copy-start | bytes 12292
  67.0 0.6 copy-start.11
  67.0 0.6 copy-start.4
  67.0 0.6 copy-start.5
  70.9 10.8 %copy-start.18 = (f32[8,128]{1,0:T(8,128)S(1)}, f32[8,128]{1,0:T(8,128)}, u32[]{:S(2)}) copy-start(f32[8,128]{1,0:T(8,128)} %get-tuple-element.41) | copy-start | bytes 12292
  70.9 18.5 %collective-permute-start.8 = (f32[64,128]{1,0:T(8,128)}, f32[64,128]{1,0:T(8,128)S(1)}, u32[]{:S(2)}, u32[]{:S(2)}) collective-permute-start(f32[64,128]{1,0:T(8,128)} %get-tuple-element.38), channel_id=1, source_target_pairs={{0,16},{16,32},{32,48},{48,64},{64,80},{80,96},{96,112},{112,128},... | collective-permute-start | bytes 98312 | tf_op jit(solution)/shard_map/ppermute | solution.py:370
  72.8 16.6 %collective-permute-start.9 = (f32[64,128]{1,0:T(8,128)}, f32[64,128]{1,0:T(8,128)S(1)}, u32[]{:S(2)}, u32[]{:S(2)}) collective-permute-start(f32[64,128]{1,0:T(8,128)} %get-tuple-element.39), channel_id=1, source_target_pairs={{16,0},{32,16},{48,32},{64,48},{80,64},{96,80},{112,96},{128,112},... | collective-permute-start | bytes 98312 | tf_op jit(solution)/shard_map/ppermute | solution.py:370
  78.8 10.5 %collective-permute-start.10 = (f32[8,128]{1,0:T(8,128)}, f32[8,128]{1,0:T(8,128)S(1)}, u32[]{:S(2)}, u32[]{:S(2)}) collective-permute-start(f32[8,128]{1,0:T(8,128)} %get-tuple-element.40), channel_id=1, source_target_pairs={{0,1},{1,2},{2,3},{3,4},{4,5},{5,6},{6,7},{7,8},{8,9},{9,10},{10,1... | collective-permute-start | bytes 12296 | tf_op jit(solution)/shard_map/ppermute | solution.py:370
  81.7 7.6 %collective-permute-start.11 = (f32[8,128]{1,0:T(8,128)S(1)}, f32[8,128]{1,0:T(8,128)S(1)}, u32[]{:S(2)}, u32[]{:S(2)}) collective-permute-start(f32[8,128]{1,0:T(8,128)S(1)} %copy-done.18), channel_id=1, source_target_pairs={{1,0},{2,1},{3,2},{4,3},{5,4},{6,5},{7,6},{8,7},{9,8},{10,9},{11,1... | collective-permute-start | bytes 12296 | tf_op jit(solution)/shard_map/ppermute | solution.py:370
  89.3 0.6 copy-start.12
  89.4 0.6 copy-start.13
  89.4 0.6 copy-start.8
  89.4 0.6 copy-start.9

commit v10 on v9

--- a/solution.py
+++ b/solution.py
@@ -199,6 +199,7 @@
 def prep_call(soil_class, soil_table, cot, slab, scales):
     nf, nz, x, y = cot.shape
     nclass = soil_table.shape[0]
+    table = soil_table.T
     nplanes = nf * nz
 
     def kernel(cls_ref, tab_ref, sc_ref, cot_ref, slab_ref, coef_ref, xf_ref, xl_ref, yf_ref, yl_ref):
@@ -207,7 +208,7 @@
         for k in range(NCOEF):
             cv = jnp.zeros(cls.shape, F32)
             for j in range(nclass):
-                cv = jnp.where(cls == j, tab_ref[j, k], cv)
+                cv = jnp.where(cls == j, tab_ref[k, j], cv)
             coef_ref[k] = cv
             coefs.append(cv)
         vals = [cot_ref[f, z] for f in range(nf) for z in range(nz)] + coefs
@@ -237,7 +238,7 @@
             pl.BlockSpec(memory_space=VMEM),
             pl.BlockSpec(memory_space=VMEM),
         ],
-    )(soil_class, soil_table, scales, cot, slab)
+    )(soil_class, table, scales, cot, slab)
 
 
 def _state0_body(sc_ref, r_ref, s_ref, xm_ref, xp_ref, ym_ref, yp_ref, per):

time: 94.1 us -> 93.5 us (level)
    unnamed x39 -> x38, local copies, waits for them, and re-layouts: 3.67 us -> 2.31 us
where the time goes in v10:
time: 93.5 us; the launch traced here: 92.6 us
  starting transfers between devices  53.4 us (57%)
  Pallas kernels  15.5 us (17%)
  blocking collectives  14 us (15%)
  local copies, waits for them, and re-layouts  5.03 us (5%)
  waiting for transfers between devices  3.54 us (4%)
  between operations  0.98 us (1%)
    ppermute x12, starting transfers between devices, _shift(): return lax.ppermute(v, axis, pairs)  47.9 us
    all_to_all x1, blocking collectives, route_blocks(): lax.all_to_all(jnp.concatenate([slab, halo, sc], axis=1), 'gy', 0, 0, til...  14 us
    pallas_call x2, Pallas kernels, adjoint_call(): pl.pallas_call(kernel, out_shape=out_shape, scratch_shapes=_halo_scratch(...  6.4 us
    all_to_all x1, starting transfers between devices, route_blocks(): return lax.all_to_all(forward, 'gy', 0, 0, tiled=True)  5.56 us
    ppermute x12, waiting for transfers between devices, _shift(): return lax.ppermute(v, axis, pairs)  3.54 us
    pallas_call x1, Pallas kernels, state0_step_call(): pl.pallas_call(kernel, out_shape=(state,) + _edge_shapes(nplanes, x, y) +...  2.93 us
    pallas_call x1, Pallas kernels, step_call(): pl.pallas_call(kernel, out_shape=out_shape, scratch_shapes=_halo_scratch(...  2.52 us
    unnamed x38, local copies, waits for them, and re-layouts  2.31 us
  transfers between devices with their start and end apart: 13, of which 4 were waited for; matrix products, arithmetic and copies ran while one was open for 1% of the time, Pallas kernels for 3%

profile of v10, /device:TPU:130, one launch (start us, length us, event | category | flops | bytes accessed | tf_op | source)
XLA Modules:
  0.0 92.6 jit_solution(4668261315067106014)
XLA Ops:
  0.6 1.3 %reshape.59.sc_ref = f32[64]{0:T(128)} reshape(bf16[2,32,1,1]{1,0,3,2:T(2,128)(2,1)} %param.7) | data formatting | bytes 384 | tf_op jit(solution)/shard_map/convert_element_type | solution.py:442
  1.9 1.8 %shard_map.77 = (f32[4,8,128]{2,1,0:T(8,128)}, f32[136,128]{1,0:T(8,128)}, f32[136,128]{1,0:T(8,128)}, f32[8,128]{1,0:T(8,128)}, f32[8,128]{1,0:T(8,128)}) custom-call(s32[8,128]{1,0:T(8,128)} %cls_ref.1, f32[4,12]{1,0:T(4,128)} %bitcast.23, f32[64]{0:T(128)} %reshape.59.sc_ref, f32[2,32,8,128]{3,2,1,0:T(8,128)} %refs_5_.1, bf16[2,32,8,128]{3,2,1,0:T(8,128)(2,1)} %slab_ref.1), custom_call_target="tpu_custom_call" | custom-call | tf_op jit(solution)/shard_map/pallas_call | solution.py:229
  3.8 3.6 %collective-permute-start = (f32[136,128]{1,0:T(8,128)}, f32[136,128]{1,0:T(8,128)S(1)}, u32[]{:S(2)}, u32[]{:S(2)}) collective-permute-start(f32[136,128]{1,0:T(8,128)} %get-tuple-element.22), channel_id=1, source_target_pairs={{0,16},{16,32},{32,48},{48,64},{64,80},{80,96},{96,112},{112,128},... | collective-permute-start | bytes 208904 | tf_op jit(solution)/shard_map/ppermute | solution.py:371
  7.4 4.5 %collective-permute-start.1 = (f32[136,128]{1,0:T(8,128)}, f32[136,128]{1,0:T(8,128)S(1)}, u32[]{:S(2)}, u32[]{:S(2)}) collective-permute-start(f32[136,128]{1,0:T(8,128)} %get-tuple-element.23), channel_id=1, source_target_pairs={{16,0},{32,16},{48,32},{64,48},{80,64},{96,80},{112,96},{128,112},... | collective-permute-start | bytes 208904 | tf_op jit(solution)/shard_map/ppermute | solution.py:371
  11.9 0.1 reshape.61
  12.0 0.6 collective-permute-done.cxm.refs_6_.refs_11_
  12.6 1.5 %collective-permute-done.1.cxp.refs_7_.refs_12_ = f32[136,128]{1,0:T(8,128)S(1)} collective-permute-done((f32[136,128]{1,0:T(8,128)}, f32[136,128]{1,0:T(8,128)S(1)}, u32[]{:S(2)}, u32[]{:S(2)}) %collective-permute-start.1) | collective-permute-done | bytes 69664 | tf_op jit(solution)/shard_map/ppermute | solution.py:371
  14.1 0.1 convert_element_type.46
  14.2 0.5 copy-done.1
  14.7 0.1 convert_element_type.47
  14.8 0.1 fusion.9
  14.9 14.0 %all_to_all.10.h_ref = bf16[16,6,8,128]{3,2,1,0:T(8,128)(2,1)} all-to-all(bf16[16,6,8,128]{3,2,1,0:T(8,128)(2,1)S(1)} %pad_maximum_fusion), channel_id=1, replica_groups=mesh['gx'=16,'gy'=16] {'gy'}, dimensions={0} | all-to-all | bytes 393216 | tf_op jit(solution)/shard_map/all_to_all | solution.py:431
  28.9 1.8 %shard_map.78 = bf16[16,8,8,128]{3,2,1,0:T(8,128)(2,1)} custom-call(s32[16]{0:T(128)} %hold_ref.1, bf16[16,6,8,128]{3,2,1,0:T(8,128)(2,1)} %all_to_all.10.h_ref), custom_call_target="tpu_custom_call" | custom-call | tf_op jit(solution)/shard_map/pallas_call | solution.py:410
  30.7 5.6 %all-to-all-start.1 = ((bf16[16,8,8,128]{3,2,1,0:T(8,128)(2,1)}), bf16[16,8,8,128]{3,2,1,0:T(8,128)(2,1)S(1)}, u32[]{:S(2)}, u32[]{:S(2)}) async-start(bf16[16,8,8,128]{3,2,1,0:T(8,128)(2,1)} %shard_map.78), calls=%async_computation.1 | async-start | bytes 524288 | tf_op jit(solution)/shard_map/all_to_all | solution.py:434
  36.3 2.1 %collective-permute-start.2 = (f32[8,128]{1,0:T(8,128)S(1)}, f32[8,128]{1,0:T(8,128)S(1)}, u32[]{:S(2)}, u32[]{:S(2)}) collective-permute-start(f32[8,128]{1,0:T(8,128)S(1)} %copy-done.16), channel_id=1, source_target_pairs={{0,1},{1,2},{2,3},{3,4},{4,5},{5,6},{6,7},{7,8},{8,9},{9,10},{10,1... | collective-permute-start | bytes 12296 | tf_op jit(solution)/shard_map/ppermute | solution.py:371
  38.4 5.9 %collective-permute-start.3 = (f32[8,128]{1,0:T(8,128)S(1)}, f32[8,128]{1,0:T(8,128)S(1)}, u32[]{:S(2)}, u32[]{:S(2)}) collective-permute-start(f32[8,128]{1,0:T(8,128)S(1)} %copy-done.15), channel_id=1, source_target_pairs={{1,0},{2,1},{3,2},{4,3},{5,4},{6,5},{7,6},{8,7},{9,8},{10,9},{11,1... | collective-permute-start | bytes 12296 | tf_op jit(solution)/shard_map/ppermute | solution.py:371
  44.3 0.0 all-to-all-done.1.r_ref
  44.3 0.0 copy-start.2
  44.3 0.1 reshape.57
  44.5 0.1 copy.30
  44.5 0.1 copy.31
  44.6 0.1 reshape.58
  44.8 0.7 reshape.60.sc_ref
  45.4 0.0 collective-permute-done.2.cym.refs_8_.refs_13_
  45.4 0.2 collective-permute-done.3.cyp.refs_9_.refs_14_
  45.6 0.4 copy-done.6
  46.0 0.2 copy-done.7
  46.2 2.9 %shard_map.79 = (f32[2,32,8,128]{3,2,1,0:T(8,128)}, f32[64,128]{1,0:T(8,128)}, f32[64,128]{1,0:T(8,128)}, f32[8,128]{1,0:T(8,128)}, f32[8,128]{1,0:T(8,128)}, /*...) custom-call(f32[320]{0:T(512)} %reshape.60.sc_ref, ...), custom_call_target="tpu_custom_call" | custom-call | tf_op jit(solution)/shard_map/pallas_call | solution.py:284
  49.1 2.8 %collective-permute-start.4 = (f32[64,128]{1,0:T(8,128)}, f32[64,128]{1,0:T(8,128)S(1)}, u32[]{:S(2)}, u32[]{:S(2)}) collective-permute-start(f32[64,128]{1,0:T(8,128)} %get-tuple-element.28), channel_id=1, source_target_pairs={{0,16},{16,32},{32,48},{48,64},{64,80},{80,96},{96,112},{112,128},... | collective-permute-start | bytes 98312 | tf_op jit(solution)/shard_map/ppermute | solution.py:371
  51.9 5.1 %collective-permute-start.5 = (f32[64,128]{1,0:T(8,128)}, f32[64,128]{1,0:T(8,128)S(1)}, u32[]{:S(2)}, u32[]{:S(2)}) collective-permute-start(f32[64,128]{1,0:T(8,128)} %get-tuple-element.29), channel_id=1, source_target_pairs={{16,0},{32,16},{48,32},{64,48},{80,64},{96,80},{112,96},{128,112},... | collective-permute-start | bytes 98312 | tf_op jit(solution)/shard_map/ppermute | solution.py:371
  57.1 3.5 %collective-permute-start.6 = (f32[8,128]{1,0:T(8,128)}, f32[8,128]{1,0:T(8,128)S(1)}, u32[]{:S(2)}, u32[]{:S(2)}) collective-permute-start(f32[8,128]{1,0:T(8,128)} %get-tuple-element.30), channel_id=1, source_target_pairs={{0,1},{1,2},{2,3},{3,4},{4,5},{5,6},{6,7},{7,8},{8,9},{9,10},{10,1... | collective-permute-start | bytes 12296 | tf_op jit(solution)/shard_map/ppermute | solution.py:371
  60.6 4.5 %collective-permute-start.7 = (f32[8,128]{1,0:T(8,128)S(1)}, f32[8,128]{1,0:T(8,128)S(1)}, u32[]{:S(2)}, u32[]{:S(2)}) collective-permute-start(f32[8,128]{1,0:T(8,128)S(1)} %copy-done.17), channel_id=1, source_target_pairs={{1,0},{2,1},{3,2},{4,3},{5,4},{6,5},{7,6},{8,7},{9,8},{10,9},{11,1... | collective-permute-start | bytes 12296 | tf_op jit(solution)/shard_map/ppermute | solution.py:371
  65.1 0.0 collective-permute-done.6.refs_3_
  65.1 1.3 %collective-permute-done.7.refs_4_ = f32[8,128]{1,0:T(8,128)S(1)} collective-permute-done((f32[8,128]{1,0:T(8,128)S(1)}, f32[8,128]{1,0:T(8,128)S(1)}, u32[]{:S(2)}, u32[]{:S(2)}) %collective-permute-start.7) | collective-permute-done | bytes 4128 | tf_op jit(solution)/shard_map/ppermute | solution.py:371
  66.4 0.0 collective-permute-done.5.refs_2_
  66.4 0.6 copy-done.11
  67.0 0.0 copy-done.4
  67.0 3.3 %shard_map.81 = (f32[2,32,8,128]{3,2,1,0:T(8,128)}, f32[64,128]{1,0:T(8,128)}, f32[64,128]{1,0:T(8,128)}, f32[8,128]{1,0:T(8,128)}, f32[8,128]{1,0:T(8,128)}) custom-call(f32[2,32,8,128]{3,2,1,0:T(8,128)} %get-tuple-element.27.refs_0_, f32[64,128]{1,0:T(8,128)} %copy-done.4, f32[64,128]{1,0:T(8,128)} %copy-done.5, f32[8,128]{1,0:T(8,128)} %copy-done.10, ...), custom_call_target="tpu_custom_call" | custom-call | tf_op jit(solution)/shard_map/pallas_call | solution.py:355
  70.3 1.9 %collective-permute-start.8 = (f32[64,128]{1,0:T(8,128)}, f32[64,128]{1,0:T(8,128)S(1)}, u32[]{:S(2)}, u32[]{:S(2)}) collective-permute-start(f32[64,128]{1,0:T(8,128)} %get-tuple-element.38), channel_id=1, source_target_pairs={{0,16},{16,32},{32,48},{48,64},{64,80},{80,96},{96,112},{112,128},... | collective-permute-start | bytes 98312 | tf_op jit(solution)/shard_map/ppermute | solution.py:371
  72.2 6.0 %collective-permute-start.9 = (f32[64,128]{1,0:T(8,128)}, f32[64,128]{1,0:T(8,128)S(1)}, u32[]{:S(2)}, u32[]{:S(2)}) collective-permute-start(f32[64,128]{1,0:T(8,128)} %get-tuple-element.39), channel_id=1, source_target_pairs={{16,0},{32,16},{48,32},{64,48},{80,64},{96,80},{112,96},{128,112},... | collective-permute-start | bytes 98312 | tf_op jit(solution)/shard_map/ppermute | solution.py:371
  78.3 2.9 %collective-permute-start.10 = (f32[8,128]{1,0:T(8,128)}, f32[8,128]{1,0:T(8,128)S(1)}, u32[]{:S(2)}, u32[]{:S(2)}) collective-permute-start(f32[8,128]{1,0:T(8,128)} %get-tuple-element.40), channel_id=1, source_target_pairs={{0,1},{1,2},{2,3},{3,4},{4,5},{5,6},{6,7},{7,8},{8,9},{9,10},{10,1... | collective-permute-start | bytes 12296 | tf_op jit(solution)/shard_map/ppermute | solution.py:371
  81.1 5.1 %collective-permute-start.11 = (f32[8,128]{1,0:T(8,128)S(1)}, f32[8,128]{1,0:T(8,128)S(1)}, u32[]{:S(2)}, u32[]{:S(2)}) collective-permute-start(f32[8,128]{1,0:T(8,128)S(1)} %copy-done.18), channel_id=1, source_target_pairs={{1,0},{2,1},{3,2},{4,3},{5,4},{6,5},{7,6},{8,7},{9,8},{10,9},{11,1... | collective-permute-start | bytes 12296 | tf_op jit(solution)/shard_map/ppermute | solution.py:371
  86.2 2.5 %shard_map.80 = f32[2,32,8,128]{3,2,1,0:T(8,128)} custom-call(f32[2,32,8,128]{3,2,1,0:T(8,128)} %get-tuple-element.27.refs_0_, f32[64,128]{1,0:T(8,128)} %copy-done.4, f32[64,128]{1,0:T(8,128)} %copy-done.5, f32[8,128]{1,0:T(8,128)} %copy-done.10, f32[8,128]{1,0:T(8,128)} %copy-done.11, f32[4,8,128]{2,1,0:T(8,128)} %get-tuple-element.24.c_ref.refs_5_.refs_10_, ...), custom_call_target="tpu_custom_call" | custom-call | tf_op jit(solution)/shard_map/pallas_call | solution.py:318
  88.8 0.5 copy-done.12
  89.4 0.0 copy-done.13
  89.4 0.0 copy-done.8
  89.4 0.0 copy-done.9
  89.4 3.1 %shard_map.82 = f32[2,32,8,128]{3,2,1,0:T(8,128)} custom-call(f32[2,32,8,128]{3,2,1,0:T(8,128)} %get-tuple-element.32.refs_0_, f32[64,128]{1,0:T(8,128)} %get-tuple-element.33.refs_1_, f32[64,128]{1,0:T(8,128)} %get-tuple-element.34.refs_2_, f32[8,128]{1,0:T(8,128)} %get-tuple-element.35.refs_3_, f32[8,128]{1,0:T(8,128)} %get-tuple-element.36.refs_4_, ...), custom_call_target="tpu_custom_call" | custom-call | tf_op jit(solution)/shard_map/pallas_call | solution.py:355
  (45 shorter events, 0.2 us)
Async XLA Ops:
  3.8 8.1 %copy-start.14 = (bf16[2,32,1,1]{1,0,3,2:T(2,128)(2,1)S(1)}, bf16[2,32,1,1]{1,0,3,2:T(2,128)(2,1)}, u32[]{:S(2)}) copy-start(bf16[2,32,1,1]{1,0,3,2:T(2,128)(2,1)} %param.7) | copy-start | bytes 388
  3.8 8.8 %collective-permute-start = (f32[136,128]{1,0:T(8,128)}, f32[136,128]{1,0:T(8,128)S(1)}, u32[]{:S(2)}, u32[]{:S(2)}) collective-permute-start(f32[136,128]{1,0:T(8,128)} %get-tuple-element.22), channel_id=1, source_target_pairs={{0,16},{16,32},{32,48},{48,64},{64,80},{80,96},{96,112},{112,128},... | collective-permute-start | bytes 208904 | tf_op jit(solution)/shard_map/ppermute | solution.py:371
  7.4 6.7 %collective-permute-start.1 = (f32[136,128]{1,0:T(8,128)}, f32[136,128]{1,0:T(8,128)S(1)}, u32[]{:S(2)}, u32[]{:S(2)}) collective-permute-start(f32[136,128]{1,0:T(8,128)} %get-tuple-element.23), channel_id=1, source_target_pairs={{16,0},{32,16},{48,32},{64,48},{80,64},{96,80},{112,96},{128,112},... | collective-permute-start | bytes 208904 | tf_op jit(solution)/shard_map/ppermute | solution.py:371
  12.5 1.6 %copy-start = (f32[136,128]{1,0:T(8,128)}, f32[136,128]{1,0:T(8,128)S(1)}, u32[]{:S(2)}) copy-start(f32[136,128]{1,0:T(8,128)S(1)} %collective-permute-done.cxm.refs_6_.refs_11_) | copy-start | bytes 208900
  12.6 2.3 %copy-start.3 = (bf16[2,32,8,128]{3,2,1,0:T(8,128)(2,1)S(1)}, bf16[2,32,8,128]{3,2,1,0:T(8,128)(2,1)}, u32[]{:S(2)}) copy-start(bf16[2,32,8,128]{3,2,1,0:T(8,128)(2,1)} %slab_ref.1) | copy-start | bytes 393220
  14.1 0.6 copy-start.1
  30.7 5.6 %copy-start.16 = (f32[8,128]{1,0:T(8,128)S(1)}, f32[8,128]{1,0:T(8,128)}, u32[]{:S(2)}) copy-start(f32[8,128]{1,0:T(8,128)} %get-tuple-element.25) | copy-start | bytes 12292
  30.7 7.6 %copy-start.15 = (f32[8,128]{1,0:T(8,128)S(1)}, f32[8,128]{1,0:T(8,128)}, u32[]{:S(2)}) copy-start(f32[8,128]{1,0:T(8,128)} %get-tuple-element.26) | copy-start | bytes 12292
  30.7 13.6 %all-to-all-start.1 = ((bf16[16,8,8,128]{3,2,1,0:T(8,128)(2,1)}), bf16[16,8,8,128]{3,2,1,0:T(8,128)(2,1)S(1)}, u32[]{:S(2)}, u32[]{:S(2)}) async-start(bf16[16,8,8,128]{3,2,1,0:T(8,128)(2,1)} %shard_map.78), calls=%async_computation.1 | async-start | bytes 524288 | tf_op jit(solution)/shard_map/all_to_all | solution.py:434
  36.3 9.1 %collective-permute-start.2 = (f32[8,128]{1,0:T(8,128)S(1)}, f32[8,128]{1,0:T(8,128)S(1)}, u32[]{:S(2)}, u32[]{:S(2)}) collective-permute-start(f32[8,128]{1,0:T(8,128)S(1)} %copy-done.16), channel_id=1, source_target_pairs={{0,1},{1,2},{2,3},{3,4},{4,5},{5,6},{6,7},{7,8},{8,9},{9,10},{10,1... | collective-permute-start | bytes 12296 | tf_op jit(solution)/shard_map/ppermute | solution.py:371
  38.4 7.2 %collective-permute-start.3 = (f32[8,128]{1,0:T(8,128)S(1)}, f32[8,128]{1,0:T(8,128)S(1)}, u32[]{:S(2)}, u32[]{:S(2)}) collective-permute-start(f32[8,128]{1,0:T(8,128)S(1)} %copy-done.15), channel_id=1, source_target_pairs={{1,0},{2,1},{3,2},{4,3},{5,4},{6,5},{7,6},{8,7},{9,8},{10,9},{11,1... | collective-permute-start | bytes 12296 | tf_op jit(solution)/shard_map/ppermute | solution.py:371
  44.3 1.3 %copy-start.2 = (bf16[16,8,8,128]{3,2,1,0:T(8,128)(2,1)}, bf16[16,8,8,128]{3,2,1,0:T(8,128)(2,1)S(1)}, u32[]{:S(2)}) copy-start(bf16[16,8,8,128]{3,2,1,0:T(8,128)(2,1)S(1)} %all-to-all-done.1.r_ref) | copy-start | bytes 786436
  45.4 0.6 copy-start.6
  45.6 0.6 copy-start.7
  49.1 11.5 %copy-start.17 = (f32[8,128]{1,0:T(8,128)S(1)}, f32[8,128]{1,0:T(8,128)}, u32[]{:S(2)}) copy-start(f32[8,128]{1,0:T(8,128)} %get-tuple-element.31) | copy-start | bytes 12292
  49.1 17.3 %collective-permute-start.4 = (f32[64,128]{1,0:T(8,128)}, f32[64,128]{1,0:T(8,128)S(1)}, u32[]{:S(2)}, u32[]{:S(2)}) collective-permute-start(f32[64,128]{1,0:T(8,128)} %get-tuple-element.28), channel_id=1, source_target_pairs={{0,16},{16,32},{32,48},{48,64},{64,80},{80,96},{96,112},{112,128},... | collective-permute-start | bytes 98312 | tf_op jit(solution)/shard_map/ppermute | solution.py:371
  51.9 14.5 %collective-permute-start.5 = (f32[64,128]{1,0:T(8,128)}, f32[64,128]{1,0:T(8,128)S(1)}, u32[]{:S(2)}, u32[]{:S(2)}) collective-permute-start(f32[64,128]{1,0:T(8,128)} %get-tuple-element.29), channel_id=1, source_target_pairs={{16,0},{32,16},{48,32},{64,48},{80,64},{96,80},{112,96},{128,112},... | collective-permute-start | bytes 98312 | tf_op jit(solution)/shard_map/ppermute | solution.py:371
  57.1 8.0 %collective-permute-start.6 = (f32[8,128]{1,0:T(8,128)}, f32[8,128]{1,0:T(8,128)S(1)}, u32[]{:S(2)}, u32[]{:S(2)}) collective-permute-start(f32[8,128]{1,0:T(8,128)} %get-tuple-element.30), channel_id=1, source_target_pairs={{0,1},{1,2},{2,3},{3,4},{4,5},{5,6},{6,7},{7,8},{8,9},{9,10},{10,1... | collective-permute-start | bytes 12296 | tf_op jit(solution)/shard_map/ppermute | solution.py:371
  60.6 5.8 %collective-permute-start.7 = (f32[8,128]{1,0:T(8,128)S(1)}, f32[8,128]{1,0:T(8,128)S(1)}, u32[]{:S(2)}, u32[]{:S(2)}) collective-permute-start(f32[8,128]{1,0:T(8,128)S(1)} %copy-done.17), channel_id=1, source_target_pairs={{1,0},{2,1},{3,2},{4,3},{5,4},{6,5},{7,6},{8,7},{9,8},{10,9},{11,1... | collective-permute-start | bytes 12296 | tf_op jit(solution)/shard_map/ppermute | solution.py:371
  65.1 1.3 %copy-start.10 = (f32[8,128]{1,0:T(8,128)}, f32[8,128]{1,0:T(8,128)S(1)}, u32[]{:S(2)}) copy-start(f32[8,128]{1,0:T(8,128)S(1)} %collective-permute-done.6.refs_3_) | copy-start | bytes 12292
  66.4 0.6 copy-start.11
  66.4 0.6 copy-start.4
  66.4 0.6 copy-start.5
  70.3 10.8 %copy-start.18 = (f32[8,128]{1,0:T(8,128)S(1)}, f32[8,128]{1,0:T(8,128)}, u32[]{:S(2)}) copy-start(f32[8,128]{1,0:T(8,128)} %get-tuple-element.41) | copy-start | bytes 12292
  70.3 18.5 %collective-permute-start.8 = (f32[64,128]{1,0:T(8,128)}, f32[64,128]{1,0:T(8,128)S(1)}, u32[]{:S(2)}, u32[]{:S(2)}) collective-permute-start(f32[64,128]{1,0:T(8,128)} %get-tuple-element.38), channel_id=1, source_target_pairs={{0,16},{16,32},{32,48},{48,64},{64,80},{80,96},{96,112},{112,128},... | collective-permute-start | bytes 98312 | tf_op jit(solution)/shard_map/ppermute | solution.py:371
  72.2 16.6 %collective-permute-start.9 = (f32[64,128]{1,0:T(8,128)}, f32[64,128]{1,0:T(8,128)S(1)}, u32[]{:S(2)}, u32[]{:S(2)}) collective-permute-start(f32[64,128]{1,0:T(8,128)} %get-tuple-element.39), channel_id=1, source_target_pairs={{16,0},{32,16},{48,32},{64,48},{80,64},{96,80},{112,96},{128,112},... | collective-permute-start | bytes 98312 | tf_op jit(solution)/shard_map/ppermute | solution.py:371
  78.3 10.5 %collective-permute-start.10 = (f32[8,128]{1,0:T(8,128)}, f32[8,128]{1,0:T(8,128)S(1)}, u32[]{:S(2)}, u32[]{:S(2)}) collective-permute-start(f32[8,128]{1,0:T(8,128)} %get-tuple-element.40), channel_id=1, source_target_pairs={{0,1},{1,2},{2,3},{3,4},{4,5},{5,6},{6,7},{7,8},{8,9},{9,10},{10,1... | collective-permute-start | bytes 12296 | tf_op jit(solution)/shard_map/ppermute | solution.py:371
  81.1 7.6 %collective-permute-start.11 = (f32[8,128]{1,0:T(8,128)S(1)}, f32[8,128]{1,0:T(8,128)S(1)}, u32[]{:S(2)}, u32[]{:S(2)}) collective-permute-start(f32[8,128]{1,0:T(8,128)S(1)} %copy-done.18), channel_id=1, source_target_pairs={{1,0},{2,1},{3,2},{4,3},{5,4},{6,5},{7,6},{8,7},{9,8},{10,9},{11,1... | collective-permute-start | bytes 12296 | tf_op jit(solution)/shard_map/ppermute | solution.py:371
  88.8 0.6 copy-start.12
  88.8 0.6 copy-start.13
  88.8 0.6 copy-start.8
  88.8 0.6 copy-start.9

commit v11 on v10

--- a/solution.py
+++ b/solution.py
@@ -220,8 +220,10 @@
             xl_ref[base + k : base + k + 1, :] = v[x - 1 : x, :]
         _, lane = _iotas((1, y))
         row = jnp.zeros((1, y), F32)
+        scv = sc_ref[...].astype(F32)
         for k in range(nplanes):
-            row = jnp.where(lane == k, sc_ref[k], row)
+            v = jnp.broadcast_to(scv[k // nz : k // nz + 1, k % nz : k % nz + 1], (1, y))
+            row = jnp.where(lane == k, v, row)
         xf_ref[base + nplanes : base + nplanes + 1, :] = row
         xl_ref[base + nplanes : base + nplanes + 1, :] = row
 
@@ -234,7 +236,7 @@
         in_specs=[
             pl.BlockSpec(memory_space=VMEM),
             pl.BlockSpec(memory_space=SMEM),
-            pl.BlockSpec(memory_space=SMEM),
+            pl.BlockSpec(memory_space=VMEM),
             pl.BlockSpec(memory_space=VMEM),
             pl.BlockSpec(memory_space=VMEM),
         ],
@@ -439,7 +441,7 @@
     nplanes = nf * nz
 
     coef, cxf, cxl, cyf, cyl = prep_call(
-        soil_class, soil_table, cotangent, stored_slab, block_scales.reshape(-1).astype(F32)
+        soil_class, soil_table, cotangent, stored_slab, block_scales.reshape(nf, nz)
     )
     c_halo = exchange(cxf, cxl, cyf, cyl)
     c_first = nplanes

time: 93.5 us -> 92.4 us (0.988)
  local copies, waits for them, and re-layouts: 5.03 us -> 3.72 us
    convert_element_type x1 -> x0, local copies, waits for them, and re-layouts: 1.31 us -> none  [on_device(): block_scales.reshape(-1).astype(F32)]
where the time goes in v11:
time: 92.4 us; the launch traced here: 91.4 us
  starting transfers between devices  53.4 us (58%)
  Pallas kernels  15.6 us (17%)
  blocking collectives  14 us (15%)
  local copies, waits for them, and re-layouts  3.72 us (4%)
  waiting for transfers between devices  3.54 us (4%)
  between operations  0.98 us (1%)
    ppermute x12, starting transfers between devices, _shift(): return lax.ppermute(v, axis, pairs)  47.9 us
    all_to_all x1, blocking collectives, route_blocks(): lax.all_to_all(jnp.concatenate([slab, halo, sc], axis=1), 'gy', 0, 0, til...  14 us
    pallas_call x2, Pallas kernels, adjoint_call(): pl.pallas_call(kernel, out_shape=out_shape, scratch_shapes=_halo_scratch(...  6.4 us
    all_to_all x1, starting transfers between devices, route_blocks(): return lax.all_to_all(forward, 'gy', 0, 0, tiled=True)  5.56 us
    ppermute x12, waiting for transfers between devices, _shift(): return lax.ppermute(v, axis, pairs)  3.54 us
    pallas_call x1, Pallas kernels, state0_step_call(): pl.pallas_call(kernel, out_shape=(state,) + _edge_shapes(nplanes, x, y) +...  2.93 us
    pallas_call x1, Pallas kernels, step_call(): pl.pallas_call(kernel, out_shape=out_shape, scratch_shapes=_halo_scratch(...  2.52 us
    unnamed x38, local copies, waits for them, and re-layouts  2.31 us
  transfers between devices with their start and end apart: 13, of which 4 were waited for; matrix products, arithmetic and copies ran while one was open for 1% of the time, Pallas kernels for 3%

profile of v11, /device:TPU:130, one launch (start us, length us, event | category | flops | bytes accessed | tf_op | source)
XLA Modules:
  0.0 91.4 jit_solution(13512854105311922740)
XLA Ops:
  0.6 2.0 %shard_map.77 = (f32[4,8,128]{2,1,0:T(8,128)}, f32[136,128]{1,0:T(8,128)}, f32[136,128]{1,0:T(8,128)}, f32[8,128]{1,0:T(8,128)}, f32[8,128]{1,0:T(8,128)}) custom-call(s32[8,128]{1,0:T(8,128)} %cls_ref.1, f32[4,12]{1,0:T(4,128)} %bitcast.22, bf16[2,32]{1,0:T(2,128)(2,1)} %bitcast.23, f32[2,32,8,128]{3,2,1,0:T(8,128)} %refs_5_.1, bf16[2,32,8,128]{3,2,1,0:T(8,128)(2,1)} %slab_ref.1), custom_call_target="tpu_custom_call" | custom-call | tf_op jit(solution)/shard_map/pallas_call | solution.py:231
  2.6 3.6 %collective-permute-start = (f32[136,128]{1,0:T(8,128)}, f32[136,128]{1,0:T(8,128)S(1)}, u32[]{:S(2)}, u32[]{:S(2)}) collective-permute-start(f32[136,128]{1,0:T(8,128)} %get-tuple-element.22), channel_id=1, source_target_pairs={{0,16},{16,32},{32,48},{48,64},{64,80},{80,96},{96,112},{112,128},... | collective-permute-start | bytes 208904 | tf_op jit(solution)/shard_map/ppermute | solution.py:373
  6.2 4.5 %collective-permute-start.1 = (f32[136,128]{1,0:T(8,128)}, f32[136,128]{1,0:T(8,128)S(1)}, u32[]{:S(2)}, u32[]{:S(2)}) collective-permute-start(f32[136,128]{1,0:T(8,128)} %get-tuple-element.23), channel_id=1, source_target_pairs={{16,0},{32,16},{48,32},{64,48},{80,64},{96,80},{112,96},{128,112},... | collective-permute-start | bytes 208904 | tf_op jit(solution)/shard_map/ppermute | solution.py:373
  10.7 0.1 reshape.61
  10.8 0.6 collective-permute-done.cxm.refs_6_.refs_11_
  11.4 1.5 %collective-permute-done.1.cxp.refs_7_.refs_12_ = f32[136,128]{1,0:T(8,128)S(1)} collective-permute-done((f32[136,128]{1,0:T(8,128)}, f32[136,128]{1,0:T(8,128)S(1)}, u32[]{:S(2)}, u32[]{:S(2)}) %collective-permute-start.1) | collective-permute-done | bytes 69664 | tf_op jit(solution)/shard_map/ppermute | solution.py:373
  13.0 0.1 convert_element_type.38
  13.1 0.5 copy-done.1
  13.5 0.1 convert_element_type.39
  13.7 0.1 fusion.9
  13.8 14.0 %all_to_all.10.h_ref = bf16[16,6,8,128]{3,2,1,0:T(8,128)(2,1)} all-to-all(bf16[16,6,8,128]{3,2,1,0:T(8,128)(2,1)S(1)} %pad_maximum_fusion), channel_id=1, replica_groups=mesh['gx'=16,'gy'=16] {'gy'}, dimensions={0} | all-to-all | bytes 393216 | tf_op jit(solution)/shard_map/all_to_all | solution.py:433
  27.7 1.8 %shard_map.78 = bf16[16,8,8,128]{3,2,1,0:T(8,128)(2,1)} custom-call(s32[16]{0:T(128)} %hold_ref.1, bf16[16,6,8,128]{3,2,1,0:T(8,128)(2,1)} %all_to_all.10.h_ref), custom_call_target="tpu_custom_call" | custom-call | tf_op jit(solution)/shard_map/pallas_call | solution.py:412
  29.5 5.6 %all-to-all-start.1 = ((bf16[16,8,8,128]{3,2,1,0:T(8,128)(2,1)}), bf16[16,8,8,128]{3,2,1,0:T(8,128)(2,1)S(1)}, u32[]{:S(2)}, u32[]{:S(2)}) async-start(bf16[16,8,8,128]{3,2,1,0:T(8,128)(2,1)} %shard_map.78), calls=%async_computation.1 | async-start | bytes 524288 | tf_op jit(solution)/shard_map/all_to_all | solution.py:436
  35.1 2.1 %collective-permute-start.2 = (f32[8,128]{1,0:T(8,128)S(1)}, f32[8,128]{1,0:T(8,128)S(1)}, u32[]{:S(2)}, u32[]{:S(2)}) collective-permute-start(f32[8,128]{1,0:T(8,128)S(1)} %copy-done.16), channel_id=1, source_target_pairs={{0,1},{1,2},{2,3},{3,4},{4,5},{5,6},{6,7},{7,8},{8,9},{9,10},{10,1... | collective-permute-start | bytes 12296 | tf_op jit(solution)/shard_map/ppermute | solution.py:373
  37.2 5.9 %collective-permute-start.3 = (f32[8,128]{1,0:T(8,128)S(1)}, f32[8,128]{1,0:T(8,128)S(1)}, u32[]{:S(2)}, u32[]{:S(2)}) collective-permute-start(f32[8,128]{1,0:T(8,128)S(1)} %copy-done.15), channel_id=1, source_target_pairs={{1,0},{2,1},{3,2},{4,3},{5,4},{6,5},{7,6},{8,7},{9,8},{10,9},{11,1... | collective-permute-start | bytes 12296 | tf_op jit(solution)/shard_map/ppermute | solution.py:373
  43.1 0.0 all-to-all-done.1.r_ref
  43.1 0.0 copy-start.2
  43.2 0.1 reshape.58
  43.3 0.1 copy.30
  43.4 0.1 copy.31
  43.5 0.1 reshape.59
  43.6 0.7 reshape.60.sc_ref
  44.3 0.0 collective-permute-done.2.cym.refs_8_.refs_13_
  44.3 0.2 collective-permute-done.3.cyp.refs_9_.refs_14_
  44.4 0.4 copy-done.6
  44.8 0.2 copy-done.7
  45.0 2.9 %shard_map.79 = (f32[2,32,8,128]{3,2,1,0:T(8,128)}, f32[64,128]{1,0:T(8,128)}, f32[64,128]{1,0:T(8,128)}, f32[8,128]{1,0:T(8,128)}, f32[8,128]{1,0:T(8,128)}, /*...) custom-call(f32[320]{0:T(512)} %reshape.60.sc_ref, ...), custom_call_target="tpu_custom_call" | custom-call | tf_op jit(solution)/shard_map/pallas_call | solution.py:286
  47.9 2.8 %collective-permute-start.4 = (f32[64,128]{1,0:T(8,128)}, f32[64,128]{1,0:T(8,128)S(1)}, u32[]{:S(2)}, u32[]{:S(2)}) collective-permute-start(f32[64,128]{1,0:T(8,128)} %get-tuple-element.28), channel_id=1, source_target_pairs={{0,16},{16,32},{32,48},{48,64},{64,80},{80,96},{96,112},{112,128},... | collective-permute-start | bytes 98312 | tf_op jit(solution)/shard_map/ppermute | solution.py:373
  50.8 5.1 %collective-permute-start.5 = (f32[64,128]{1,0:T(8,128)}, f32[64,128]{1,0:T(8,128)S(1)}, u32[]{:S(2)}, u32[]{:S(2)}) collective-permute-start(f32[64,128]{1,0:T(8,128)} %get-tuple-element.29), channel_id=1, source_target_pairs={{16,0},{32,16},{48,32},{64,48},{80,64},{96,80},{112,96},{128,112},... | collective-permute-start | bytes 98312 | tf_op jit(solution)/shard_map/ppermute | solution.py:373
  55.9 3.5 %collective-permute-start.6 = (f32[8,128]{1,0:T(8,128)}, f32[8,128]{1,0:T(8,128)S(1)}, u32[]{:S(2)}, u32[]{:S(2)}) collective-permute-start(f32[8,128]{1,0:T(8,128)} %get-tuple-element.30), channel_id=1, source_target_pairs={{0,1},{1,2},{2,3},{3,4},{4,5},{5,6},{6,7},{7,8},{8,9},{9,10},{10,1... | collective-permute-start | bytes 12296 | tf_op jit(solution)/shard_map/ppermute | solution.py:373
  59.4 4.5 %collective-permute-start.7 = (f32[8,128]{1,0:T(8,128)S(1)}, f32[8,128]{1,0:T(8,128)S(1)}, u32[]{:S(2)}, u32[]{:S(2)}) collective-permute-start(f32[8,128]{1,0:T(8,128)S(1)} %copy-done.17), channel_id=1, source_target_pairs={{1,0},{2,1},{3,2},{4,3},{5,4},{6,5},{7,6},{8,7},{9,8},{10,9},{11,1... | collective-permute-start | bytes 12296 | tf_op jit(solution)/shard_map/ppermute | solution.py:373
  63.9 1.3 %collective-permute-done.7.refs_4_ = f32[8,128]{1,0:T(8,128)S(1)} collective-permute-done((f32[8,128]{1,0:T(8,128)S(1)}, f32[8,128]{1,0:T(8,128)S(1)}, u32[]{:S(2)}, u32[]{:S(2)}) %collective-permute-start.7) | collective-permute-done | bytes 4128 | tf_op jit(solution)/shard_map/ppermute | solution.py:373
  65.2 0.0 collective-permute-done.4.refs_1_
  65.2 0.0 collective-permute-done.5.refs_2_
  65.2 0.6 copy-done.11
  65.8 0.0 copy-done.4
  65.8 3.3 %shard_map.81 = (f32[2,32,8,128]{3,2,1,0:T(8,128)}, f32[64,128]{1,0:T(8,128)}, f32[64,128]{1,0:T(8,128)}, f32[8,128]{1,0:T(8,128)}, f32[8,128]{1,0:T(8,128)}) custom-call(f32[2,32,8,128]{3,2,1,0:T(8,128)} %get-tuple-element.27.refs_0_, f32[64,128]{1,0:T(8,128)} %copy-done.4, f32[64,128]{1,0:T(8,128)} %copy-done.5, f32[8,128]{1,0:T(8,128)} %copy-done.10, ...), custom_call_target="tpu_custom_call" | custom-call | tf_op jit(solution)/shard_map/pallas_call | solution.py:357
  69.1 1.9 %collective-permute-start.8 = (f32[64,128]{1,0:T(8,128)}, f32[64,128]{1,0:T(8,128)S(1)}, u32[]{:S(2)}, u32[]{:S(2)}) collective-permute-start(f32[64,128]{1,0:T(8,128)} %get-tuple-element.38), channel_id=1, source_target_pairs={{0,16},{16,32},{32,48},{48,64},{64,80},{80,96},{96,112},{112,128},... | collective-permute-start | bytes 98312 | tf_op jit(solution)/shard_map/ppermute | solution.py:373
  71.0 6.0 %collective-permute-start.9 = (f32[64,128]{1,0:T(8,128)}, f32[64,128]{1,0:T(8,128)S(1)}, u32[]{:S(2)}, u32[]{:S(2)}) collective-permute-start(f32[64,128]{1,0:T(8,128)} %get-tuple-element.39), channel_id=1, source_target_pairs={{16,0},{32,16},{48,32},{64,48},{80,64},{96,80},{112,96},{128,112},... | collective-permute-start | bytes 98312 | tf_op jit(solution)/shard_map/ppermute | solution.py:373
  77.1 2.9 %collective-permute-start.10 = (f32[8,128]{1,0:T(8,128)}, f32[8,128]{1,0:T(8,128)S(1)}, u32[]{:S(2)}, u32[]{:S(2)}) collective-permute-start(f32[8,128]{1,0:T(8,128)} %get-tuple-element.40), channel_id=1, source_target_pairs={{0,1},{1,2},{2,3},{3,4},{4,5},{5,6},{6,7},{7,8},{8,9},{9,10},{10,1... | collective-permute-start | bytes 12296 | tf_op jit(solution)/shard_map/ppermute | solution.py:373
  79.9 5.1 %collective-permute-start.11 = (f32[8,128]{1,0:T(8,128)S(1)}, f32[8,128]{1,0:T(8,128)S(1)}, u32[]{:S(2)}, u32[]{:S(2)}) collective-permute-start(f32[8,128]{1,0:T(8,128)S(1)} %copy-done.18), channel_id=1, source_target_pairs={{1,0},{2,1},{3,2},{4,3},{5,4},{6,5},{7,6},{8,7},{9,8},{10,9},{11,1... | collective-permute-start | bytes 12296 | tf_op jit(solution)/shard_map/ppermute | solution.py:373
  85.1 2.5 %shard_map.80 = f32[2,32,8,128]{3,2,1,0:T(8,128)} custom-call(f32[2,32,8,128]{3,2,1,0:T(8,128)} %get-tuple-element.27.refs_0_, f32[64,128]{1,0:T(8,128)} %copy-done.4, f32[64,128]{1,0:T(8,128)} %copy-done.5, f32[8,128]{1,0:T(8,128)} %copy-done.10, f32[8,128]{1,0:T(8,128)} %copy-done.11, f32[4,8,128]{2,1,0:T(8,128)} %get-tuple-element.24.c_ref.refs_5_.refs_10_, ...), custom_call_target="tpu_custom_call" | custom-call | tf_op jit(solution)/shard_map/pallas_call | solution.py:320
  87.6 0.0 collective-permute-done.9.refs_7_
  87.7 0.5 copy-done.12
  88.2 0.0 copy-done.13
  88.2 0.0 copy-done.8
  88.2 0.0 copy-done.9
  88.3 3.1 %shard_map.82 = f32[2,32,8,128]{3,2,1,0:T(8,128)} custom-call(f32[2,32,8,128]{3,2,1,0:T(8,128)} %get-tuple-element.32.refs_0_, f32[64,128]{1,0:T(8,128)} %get-tuple-element.33.refs_1_, f32[64,128]{1,0:T(8,128)} %get-tuple-element.34.refs_2_, f32[8,128]{1,0:T(8,128)} %get-tuple-element.35.refs_3_, f32[8,128]{1,0:T(8,128)} %get-tuple-element.36.refs_4_, ...), custom_call_target="tpu_custom_call" | custom-call | tf_op jit(solution)/shard_map/pallas_call | solution.py:357
  (44 shorter events, 0.2 us)
Async XLA Ops:
  2.6 8.1 %copy-start.14 = (bf16[2,32,1,1]{1,0,3,2:T(2,128)(2,1)S(1)}, bf16[2,32,1,1]{1,0,3,2:T(2,128)(2,1)}, u32[]{:S(2)}) copy-start(bf16[2,32,1,1]{1,0,3,2:T(2,128)(2,1)} %param.7) | copy-start | bytes 388
  2.6 8.8 %collective-permute-start = (f32[136,128]{1,0:T(8,128)}, f32[136,128]{1,0:T(8,128)S(1)}, u32[]{:S(2)}, u32[]{:S(2)}) collective-permute-start(f32[136,128]{1,0:T(8,128)} %get-tuple-element.22), channel_id=1, source_target_pairs={{0,16},{16,32},{32,48},{48,64},{64,80},{80,96},{96,112},{112,128},... | collective-permute-start | bytes 208904 | tf_op jit(solution)/shard_map/ppermute | solution.py:373
  6.2 6.7 %collective-permute-start.1 = (f32[136,128]{1,0:T(8,128)}, f32[136,128]{1,0:T(8,128)S(1)}, u32[]{:S(2)}, u32[]{:S(2)}) collective-permute-start(f32[136,128]{1,0:T(8,128)} %get-tuple-element.23), channel_id=1, source_target_pairs={{16,0},{32,16},{48,32},{64,48},{80,64},{96,80},{112,96},{128,112},... | collective-permute-start | bytes 208904 | tf_op jit(solution)/shard_map/ppermute | solution.py:373
  11.3 1.6 %copy-start = (f32[136,128]{1,0:T(8,128)}, f32[136,128]{1,0:T(8,128)S(1)}, u32[]{:S(2)}) copy-start(f32[136,128]{1,0:T(8,128)S(1)} %collective-permute-done.cxm.refs_6_.refs_11_) | copy-start | bytes 208900
  11.4 2.3 %copy-start.3 = (bf16[2,32,8,128]{3,2,1,0:T(8,128)(2,1)S(1)}, bf16[2,32,8,128]{3,2,1,0:T(8,128)(2,1)}, u32[]{:S(2)}) copy-start(bf16[2,32,8,128]{3,2,1,0:T(8,128)(2,1)} %slab_ref.1) | copy-start | bytes 393220
  12.9 0.6 copy-start.1
  29.5 5.6 %copy-start.16 = (f32[8,128]{1,0:T(8,128)S(1)}, f32[8,128]{1,0:T(8,128)}, u32[]{:S(2)}) copy-start(f32[8,128]{1,0:T(8,128)} %get-tuple-element.25) | copy-start | bytes 12292
  29.5 7.6 %copy-start.15 = (f32[8,128]{1,0:T(8,128)S(1)}, f32[8,128]{1,0:T(8,128)}, u32[]{:S(2)}) copy-start(f32[8,128]{1,0:T(8,128)} %get-tuple-element.26) | copy-start | bytes 12292
  29.5 13.6 %all-to-all-start.1 = ((bf16[16,8,8,128]{3,2,1,0:T(8,128)(2,1)}), bf16[16,8,8,128]{3,2,1,0:T(8,128)(2,1)S(1)}, u32[]{:S(2)}, u32[]{:S(2)}) async-start(bf16[16,8,8,128]{3,2,1,0:T(8,128)(2,1)} %shard_map.78), calls=%async_computation.1 | async-start | bytes 524288 | tf_op jit(solution)/shard_map/all_to_all | solution.py:436
  35.1 9.1 %collective-permute-start.2 = (f32[8,128]{1,0:T(8,128)S(1)}, f32[8,128]{1,0:T(8,128)S(1)}, u32[]{:S(2)}, u32[]{:S(2)}) collective-permute-start(f32[8,128]{1,0:T(8,128)S(1)} %copy-done.16), channel_id=1, source_target_pairs={{0,1},{1,2},{2,3},{3,4},{4,5},{5,6},{6,7},{7,8},{8,9},{9,10},{10,1... | collective-permute-start | bytes 12296 | tf_op jit(solution)/shard_map/ppermute | solution.py:373
  37.2 7.2 %collective-permute-start.3 = (f32[8,128]{1,0:T(8,128)S(1)}, f32[8,128]{1,0:T(8,128)S(1)}, u32[]{:S(2)}, u32[]{:S(2)}) collective-permute-start(f32[8,128]{1,0:T(8,128)S(1)} %copy-done.15), channel_id=1, source_target_pairs={{1,0},{2,1},{3,2},{4,3},{5,4},{6,5},{7,6},{8,7},{9,8},{10,9},{11,1... | collective-permute-start | bytes 12296 | tf_op jit(solution)/shard_map/ppermute | solution.py:373
  43.1 1.3 %copy-start.2 = (bf16[16,8,8,128]{3,2,1,0:T(8,128)(2,1)}, bf16[16,8,8,128]{3,2,1,0:T(8,128)(2,1)S(1)}, u32[]{:S(2)}) copy-start(bf16[16,8,8,128]{3,2,1,0:T(8,128)(2,1)S(1)} %all-to-all-done.1.r_ref) | copy-start | bytes 786436
  44.3 0.6 copy-start.6
  44.4 0.6 copy-start.7
  47.9 11.5 %copy-start.17 = (f32[8,128]{1,0:T(8,128)S(1)}, f32[8,128]{1,0:T(8,128)}, u32[]{:S(2)}) copy-start(f32[8,128]{1,0:T(8,128)} %get-tuple-element.31) | copy-start | bytes 12292
  47.9 17.3 %collective-permute-start.4 = (f32[64,128]{1,0:T(8,128)}, f32[64,128]{1,0:T(8,128)S(1)}, u32[]{:S(2)}, u32[]{:S(2)}) collective-permute-start(f32[64,128]{1,0:T(8,128)} %get-tuple-element.28), channel_id=1, source_target_pairs={{0,16},{16,32},{32,48},{48,64},{64,80},{80,96},{96,112},{112,128},... | collective-permute-start | bytes 98312 | tf_op jit(solution)/shard_map/ppermute | solution.py:373
  50.8 14.5 %collective-permute-start.5 = (f32[64,128]{1,0:T(8,128)}, f32[64,128]{1,0:T(8,128)S(1)}, u32[]{:S(2)}, u32[]{:S(2)}) collective-permute-start(f32[64,128]{1,0:T(8,128)} %get-tuple-element.29), channel_id=1, source_target_pairs={{16,0},{32,16},{48,32},{64,48},{80,64},{96,80},{112,96},{128,112},... | collective-permute-start | bytes 98312 | tf_op jit(solution)/shard_map/ppermute | solution.py:373
  55.9 8.0 %collective-permute-start.6 = (f32[8,128]{1,0:T(8,128)}, f32[8,128]{1,0:T(8,128)S(1)}, u32[]{:S(2)}, u32[]{:S(2)}) collective-permute-start(f32[8,128]{1,0:T(8,128)} %get-tuple-element.30), channel_id=1, source_target_pairs={{0,1},{1,2},{2,3},{3,4},{4,5},{5,6},{6,7},{7,8},{8,9},{9,10},{10,1... | collective-permute-start | bytes 12296 | tf_op jit(solution)/shard_map/ppermute | solution.py:373
  59.4 5.8 %collective-permute-start.7 = (f32[8,128]{1,0:T(8,128)S(1)}, f32[8,128]{1,0:T(8,128)S(1)}, u32[]{:S(2)}, u32[]{:S(2)}) collective-permute-start(f32[8,128]{1,0:T(8,128)S(1)} %copy-done.17), channel_id=1, source_target_pairs={{1,0},{2,1},{3,2},{4,3},{5,4},{6,5},{7,6},{8,7},{9,8},{10,9},{11,1... | collective-permute-start | bytes 12296 | tf_op jit(solution)/shard_map/ppermute | solution.py:373
  63.9 1.3 %copy-start.10 = (f32[8,128]{1,0:T(8,128)}, f32[8,128]{1,0:T(8,128)S(1)}, u32[]{:S(2)}) copy-start(f32[8,128]{1,0:T(8,128)S(1)} %collective-permute-done.6.refs_3_) | copy-start | bytes 12292
  65.2 0.6 copy-start.11
  65.2 0.6 copy-start.4
  65.2 0.6 copy-start.5
  69.1 10.8 %copy-start.18 = (f32[8,128]{1,0:T(8,128)S(1)}, f32[8,128]{1,0:T(8,128)}, u32[]{:S(2)}) copy-start(f32[8,128]{1,0:T(8,128)} %get-tuple-element.41) | copy-start | bytes 12292
  69.1 18.5 %collective-permute-start.8 = (f32[64,128]{1,0:T(8,128)}, f32[64,128]{1,0:T(8,128)S(1)}, u32[]{:S(2)}, u32[]{:S(2)}) collective-permute-start(f32[64,128]{1,0:T(8,128)} %get-tuple-element.38), channel_id=1, source_target_pairs={{0,16},{16,32},{32,48},{48,64},{64,80},{80,96},{96,112},{112,128},... | collective-permute-start | bytes 98312 | tf_op jit(solution)/shard_map/ppermute | solution.py:373
  71.0 16.6 %collective-permute-start.9 = (f32[64,128]{1,0:T(8,128)}, f32[64,128]{1,0:T(8,128)S(1)}, u32[]{:S(2)}, u32[]{:S(2)}) collective-permute-start(f32[64,128]{1,0:T(8,128)} %get-tuple-element.39), channel_id=1, source_target_pairs={{16,0},{32,16},{48,32},{64,48},{80,64},{96,80},{112,96},{128,112},... | collective-permute-start | bytes 98312 | tf_op jit(solution)/shard_map/ppermute | solution.py:373
  77.1 10.5 %collective-permute-start.10 = (f32[8,128]{1,0:T(8,128)}, f32[8,128]{1,0:T(8,128)S(1)}, u32[]{:S(2)}, u32[]{:S(2)}) collective-permute-start(f32[8,128]{1,0:T(8,128)} %get-tuple-element.40), channel_id=1, source_target_pairs={{0,1},{1,2},{2,3},{3,4},{4,5},{5,6},{6,7},{7,8},{8,9},{9,10},{10,1... | collective-permute-start | bytes 12296 | tf_op jit(solution)/shard_map/ppermute | solution.py:373
  79.9 7.6 %collective-permute-start.11 = (f32[8,128]{1,0:T(8,128)S(1)}, f32[8,128]{1,0:T(8,128)S(1)}, u32[]{:S(2)}, u32[]{:S(2)}) collective-permute-start(f32[8,128]{1,0:T(8,128)S(1)} %copy-done.18), channel_id=1, source_target_pairs={{1,0},{2,1},{3,2},{4,3},{5,4},{6,5},{7,6},{8,7},{9,8},{10,9},{11,1... | collective-permute-start | bytes 12296 | tf_op jit(solution)/shard_map/ppermute | solution.py:373
  87.6 0.6 copy-start.12
  87.6 0.6 copy-start.13
  87.6 0.6 copy-start.8
  87.6 0.6 copy-start.9

commit v12 on v11

--- a/solution.py
+++ b/solution.py
@@ -251,13 +251,18 @@
     yp = jnp.zeros((x, y), F32)
     for k in range(nplanes):
         p, i = k // per, k % per
-        s_ref[k // nz, k % nz] = r_ref[p, i].astype(F32) * sc_ref[k]
+        sp = r_ref[p, per + 1].astype(F32)
+        sq = r_ref[p, per + 3].astype(F32)
+        own = jnp.broadcast_to(sp[0:1, i : i + 1], (x, y))
+        s_ref[k // nz, k % nz] = r_ref[p, i].astype(F32) * own
         hx = r_ref[p, per].astype(F32)
-        xm_ref[k : k + 1, :] = hx[i : i + 1, :] * sc_ref[nplanes + k]
-        xp_ref[k : k + 1, :] = hx[per + i : per + i + 1, :] * sc_ref[2 * nplanes + k]
+        xm_ref[k : k + 1, :] = hx[i : i + 1, :] * jnp.broadcast_to(sp[1:2, i : i + 1], (1, y))
+        xp_ref[k : k + 1, :] = hx[per + i : per + i + 1, :] * jnp.broadcast_to(sp[2:3, i : i + 1], (1, y))
         hy = r_ref[p, per + 2].astype(F32)
-        ym = jnp.where(lane == k, _roll(hy, k - i, 1) * sc_ref[3 * nplanes + k], ym)
-        yp = jnp.where(lane == k, _roll(hy, k - (per + i), 1) * sc_ref[4 * nplanes + k], yp)
+        sm = jnp.broadcast_to(sq[0:1, i : i + 1], (x, y))
+        spp = jnp.broadcast_to(sq[0:1, per + i : per + i + 1], (x, y))
+        ym = jnp.where(lane == k, _roll(hy, k - i, 1) * sm, ym)
+        yp = jnp.where(lane == k, _roll(hy, k - (per + i), 1) * spp, yp)
     ym_ref[...] = ym
     yp_ref[...] = yp
 
@@ -267,13 +272,13 @@
     nplanes = npiece * per
     nz = nplanes // nf
 
-    def kernel(sc_ref, r_ref, c_ref, cxm, cxp, cym, cyp, *refs):
+    def kernel(r_ref, c_ref, cxm, cxp, cym, cyp, *refs):
         s0_ref, xm_ref, xp_ref, ym_ref, yp_ref = refs[:5]
         s1_ref, xf_ref, xl_ref, yf_ref, yl_ref = refs[5:10]
         scratch = refs[10:]
         sh_all = scratch[0:4]
         cs = scratch[4]
-        _state0_body(sc_ref, r_ref, s0_ref, xm_ref, xp_ref, ym_ref, yp_ref, per)
+        _state0_body(None, r_ref, s0_ref, xm_ref, xp_ref, ym_ref, yp_ref, per)
         _expand_halo(xm_ref, xp_ref, ym_ref, yp_ref, 0, nf, nz, sh_all)
         _coef_table(c_ref, cxm, cxp, cym, cyp, c_first, cs)
         masks = _iotas((x, y))
@@ -286,9 +291,9 @@
     return pl.pallas_call(
         kernel,
         out_shape=(state,) + _edge_shapes(nplanes, x, y) + (state,) + _edge_shapes(_rows(nplanes), x, y),
-        in_specs=[pl.BlockSpec(memory_space=SMEM)] + [pl.BlockSpec(memory_space=VMEM)] * 6,
+        in_specs=[pl.BlockSpec(memory_space=VMEM)] * 6,
         scratch_shapes=_halo_scratch(nf, nz, x, y) + [pltpu.VMEM((5 * NCOEF, x, y), F32)],
-    )(scales, pieces, coef, *c_halo)
+    )(pieces, coef, *c_halo)
 
 
 def step_call(s, s_halo, coef, c_halo, c_first, with_edges):

time: 92.4 us -> 92.4 us (level)
  waiting for transfers between devices: 3.54 us -> 4.68 us
  local copies, waits for them, and re-layouts: 3.72 us -> 2.75 us
    ppermute x12, waiting for transfers between devices: 3.54 us -> 4.67 us  [_shift(): return lax.ppermute(v, axis, pairs)]
  transfers between devices with their start and end apart: 13 -> 13, of which waited for: 4 -> 4; matrix products, arithmetic and copies ran while one was open for 1% -> 0% of each run, Pallas kernels for 3% -> 3%
where the time goes in v12:
time: 92.4 us; the launch traced here: 91.5 us
  starting transfers between devices  53.4 us (58%)
  Pallas kernels  15.6 us (17%)
  blocking collectives  14 us (15%)
  waiting for transfers between devices  4.68 us (5%)
  local copies, waits for them, and re-layouts  2.75 us (3%)
  between operations  0.95 us (1%)
    ppermute x12, starting transfers between devices, _shift(): return lax.ppermute(v, axis, pairs)  47.9 us
    all_to_all x1, blocking collectives, route_blocks(): lax.all_to_all(jnp.concatenate([slab, halo, sc], axis=1), 'gy', 0, 0, til...  14 us
    pallas_call x2, Pallas kernels, adjoint_call(): pl.pallas_call(kernel, out_shape=out_shape, scratch_shapes=_halo_scratch(...  6.4 us
    all_to_all x1, starting transfers between devices, route_blocks(): return lax.all_to_all(forward, 'gy', 0, 0, tiled=True)  5.56 us
    ppermute x12, waiting for transfers between devices, _shift(): return lax.ppermute(v, axis, pairs)  4.67 us
    pallas_call x1, Pallas kernels, state0_step_call(): pl.pallas_call(kernel, out_shape=(state,) + _edge_shapes(nplanes, x, y) +...  2.89 us
    pallas_call x1, Pallas kernels, step_call(): pl.pallas_call(kernel, out_shape=out_shape, scratch_shapes=_halo_scratch(...  2.52 us
    unnamed x38, local copies, waits for them, and re-layouts  2.41 us
  transfers between devices with their start and end apart: 13, of which 4 were waited for; matrix products, arithmetic and copies ran while one was open for 0% of the time, Pallas kernels for 3%

profile of v12, /device:TPU:130, one launch (start us, length us, event | category | flops | bytes accessed | tf_op | source)
XLA Modules:
  0.0 91.5 jit_solution(17729843006361315776)
XLA Ops:
  0.6 2.0 %shard_map.77 = (f32[4,8,128]{2,1,0:T(8,128)}, f32[136,128]{1,0:T(8,128)}, f32[136,128]{1,0:T(8,128)}, f32[8,128]{1,0:T(8,128)}, f32[8,128]{1,0:T(8,128)}) custom-call(s32[8,128]{1,0:T(8,128)} %cls_ref.1, f32[4,12]{1,0:T(4,128)} %bitcast.14, bf16[2,32]{1,0:T(2,128)(2,1)} %bitcast.15, f32[2,32,8,128]{3,2,1,0:T(8,128)} %refs_5_.1, bf16[2,32,8,128]{3,2,1,0:T(8,128)(2,1)} %slab_ref.1), custom_call_target="tpu_custom_call" | custom-call | tf_op jit(solution)/shard_map/pallas_call | solution.py:231
  2.6 3.6 %collective-permute-start = (f32[136,128]{1,0:T(8,128)}, f32[136,128]{1,0:T(8,128)S(1)}, u32[]{:S(2)}, u32[]{:S(2)}) collective-permute-start(f32[136,128]{1,0:T(8,128)} %get-tuple-element.22), channel_id=1, source_target_pairs={{0,16},{16,32},{32,48},{48,64},{64,80},{80,96},{96,112},{112,128},... | collective-permute-start | bytes 208904 | tf_op jit(solution)/shard_map/ppermute | solution.py:378
  6.2 4.5 %collective-permute-start.1 = (f32[136,128]{1,0:T(8,128)}, f32[136,128]{1,0:T(8,128)S(1)}, u32[]{:S(2)}, u32[]{:S(2)}) collective-permute-start(f32[136,128]{1,0:T(8,128)} %get-tuple-element.23), channel_id=1, source_target_pairs={{16,0},{32,16},{48,32},{64,48},{80,64},{96,80},{112,96},{128,112},... | collective-permute-start | bytes 208904 | tf_op jit(solution)/shard_map/ppermute | solution.py:378
  10.7 0.1 reshape.48
  10.8 0.6 collective-permute-done.cxm.refs_6_.refs_11_
  11.4 1.5 %collective-permute-done.1.cxp.refs_7_.refs_12_ = f32[136,128]{1,0:T(8,128)S(1)} collective-permute-done((f32[136,128]{1,0:T(8,128)}, f32[136,128]{1,0:T(8,128)S(1)}, u32[]{:S(2)}, u32[]{:S(2)}) %collective-permute-start.1) | collective-permute-done | bytes 69664 | tf_op jit(solution)/shard_map/ppermute | solution.py:378
  13.0 0.1 convert_element_type.28
  13.1 0.5 copy-done.1
  13.5 0.1 convert_element_type.29
  13.7 0.1 fusion.9
  13.8 14.0 %all_to_all.10.h_ref = bf16[16,6,8,128]{3,2,1,0:T(8,128)(2,1)} all-to-all(bf16[16,6,8,128]{3,2,1,0:T(8,128)(2,1)S(1)} %pad_maximum_fusion), channel_id=1, replica_groups=mesh['gx'=16,'gy'=16] {'gy'}, dimensions={0} | all-to-all | bytes 393216 | tf_op jit(solution)/shard_map/all_to_all | solution.py:438
  27.7 1.8 %shard_map.78 = bf16[16,8,8,128]{3,2,1,0:T(8,128)(2,1)} custom-call(s32[16]{0:T(128)} %hold_ref.1, bf16[16,6,8,128]{3,2,1,0:T(8,128)(2,1)} %all_to_all.10.h_ref), custom_call_target="tpu_custom_call" | custom-call | tf_op jit(solution)/shard_map/pallas_call | solution.py:417
  29.5 5.6 %all-to-all-start.1 = ((bf16[16,8,8,128]{3,2,1,0:T(8,128)(2,1)}), bf16[16,8,8,128]{3,2,1,0:T(8,128)(2,1)S(1)}, u32[]{:S(2)}, u32[]{:S(2)}) async-start(bf16[16,8,8,128]{3,2,1,0:T(8,128)(2,1)} %shard_map.78), calls=%async_computation.1 | async-start | bytes 524288 | tf_op jit(solution)/shard_map/all_to_all | solution.py:441
  35.1 0.0 copy-done.16
  35.1 2.1 %collective-permute-start.2 = (f32[8,128]{1,0:T(8,128)S(1)}, f32[8,128]{1,0:T(8,128)S(1)}, u32[]{:S(2)}, u32[]{:S(2)}) collective-permute-start(f32[8,128]{1,0:T(8,128)S(1)} %copy-done.16), channel_id=1, source_target_pairs={{0,1},{1,2},{2,3},{3,4},{4,5},{5,6},{6,7},{7,8},{8,9},{9,10},{10,1... | collective-permute-start | bytes 12296 | tf_op jit(solution)/shard_map/ppermute | solution.py:378
  37.2 5.9 %collective-permute-start.3 = (f32[8,128]{1,0:T(8,128)S(1)}, f32[8,128]{1,0:T(8,128)S(1)}, u32[]{:S(2)}, u32[]{:S(2)}) collective-permute-start(f32[8,128]{1,0:T(8,128)S(1)} %copy-done.15), channel_id=1, source_target_pairs={{1,0},{2,1},{3,2},{4,3},{5,4},{6,5},{7,6},{8,7},{9,8},{10,9},{11,1... | collective-permute-start | bytes 12296 | tf_op jit(solution)/shard_map/ppermute | solution.py:378
  43.1 0.0 collective-permute-done.2.cym.refs_8_.refs_13_
  43.1 1.3 %collective-permute-done.3.cyp.refs_9_.refs_14_ = f32[8,128]{1,0:T(8,128)S(1)} collective-permute-done((f32[8,128]{1,0:T(8,128)S(1)}, f32[8,128]{1,0:T(8,128)S(1)}, u32[]{:S(2)}, u32[]{:S(2)}) %collective-permute-start.3) | collective-permute-done | bytes 4128 | tf_op jit(solution)/shard_map/ppermute | solution.py:378
  44.4 0.0 all-to-all-done.1.r_ref
  44.4 0.6 copy-done.7
  45.0 0.1 copy-done.2
  45.1 2.9 %shard_map.79 = (f32[2,32,8,128]{3,2,1,0:T(8,128)}, f32[64,128]{1,0:T(8,128)}, f32[64,128]{1,0:T(8,128)}, f32[8,128]{1,0:T(8,128)}, f32[8,128]{1,0:T(8,128)}, /*...) custom-call(bf16[16,8,8,128]{3,2,1,0:T(8,128)(2,1)} %copy-done.2, ...), custom_call_target="tpu_custom_call" | custom-call | tf_op jit(solution)/shard_map/pallas_call | solution.py:291
  48.0 2.8 %collective-permute-start.4 = (f32[64,128]{1,0:T(8,128)}, f32[64,128]{1,0:T(8,128)S(1)}, u32[]{:S(2)}, u32[]{:S(2)}) collective-permute-start(f32[64,128]{1,0:T(8,128)} %get-tuple-element.28), channel_id=1, source_target_pairs={{0,16},{16,32},{32,48},{48,64},{64,80},{80,96},{96,112},{112,128},... | collective-permute-start | bytes 98312 | tf_op jit(solution)/shard_map/ppermute | solution.py:378
  50.8 5.1 %collective-permute-start.5 = (f32[64,128]{1,0:T(8,128)}, f32[64,128]{1,0:T(8,128)S(1)}, u32[]{:S(2)}, u32[]{:S(2)}) collective-permute-start(f32[64,128]{1,0:T(8,128)} %get-tuple-element.29), channel_id=1, source_target_pairs={{16,0},{32,16},{48,32},{64,48},{80,64},{96,80},{112,96},{128,112},... | collective-permute-start | bytes 98312 | tf_op jit(solution)/shard_map/ppermute | solution.py:378
  56.0 3.5 %collective-permute-start.6 = (f32[8,128]{1,0:T(8,128)}, f32[8,128]{1,0:T(8,128)S(1)}, u32[]{:S(2)}, u32[]{:S(2)}) collective-permute-start(f32[8,128]{1,0:T(8,128)} %get-tuple-element.30), channel_id=1, source_target_pairs={{0,1},{1,2},{2,3},{3,4},{4,5},{5,6},{6,7},{7,8},{8,9},{9,10},{10,1... | collective-permute-start | bytes 12296 | tf_op jit(solution)/shard_map/ppermute | solution.py:378
  59.5 4.5 %collective-permute-start.7 = (f32[8,128]{1,0:T(8,128)S(1)}, f32[8,128]{1,0:T(8,128)S(1)}, u32[]{:S(2)}, u32[]{:S(2)}) collective-permute-start(f32[8,128]{1,0:T(8,128)S(1)} %copy-done.17), channel_id=1, source_target_pairs={{1,0},{2,1},{3,2},{4,3},{5,4},{6,5},{7,6},{8,7},{9,8},{10,9},{11,1... | collective-permute-start | bytes 12296 | tf_op jit(solution)/shard_map/ppermute | solution.py:378
  64.0 0.0 collective-permute-done.6.refs_3_
  64.0 1.3 %collective-permute-done.7.refs_4_ = f32[8,128]{1,0:T(8,128)S(1)} collective-permute-done((f32[8,128]{1,0:T(8,128)S(1)}, f32[8,128]{1,0:T(8,128)S(1)}, u32[]{:S(2)}, u32[]{:S(2)}) %collective-permute-start.7) | collective-permute-done | bytes 4128 | tf_op jit(solution)/shard_map/ppermute | solution.py:378
  65.3 0.0 collective-permute-done.4.refs_1_
  65.3 0.0 collective-permute-done.5.refs_2_
  65.3 0.6 copy-done.11
  65.9 0.0 copy-done.4
  65.9 0.0 copy-done.5
  65.9 3.3 %shard_map.81 = (f32[2,32,8,128]{3,2,1,0:T(8,128)}, f32[64,128]{1,0:T(8,128)}, f32[64,128]{1,0:T(8,128)}, f32[8,128]{1,0:T(8,128)}, f32[8,128]{1,0:T(8,128)}) custom-call(f32[2,32,8,128]{3,2,1,0:T(8,128)} %get-tuple-element.27.refs_0_, f32[64,128]{1,0:T(8,128)} %copy-done.4, f32[64,128]{1,0:T(8,128)} %copy-done.5, f32[8,128]{1,0:T(8,128)} %copy-done.10, ...), custom_call_target="tpu_custom_call" | custom-call | tf_op jit(solution)/shard_map/pallas_call | solution.py:362
  69.2 1.9 %collective-permute-start.8 = (f32[64,128]{1,0:T(8,128)}, f32[64,128]{1,0:T(8,128)S(1)}, u32[]{:S(2)}, u32[]{:S(2)}) collective-permute-start(f32[64,128]{1,0:T(8,128)} %get-tuple-element.38), channel_id=1, source_target_pairs={{0,16},{16,32},{32,48},{48,64},{64,80},{80,96},{96,112},{112,128},... | collective-permute-start | bytes 98312 | tf_op jit(solution)/shard_map/ppermute | solution.py:378
  71.1 6.0 %collective-permute-start.9 = (f32[64,128]{1,0:T(8,128)}, f32[64,128]{1,0:T(8,128)S(1)}, u32[]{:S(2)}, u32[]{:S(2)}) collective-permute-start(f32[64,128]{1,0:T(8,128)} %get-tuple-element.39), channel_id=1, source_target_pairs={{16,0},{32,16},{48,32},{64,48},{80,64},{96,80},{112,96},{128,112},... | collective-permute-start | bytes 98312 | tf_op jit(solution)/shard_map/ppermute | solution.py:378
  77.1 2.9 %collective-permute-start.10 = (f32[8,128]{1,0:T(8,128)}, f32[8,128]{1,0:T(8,128)S(1)}, u32[]{:S(2)}, u32[]{:S(2)}) collective-permute-start(f32[8,128]{1,0:T(8,128)} %get-tuple-element.40), channel_id=1, source_target_pairs={{0,1},{1,2},{2,3},{3,4},{4,5},{5,6},{6,7},{7,8},{8,9},{9,10},{10,1... | collective-permute-start | bytes 12296 | tf_op jit(solution)/shard_map/ppermute | solution.py:378
  80.0 5.1 %collective-permute-start.11 = (f32[8,128]{1,0:T(8,128)S(1)}, f32[8,128]{1,0:T(8,128)S(1)}, u32[]{:S(2)}, u32[]{:S(2)}) collective-permute-start(f32[8,128]{1,0:T(8,128)S(1)} %copy-done.18), channel_id=1, source_target_pairs={{1,0},{2,1},{3,2},{4,3},{5,4},{6,5},{7,6},{8,7},{9,8},{10,9},{11,1... | collective-permute-start | bytes 12296 | tf_op jit(solution)/shard_map/ppermute | solution.py:378
  85.1 2.5 %shard_map.80 = f32[2,32,8,128]{3,2,1,0:T(8,128)} custom-call(f32[2,32,8,128]{3,2,1,0:T(8,128)} %get-tuple-element.27.refs_0_, f32[64,128]{1,0:T(8,128)} %copy-done.4, f32[64,128]{1,0:T(8,128)} %copy-done.5, f32[8,128]{1,0:T(8,128)} %copy-done.10, f32[8,128]{1,0:T(8,128)} %copy-done.11, f32[4,8,128]{2,1,0:T(8,128)} %get-tuple-element.24.c_ref.refs_5_.refs_10_, ...), custom_call_target="tpu_custom_call" | custom-call | tf_op jit(solution)/shard_map/pallas_call | solution.py:325
  87.7 0.0 collective-permute-done.10.refs_8_
  87.7 0.0 collective-permute-done.11.refs_9_
  87.7 0.0 collective-permute-done.8.refs_6_
  87.7 0.0 collective-permute-done.9.refs_7_
  87.7 0.5 copy-done.12
  88.3 0.0 copy-done.13
  88.3 0.0 copy-done.8
  88.3 0.0 copy-done.9
  88.3 3.1 %shard_map.82 = f32[2,32,8,128]{3,2,1,0:T(8,128)} custom-call(f32[2,32,8,128]{3,2,1,0:T(8,128)} %get-tuple-element.32.refs_0_, f32[64,128]{1,0:T(8,128)} %get-tuple-element.33.refs_1_, f32[64,128]{1,0:T(8,128)} %get-tuple-element.34.refs_2_, f32[8,128]{1,0:T(8,128)} %get-tuple-element.35.refs_3_, f32[8,128]{1,0:T(8,128)} %get-tuple-element.36.refs_4_, ...), custom_call_target="tpu_custom_call" | custom-call | tf_op jit(solution)/shard_map/pallas_call | solution.py:362
  (35 shorter events, 0.2 us)
Async XLA Ops:
  2.6 8.1 %copy-start.14 = (bf16[2,32,1,1]{1,0,3,2:T(2,128)(2,1)S(1)}, bf16[2,32,1,1]{1,0,3,2:T(2,128)(2,1)}, u32[]{:S(2)}) copy-start(bf16[2,32,1,1]{1,0,3,2:T(2,128)(2,1)} %param.7) | copy-start | bytes 388
  2.6 8.8 %collective-permute-start = (f32[136,128]{1,0:T(8,128)}, f32[136,128]{1,0:T(8,128)S(1)}, u32[]{:S(2)}, u32[]{:S(2)}) collective-permute-start(f32[136,128]{1,0:T(8,128)} %get-tuple-element.22), channel_id=1, source_target_pairs={{0,16},{16,32},{32,48},{48,64},{64,80},{80,96},{96,112},{112,128},... | collective-permute-start | bytes 208904 | tf_op jit(solution)/shard_map/ppermute | solution.py:378
  6.2 6.7 %collective-permute-start.1 = (f32[136,128]{1,0:T(8,128)}, f32[136,128]{1,0:T(8,128)S(1)}, u32[]{:S(2)}, u32[]{:S(2)}) collective-permute-start(f32[136,128]{1,0:T(8,128)} %get-tuple-element.23), channel_id=1, source_target_pairs={{16,0},{32,16},{48,32},{64,48},{80,64},{96,80},{112,96},{128,112},... | collective-permute-start | bytes 208904 | tf_op jit(solution)/shard_map/ppermute | solution.py:378
  11.3 1.6 %copy-start = (f32[136,128]{1,0:T(8,128)}, f32[136,128]{1,0:T(8,128)S(1)}, u32[]{:S(2)}) copy-start(f32[136,128]{1,0:T(8,128)S(1)} %collective-permute-done.cxm.refs_6_.refs_11_) | copy-start | bytes 208900
  11.4 2.3 %copy-start.3 = (bf16[2,32,8,128]{3,2,1,0:T(8,128)(2,1)S(1)}, bf16[2,32,8,128]{3,2,1,0:T(8,128)(2,1)}, u32[]{:S(2)}) copy-start(bf16[2,32,8,128]{3,2,1,0:T(8,128)(2,1)} %slab_ref.1) | copy-start | bytes 393220
  12.9 0.6 copy-start.1
  29.5 5.6 %copy-start.16 = (f32[8,128]{1,0:T(8,128)S(1)}, f32[8,128]{1,0:T(8,128)}, u32[]{:S(2)}) copy-start(f32[8,128]{1,0:T(8,128)} %get-tuple-element.25) | copy-start | bytes 12292
  29.5 7.6 %copy-start.15 = (f32[8,128]{1,0:T(8,128)S(1)}, f32[8,128]{1,0:T(8,128)}, u32[]{:S(2)}) copy-start(f32[8,128]{1,0:T(8,128)} %get-tuple-element.26) | copy-start | bytes 12292
  29.5 14.9 %all-to-all-start.1 = ((bf16[16,8,8,128]{3,2,1,0:T(8,128)(2,1)}), bf16[16,8,8,128]{3,2,1,0:T(8,128)(2,1)S(1)}, u32[]{:S(2)}, u32[]{:S(2)}) async-start(bf16[16,8,8,128]{3,2,1,0:T(8,128)(2,1)} %shard_map.78), calls=%async_computation.1 | async-start | bytes 524288 | tf_op jit(solution)/shard_map/all_to_all | solution.py:441
  35.1 8.0 %collective-permute-start.2 = (f32[8,128]{1,0:T(8,128)S(1)}, f32[8,128]{1,0:T(8,128)S(1)}, u32[]{:S(2)}, u32[]{:S(2)}) collective-permute-start(f32[8,128]{1,0:T(8,128)S(1)} %copy-done.16), channel_id=1, source_target_pairs={{0,1},{1,2},{2,3},{3,4},{4,5},{5,6},{6,7},{7,8},{8,9},{9,10},{10,1... | collective-permute-start | bytes 12296 | tf_op jit(solution)/shard_map/ppermute | solution.py:378
  37.2 7.2 %collective-permute-start.3 = (f32[8,128]{1,0:T(8,128)S(1)}, f32[8,128]{1,0:T(8,128)S(1)}, u32[]{:S(2)}, u32[]{:S(2)}) collective-permute-start(f32[8,128]{1,0:T(8,128)S(1)} %copy-done.15), channel_id=1, source_target_pairs={{1,0},{2,1},{3,2},{4,3},{5,4},{6,5},{7,6},{8,7},{9,8},{10,9},{11,1... | collective-permute-start | bytes 12296 | tf_op jit(solution)/shard_map/ppermute | solution.py:378
  43.1 1.3 %copy-start.6 = (f32[8,128]{1,0:T(8,128)}, f32[8,128]{1,0:T(8,128)S(1)}, u32[]{:S(2)}) copy-start(f32[8,128]{1,0:T(8,128)S(1)} %collective-permute-done.2.cym.refs_8_.refs_13_) | copy-start | bytes 12292
  44.4 0.6 copy-start.7
  44.4 0.7 copy-start.2
  48.0 11.5 %copy-start.17 = (f32[8,128]{1,0:T(8,128)S(1)}, f32[8,128]{1,0:T(8,128)}, u32[]{:S(2)}) copy-start(f32[8,128]{1,0:T(8,128)} %get-tuple-element.31) | copy-start | bytes 12292
  48.0 17.3 %collective-permute-start.4 = (f32[64,128]{1,0:T(8,128)}, f32[64,128]{1,0:T(8,128)S(1)}, u32[]{:S(2)}, u32[]{:S(2)}) collective-permute-start(f32[64,128]{1,0:T(8,128)} %get-tuple-element.28), channel_id=1, source_target_pairs={{0,16},{16,32},{32,48},{48,64},{64,80},{80,96},{96,112},{112,128},... | collective-permute-start | bytes 98312 | tf_op jit(solution)/shard_map/ppermute | solution.py:378
  50.8 14.5 %collective-permute-start.5 = (f32[64,128]{1,0:T(8,128)}, f32[64,128]{1,0:T(8,128)S(1)}, u32[]{:S(2)}, u32[]{:S(2)}) collective-permute-start(f32[64,128]{1,0:T(8,128)} %get-tuple-element.29), channel_id=1, source_target_pairs={{16,0},{32,16},{48,32},{64,48},{80,64},{96,80},{112,96},{128,112},... | collective-permute-start | bytes 98312 | tf_op jit(solution)/shard_map/ppermute | solution.py:378
  56.0 8.0 %collective-permute-start.6 = (f32[8,128]{1,0:T(8,128)}, f32[8,128]{1,0:T(8,128)S(1)}, u32[]{:S(2)}, u32[]{:S(2)}) collective-permute-start(f32[8,128]{1,0:T(8,128)} %get-tuple-element.30), channel_id=1, source_target_pairs={{0,1},{1,2},{2,3},{3,4},{4,5},{5,6},{6,7},{7,8},{8,9},{9,10},{10,1... | collective-permute-start | bytes 12296 | tf_op jit(solution)/shard_map/ppermute | solution.py:378
  59.5 5.8 %collective-permute-start.7 = (f32[8,128]{1,0:T(8,128)S(1)}, f32[8,128]{1,0:T(8,128)S(1)}, u32[]{:S(2)}, u32[]{:S(2)}) collective-permute-start(f32[8,128]{1,0:T(8,128)S(1)} %copy-done.17), channel_id=1, source_target_pairs={{1,0},{2,1},{3,2},{4,3},{5,4},{6,5},{7,6},{8,7},{9,8},{10,9},{11,1... | collective-permute-start | bytes 12296 | tf_op jit(solution)/shard_map/ppermute | solution.py:378
  64.0 1.3 %copy-start.10 = (f32[8,128]{1,0:T(8,128)}, f32[8,128]{1,0:T(8,128)S(1)}, u32[]{:S(2)}) copy-start(f32[8,128]{1,0:T(8,128)S(1)} %collective-permute-done.6.refs_3_) | copy-start | bytes 12292
  65.3 0.6 copy-start.11
  65.3 0.6 copy-start.4
  65.3 0.6 copy-start.5
  69.2 10.8 %copy-start.18 = (f32[8,128]{1,0:T(8,128)S(1)}, f32[8,128]{1,0:T(8,128)}, u32[]{:S(2)}) copy-start(f32[8,128]{1,0:T(8,128)} %get-tuple-element.41) | copy-start | bytes 12292
  69.2 18.5 %collective-permute-start.8 = (f32[64,128]{1,0:T(8,128)}, f32[64,128]{1,0:T(8,128)S(1)}, u32[]{:S(2)}, u32[]{:S(2)}) collective-permute-start(f32[64,128]{1,0:T(8,128)} %get-tuple-element.38), channel_id=1, source_target_pairs={{0,16},{16,32},{32,48},{48,64},{64,80},{80,96},{96,112},{112,128},... | collective-permute-start | bytes 98312 | tf_op jit(solution)/shard_map/ppermute | solution.py:378
  71.1 16.6 %collective-permute-start.9 = (f32[64,128]{1,0:T(8,128)}, f32[64,128]{1,0:T(8,128)S(1)}, u32[]{:S(2)}, u32[]{:S(2)}) collective-permute-start(f32[64,128]{1,0:T(8,128)} %get-tuple-element.39), channel_id=1, source_target_pairs={{16,0},{32,16},{48,32},{64,48},{80,64},{96,80},{112,96},{128,112},... | collective-permute-start | bytes 98312 | tf_op jit(solution)/shard_map/ppermute | solution.py:378
  77.1 10.5 %collective-permute-start.10 = (f32[8,128]{1,0:T(8,128)}, f32[8,128]{1,0:T(8,128)S(1)}, u32[]{:S(2)}, u32[]{:S(2)}) collective-permute-start(f32[8,128]{1,0:T(8,128)} %get-tuple-element.40), channel_id=1, source_target_pairs={{0,1},{1,2},{2,3},{3,4},{4,5},{5,6},{6,7},{7,8},{8,9},{9,10},{10,1... | collective-permute-start | bytes 12296 | tf_op jit(solution)/shard_map/ppermute | solution.py:378
  80.0 7.6 %collective-permute-start.11 = (f32[8,128]{1,0:T(8,128)S(1)}, f32[8,128]{1,0:T(8,128)S(1)}, u32[]{:S(2)}, u32[]{:S(2)}) collective-permute-start(f32[8,128]{1,0:T(8,128)S(1)} %copy-done.18), channel_id=1, source_target_pairs={{1,0},{2,1},{3,2},{4,3},{5,4},{6,5},{7,6},{8,7},{9,8},{10,9},{11,1... | collective-permute-start | bytes 12296 | tf_op jit(solution)/shard_map/ppermute | solution.py:378
  87.7 0.6 copy-start.12
  87.7 0.6 copy-start.13
  87.7 0.6 copy-start.8
  87.7 0.6 copy-start.9
